TPU v7x, 512 devices: a whole 4x8x8 slice. The times are simulated.
512 devices in a mesh: blk: 64 (over y_lo, z, core), tp: 8 (over y_hi, x).
Axes of the slice: x: 4, y: 8 (y_hi: 2, y_lo: 4; y = y_hi * 4 + y_lo), z: 8, core: 2. Of those that a mesh axis runs over, the one named last changes fastest.
Arguments:
- embeds: bfloat16 [8192, 5120], P('blk', 'tp')
- given_embeds: bfloat16 [8192, 5120], P('blk', 'tp')
- accept: int32 [8192], P('blk'), may hold values 0 or 1
- lengths: int32 [64], P('blk'), may hold values from 4 to 4096, as said below
- block_keep: int32 [64, 64], P('blk'), may hold values from 0 to 1
- norm_gain: bfloat16 [5120], replicated, may hold values from 0.25 to 1.75
- w_query: bfloat16 [5120, 5120], P('blk', 'tp'), may hold values from -0.078125 to 0.078125
- b_query: bfloat16 [5120], P('tp'), may hold values from -4 to 4
- w_key: bfloat16 [5120, 1024], P('blk', 'tp'), may hold values from -0.078125 to 0.078125
- b_key: bfloat16 [1024], P('tp'), may hold values from -4 to 4
- w_value: bfloat16 [5120, 1024], P('blk', 'tp'), may hold values from -0.078125 to 0.078125
- b_value: bfloat16 [1024], P('tp'), may hold values from -4 to 4
- cache_keys: bfloat16 [4096, 1024], P('blk', 'tp'), as said below
- cache_values: bfloat16 [4096, 1024], P('blk', 'tp'), may hold values from -6 to 6
Outputs:
- first_pass: bfloat16 [8192, 5120], P('blk', 'tp')
- second_pass: bfloat16 [8192, 5120], P('blk', 'tp')
Inputs may be any that keep to these rules, and one draw needn't show every extreme that they name: `lengths`: every request sees at least the first 4 prompt positions; some request sees all 4096. `cache_keys`: entries lie between -160 and 160.
All inputs are finite; a program needn't handle non-finite values. No bound on the sum of `accept` on one device may be relied on, other than what follows from the above.
Results may differ from a plain program's by a relative error of at most 0.012.
The roundings to bfloat16 on the way count: a program that leaves them out, or rounds other values in their place, can miss the bound.
Values may be sent and summed in bfloat16 or wider, within the bound.
No kernel may reach another device: no remote copies, remote signals or barrier semaphores. Data moves between devices by JAX's collectives and lax.ppermute only.
A program may use at most 64 MiB of HBM per device.

v0:
```python
import math

import jax
import jax.numpy as jnp
from jax import lax
from jax.sharding import PartitionSpec as P

KVH = 8
HD = 128
HQ = 40
CB = 64


def rotate(vectors, positions):
    halfway = HD // 2
    frequency = 1000000.0 ** (-(jnp.arange(halfway, dtype=jnp.float32) * (2.0 / HD)))
    angles = positions[..., None] * frequency
    cosine = jnp.cos(angles)[..., None, :]
    sine_part = jnp.sin(angles)[..., None, :]
    front_part = vectors[..., :halfway]
    back_part = vectors[..., halfway:]
    return jnp.concatenate(
        [front_part * cosine - back_part * sine_part, back_part * cosine + front_part * sine_part],
        axis=-1,
    )


def normalize(rows_in, norm_gain):
    widened = rows_in.astype(jnp.float32)
    inverse = lax.rsqrt(jnp.mean(widened * widened, axis=-1, keepdims=True) + 1e-06)
    return (widened * inverse * norm_gain.astype(jnp.float32)).astype(jnp.bfloat16)


def local(
    embeds,
    given_embeds,
    accept,
    lengths,
    block_keep,
    norm_gain,
    w_query,
    b_query,
    w_key,
    b_key,
    w_value,
    b_value,
    cache_keys,
    cache_values,
):
    grouping = HQ // KVH
    local_kv = w_key.shape[1] // HD
    local_q = local_kv * grouping
    block_rows = embeds.shape[0]
    blocks_all = block_keep.shape[1]
    inv_root = 1.0 / math.sqrt(HD)
    first_rows, given_rows = (
        lax.all_gather(embeds, "tp", axis=1, tiled=True),
        lax.all_gather(given_embeds, "tp", axis=1, tiled=True),
    )
    revised = jnp.where(accept[:, None] == 1, given_rows, first_rows)
    normed = normalize(jnp.concatenate([first_rows, revised], axis=0), norm_gain)
    pieces = (
        lax.all_gather(w_query, "blk", axis=0, tiled=True),
        lax.all_gather(w_key, "blk", axis=0, tiled=True),
        lax.all_gather(w_value, "blk", axis=0, tiled=True),
    )
    queries, key_proj, value_proj = tuple(
        (
            jnp.dot(normed, weight_piece, preferred_element_type=jnp.float32)
            for weight_piece in pieces
        )
    )
    queries = queries + b_query.astype(jnp.float32)
    key_proj = key_proj + b_key.astype(jnp.float32)
    value_proj = value_proj + b_value.astype(jnp.float32)
    length = lengths[0]
    keep_row = block_keep[0]
    positions = length.astype(jnp.float32) + jnp.arange(block_rows, dtype=jnp.float32)
    q_rot = rotate(queries.reshape(2, block_rows, local_q, HD), positions).astype(jnp.bfloat16)
    q_rot = q_rot.reshape(2, block_rows, local_kv, grouping, HD)
    k_rot = rotate(key_proj.reshape(2, block_rows, local_kv, HD), positions).astype(jnp.bfloat16)
    value_rows = value_proj.astype(jnp.bfloat16).reshape(2, block_rows, local_kv, HD)
    own_scores = (
        jnp.einsum("pqkgd,pjkd->pkgqj", q_rot, k_rot, preferred_element_type=jnp.float32) * inv_root
    )
    highest = jnp.max(own_scores, axis=-1)
    own_weights = jnp.exp(own_scores - highest[..., None])
    totals = jnp.sum(own_weights, axis=-1)
    mixture = jnp.einsum(
        "pkgqj,pjkd->pkgqd",
        own_weights.astype(jnp.bfloat16),
        value_rows,
        preferred_element_type=jnp.float32,
    )
    running = (highest, totals, mixture)
    key_piece = lax.all_gather(cache_keys, "blk", axis=0, tiled=True)
    value_piece = lax.all_gather(cache_values, "blk", axis=0, tiled=True)
    piece_rows = key_piece.shape[0]
    sub_rows = math.gcd(piece_rows, CB)
    count = piece_rows // sub_rows
    key_blocks = key_piece.reshape(count, sub_rows, local_kv, HD)
    value_blocks = value_piece.reshape(count, sub_rows, local_kv, HD)
    block_starts = jnp.arange(count, dtype=jnp.int32) * sub_rows

    def visit(running_now, inputs):
        key_rows, value_block, position = inputs
        cache_index = position + jnp.arange(sub_rows, dtype=jnp.int32)
        block_index = cache_index // CB
        matches = block_index[:, None] == jnp.arange(blocks_all, dtype=jnp.int32)[None, :]
        kept = jnp.sum(jnp.where(matches, keep_row[None, :], 0), axis=1)
        visible = (cache_index < length) & (kept == 1)
        best_old, sums_old, mixed_old = running_now
        scores = (
            jnp.einsum("pqkgd,ckd->pkgqc", q_rot, key_rows, preferred_element_type=jnp.float32)
            * inv_root
        )
        scores = jnp.where(visible, scores, -jnp.inf)
        best_new = jnp.maximum(best_old, jnp.max(scores, axis=-1))
        weights = jnp.where(visible, jnp.exp(scores - best_new[..., None]), 0.0)
        factor = jnp.exp(best_old - best_new)
        sums_new = sums_old * factor + jnp.sum(weights, axis=-1)
        mixed_new = mixed_old * factor[..., None] + jnp.einsum(
            "pkgqc,ckd->pkgqd",
            weights.astype(jnp.bfloat16),
            value_block,
            preferred_element_type=jnp.float32,
        )
        return ((best_new, sums_new, mixed_new), None)

    result, ignored = lax.scan(visit, running, (key_blocks, value_blocks, block_starts))
    running = result
    highest, totals, mixture = running
    attended = mixture / totals[..., None]
    attended = (
        jnp.transpose(attended, (0, 3, 1, 2, 4))
        .reshape(2 * block_rows, local_q * HD)
        .astype(jnp.bfloat16)
    )
    return (attended[:block_rows], attended[block_rows:])


def solution(mesh):
    return jax.shard_map(
        local,
        mesh=mesh,
        in_specs=(
            P("blk", "tp"),
            P("blk", "tp"),
            P("blk"),
            P("blk"),
            P("blk", None),
            P(),
            P("blk", "tp"),
            P("tp"),
            P("blk", "tp"),
            P("tp"),
            P("blk", "tp"),
            P("tp"),
            P("blk", "tp"),
            P("blk", "tp"),
        ),
        out_specs=(P("blk", "tp"), P("blk", "tp")),
        check_vma=False,
    )
```

profile of v0, /device:TPU:1, one launch (start us, length us, event | category | flops | bytes accessed | tf_op | source)
XLA Modules:
  0.0 1078.7 jit_solution(2611596930218597881)
XLA Ops:
  16.3 68.1 %all-gather.8.cloned.1.call-done = bf16[128,5120]{1,0:T(8,128)(2,1)} async-done(((bf16[128,640]{1,0:T(8,128)(2,1)}), bf16[128,5120]{1,0:T(8,128)(2,1)}) %all-gather.8.cloned.1.call-update) | async-done | bytes 1310736 | tf_op jit(solution)/shard_map/all_gather | solution.py:57
  84.4 69.6 %all-gather.10.cloned.1.call-done = bf16[128,5120]{1,0:T(8,128)(2,1)} async-done(((bf16[128,640]{1,0:T(8,128)(2,1)}), bf16[128,5120]{1,0:T(8,128)(2,1)}) %all-gather.10.cloned.1.call-update) | async-done | bytes 1310736 | tf_op jit(solution)/shard_map/all_gather | solution.py:58
  154.0 1.9 broadcast_select_fusion
  156.5 115.4 %all-gather.12.cloned.1.call-done = bf16[5120,128]{1,0:T(8,128)(2,1)} async-done(((bf16[80,128]{1,0:T(8,128)(2,1)}), bf16[5120,128]{1,0:T(8,128)(2,1)}) %all-gather.12.cloned.1.call-update) | async-done | bytes 1310736 | tf_op jit(solution)/shard_map/all_gather | solution.py:64
  271.9 2.3 convolution_add_fusion.2
  274.3 115.1 %all-gather.16.cloned.1.call-done = bf16[5120,128]{1,0:T(8,128)(2,1)} async-done(((bf16[80,128]{1,0:T(8,128)(2,1)}), bf16[5120,128]{1,0:T(8,128)(2,1)}) %all-gather.16.cloned.1.call-update) | async-done | bytes 1310736 | tf_op jit(solution)/shard_map/all_gather | solution.py:65
  389.4 2.9 fusion.24
  392.3 120.0 %all-gather.14.cloned.1.call-done = bf16[5120,640]{1,0:T(8,128)(2,1)} async-done(((bf16[80,640]{1,0:T(8,128)(2,1)}), bf16[5120,640]{1,0:T(8,128)(2,1)}) %all-gather.14.cloned.1.call-update) | async-done | bytes 6553616 | tf_op jit(solution)/shard_map/all_gather | solution.py:63
  512.4 5.1 convolution_add_fusion
  519.2 109.8 %all-gather.18.cloned.1.call-done = bf16[4096,128]{1,0:T(8,128)(2,1)} async-done(((bf16[64,128]{1,0:T(8,128)(2,1)}), bf16[4096,128]{1,0:T(8,128)(2,1)}) %all-gather.18.cloned.1.call-update) | async-done | bytes 1048592 | tf_op jit(solution)/shard_map/all_gather | solution.py:96
  629.1 116.8 %all-gather.20.cloned.1.call-done = bf16[4096,128]{1,0:T(8,128)(2,1)} async-done(((bf16[64,128]{1,0:T(8,128)(2,1)}), bf16[4096,128]{1,0:T(8,128)(2,1)}) %all-gather.20.cloned.1.call-update) | async-done | bytes 1048592 | tf_op jit(solution)/shard_map/all_gather | solution.py:97
  745.8 324.3 %while.16 = (s32[]{:T(128)}, f32[2,1,5,128]{3,2,0,1:T(8,128)S(1)}, f32[2,1,5,128]{3,2,0,1:T(8,128)S(1)}, f32[2,1,5,128,128]{3,4,2,0,1:T(8,128)S(1)}, s32[64]{0:T...) while((s32[]{:T(128)}, f32[2,1,5,128]{3,2,0,1:T(8,128)S(1)}, ...), condition=%wide.region_7.8_spmd, body=%wide.region_3.7_spmd.sunk | while | flops 43025344 | bytes 2738821 | solution.py:130
  747.3 1.3 compare_and_fusion.2
  752.3 1.3 compare_and_fusion.2
  757.4 1.3 compare_and_fusion.2
  762.5 1.3 compare_and_fusion.2
  767.5 1.3 compare_and_fusion.2
  772.6 1.3 compare_and_fusion.2
  777.7 1.3 compare_and_fusion.2
  782.7 1.3 compare_and_fusion.2
  787.8 1.3 compare_and_fusion.2
  792.9 1.3 compare_and_fusion.2
  797.9 1.3 compare_and_fusion.2
  803.0 1.3 compare_and_fusion.2
  808.1 1.3 compare_and_fusion.2
  813.1 1.3 compare_and_fusion.2
  818.2 1.3 compare_and_fusion.2
  823.3 1.3 compare_and_fusion.2
  828.3 1.3 compare_and_fusion.2
  833.4 1.3 compare_and_fusion.2
  838.5 1.3 compare_and_fusion.2
  843.5 1.3 compare_and_fusion.2
  848.6 1.3 compare_and_fusion.2
  853.7 1.3 compare_and_fusion.2
  858.7 1.3 compare_and_fusion.2
  863.8 1.3 compare_and_fusion.2
  868.9 1.3 compare_and_fusion.2
  873.9 1.3 compare_and_fusion.2
  879.0 1.3 compare_and_fusion.2
  884.1 1.3 compare_and_fusion.2
  889.1 1.3 compare_and_fusion.2
  894.2 1.3 compare_and_fusion.2
  899.3 1.3 compare_and_fusion.2
  904.4 1.3 compare_and_fusion.2
  909.4 1.3 compare_and_fusion.2
  924.6 1.3 compare_and_fusion.2
  1000.6 1.3 compare_and_fusion.2
  1061.4 1.3 compare_and_fusion.2
  (649 shorter events, 285.3 us)
Async XLA Ops:
  7.2 77.2 %all-gather.8.cloned.1.call-start = ((), (), s32[]{:S(2)}) async-start(), calls=%async_computation | async-start | bytes 1474560 | tf_op jit(solution)/shard_map/all_gather | solution.py:57
  7.9 146.1 %all-gather.10.cloned.1.call-start = ((), (), s32[]{:S(2)}) async-start(), calls=%async_computation.1 | async-start | bytes 1474560 | tf_op jit(solution)/shard_map/all_gather | solution.py:58
  8.6 263.3 %all-gather.12.cloned.1.call-start = ((), (), s32[]{:S(2)}) async-start(), calls=%async_computation.2 | async-start | bytes 1331200 | tf_op jit(solution)/shard_map/all_gather | solution.py:64
  9.4 380.0 %all-gather.16.cloned.1.call-start = ((), (), s32[]{:S(2)}) async-start(), calls=%async_computation.4 | async-start | bytes 1331200 | tf_op jit(solution)/shard_map/all_gather | solution.py:65
  10.0 502.4 %all-gather.14.cloned.1.call-start = ((), (), s32[]{:S(2)}) async-start(), calls=%async_computation.3 | async-start | bytes 6656000 | tf_op jit(solution)/shard_map/all_gather | solution.py:63
  10.5 618.5 %all-gather.18.cloned.1.call-start = ((), (), s32[]{:S(2)}) async-start(), calls=%async_computation.5 | async-start | bytes 1064960 | tf_op jit(solution)/shard_map/all_gather | solution.py:96
  11.1 734.7 %all-gather.20.cloned.1.call-start = ((), (), s32[]{:S(2)}) async-start(), calls=%async_computation.6 | async-start | bytes 1064960 | tf_op jit(solution)/shard_map/all_gather | solution.py:97
  13.3 376.1 %copy-start.2 = (f32[5120]{0:T(1024)}, f32[5120]{0:T(1024)S(1)}, u32[]{:S(2)}) copy-start(f32[5120]{0:T(1024)S(1)} %convert_element_type.54) | copy-start | bytes 61444
  84.4 71.6 %copy-start = (bf16[128,5120]{1,0:T(8,128)(2,1)S(1)}, bf16[128,5120]{1,0:T(8,128)(2,1)}, u32[]{:S(2)}) copy-start(bf16[128,5120]{1,0:T(8,128)(2,1)} %all-gather.8.cloned.1.call-done) | copy-start | bytes 3932164
  517.9 1.0 copy-start.1
  518.2 227.6 %copy-start.3 = (s32[1,64]{1,0:T(1,128)S(1)}, s32[1,64]{1,0:T(1,128)}, u32[]{:S(2)}) copy-start(s32[1,64]{1,0:T(1,128)} %param.20) | copy-start | bytes 772
Sparse Core Ops, SparseCore 0:
  11.2 73.0 all-gather.7
  87.6 66.3 all-gather.9
  156.2 115.7 all-gather.11
  273.9 115.4 all-gather.15
  391.4 120.9 all-gather.13
  514.4 114.6 all-gather.17
  631.2 114.5 all-gather.19
where the time goes:
time: 1090 us; the launch traced here: 1080 us
  waiting for transfers between devices  719 us (66%)
  other arithmetic  152 us (14%)
  matrix products  149 us (14%)
  local copies, waits for them, and re-layouts  39.8 us (4%)
  between operations  14.9 us (1%)
    all_gather x1, waiting for transfers between devices, local(): lax.all_gather(w_query, 'blk', axis=0, tiled=True)  120 us
    all_gather x1, waiting for transfers between devices, local(): value_piece = lax.all_gather(cache_values, 'blk', axis=0, tiled=True)  117 us
    all_gather x1, waiting for transfers between devices, local(): lax.all_gather(w_key, 'blk', axis=0, tiled=True)  115 us
    all_gather x1, waiting for transfers between devices, local(): lax.all_gather(w_value, 'blk', axis=0, tiled=True)  115 us
    all_gather x1, waiting for transfers between devices, local(): key_piece = lax.all_gather(cache_keys, 'blk', axis=0, tiled=True)  110 us
    and x64, other arithmetic, visit(): visible = (cache_index < length) & (kept == 1)  83.6 us
    dot_general x64, matrix products, visit(): jnp.einsum('pkgqc,ckd->pkgqd', weights.astype(jnp.bfloat16), value_block,...  75.1 us
    all_gather x1, waiting for transfers between devices, local(): lax.all_gather(given_embeds, 'tp', axis=1, tiled=True)  69.6 us
  transfers between devices with their start and end apart: 7, of which 7 were waited for; matrix products, arithmetic and copies ran while one was open for 2% of the time, Pallas kernels for 0%

commit v1 on v0

v1 whole, which is shorter than its diff:
```python
import math

import jax
import jax.numpy as jnp
from jax import lax
from jax.experimental import pallas as pl
from jax.experimental.pallas import tpu as pltpu
from jax.sharding import PartitionSpec as P

KVH = 8
HD = 128
HQ = 40
CB = 64


def rotate(vectors, positions):
    halfway = HD // 2
    frequency = 1000000.0 ** (-(jnp.arange(halfway, dtype=jnp.float32) * (2.0 / HD)))
    angles = positions[..., None] * frequency
    cosine = jnp.cos(angles)[..., None, :]
    sine_part = jnp.sin(angles)[..., None, :]
    front_part = vectors[..., :halfway]
    back_part = vectors[..., halfway:]
    return jnp.concatenate(
        [front_part * cosine - back_part * sine_part, back_part * cosine + front_part * sine_part],
        axis=-1,
    )


def normalize(rows_in, norm_gain):
    widened = rows_in.astype(jnp.float32)
    inverse = lax.rsqrt(jnp.mean(widened * widened, axis=-1, keepdims=True) + 1e-06)
    return (widened * inverse * norm_gain.astype(jnp.float32)).astype(jnp.bfloat16)


def attend_kernel(q_ref, ko_ref, vo_ref, kc_ref, vc_ref, bias_ref, out_ref):
    inv_root = 1.0 / math.sqrt(HD)
    q = q_ref[...]
    contract = (((1,), (1,)), ((), ()))
    own = lax.dot_general(q, ko_ref[...], contract, preferred_element_type=jnp.float32) * inv_root
    far = lax.dot_general(q, kc_ref[...], contract, preferred_element_type=jnp.float32) * inv_root
    far = far + bias_ref[...]
    highest = jnp.maximum(jnp.max(own, axis=-1, keepdims=True), jnp.max(far, axis=-1, keepdims=True))
    own_w = jnp.exp(own - highest)
    far_w = jnp.exp(far - highest)
    totals = jnp.sum(own_w, axis=-1, keepdims=True) + jnp.sum(far_w, axis=-1, keepdims=True)
    mixture = jnp.dot(own_w.astype(jnp.bfloat16), vo_ref[...], preferred_element_type=jnp.float32)
    mixture = mixture + jnp.dot(far_w.astype(jnp.bfloat16), vc_ref[...], preferred_element_type=jnp.float32)
    out_ref[...] = (mixture / totals).astype(out_ref.dtype)


def attend(q_rot, k_rot, value_rows, cache_k, cache_v, bias):
    passes, rows, width = q_rot.shape
    heads = width // HD
    ctx = cache_k.shape[0]
    return pl.pallas_call(
        attend_kernel,
        grid=(passes, heads),
        in_specs=[
            pl.BlockSpec((None, rows, HD), lambda p, h: (p, 0, h)),
            pl.BlockSpec((None, rows, HD), lambda p, h: (p, 0, 0)),
            pl.BlockSpec((None, rows, HD), lambda p, h: (p, 0, 0)),
            pl.BlockSpec((ctx, HD), lambda p, h: (0, 0)),
            pl.BlockSpec((ctx, HD), lambda p, h: (0, 0)),
            pl.BlockSpec((1, ctx), lambda p, h: (0, 0)),
        ],
        out_specs=pl.BlockSpec((None, rows, HD), lambda p, h: (p, 0, h)),
        out_shape=jax.ShapeDtypeStruct((passes, rows, width), jnp.bfloat16),
        cost_estimate=pl.CostEstimate(
            flops=4 * passes * heads * rows * (ctx + rows) * HD,
            transcendentals=passes * heads * rows * (ctx + rows),
            bytes_accessed=2 * (2 * ctx * HD + 4 * passes * rows * width),
        ),
    )(q_rot, k_rot, value_rows, cache_k, cache_v, bias)


def local(
    embeds,
    given_embeds,
    accept,
    lengths,
    block_keep,
    norm_gain,
    w_query,
    b_query,
    w_key,
    b_key,
    w_value,
    b_value,
    cache_keys,
    cache_values,
):
    local_kv = w_key.shape[1] // HD
    block_rows = embeds.shape[0]
    ctx_rows = cache_keys.shape[0]
    q_cols = w_query.shape[1]
    w_rows = w_query.shape[0]

    both = lax.all_gather(jnp.stack([embeds, given_embeds]), "tp", axis=2, tiled=True)
    first_rows, given_rows = both[0], both[1]

    w_piece = jnp.concatenate([w_query, w_key, w_value], axis=1)
    c_piece = jnp.concatenate([cache_keys, cache_values], axis=1)
    w_size = w_piece.size
    packed = jnp.concatenate([w_piece.reshape(-1), c_piece.reshape(-1)])
    gathered = lax.all_gather(packed, "blk", axis=0, tiled=False)
    shards = gathered.shape[0]
    w_all = gathered[:, :w_size].reshape(shards * w_rows, w_piece.shape[1])
    c_all = gathered[:, w_size:].reshape(shards * ctx_rows, c_piece.shape[1])
    cache_k = c_all[:, : local_kv * HD]
    cache_v = c_all[:, local_kv * HD :]

    revised = jnp.where(accept[:, None] == 1, given_rows, first_rows)
    normed = normalize(jnp.concatenate([first_rows, revised], axis=0), norm_gain)
    proj = jnp.dot(normed, w_all, preferred_element_type=jnp.float32)
    queries = proj[:, :q_cols] + b_query.astype(jnp.float32)
    key_proj = proj[:, q_cols : q_cols + local_kv * HD] + b_key.astype(jnp.float32)
    value_proj = proj[:, q_cols + local_kv * HD :] + b_value.astype(jnp.float32)

    length = lengths[0]
    keep_row = block_keep[0]
    positions = length.astype(jnp.float32) + jnp.arange(block_rows, dtype=jnp.float32)
    q_rot = rotate(queries.reshape(2, block_rows, q_cols // HD, HD), positions).astype(jnp.bfloat16)
    k_rot = rotate(key_proj.reshape(2, block_rows, local_kv, HD), positions).astype(jnp.bfloat16)
    value_rows = value_proj.astype(jnp.bfloat16)

    total_ctx = shards * ctx_rows
    cache_index = jnp.arange(total_ctx, dtype=jnp.int32)
    visible = (cache_index < length) & (jnp.repeat(keep_row, CB, total_repeat_length=total_ctx) == 1)
    bias = jnp.where(visible, 0.0, -jnp.inf).astype(jnp.float32).reshape(1, total_ctx)

    attended = attend(
        q_rot.reshape(2, block_rows, q_cols),
        k_rot.reshape(2, block_rows, local_kv * HD),
        value_rows.reshape(2, block_rows, local_kv * HD),
        cache_k,
        cache_v,
        bias,
    )
    return (attended[0], attended[1])


def solution(mesh):
    return jax.shard_map(
        local,
        mesh=mesh,
        in_specs=(
            P("blk", "tp"),
            P("blk", "tp"),
            P("blk"),
            P("blk"),
            P("blk", None),
            P(),
            P("blk", "tp"),
            P("tp"),
            P("blk", "tp"),
            P("tp"),
            P("blk", "tp"),
            P("tp"),
            P("blk", "tp"),
            P("blk", "tp"),
        ),
        out_specs=(P("blk", "tp"), P("blk", "tp")),
        check_vma=False,
    )
```

time: 1090 us -> 308 us (0.28)
  waiting for transfers between devices: 719 us -> 159 us
  matrix products: 149 us -> 6.56 us
  other arithmetic: 152 us -> 56.7 us
  Pallas kernels: 0 us -> 15.5 us
  local copies, waits for them, and re-layouts: 39.8 us -> 54 us
    all_gather x7 -> x2, waiting for transfers between devices: 715 us -> 158 us  [the longest x1 129 us: local(): gathered = lax.all_gather(packed, 'blk', axis=0, tiled=False)]
    dot_general x133 -> x1, matrix products: 149 us -> 6.56 us  [local(): proj = jnp.dot(normed, w_all, preferred_element_type=jnp.float32)]
    and x64 -> x0, other arithmetic: 83.6 us -> none  [visit(): visible = (cache_index < length) & (kept == 1)]
    gather x0 -> x3, other arithmetic: none -> 44.2 us  [local(): jnp.repeat(keep_row, CB, total_repeat_length=total_ctx) == 1]
    select_n x64 -> x1, other arithmetic: 41.8 us -> 0.65 us  [local(): jnp.where(visible, 0.0, -jnp.inf).astype(jnp.float32).reshape(1, total_ctx)]
    dynamic_slice x64 -> x0, local copies, waits for them, and re-layouts: 37.5 us -> none  [local(): lax.scan(visit, running, (key_blocks, value_blocks, block_starts))]
    reduce_sum x129 -> x0, other arithmetic: 18 us -> none  [the longest x64 11 us: visit(): kept = jnp.sum(jnp.where(matches, keep_row[None, :], 0), axis=1)]
    pallas_call x0 -> x1, Pallas kernels: none -> 15.5 us  [attend(): pl.pallas_call(attend_kernel, grid=(passes, heads), in_specs=[pl.BlockSpe...]
  transfers between devices with their start and end apart: 7 -> 2, of which waited for: 7 -> 2; matrix products, arithmetic and copies ran while one was open for 2% -> 20% of each run, Pallas kernels for 0% -> 0%
where the time goes in v1:
time: 308 us; the launch traced here: 306 us
  waiting for transfers between devices  159 us (52%)
  other arithmetic  56.7 us (18%)
  local copies, waits for them, and re-layouts  54 us (18%)
  Pallas kernels  15.5 us (5%)
  between operations  14.9 us (5%)
  matrix products  6.56 us (2%)
    all_gather x1, waiting for transfers between devices, local(): gathered = lax.all_gather(packed, 'blk', axis=0, tiled=False)  129 us
    gather x3, other arithmetic, local(): jnp.repeat(keep_row, CB, total_repeat_length=total_ctx) == 1  44.2 us
    all_gather x1, waiting for transfers between devices, local(): lax.all_gather(jnp.stack([embeds, given_embeds]), 'tp', axis=2, tiled=True)  29.8 us
    pallas_call x1, Pallas kernels, attend(): pl.pallas_call(attend_kernel, grid=(passes, heads), in_specs=[pl.BlockSpe...  15.5 us
    all_gather x1, local copies, waits for them, and re-layouts, local(): gathered = lax.all_gather(packed, 'blk', axis=0, tiled=False)  12.6 us
    reshape x1, local copies, waits for them, and re-layouts, local(): w_all = gathered[:, :w_size].reshape(shards * w_rows, w_piece.shape[1])  11.4 us
    gather x4, local copies, waits for them, and re-layouts, local(): jnp.repeat(keep_row, CB, total_repeat_length=total_ctx) == 1  7.8 us
    slice x1, local copies, waits for them, and re-layouts, local(): w_all = gathered[:, :w_size].reshape(shards * w_rows, w_piece.shape[1])  7.74 us
  transfers between devices with their start and end apart: 2, of which 2 were waited for; matrix products, arithmetic and copies ran while one was open for 20% of the time, Pallas kernels for 0%

profile of v1, /device:TPU:1, one launch (start us, length us, event | category | flops | bytes accessed | tf_op | source)
XLA Modules:
  0.0 306.3 jit_solution(6695729438255710342)
XLA Ops:
  7.2 0.0 all-gather.4.cloned.1.call-start
  7.2 1.8 pad_maximum_fusion.2
  9.0 0.0 all-gather.6.cloned.1.call-start
  9.1 0.7 maximum_bitcast_fusion
  9.8 0.9 pad_maximum_fusion.5
  10.8 0.2 reshape.232
  10.9 0.7 pad_maximum_fusion.4
  11.6 0.0 all-gather.6.cloned.1.call-update
  12.3 0.7 convert_element_type.39
  13.0 0.7 convert_element_type.40
  13.6 0.7 convert_element_type.36
  14.3 1.3 convert_element_type.34
  15.6 0.2 multiply_cosine_fusion
  15.8 0.1 copy.28
  15.9 0.7 copy.29
  16.7 1.6 fusion.16
  18.3 2.1 fusion.14
  20.3 2.1 fusion.15
  22.4 2.1 fusion.13
  24.5 0.1 add_add_fusion.1
  24.6 4.5 %compare_select_fusion.2 = (s32[4096,1]{0,1:T(1,128)S(1)}, s32[4096,1]{0,1:T(1,128)S(1)}) fusion(s32[]{:T(128)} %bitcast.71, s32[]{:T(128)} %bitcast.72, s32[]{:T(128)} %bitcast.73, s32[]{:T(128)} %bitcast.74, s32[]{:T(128)} %bitcast.75, s32[]{:T(128)} %bitcast.77, s32[]{:T(128)} %bitcast.76, s32[4096,1]{0,1:T(1,128)S(1)} %bitcast.106, ...), kind=kLoop, calls=%fused_computation.88 | loop fusion | flops 57344 | bytes 65564 | tf_op jit(solution)/shard_map/jit(_take)/gather | solution.py:129
  29.1 2.9 compare_reduce_fusion.56
  32.0 36.9 %select_select_fusion = s32[4096]{0:T(1024)S(1)} fusion(pred[4096]{0:T(1024)(128)(4,1)S(1)} %get-tuple-element.70, pred[4096]{0:T(1024)(128)(4,1)S(1)} %get-tuple-element.69, pred[4096]{0:T(1024)(128)(4,1)S(1)} %get-tuple-element.68, pred[4096]{0:T(1024)(128)(4,1)S(1)} %get-tuple-element.67, pred[4096]{0:T(1024)(128)(4,1)S(1)} %get-tuple-element.66, ...), kind=kLoop, calls=%fused_computation.101 | loop fusion | flops 233472 | bytes 266468 | tf_op jit(solution)/shard_map/jit(_take)/gather | solution.py:129
  68.9 0.7 and_select_fusion.bias_ref
  69.5 29.8 %all-gather.4.cloned.1.call-done = bf16[2,128,5120]{2,1,0:T(8,128)(2,1)} async-done(((bf16[2,128,640]{2,1,0:T(8,128)(2,1)}), bf16[2,128,5120]{2,1,0:T(8,128)(2,1)}) %all-gather.4.cloned.1.call-update) | async-done | bytes 2621456 | tf_op jit(solution)/shard_map/all_gather | solution.py:99
  99.3 1.6 slice_bitcast_fusion.1
  100.9 0.6 copy-done
  101.4 0.2 fusion.7
  101.7 1.1 copy-done.1
  102.7 0.6 fusion
  103.4 128.7 %all-gather.6.cloned.1.call-done = bf16[5636096]{0:T(1024)(128)(2,1)} async-done(((bf16[88064]{0:T(1024)(128)(2,1)}), bf16[5636096]{0:T(1024)(128)(2,1)}) %all-gather.6.cloned.1.call-update) | async-done | bytes 11272208 | tf_op jit(solution)/shard_map/all_gather | solution.py:106
  232.0 12.6 %reshape.310 = bf16[64,88064]{1,0:T(8,128)(2,1)} reshape(bf16[5636096]{0:T(1024)(128)(2,1)} %all-gather.6.cloned.1.call-done) | data formatting | bytes 22544384 | tf_op jit(solution)/shard_map/all_gather | solution.py:106
  244.6 7.7 %slice.208 = bf16[64,71680]{1,0:T(8,128)(2,1)} slice(bf16[64,88064]{1,0:T(8,128)(2,1)} %reshape.310), slice={[0:64], [0:71680]} | slice | bytes 18350080 | tf_op jit(solution)/shard_map/slice | solution.py:108
  252.4 11.4 %reshape.234 = bf16[5120,896]{1,0:T(8,128)(2,1)} reshape(bf16[64,71680]{1,0:T(8,128)(2,1)} %slice.208) | data formatting | bytes 18350080 | tf_op jit(solution)/shard_map/reshape | solution.py:108
  263.8 2.4 reshape.238
  266.1 3.2 %fusion.12 = (bf16[4096,128]{1,0:T(8,128)(2,1)}, bf16[4096,128]{1,0:T(8,128)(2,1)}) fusion(bf16[4096,256]{1,0:T(8,128)(2,1)} %reshape.238), kind=kLoop, calls=%fused_computation.108 | loop fusion | bytes 4194304 | tf_op jit(solution)/shard_map/slice | solution.py:111
  269.3 6.6 %fusion.3 = f32[256,896]{1,0:T(8,128)S(1)} fusion(bf16[5120,896]{1,0:T(8,128)(2,1)} %reshape.234, f32[5120]{0:T(1024)S(1)} %copy-done.5, f32[256]{0:T(256)S(1)} %add_rsqrt_fusion, bf16[128,5120]{1,0:T(8,128)(2,1)S(1)} %copy-done.2, bf16[128,5120]{1,0:T(8,128)(2,1)S(1)} %slice_bitcast_fusion.1), kind=kOutput, calls=%fused_computation.5 | convolution fusion | flops 2357985280 | bytes 12735488 | tf_op jit(solution)/shard_map/dot_general | solution.py:115
  275.9 0.9 copy-done.3
  276.9 0.2 copy.26
  277.1 0.3 reshape.235
  277.4 0.3 subtract_convert_fusion
  277.8 0.4 pad_maximum_fusion.3
  278.2 1.5 copy.30.q_ref
  279.7 1.6 fusion.8
  281.3 0.1 fusion.9
  281.4 0.7 pad_maximum_fusion.6.ko_ref
  282.2 15.5 %shard_map.149 = bf16[2,128,640]{2,1,0:T(8,128)(2,1)} custom-call(bf16[2,128,640]{2,1,0:T(8,128)(2,1)} %copy.30.q_ref, bf16[2,128,128]{2,1,0:T(8,128)(2,1)} %pad_maximum_fusion.6.ko_ref, bf16[2,128,128]{2,1,0:T(8,128)(2,1)} %bitcast.109, bf16[4096,128]{1,0:T(8,128)(2,1)} %get-tuple-element.74.kc_ref, bf16[4096,128]{1,0:T(8,128)(2,1)} %get-tuple-element.73.vc_ref, ...), custom_call_target="tpu_custom_call" | custom-call | flops 2768240640 | bytes 3407872 | tf_op jit(solution)/shard_map/pallas_call | solution.py:56
  297.7 1.7 slice_bitcast_fusion.2
  (23 shorter events, 0.2 us)
Async XLA Ops:
  7.2 17.3 %copy-start.6 = (s32[32,128]{1,0:T(8,128)S(1)}, s32[32,128]{1,0:T(8,128)}, u32[]{:S(2)}) copy-start(s32[32,128]{1,0:T(8,128)} %constant.102.clone.1) | copy-start | bytes 49156
  7.2 24.8 %copy-start.7 = (s32[128]{0:T(128)S(1)}, s32[128]{0:T(128)}, u32[]{:S(2)}) copy-start(s32[128]{0:T(128)} %param.18) | copy-start | bytes 1540
  7.2 92.1 %all-gather.4.cloned.1.call-start = ((), (), s32[]{:S(2)}) async-start(), calls=%async_computation | async-start | bytes 2949120 | tf_op jit(solution)/shard_map/all_gather | solution.py:99
  9.0 223.0 %all-gather.6.cloned.1.call-start = ((), (), s32[]{:S(2)}) async-start(), calls=%async_computation.1 | async-start | bytes 11448320 | tf_op jit(solution)/shard_map/all_gather | solution.py:106
  99.3 2.1 copy-start
  101.7 1.1 copy-start.1
  252.4 11.4 %slice-start = ((bf16[64,88064]{1,0:T(8,128)(2,1)}), bf16[64,16384]{1,0:T(8,128)(2,1)S(1)}, s32[]{:S(2)}) async-start(bf16[64,88064]{1,0:T(8,128)(2,1)} %reshape.310), calls=%async_computation.2 | async-start | bytes 4194304 | tf_op jit(solution)/shard_map/slice | solution.py:109
  266.1 3.2 %copy-start.2 = (bf16[128,5120]{1,0:T(8,128)(2,1)S(1)}, bf16[128,5120]{1,0:T(8,128)(2,1)}, u32[]{:S(2)}) copy-start(bf16[128,5120]{1,0:T(8,128)(2,1)} %copy-done.1) | copy-start | bytes 3932164
  266.1 3.2 %copy-start.5 = (f32[5120]{0:T(1024)S(1)}, f32[5120]{0:T(1024)}, u32[]{:S(2)}) copy-start(f32[5120]{0:T(1024)} %convert_element_type.34) | copy-start | bytes 61444
  275.9 0.9 copy-start.3
  276.8 4.5 %copy-start.4 = (f32[128,64]{1,0:T(8,128)S(1)}, f32[128,64]{1,0:T(8,128)}, u32[]{:S(2)}) copy-start(f32[128,64]{1,0:T(8,128)} %copy.29) | copy-start | bytes 98308
Sparse Core Ops, SparseCore 0:
  11.2 88.0 all-gather.3
  101.5 130.5 all-gather.5

commit v2 on v1

--- a/solution.py
+++ b/solution.py
@@ -36,23 +36,28 @@
 def attend_kernel(q_ref, ko_ref, vo_ref, kc_ref, vc_ref, bias_ref, out_ref):
     inv_root = 1.0 / math.sqrt(HD)
     q = q_ref[...]
+    shards, ctx_rows, width = kc_ref.shape
+    cache_k = kc_ref[...].reshape(shards * ctx_rows, width)
+    cache_v = vc_ref[...].reshape(shards * ctx_rows, width)
     contract = (((1,), (1,)), ((), ()))
     own = lax.dot_general(q, ko_ref[...], contract, preferred_element_type=jnp.float32) * inv_root
-    far = lax.dot_general(q, kc_ref[...], contract, preferred_element_type=jnp.float32) * inv_root
+    far = lax.dot_general(q, cache_k, contract, preferred_element_type=jnp.float32) * inv_root
     far = far + bias_ref[...]
     highest = jnp.maximum(jnp.max(own, axis=-1, keepdims=True), jnp.max(far, axis=-1, keepdims=True))
     own_w = jnp.exp(own - highest)
     far_w = jnp.exp(far - highest)
     totals = jnp.sum(own_w, axis=-1, keepdims=True) + jnp.sum(far_w, axis=-1, keepdims=True)
     mixture = jnp.dot(own_w.astype(jnp.bfloat16), vo_ref[...], preferred_element_type=jnp.float32)
-    mixture = mixture + jnp.dot(far_w.astype(jnp.bfloat16), vc_ref[...], preferred_element_type=jnp.float32)
+    mixture = mixture + jnp.dot(far_w.astype(jnp.bfloat16), cache_v, preferred_element_type=jnp.float32)
     out_ref[...] = (mixture / totals).astype(out_ref.dtype)
 
 
-def attend(q_rot, k_rot, value_rows, cache_k, cache_v, bias):
+def attend(q_rot, k_rot, value_rows, gathered, bias):
     passes, rows, width = q_rot.shape
     heads = width // HD
-    ctx = cache_k.shape[0]
+    shards, ignored, lanes = gathered.shape
+    ctx = bias.shape[1]
+    ctx_rows = ctx // shards
     return pl.pallas_call(
         attend_kernel,
         grid=(passes, heads),
@@ -60,8 +65,8 @@
             pl.BlockSpec((None, rows, HD), lambda p, h: (p, 0, h)),
             pl.BlockSpec((None, rows, HD), lambda p, h: (p, 0, 0)),
             pl.BlockSpec((None, rows, HD), lambda p, h: (p, 0, 0)),
-            pl.BlockSpec((ctx, HD), lambda p, h: (0, 0)),
-            pl.BlockSpec((ctx, HD), lambda p, h: (0, 0)),
+            pl.BlockSpec((shards, ctx_rows, lanes), lambda p, h: (0, 0, 0)),
+            pl.BlockSpec((shards, ctx_rows, lanes), lambda p, h: (0, 1, 0)),
             pl.BlockSpec((1, ctx), lambda p, h: (0, 0)),
         ],
         out_specs=pl.BlockSpec((None, rows, HD), lambda p, h: (p, 0, h)),
@@ -71,7 +76,7 @@
             transcendentals=passes * heads * rows * (ctx + rows),
             bytes_accessed=2 * (2 * ctx * HD + 4 * passes * rows * width),
         ),
-    )(q_rot, k_rot, value_rows, cache_k, cache_v, bias)
+    )(q_rot, k_rot, value_rows, gathered, gathered, bias)
 
 
 def local(
@@ -96,27 +101,35 @@
     q_cols = w_query.shape[1]
     w_rows = w_query.shape[0]
 
-    both = lax.all_gather(jnp.stack([embeds, given_embeds]), "tp", axis=2, tiled=True)
+    tp_size = lax.axis_size("tp")
+    me_tp = lax.axis_index("tp")
+    mine = jnp.stack([embeds, given_embeds])
+    pieces = [mine]
+    for shift in range(1, tp_size):
+        pairs = [(i, (i - shift) % tp_size) for i in range(tp_size)]
+        pieces.append(lax.ppermute(mine, "tp", pairs))
+    ordered = jnp.roll(jnp.stack(pieces), me_tp, axis=0)
+    both = jnp.concatenate([ordered[i] for i in range(tp_size)], axis=-1)
     first_rows, given_rows = both[0], both[1]
 
-    w_piece = jnp.concatenate([w_query, w_key, w_value], axis=1)
-    c_piece = jnp.concatenate([cache_keys, cache_values], axis=1)
-    w_size = w_piece.size
-    packed = jnp.concatenate([w_piece.reshape(-1), c_piece.reshape(-1)])
+    w_cols = w_query.shape[1] // HD + 2 * local_kv
+    w_parts = [w_query[:, j * HD : (j + 1) * HD] for j in range(q_cols // HD)] + [w_key, w_value]
+    packed = jnp.concatenate([cache_keys, cache_values] + w_parts, axis=0)
     gathered = lax.all_gather(packed, "blk", axis=0, tiled=False)
     shards = gathered.shape[0]
-    w_all = gathered[:, :w_size].reshape(shards * w_rows, w_piece.shape[1])
-    c_all = gathered[:, w_size:].reshape(shards * ctx_rows, c_piece.shape[1])
-    cache_k = c_all[:, : local_kv * HD]
-    cache_v = c_all[:, local_kv * HD :]
-
+    cache_rows = 2 * ctx_rows
+    w_blocks = gathered[:, cache_rows:, :].reshape(shards, w_cols, w_rows, HD)
     revised = jnp.where(accept[:, None] == 1, given_rows, first_rows)
     normed = normalize(jnp.concatenate([first_rows, revised], axis=0), norm_gain)
-    proj = jnp.dot(normed, w_all, preferred_element_type=jnp.float32)
-    queries = proj[:, :q_cols] + b_query.astype(jnp.float32)
-    key_proj = proj[:, q_cols : q_cols + local_kv * HD] + b_key.astype(jnp.float32)
-    value_proj = proj[:, q_cols + local_kv * HD :] + b_value.astype(jnp.float32)
-
+    proj = jnp.einsum(
+        "rsi,sjic->rjc",
+        normed.reshape(normed.shape[0], shards, w_rows),
+        w_blocks,
+        preferred_element_type=jnp.float32,
+    )
+    queries = proj[:, : q_cols // HD, :].reshape(-1, q_cols) + b_query.astype(jnp.float32)
+    key_proj = proj[:, q_cols // HD, :] + b_key.astype(jnp.float32)
+    value_proj = proj[:, q_cols // HD + 1, :] + b_value.astype(jnp.float32)
     length = lengths[0]
     keep_row = block_keep[0]
     positions = length.astype(jnp.float32) + jnp.arange(block_rows, dtype=jnp.float32)
@@ -125,16 +138,15 @@
     value_rows = value_proj.astype(jnp.bfloat16)
 
     total_ctx = shards * ctx_rows
-    cache_index = jnp.arange(total_ctx, dtype=jnp.int32)
-    visible = (cache_index < length) & (jnp.repeat(keep_row, CB, total_repeat_length=total_ctx) == 1)
+    cache_index = jnp.arange(total_ctx, dtype=jnp.int32).reshape(-1, CB)
+    kept = jnp.broadcast_to(keep_row.reshape(-1, 1), cache_index.shape) == 1
+    visible = (cache_index < length) & kept
     bias = jnp.where(visible, 0.0, -jnp.inf).astype(jnp.float32).reshape(1, total_ctx)
-
     attended = attend(
         q_rot.reshape(2, block_rows, q_cols),
         k_rot.reshape(2, block_rows, local_kv * HD),
         value_rows.reshape(2, block_rows, local_kv * HD),
-        cache_k,
-        cache_v,
+        gathered,
         bias,
     )
     return (attended[0], attended[1])

time: 308 us -> 236 us (0.77)
  other arithmetic: 56.7 us -> 6.5 us
  starting transfers between devices: 0.08 us -> 31.2 us
  local copies, waits for them, and re-layouts: 54 us -> 23.1 us
  waiting for transfers between devices: 159 us -> 134 us
    ppermute x0 -> x7, waiting for transfers between devices: none -> 62.9 us  [local(): pieces.append(lax.ppermute(mine, 'tp', pairs))]
    all_gather x1, waiting for transfers between devices: 129 us -> 71.2 us  [local(): gathered = lax.all_gather(packed, 'blk', axis=0, tiled=False)]
    gather x3 -> x0, other arithmetic: 44.2 us -> none  [local(): jnp.repeat(keep_row, CB, total_repeat_length=total_ctx) == 1]
    ppermute x0 -> x7, starting transfers between devices: none -> 31.2 us  [local(): pieces.append(lax.ppermute(mine, 'tp', pairs))]
    all_gather x1 -> x0, waiting for transfers between devices: 29.8 us -> none  [local(): lax.all_gather(jnp.stack([embeds, given_embeds]), 'tp', axis=2, tiled=True)]
    reshape x4 -> x1, local copies, waits for them, and re-layouts: 14.3 us -> 0.23 us  [local(): proj[:, :q_cols // HD, :].reshape(-1, q_cols) + b_query.astype(jnp.float32)]
    all_gather x1 -> x0, local copies, waits for them, and re-layouts: 12.6 us -> none  [local(): gathered = lax.all_gather(packed, 'blk', axis=0, tiled=False)]
    gather x4 -> x0, local copies, waits for them, and re-layouts: 7.8 us -> none  [local(): jnp.repeat(keep_row, CB, total_repeat_length=total_ctx) == 1]
  transfers between devices with their start and end apart: 2 -> 8, of which waited for: 2 -> 6; matrix products, arithmetic and copies ran while one was open for 20% -> 4% of each run, Pallas kernels for 0% -> 0%
where the time goes in v2:
time: 236 us; the launch traced here: 232 us
  waiting for transfers between devices  134 us (57%)
  starting transfers between devices  31.2 us (13%)
  local copies, waits for them, and re-layouts  23.1 us (10%)
  Pallas kernels  15.6 us (7%)
  between operations  15.1 us (6%)
  matrix products  6.65 us (3%)
  other arithmetic  6.5 us (3%)
    all_gather x1, waiting for transfers between devices, local(): gathered = lax.all_gather(packed, 'blk', axis=0, tiled=False)  71.2 us
    ppermute x7, waiting for transfers between devices, local(): pieces.append(lax.ppermute(mine, 'tp', pairs))  62.9 us
    ppermute x7, starting transfers between devices, local(): pieces.append(lax.ppermute(mine, 'tp', pairs))  31.2 us
    pallas_call x1, Pallas kernels, attend(): pl.pallas_call(attend_kernel, grid=(passes, heads), in_specs=[pl.BlockSpe...  15.6 us
    unnamed x32, local copies, waits for them, and re-layouts  9.6 us
    slice x1, local copies, waits for them, and re-layouts, local(): w_blocks = gathered[:, cache_rows:, :].reshape(shards, w_cols, w_rows, HD)  7.67 us
    dot_general x1, matrix products, local(): jnp.einsum('rsi,sjic->rjc', normed.reshape(normed.shape[0], shards, w_row...  6.65 us
  transfers between devices with their start and end apart: 8, of which 6 were waited for; matrix products, arithmetic and copies ran while one was open for 4% of the time, Pallas kernels for 0%

profile of v2, /device:TPU:1, one launch (start us, length us, event | category | flops | bytes accessed | tf_op | source)
XLA Modules:
  0.0 232.4 jit_solution(14575445441256073149)
XLA Ops:
  7.2 0.7 constant_dynamic-update-slice_fusion.8
  7.9 0.7 constant_dynamic-update-slice_fusion.7
  8.7 0.7 constant_dynamic-update-slice_fusion.6
  9.4 0.7 constant_dynamic-update-slice_fusion.5
  10.1 0.7 constant_dynamic-update-slice_fusion.4
  10.9 0.7 constant_dynamic-update-slice_fusion.3
  11.6 0.7 constant_dynamic-update-slice_fusion.2
  12.3 0.7 constant_dynamic-update-slice_fusion.1
  13.1 0.7 constant_dynamic-update-slice_fusion
  13.8 0.7 copy-done
  14.5 1.1 copy.28
  15.6 1.1 copy.29
  16.7 10.5 %collective-permute-start = (bf16[2,128,640]{1,2,0:T(8,128)(2,1)S(1)}, bf16[2,128,640]{1,2,0:T(8,128)(2,1)S(1)}, u32[]{:S(2)}, u32[]{:S(2)}) collective-permute-start(bf16[2,128,640]{1,2,0:T(8,128)(2,1)S(1)} %pad_maximum_fusion), channel_id=1, source_target_pairs={{0,7},{1,0},{2,1},{3,2},{4,3},{5,4},{6,5},{7,6},{8,15},{9,8},{10,9... | collective-permute-start | bytes 983048 | tf_op jit(solution)/shard_map/ppermute | solution.py:110
  27.2 2.4 %collective-permute-start.1 = (bf16[2,128,640]{1,2,0:T(8,128)(2,1)S(1)}, bf16[2,128,640]{1,2,0:T(8,128)(2,1)S(1)}, u32[]{:S(2)}, u32[]{:S(2)}) collective-permute-start(bf16[2,128,640]{1,2,0:T(8,128)(2,1)S(1)} %pad_maximum_fusion), channel_id=1, source_target_pairs={{0,6},{1,7},{2,0},{3,1},{4,2},{5,3},{6,4},{7,5},{8,14},{9,15},{10,... | collective-permute-start | bytes 983048 | tf_op jit(solution)/shard_map/ppermute | solution.py:110
  29.6 2.1 collective-permute-start.2
  31.7 7.5 %collective-permute-start.3 = (bf16[2,128,640]{1,2,0:T(8,128)(2,1)S(1)}, bf16[2,128,640]{1,2,0:T(8,128)(2,1)S(1)}, u32[]{:S(2)}, u32[]{:S(2)}) collective-permute-start(bf16[2,128,640]{1,2,0:T(8,128)(2,1)S(1)} %pad_maximum_fusion), channel_id=1, source_target_pairs={{0,4},{1,5},{2,6},{3,7},{4,0},{5,1},{6,2},{7,3},{8,12},{9,13},{10,... | collective-permute-start | bytes 983048 | tf_op jit(solution)/shard_map/ppermute | solution.py:110
  39.1 1.9 collective-permute-start.4
  41.1 0.8 reshape.197
  41.9 0.7 convert_element_type.39
  43.2 0.2 multiply_cosine_fusion
  43.6 0.7 convert_element_type.40
  44.3 0.7 compare_bitcast_fusion
  45.0 0.7 reshape.201.bias_ref
  45.7 0.7 bitcast_convert_fusion
  46.4 0.7 broadcast_compare_fusion
  47.1 4.9 %collective-permute-start.5 = (bf16[2,128,640]{1,2,0:T(8,128)(2,1)S(1)}, bf16[2,128,640]{1,2,0:T(8,128)(2,1)S(1)}, u32[]{:S(2)}, u32[]{:S(2)}) collective-permute-start(bf16[2,128,640]{1,2,0:T(8,128)(2,1)S(1)} %pad_maximum_fusion), channel_id=1, source_target_pairs={{0,2},{1,3},{2,4},{3,5},{4,6},{5,7},{6,0},{7,1},{8,10},{9,11},{10,... | collective-permute-start | bytes 983048 | tf_op jit(solution)/shard_map/ppermute | solution.py:110
  52.1 3.5 %collective-permute-done.1 = bf16[2,128,640]{1,2,0:T(8,128)(2,1)S(1)} collective-permute-done((bf16[2,128,640]{1,2,0:T(8,128)(2,1)S(1)}, bf16[2,128,640]{1,2,0:T(8,128)(2,1)S(1)}, u32[]{:S(2)}, u32[]{:S(2)}) %collective-permute-start.1) | collective-permute-done | bytes 327712 | tf_op jit(solution)/shard_map/ppermute | solution.py:110
  55.6 1.9 collective-permute-start.6
  57.5 19.5 %collective-permute-done.2 = bf16[2,128,640]{1,2,0:T(8,128)(2,1)S(1)} collective-permute-done((bf16[2,128,640]{1,2,0:T(8,128)(2,1)S(1)}, bf16[2,128,640]{1,2,0:T(8,128)(2,1)S(1)}, u32[]{:S(2)}, u32[]{:S(2)}) %collective-permute-start.2) | collective-permute-done | bytes 327712 | tf_op jit(solution)/shard_map/ppermute | solution.py:110
  77.1 21.2 %collective-permute-done.3 = bf16[2,128,640]{1,2,0:T(8,128)(2,1)S(1)} collective-permute-done((bf16[2,128,640]{1,2,0:T(8,128)(2,1)S(1)}, bf16[2,128,640]{1,2,0:T(8,128)(2,1)S(1)}, u32[]{:S(2)}, u32[]{:S(2)}) %collective-permute-start.3) | collective-permute-done | bytes 327712 | tf_op jit(solution)/shard_map/ppermute | solution.py:110
  98.4 7.6 %collective-permute-done.5 = bf16[2,128,640]{1,2,0:T(8,128)(2,1)S(1)} collective-permute-done((bf16[2,128,640]{1,2,0:T(8,128)(2,1)S(1)}, bf16[2,128,640]{1,2,0:T(8,128)(2,1)S(1)}, u32[]{:S(2)}, u32[]{:S(2)}) %collective-permute-start.5) | collective-permute-done | bytes 327712 | tf_op jit(solution)/shard_map/ppermute | solution.py:110
  106.0 11.1 %collective-permute-done.6 = bf16[2,128,640]{1,2,0:T(8,128)(2,1)S(1)} collective-permute-done((bf16[2,128,640]{1,2,0:T(8,128)(2,1)S(1)}, bf16[2,128,640]{1,2,0:T(8,128)(2,1)S(1)}, u32[]{:S(2)}, u32[]{:S(2)}) %collective-permute-start.6) | collective-permute-done | bytes 327712 | tf_op jit(solution)/shard_map/ppermute | solution.py:110
  118.1 0.4 slice_bitcast_fusion.2
  118.5 0.1 bitcast_select_fusion
  118.7 0.7 multiply_reduce_fusion
  119.4 0.1 broadcast_select_fusion
  119.6 71.2 %all-gather.3.cloned.1.call-done = bf16[44032,128]{1,0:T(8,128)(2,1)} async-done(((bf16[688,128]{1,0:T(8,128)(2,1)}), bf16[44032,128]{1,0:T(8,128)(2,1)}) %all-gather.3.cloned.1.call-update) | async-done | bytes 11272208 | tf_op jit(solution)/shard_map/all_gather | solution.py:118
  190.8 7.7 %slice.102 = bf16[64,560,128]{2,1,0:T(8,128)(2,1)} slice(bf16[64,688,128]{2,1,0:T(8,128)(2,1)} %bitcast.100), slice={[0:64], [128:688], [0:128]} | slice | bytes 18350080 | tf_op jit(solution)/shard_map/slice | solution.py:121
  198.5 6.6 %fusion.8 = f32[256,7,128]{2,0,1:T(8,128)S(1)} fusion(bf16[64,7,80,128]{3,2,1,0:T(8,128)(2,1)} %bitcast.103, bf16[128,64,80]{0,2,1:T(8,128)(2,1)S(1)} %broadcast_select_fusion, bf16[128,64,80]{0,2,1:T(8,128)(2,1)S(1)} %bitcast.105, f32[64,80]{1,0:T(8,128)S(1)} %reshape.197, f32[256]{0:T(256)S(1)} %add_rsqrt_fusion), kind=kOutput, calls=%fused_computation.9 | convolution fusion | flops 2357985280 | bytes 12735488 | tf_op jit(solution)/shard_map/rsi,sjic->rjc/dot_general | solution.py:124
  205.2 0.2 copy.31
  205.4 0.1 broadcast_add_fusion
  205.6 0.1 subtract_convert_fusion
  205.7 0.9 copy.34.q_ref
  206.7 0.1 fusion.19
  206.8 0.7 pad_maximum_fusion.2.ko_ref
  207.5 0.6 add_convert_fusion.1.vo_ref
  208.1 15.6 %shard_map.149 = bf16[2,128,640]{2,1,0:T(8,128)(2,1)} custom-call(bf16[2,128,640]{2,1,0:T(8,128)(2,1)} %copy.34.q_ref, bf16[2,128,128]{2,1,0:T(8,128)(2,1)} %pad_maximum_fusion.2.ko_ref, bf16[2,128,128]{2,1,0:T(8,128)(2,1)} %add_convert_fusion.1.vo_ref, bf16[64,688,128]{2,1,0:T(8,128)(2,1)} %bitcast.101, bf16[64,688,128]{2,1,0:T(8,128)(2,1)} %bitcast.102, ...), custom_call_target="tpu_custom_call" | custom-call | flops 2768240640 | bytes 3407872 | tf_op jit(solution)/shard_map/pallas_call | solution.py:61
  223.8 1.7 slice_bitcast_fusion
  (40 shorter events, 1.6 us)
Async XLA Ops:
  7.2 183.6 %all-gather.3.cloned.1.call-start = ((), (), s32[]{:S(2)}) async-start(), calls=%async_computation | async-start | bytes 11448320 | tf_op jit(solution)/shard_map/all_gather | solution.py:118
  13.8 0.7 copy-start
  16.7 30.4 %collective-permute-start = (bf16[2,128,640]{1,2,0:T(8,128)(2,1)S(1)}, bf16[2,128,640]{1,2,0:T(8,128)(2,1)S(1)}, u32[]{:S(2)}, u32[]{:S(2)}) collective-permute-start(bf16[2,128,640]{1,2,0:T(8,128)(2,1)S(1)} %pad_maximum_fusion), channel_id=1, source_target_pairs={{0,7},{1,0},{2,1},{3,2},{4,3},{5,4},{6,5},{7,6},{8,15},{9,8},{10,9... | collective-permute-start | bytes 983048 | tf_op jit(solution)/shard_map/ppermute | solution.py:110
  27.2 28.4 %collective-permute-start.1 = (bf16[2,128,640]{1,2,0:T(8,128)(2,1)S(1)}, bf16[2,128,640]{1,2,0:T(8,128)(2,1)S(1)}, u32[]{:S(2)}, u32[]{:S(2)}) collective-permute-start(bf16[2,128,640]{1,2,0:T(8,128)(2,1)S(1)} %pad_maximum_fusion), channel_id=1, source_target_pairs={{0,6},{1,7},{2,0},{3,1},{4,2},{5,3},{6,4},{7,5},{8,14},{9,15},{10,... | collective-permute-start | bytes 983048 | tf_op jit(solution)/shard_map/ppermute | solution.py:110
  29.6 47.4 %collective-permute-start.2 = (bf16[2,128,640]{1,2,0:T(8,128)(2,1)S(1)}, bf16[2,128,640]{1,2,0:T(8,128)(2,1)S(1)}, u32[]{:S(2)}, u32[]{:S(2)}) collective-permute-start(bf16[2,128,640]{1,2,0:T(8,128)(2,1)S(1)} %pad_maximum_fusion), channel_id=1, source_target_pairs={{0,5},{1,6},{2,7},{3,0},{4,1},{5,2},{6,3},{7,4},{8,13},{9,14},{10,... | collective-permute-start | bytes 983048 | tf_op jit(solution)/shard_map/ppermute | solution.py:110
  31.7 66.6 %collective-permute-start.3 = (bf16[2,128,640]{1,2,0:T(8,128)(2,1)S(1)}, bf16[2,128,640]{1,2,0:T(8,128)(2,1)S(1)}, u32[]{:S(2)}, u32[]{:S(2)}) collective-permute-start(bf16[2,128,640]{1,2,0:T(8,128)(2,1)S(1)} %pad_maximum_fusion), channel_id=1, source_target_pairs={{0,4},{1,5},{2,6},{3,7},{4,0},{5,1},{6,2},{7,3},{8,12},{9,13},{10,... | collective-permute-start | bytes 983048 | tf_op jit(solution)/shard_map/ppermute | solution.py:110
  39.1 59.2 %collective-permute-start.4 = (bf16[2,128,640]{1,2,0:T(8,128)(2,1)S(1)}, bf16[2,128,640]{1,2,0:T(8,128)(2,1)S(1)}, u32[]{:S(2)}, u32[]{:S(2)}) collective-permute-start(bf16[2,128,640]{1,2,0:T(8,128)(2,1)S(1)} %pad_maximum_fusion), channel_id=1, source_target_pairs={{0,3},{1,4},{2,5},{3,6},{4,7},{5,0},{6,1},{7,2},{8,11},{9,12},{10,... | collective-permute-start | bytes 983048 | tf_op jit(solution)/shard_map/ppermute | solution.py:110
  47.1 58.9 %collective-permute-start.5 = (bf16[2,128,640]{1,2,0:T(8,128)(2,1)S(1)}, bf16[2,128,640]{1,2,0:T(8,128)(2,1)S(1)}, u32[]{:S(2)}, u32[]{:S(2)}) collective-permute-start(bf16[2,128,640]{1,2,0:T(8,128)(2,1)S(1)} %pad_maximum_fusion), channel_id=1, source_target_pairs={{0,2},{1,3},{2,4},{3,5},{4,6},{5,7},{6,0},{7,1},{8,10},{9,11},{10,... | collective-permute-start | bytes 983048 | tf_op jit(solution)/shard_map/ppermute | solution.py:110
  55.6 61.6 %collective-permute-start.6 = (bf16[2,128,640]{1,2,0:T(8,128)(2,1)S(1)}, bf16[2,128,640]{1,2,0:T(8,128)(2,1)S(1)}, u32[]{:S(2)}, u32[]{:S(2)}) collective-permute-start(bf16[2,128,640]{1,2,0:T(8,128)(2,1)S(1)} %pad_maximum_fusion), channel_id=1, source_target_pairs={{0,1},{1,2},{2,3},{3,4},{4,5},{5,6},{6,7},{7,0},{8,9},{9,10},{10,1... | collective-permute-start | bytes 983048 | tf_op jit(solution)/shard_map/ppermute | solution.py:110
Sparse Core Ops, SparseCore 0:
  14.6 176.1 all-gather.2

commit v3 on v2

v3 whole, which is shorter than its diff:
```python
import math

import jax
import jax.numpy as jnp
from jax import lax
from jax.experimental import pallas as pl
from jax.experimental.pallas import tpu as pltpu
from jax.sharding import Mesh
from jax.sharding import PartitionSpec as P

KVH = 8
HD = 128
HQ = 40
CB = 64


def rotate(vectors, positions):
    halfway = HD // 2
    frequency = 1000000.0 ** (-(jnp.arange(halfway, dtype=jnp.float32) * (2.0 / HD)))
    angles = positions[..., None] * frequency
    cosine = jnp.cos(angles)[..., None, :]
    sine_part = jnp.sin(angles)[..., None, :]
    front_part = vectors[..., :halfway]
    back_part = vectors[..., halfway:]
    return jnp.concatenate(
        [front_part * cosine - back_part * sine_part, back_part * cosine + front_part * sine_part],
        axis=-1,
    )


def normalize(rows_in, norm_gain):
    widened = rows_in.astype(jnp.float32)
    inverse = lax.rsqrt(jnp.mean(widened * widened, axis=-1, keepdims=True) + 1e-06)
    return (widened * inverse * norm_gain.astype(jnp.float32)).astype(jnp.bfloat16)


def attend_kernel(q_ref, ko_ref, vo_ref, ka_ref, va_ref, kb_ref, vb_ref, bias_ref, out_ref):
    inv_root = 1.0 / math.sqrt(HD)
    q = q_ref[...]
    contract = (((1,), (1,)), ((), ()))
    own = lax.dot_general(q, ko_ref[...], contract, preferred_element_type=jnp.float32) * inv_root
    halves = []
    for index, (k_ref, v_ref) in enumerate(((ka_ref, va_ref), (kb_ref, vb_ref))):
        shards, ctx_rows, width = k_ref.shape
        keys = k_ref[...].reshape(shards * ctx_rows, width)
        values = v_ref[...].reshape(shards * ctx_rows, width)
        far = lax.dot_general(q, keys, contract, preferred_element_type=jnp.float32) * inv_root
        halves.append((far + bias_ref[index], values))
    highest = jnp.max(own, axis=-1, keepdims=True)
    for far, ignored in halves:
        highest = jnp.maximum(highest, jnp.max(far, axis=-1, keepdims=True))
    own_w = jnp.exp(own - highest)
    totals = jnp.sum(own_w, axis=-1, keepdims=True)
    mixture = jnp.dot(own_w.astype(jnp.bfloat16), vo_ref[...], preferred_element_type=jnp.float32)
    for far, values in halves:
        far_w = jnp.exp(far - highest)
        totals = totals + jnp.sum(far_w, axis=-1, keepdims=True)
        mixture = mixture + jnp.dot(far_w.astype(jnp.bfloat16), values, preferred_element_type=jnp.float32)
    out_ref[...] = (mixture / totals).astype(out_ref.dtype)


def attend(q_rot, k_rot, value_rows, own_half, other_half, bias, key_block, value_block):
    passes, rows, width = q_rot.shape
    heads = width // HD
    shards, ignored, lanes = own_half.shape
    ctx_rows = bias.shape[2] // shards
    cache_spec_k = pl.BlockSpec((shards, ctx_rows, lanes), lambda p, h: (0, key_block, 0))
    cache_spec_v = pl.BlockSpec((shards, ctx_rows, lanes), lambda p, h: (0, value_block, 0))
    ctx = 2 * shards * ctx_rows
    return pl.pallas_call(
        attend_kernel,
        grid=(passes, heads),
        in_specs=[
            pl.BlockSpec((None, rows, HD), lambda p, h: (p, 0, h)),
            pl.BlockSpec((None, rows, HD), lambda p, h: (p, 0, 0)),
            pl.BlockSpec((None, rows, HD), lambda p, h: (p, 0, 0)),
            cache_spec_k,
            cache_spec_v,
            cache_spec_k,
            cache_spec_v,
            pl.BlockSpec(bias.shape, lambda p, h: (0, 0, 0)),
        ],
        out_specs=pl.BlockSpec((None, rows, HD), lambda p, h: (p, 0, h)),
        out_shape=jax.ShapeDtypeStruct((passes, rows, width), jnp.bfloat16),
        cost_estimate=pl.CostEstimate(
            flops=4 * passes * heads * rows * (ctx + rows) * HD,
            transcendentals=passes * heads * rows * (ctx + rows),
            bytes_accessed=2 * (2 * ctx * HD + 4 * passes * rows * width),
        ),
    )(q_rot, k_rot, value_rows, own_half, own_half, other_half, other_half, bias)


def local(
    embeds,
    given_embeds,
    accept,
    lengths,
    block_keep,
    norm_gain,
    w_query,
    b_query,
    w_key,
    b_key,
    w_value,
    b_value,
    cache_keys,
    cache_values,
):
    local_kv = w_key.shape[1] // HD
    block_rows = embeds.shape[0]
    ctx_rows = cache_keys.shape[0]
    q_cols = w_query.shape[1]
    w_rows = w_query.shape[0]

    tp_size = lax.axis_size("tp")
    me_tp = lax.axis_index("tp")
    mine = jnp.stack([embeds, given_embeds])
    pieces = [mine]
    for shift in range(1, tp_size):
        pairs = [(i, (i - shift) % tp_size) for i in range(tp_size)]
        pieces.append(lax.ppermute(mine, "tp", pairs))
    ordered = jnp.roll(jnp.stack(pieces), me_tp, axis=0)
    both = jnp.concatenate([ordered[i] for i in range(tp_size)], axis=-1)
    first_rows, given_rows = both[0], both[1]

    w_parts = [w_query[:, j * HD : (j + 1) * HD] for j in range(q_cols // HD)] + [w_key, w_value]
    w_len = len(w_parts) * w_rows
    key_block = -(-w_len // ctx_rows)
    value_block = key_block + 1
    used = (value_block + 1) * ctx_rows
    total_blocks = -(-used // w_rows)
    lead = jnp.zeros((key_block * ctx_rows - w_len, HD), w_query.dtype)
    tail = jnp.zeros((total_blocks * w_rows - used, HD), w_query.dtype)
    packed = jnp.concatenate(w_parts + [lead, cache_keys, cache_values, tail], axis=0)
    own_half = lax.all_gather(packed, "chip", axis=0, tiled=False)
    other_half = lax.ppermute(own_half, "core", [(0, 1), (1, 0)])
    chips = own_half.shape[0]
    me_core = lax.axis_index("core")

    revised = jnp.where(accept[:, None] == 1, given_rows, first_rows)
    normed = normalize(jnp.concatenate([first_rows, revised], axis=0), norm_gain)
    normed4 = normed.reshape(normed.shape[0], chips, 2, w_rows)
    proj = None
    for half, core in ((own_half, me_core), (other_half, 1 - me_core)):
        part = jnp.einsum(
            "rsi,sjic->rjc",
            lax.dynamic_index_in_dim(normed4, core, axis=2, keepdims=False),
            half.reshape(chips, total_blocks, w_rows, HD),
            preferred_element_type=jnp.float32,
        )
        proj = part if proj is None else proj + part
    queries = proj[:, : q_cols // HD, :].reshape(-1, q_cols) + b_query.astype(jnp.float32)
    key_proj = proj[:, q_cols // HD, :] + b_key.astype(jnp.float32)
    value_proj = proj[:, q_cols // HD + 1, :] + b_value.astype(jnp.float32)
    length = lengths[0]
    keep_row = block_keep[0]
    positions = length.astype(jnp.float32) + jnp.arange(block_rows, dtype=jnp.float32)
    q_rot = rotate(queries.reshape(2, block_rows, q_cols // HD, HD), positions).astype(jnp.bfloat16)
    k_rot = rotate(key_proj.reshape(2, block_rows, local_kv, HD), positions).astype(jnp.bfloat16)
    value_rows = value_proj.astype(jnp.bfloat16)

    blocks_all = keep_row.shape[0]
    cache_index = jnp.arange(blocks_all * ctx_rows, dtype=jnp.int32).reshape(chips, 2, ctx_rows)
    kept = jnp.broadcast_to(keep_row.reshape(chips, 2, 1), cache_index.shape) == 1
    visible = (cache_index < length) & kept
    bias3 = jnp.where(visible, 0.0, -jnp.inf).astype(jnp.float32)
    bias = jnp.stack(
        [
            lax.dynamic_index_in_dim(bias3, me_core, axis=1, keepdims=False).reshape(1, -1),
            lax.dynamic_index_in_dim(bias3, 1 - me_core, axis=1, keepdims=False).reshape(1, -1),
        ]
    )
    attended = attend(
        q_rot.reshape(2, block_rows, q_cols),
        k_rot.reshape(2, block_rows, local_kv * HD),
        value_rows.reshape(2, block_rows, local_kv * HD),
        own_half,
        other_half,
        bias,
        key_block,
        value_block,
    )
    return (attended[0], attended[1])


def solution(mesh):
    blk_size, tp_size = mesh.devices.shape
    fine = Mesh(mesh.devices.reshape(blk_size // 2, 2, tp_size), ("chip", "core", "tp"))
    rows = ("chip", "core")
    return jax.shard_map(
        local,
        mesh=fine,
        in_specs=(
            P(rows, "tp"),
            P(rows, "tp"),
            P(rows),
            P(rows),
            P(rows, None),
            P(),
            P(rows, "tp"),
            P("tp"),
            P(rows, "tp"),
            P("tp"),
            P(rows, "tp"),
            P("tp"),
            P(rows, "tp"),
            P(rows, "tp"),
        ),
        out_specs=(P(rows, "tp"), P(rows, "tp")),
        check_vma=False,
    )
```

time: 236 us -> 274 us (1.16)
  the two profiles are of different devices: /device:TPU:1 before, /device:TPU:35 now
where the time goes in v3:
time: 274 us; the launch traced here: 272 us
  waiting for transfers between devices  145 us (53%)
  starting transfers between devices  48.4 us (18%)
  local copies, waits for them, and re-layouts  34.8 us (13%)
  Pallas kernels  16 us (6%)
  between operations  15 us (5%)
  other arithmetic  9.46 us (3%)
  matrix products  3.8 us (1%)
    all_gather x1, waiting for transfers between devices, local(): own_half = lax.all_gather(packed, 'chip', axis=0, tiled=False)  103 us
    ppermute x7, waiting for transfers between devices, local(): pieces.append(lax.ppermute(mine, 'tp', pairs))  42.1 us
    ppermute x7, starting transfers between devices, local(): pieces.append(lax.ppermute(mine, 'tp', pairs))  29.7 us
    unnamed x40, local copies, waits for them, and re-layouts  28.2 us
    ppermute x1, starting transfers between devices, local(): other_half = lax.ppermute(own_half, 'core', [(0, 1), (1, 0)])  18.8 us
    pallas_call x1, Pallas kernels, attend(): pl.pallas_call(attend_kernel, grid=(passes, heads), in_specs=[pl.BlockSpe...  16 us
  transfers between devices with their start and end apart: 9, of which 4 were waited for; matrix products, arithmetic and copies ran while one was open for 12% of the time, Pallas kernels for 0%

profile of v3, /device:TPU:35, one launch (start us, length us, event | category | flops | bytes accessed | tf_op | source)
XLA Modules:
  0.0 272.5 jit_solution(7866244011331187107)
XLA Ops:
  8.7 0.7 constant_dynamic-update-slice_fusion.8
  9.4 0.7 constant_dynamic-update-slice_fusion.7
  10.1 0.7 constant_dynamic-update-slice_fusion.6
  10.9 0.7 constant_dynamic-update-slice_fusion.5
  14.5 1.1 copy.31
  15.6 1.1 copy.32
  16.7 2.2 collective-permute-start
  18.9 3.6 %collective-permute-start.1 = (bf16[2,128,640]{1,2,0:T(8,128)(2,1)S(1)}, bf16[2,128,640]{1,2,0:T(8,128)(2,1)S(1)}, u32[]{:S(2)}, u32[]{:S(2)}) collective-permute-start(bf16[2,128,640]{1,2,0:T(8,128)(2,1)S(1)} %pad_maximum_fusion), channel_id=1, source_target_pairs={{0,6},{1,7},{2,0},{3,1},{4,2},{5,3},{6,4},{7,5},{8,14},{9,15},{10,... | collective-permute-start | bytes 983048 | tf_op jit(solution)/shard_map/ppermute | solution.py:121
  22.5 8.7 %collective-permute-start.2 = (bf16[2,128,640]{1,2,0:T(8,128)(2,1)S(1)}, bf16[2,128,640]{1,2,0:T(8,128)(2,1)S(1)}, u32[]{:S(2)}, u32[]{:S(2)}) collective-permute-start(bf16[2,128,640]{1,2,0:T(8,128)(2,1)S(1)} %pad_maximum_fusion), channel_id=1, source_target_pairs={{0,5},{1,6},{2,7},{3,0},{4,1},{5,2},{6,3},{7,4},{8,13},{9,14},{10,... | collective-permute-start | bytes 983048 | tf_op jit(solution)/shard_map/ppermute | solution.py:121
  31.2 1.9 collective-permute-start.3
  33.1 6.9 %collective-permute-start.4 = (bf16[2,128,640]{1,2,0:T(8,128)(2,1)S(1)}, bf16[2,128,640]{1,2,0:T(8,128)(2,1)S(1)}, u32[]{:S(2)}, u32[]{:S(2)}) collective-permute-start(bf16[2,128,640]{1,2,0:T(8,128)(2,1)S(1)} %pad_maximum_fusion), channel_id=1, source_target_pairs={{0,3},{1,4},{2,5},{3,6},{4,7},{5,0},{6,1},{7,2},{8,11},{9,12},{10,... | collective-permute-start | bytes 983048 | tf_op jit(solution)/shard_map/ppermute | solution.py:121
  40.1 0.8 reshape.163
  46.4 0.8 bitcast_dynamic-update-slice_fusion.14
  47.2 1.9 collective-permute-start.5
  49.1 0.8 bitcast_dynamic-update-slice_fusion.12
  49.9 4.4 %collective-permute-start.6 = (bf16[2,128,640]{1,2,0:T(8,128)(2,1)S(1)}, bf16[2,128,640]{1,2,0:T(8,128)(2,1)S(1)}, u32[]{:S(2)}, u32[]{:S(2)}) collective-permute-start(bf16[2,128,640]{1,2,0:T(8,128)(2,1)S(1)} %pad_maximum_fusion), channel_id=1, source_target_pairs={{0,1},{1,2},{2,3},{3,4},{4,5},{5,6},{6,7},{7,0},{8,9},{9,10},{10,1... | collective-permute-start | bytes 983048 | tf_op jit(solution)/shard_map/ppermute | solution.py:121
  54.3 0.7 bitcast_dynamic-update-slice_fusion.10
  55.1 11.2 %collective-permute-done.2 = bf16[2,128,640]{1,2,0:T(8,128)(2,1)S(1)} collective-permute-done((bf16[2,128,640]{1,2,0:T(8,128)(2,1)S(1)}, bf16[2,128,640]{1,2,0:T(8,128)(2,1)S(1)}, u32[]{:S(2)}, u32[]{:S(2)}) %collective-permute-start.2) | collective-permute-done | bytes 327712 | tf_op jit(solution)/shard_map/ppermute | solution.py:121
  66.2 0.8 bitcast_dynamic-update-slice_fusion.8
  67.0 0.7 bitcast_dynamic-update-slice_fusion.6
  67.7 25.1 %collective-permute-done.4 = bf16[2,128,640]{1,2,0:T(8,128)(2,1)S(1)} collective-permute-done((bf16[2,128,640]{1,2,0:T(8,128)(2,1)S(1)}, bf16[2,128,640]{1,2,0:T(8,128)(2,1)S(1)}, u32[]{:S(2)}, u32[]{:S(2)}) %collective-permute-start.4) | collective-permute-done | bytes 327712 | tf_op jit(solution)/shard_map/ppermute | solution.py:121
  92.9 0.8 bitcast_dynamic-update-slice_fusion.4
  93.6 5.8 %collective-permute-done.5 = bf16[2,128,640]{1,2,0:T(8,128)(2,1)S(1)} collective-permute-done((bf16[2,128,640]{1,2,0:T(8,128)(2,1)S(1)}, bf16[2,128,640]{1,2,0:T(8,128)(2,1)S(1)}, u32[]{:S(2)}, u32[]{:S(2)}) %collective-permute-start.5) | collective-permute-done | bytes 327712 | tf_op jit(solution)/shard_map/ppermute | solution.py:121
  99.4 0.8 bitcast_dynamic-update-slice_fusion.2
  100.2 0.8 bitcast_dynamic-update-slice_fusion
  101.0 0.8 bitcast_dynamic-update-slice_fusion.15
  101.8 0.8 bitcast_dynamic-update-slice_fusion.13
  103.3 0.8 bitcast_dynamic-update-slice_fusion.9
  104.0 102.8 %all-gather.3.cloned.1.call-done = bf16[23040,128]{1,0:T(8,128)(2,1)} async-done(((bf16[720,128]{1,0:T(8,128)(2,1)}), bf16[23040,128]{1,0:T(8,128)(2,1)}) %all-gather.3.cloned.1.call-update) | async-done | bytes 5898256 | tf_op jit(solution)/shard_map/all_gather | solution.py:135
  206.9 18.8 %collective-permute-start.7 = (bf16[32,720,128]{2,1,0:T(8,128)(2,1)}, bf16[32,720,128]{2,1,0:T(8,128)(2,1)S(1)}, u32[]{:S(2)}, u32[]{:S(2)}) collective-permute-start(bf16[32,720,128]{2,1,0:T(8,128)(2,1)} %bitcast.116), channel_id=1, source_target_pairs={{0,8},{8,0},{1,9},{9,1},{2,10},{10,2},{3,11},{11,3},{4,12},{12,4},... | collective-permute-start | bytes 17694728 | tf_op jit(solution)/shard_map/ppermute | solution.py:136
  225.6 0.8 bitcast_dynamic-update-slice_fusion.7
  226.4 0.8 bitcast_dynamic-update-slice_fusion.5
  227.2 0.8 bitcast_dynamic-update-slice_fusion.3
  227.9 0.8 bitcast_dynamic-update-slice_fusion.1
  228.7 1.0 fusion.12
  229.7 1.0 fusion.11
  230.7 1.0 fusion.10
  231.8 1.0 fusion.9
  232.8 1.0 fusion.8
  233.8 1.0 fusion.7
  234.8 1.0 fusion.6
  235.9 1.0 fusion.5
  238.4 0.9 multiply_convert_fusion
  240.4 1.9 convolution_bitcast_fusion.1
  242.3 1.9 fusion
  245.5 0.9 copy.39.q_ref
  247.9 16.0 %shard_map.149 = bf16[2,128,640]{2,1,0:T(8,128)(2,1)} custom-call(bf16[2,128,640]{2,1,0:T(8,128)(2,1)} %copy.39.q_ref, bf16[2,128,128]{2,1,0:T(8,128)(2,1)} %pad_maximum_fusion.2.ko_ref, bf16[2,128,128]{2,1,0:T(8,128)(2,1)} %add_convert_fusion.1.vo_ref, bf16[32,720,128]{2,1,0:T(8,128)(2,1)} %bitcast.117, bf16[32,720,128]{2,1,0:T(8,128)(2,1)} %bitcast.118, ...), custom_call_target="tpu_custom_call" | custom-call | flops 2768240640 | bytes 3407872 | tf_op jit(solution)/shard_map/pallas_call | solution.py:70
  263.9 1.7 slice_bitcast_fusion
  (57 shorter events, 15.2 us)
Async XLA Ops:
  7.2 199.7 %all-gather.3.cloned.1.call-start = ((), (), s32[]{:S(2)}) async-start(), calls=%async_computation | async-start | bytes 6082560 | tf_op jit(solution)/shard_map/all_gather | solution.py:135
  13.8 0.7 copy-start.1
  16.7 30.5 %collective-permute-start = (bf16[2,128,640]{1,2,0:T(8,128)(2,1)S(1)}, bf16[2,128,640]{1,2,0:T(8,128)(2,1)S(1)}, u32[]{:S(2)}, u32[]{:S(2)}) collective-permute-start(bf16[2,128,640]{1,2,0:T(8,128)(2,1)S(1)} %pad_maximum_fusion), channel_id=1, source_target_pairs={{0,7},{1,0},{2,1},{3,2},{4,3},{5,4},{6,5},{7,6},{8,15},{9,8},{10,9... | collective-permute-start | bytes 983048 | tf_op jit(solution)/shard_map/ppermute | solution.py:121
  18.9 31.0 %collective-permute-start.1 = (bf16[2,128,640]{1,2,0:T(8,128)(2,1)S(1)}, bf16[2,128,640]{1,2,0:T(8,128)(2,1)S(1)}, u32[]{:S(2)}, u32[]{:S(2)}) collective-permute-start(bf16[2,128,640]{1,2,0:T(8,128)(2,1)S(1)} %pad_maximum_fusion), channel_id=1, source_target_pairs={{0,6},{1,7},{2,0},{3,1},{4,2},{5,3},{6,4},{7,5},{8,14},{9,15},{10,... | collective-permute-start | bytes 983048 | tf_op jit(solution)/shard_map/ppermute | solution.py:121
  22.5 43.7 %collective-permute-start.2 = (bf16[2,128,640]{1,2,0:T(8,128)(2,1)S(1)}, bf16[2,128,640]{1,2,0:T(8,128)(2,1)S(1)}, u32[]{:S(2)}, u32[]{:S(2)}) collective-permute-start(bf16[2,128,640]{1,2,0:T(8,128)(2,1)S(1)} %pad_maximum_fusion), channel_id=1, source_target_pairs={{0,5},{1,6},{2,7},{3,0},{4,1},{5,2},{6,3},{7,4},{8,13},{9,14},{10,... | collective-permute-start | bytes 983048 | tf_op jit(solution)/shard_map/ppermute | solution.py:121
  31.2 35.8 %collective-permute-start.3 = (bf16[2,128,640]{1,2,0:T(8,128)(2,1)S(1)}, bf16[2,128,640]{1,2,0:T(8,128)(2,1)S(1)}, u32[]{:S(2)}, u32[]{:S(2)}) collective-permute-start(bf16[2,128,640]{1,2,0:T(8,128)(2,1)S(1)} %pad_maximum_fusion), channel_id=1, source_target_pairs={{0,4},{1,5},{2,6},{3,7},{4,0},{5,1},{6,2},{7,3},{8,12},{9,13},{10,... | collective-permute-start | bytes 983048 | tf_op jit(solution)/shard_map/ppermute | solution.py:121
  33.1 59.7 %collective-permute-start.4 = (bf16[2,128,640]{1,2,0:T(8,128)(2,1)S(1)}, bf16[2,128,640]{1,2,0:T(8,128)(2,1)S(1)}, u32[]{:S(2)}, u32[]{:S(2)}) collective-permute-start(bf16[2,128,640]{1,2,0:T(8,128)(2,1)S(1)} %pad_maximum_fusion), channel_id=1, source_target_pairs={{0,3},{1,4},{2,5},{3,6},{4,7},{5,0},{6,1},{7,2},{8,11},{9,12},{10,... | collective-permute-start | bytes 983048 | tf_op jit(solution)/shard_map/ppermute | solution.py:121
  47.2 52.2 %collective-permute-start.5 = (bf16[2,128,640]{1,2,0:T(8,128)(2,1)S(1)}, bf16[2,128,640]{1,2,0:T(8,128)(2,1)S(1)}, u32[]{:S(2)}, u32[]{:S(2)}) collective-permute-start(bf16[2,128,640]{1,2,0:T(8,128)(2,1)S(1)} %pad_maximum_fusion), channel_id=1, source_target_pairs={{0,2},{1,3},{2,4},{3,5},{4,6},{5,7},{6,0},{7,1},{8,10},{9,11},{10,... | collective-permute-start | bytes 983048 | tf_op jit(solution)/shard_map/ppermute | solution.py:121
  49.9 50.3 %collective-permute-start.6 = (bf16[2,128,640]{1,2,0:T(8,128)(2,1)S(1)}, bf16[2,128,640]{1,2,0:T(8,128)(2,1)S(1)}, u32[]{:S(2)}, u32[]{:S(2)}) collective-permute-start(bf16[2,128,640]{1,2,0:T(8,128)(2,1)S(1)} %pad_maximum_fusion), channel_id=1, source_target_pairs={{0,1},{1,2},{2,3},{3,4},{4,5},{5,6},{6,7},{7,0},{8,9},{9,10},{10,1... | collective-permute-start | bytes 983048 | tf_op jit(solution)/shard_map/ppermute | solution.py:121
  206.9 35.4 %collective-permute-start.7 = (bf16[32,720,128]{2,1,0:T(8,128)(2,1)}, bf16[32,720,128]{2,1,0:T(8,128)(2,1)S(1)}, u32[]{:S(2)}, u32[]{:S(2)}) collective-permute-start(bf16[32,720,128]{2,1,0:T(8,128)(2,1)} %bitcast.116), channel_id=1, source_target_pairs={{0,8},{8,0},{1,9},{9,1},{2,10},{10,2},{3,11},{11,3},{4,12},{12,4},... | collective-permute-start | bytes 17694728 | tf_op jit(solution)/shard_map/ppermute | solution.py:136
  237.5 2.2 slice-start
  238.2 2.2 slice-start.1
  242.3 2.6 copy-start
Sparse Core Ops, SparseCore 0:
  14.6 192.1 all-gather.2

commit v4 on v1

--- a/solution.py
+++ b/solution.py
@@ -5,6 +5,7 @@
 from jax import lax
 from jax.experimental import pallas as pl
 from jax.experimental.pallas import tpu as pltpu
+from jax.sharding import Mesh
 from jax.sharding import PartitionSpec as P
 
 KVH = 8
@@ -74,6 +75,11 @@
     )(q_rot, k_rot, value_rows, cache_k, cache_v, bias)
 
 
+def shifted(x, axis, size, shift):
+    pairs = [(j, (j - shift) % size) for j in range(size)]
+    return lax.ppermute(x, axis, pairs)
+
+
 def local(
     embeds,
     given_embeds,
@@ -96,27 +102,61 @@
     q_cols = w_query.shape[1]
     w_rows = w_query.shape[0]
 
-    both = lax.all_gather(jnp.stack([embeds, given_embeds]), "tp", axis=2, tiled=True)
+    tp_size = lax.axis_size("tp")
+    me_tp = lax.axis_index("tp")
+    mine = jnp.stack([embeds, given_embeds])
+    pieces = [mine] + [shifted(mine, "tp", tp_size, k) for k in range(1, tp_size)]
+    ordered = jnp.roll(jnp.stack(pieces), me_tp, axis=0)
+    both = jnp.concatenate([ordered[i] for i in range(tp_size)], axis=-1)
     first_rows, given_rows = both[0], both[1]
 
-    w_piece = jnp.concatenate([w_query, w_key, w_value], axis=1)
-    c_piece = jnp.concatenate([cache_keys, cache_values], axis=1)
-    w_size = w_piece.size
-    packed = jnp.concatenate([w_piece.reshape(-1), c_piece.reshape(-1)])
-    gathered = lax.all_gather(packed, "blk", axis=0, tiled=False)
-    shards = gathered.shape[0]
-    w_all = gathered[:, :w_size].reshape(shards * w_rows, w_piece.shape[1])
-    c_all = gathered[:, w_size:].reshape(shards * ctx_rows, c_piece.shape[1])
-    cache_k = c_all[:, : local_kv * HD]
-    cache_v = c_all[:, local_kv * HD :]
+    w_parts = [w_query[:, j * HD : (j + 1) * HD] for j in range(q_cols // HD)] + [w_key, w_value]
+    w_len = len(w_parts) * w_rows
+    key_start = -(-w_len // ctx_rows) * ctx_rows
+    value_start = key_start + ctx_rows
+    used = value_start + ctx_rows
+    total_blocks = -(-used // w_rows)
+    lead = jnp.zeros((key_start - w_len, HD), w_query.dtype)
+    tail = jnp.zeros((total_blocks * w_rows - used, HD), w_query.dtype)
+    packed = jnp.concatenate(w_parts + [lead, cache_keys, cache_values, tail], axis=0)
+
+    n_ylo = lax.axis_size("ylo")
+    n_z = lax.axis_size("z")
+    me_ylo = lax.axis_index("ylo")
+    me_z = lax.axis_index("z")
+    me_core = lax.axis_index("core")
+
+    line = jnp.stack([packed] + [shifted(packed, "ylo", n_ylo, k) for k in range(1, n_ylo)])
+    arrived = [(0, line)]
+    forward = line
+    backward = line
+    for step in range(1, n_z // 2 + 1):
+        forward = shifted(forward, "z", n_z, -1)
+        arrived.append((-step, forward))
+        if step < n_z - n_z // 2:
+            backward = shifted(backward, "z", n_z, 1)
+            arrived.append((step, backward))
+    held = [(offset, 0, piece) for offset, piece in arrived]
+    held += [(offset, 1, shifted(piece, "core", 2, 1)) for offset, piece in arrived]
 
     revised = jnp.where(accept[:, None] == 1, given_rows, first_rows)
     normed = normalize(jnp.concatenate([first_rows, revised], axis=0), norm_gain)
-    proj = jnp.dot(normed, w_all, preferred_element_type=jnp.float32)
-    queries = proj[:, :q_cols] + b_query.astype(jnp.float32)
-    key_proj = proj[:, q_cols : q_cols + local_kv * HD] + b_key.astype(jnp.float32)
-    value_proj = proj[:, q_cols + local_kv * HD :] + b_value.astype(jnp.float32)
-
+    normed5 = normed.reshape(normed.shape[0], n_ylo, n_z, 2, w_rows)
+    normed5 = jnp.roll(normed5, -me_ylo, axis=1)
+    normed5 = jnp.roll(normed5, -me_z, axis=2)
+    normed5 = jnp.roll(normed5, -me_core, axis=3)
+    proj = None
+    for offset, core, piece in held:
+        part = jnp.einsum(
+            "rki,kjid->rjd",
+            normed5[:, :, offset % n_z, core, :],
+            piece.reshape(n_ylo, total_blocks, w_rows, HD),
+            preferred_element_type=jnp.float32,
+        )
+        proj = part if proj is None else proj + part
+    queries = proj[:, : q_cols // HD, :].reshape(-1, q_cols) + b_query.astype(jnp.float32)
+    key_proj = proj[:, q_cols // HD, :] + b_key.astype(jnp.float32)
+    value_proj = proj[:, q_cols // HD + 1, :] + b_value.astype(jnp.float32)
     length = lengths[0]
     keep_row = block_keep[0]
     positions = length.astype(jnp.float32) + jnp.arange(block_rows, dtype=jnp.float32)
@@ -124,11 +164,21 @@
     k_rot = rotate(key_proj.reshape(2, block_rows, local_kv, HD), positions).astype(jnp.bfloat16)
     value_rows = value_proj.astype(jnp.bfloat16)
 
-    total_ctx = shards * ctx_rows
-    cache_index = jnp.arange(total_ctx, dtype=jnp.int32)
-    visible = (cache_index < length) & (jnp.repeat(keep_row, CB, total_repeat_length=total_ctx) == 1)
-    bias = jnp.where(visible, 0.0, -jnp.inf).astype(jnp.float32).reshape(1, total_ctx)
-
+    blocks_all = keep_row.shape[0]
+    cache_index = jnp.arange(blocks_all * ctx_rows, dtype=jnp.int32).reshape(n_ylo, n_z, 2, ctx_rows)
+    kept = jnp.broadcast_to(keep_row.reshape(n_ylo, n_z, 2, 1), cache_index.shape) == 1
+    visible = (cache_index < length) & kept
+    bias4 = jnp.where(visible, 0.0, -jnp.inf).astype(jnp.float32)
+    bias4 = jnp.roll(bias4, -me_ylo, axis=0)
+    bias4 = jnp.roll(bias4, -me_z, axis=1)
+    bias4 = jnp.roll(bias4, -me_core, axis=2)
+    bias = jnp.concatenate([bias4[:, offset % n_z, core, :].reshape(1, -1) for offset, core, ignored in held], axis=1)
+    cache_k = jnp.concatenate(
+        [piece[:, key_start:value_start, :].reshape(-1, HD) for ignored, ignored2, piece in held], axis=0
+    )
+    cache_v = jnp.concatenate(
+        [piece[:, value_start:used, :].reshape(-1, HD) for ignored, ignored2, piece in held], axis=0
+    )
     attended = attend(
         q_rot.reshape(2, block_rows, q_cols),
         k_rot.reshape(2, block_rows, local_kv * HD),
@@ -141,25 +191,28 @@
 
 
 def solution(mesh):
+    blk_size, tp_size = mesh.devices.shape
+    fine = Mesh(mesh.devices.reshape(4, blk_size // 8, 2, tp_size), ("ylo", "z", "core", "tp"))
+    rows = ("ylo", "z", "core")
     return jax.shard_map(
         local,
-        mesh=mesh,
+        mesh=fine,
         in_specs=(
-            P("blk", "tp"),
-            P("blk", "tp"),
-            P("blk"),
-            P("blk"),
-            P("blk", None),
+            P(rows, "tp"),
+            P(rows, "tp"),
+            P(rows),
+            P(rows),
+            P(rows, None),
             P(),
-            P("blk", "tp"),
+            P(rows, "tp"),
             P("tp"),
-            P("blk", "tp"),
+            P(rows, "tp"),
             P("tp"),
-            P("blk", "tp"),
+            P(rows, "tp"),
             P("tp"),
-            P("blk", "tp"),
-            P("blk", "tp"),
+            P(rows, "tp"),
+            P(rows, "tp"),
         ),
-        out_specs=(P("blk", "tp"), P("blk", "tp")),
+        out_specs=(P(rows, "tp"), P(rows, "tp")),
         check_vma=False,
     )

time: 308 us -> 237 us (0.77)
  the two profiles are of different devices: /device:TPU:1 before, /device:TPU:57 now
where the time goes in v4:
time: 237 us; the launch traced here: 236 us
  starting transfers between devices  97.4 us (41%)
  waiting for transfers between devices  67.5 us (28%)
  local copies, waits for them, and re-layouts  34.8 us (15%)
  Pallas kernels  15.5 us (7%)
  other arithmetic  9.25 us (4%)
  matrix products  8.75 us (4%)
  between operations  2.46 us (1%)
    ppermute x25, starting transfers between devices, shifted(): return lax.ppermute(x, axis, pairs)  97.4 us
    ppermute x25, waiting for transfers between devices, shifted(): return lax.ppermute(x, axis, pairs)  67.5 us
    unnamed x91, local copies, waits for them, and re-layouts  26.2 us
    pallas_call x1, Pallas kernels, attend(): pl.pallas_call(attend_kernel, grid=(passes, heads), in_specs=[pl.BlockSpe...  15.5 us
    dot_general x16, matrix products, local(): jnp.einsum('rki,kjid->rjd', normed5[:, :, offset % n_z, core, :], piece.r...  8.75 us
  transfers between devices with their start and end apart: 25, of which 7 were waited for; matrix products, arithmetic and copies ran while one was open for 17% of the time, Pallas kernels for 0%

profile of v4, /device:TPU:57, one launch (start us, length us, event | category | flops | bytes accessed | tf_op | source)
XLA Modules:
  0.0 235.7 jit_solution(598128373422272360)
XLA Ops:
  7.3 4.5 %collective-permute-start.9 = (bf16[720,128]{1,0:T(8,128)(2,1)S(1)}, bf16[720,128]{1,0:T(8,128)(2,1)S(1)}, u32[]{:S(2)}, u32[]{:S(2)}) collective-permute-start(bf16[720,128]{1,0:T(8,128)(2,1)S(1)} %constant_dynamic-update-slice_fusion), channel_id=1, source_target_pairs={{0,128},{128,256},{256,384},{384,0},{1,129},{129,257},{257,385},{3... | collective-permute-start | bytes 552968 | tf_op jit(solution)/shard_map/ppermute | solution.py:80
  11.8 1.9 collective-permute-start.8
  13.8 2.6 %collective-permute-start.7 = (bf16[720,128]{1,0:T(8,128)(2,1)S(1)}, bf16[720,128]{1,0:T(8,128)(2,1)S(1)}, u32[]{:S(2)}, u32[]{:S(2)}) collective-permute-start(bf16[720,128]{1,0:T(8,128)(2,1)S(1)} %constant_dynamic-update-slice_fusion), channel_id=1, source_target_pairs={{0,384},{128,0},{256,128},{384,256},{1,385},{129,1},{257,129},{385... | collective-permute-start | bytes 552968 | tf_op jit(solution)/shard_map/ppermute | solution.py:80
  16.4 1.1 copy.45
  17.4 1.1 copy.44
  18.6 4.8 %collective-permute-start = (bf16[2,128,640]{1,2,0:T(8,128)(2,1)S(1)}, bf16[2,128,640]{1,2,0:T(8,128)(2,1)S(1)}, u32[]{:S(2)}, u32[]{:S(2)}) collective-permute-start(bf16[2,128,640]{1,2,0:T(8,128)(2,1)S(1)} %pad_maximum_fusion.1), channel_id=1, source_target_pairs={{0,7},{1,0},{2,1},{3,2},{4,3},{5,4},{6,5},{7,6},{8,15},{9,8},{10,9... | collective-permute-start | bytes 983048 | tf_op jit(solution)/shard_map/ppermute | solution.py:80
  23.4 2.4 %collective-permute-start.1 = (bf16[2,128,640]{1,2,0:T(8,128)(2,1)S(1)}, bf16[2,128,640]{1,2,0:T(8,128)(2,1)S(1)}, u32[]{:S(2)}, u32[]{:S(2)}) collective-permute-start(bf16[2,128,640]{1,2,0:T(8,128)(2,1)S(1)} %pad_maximum_fusion.1), channel_id=1, source_target_pairs={{0,6},{1,7},{2,0},{3,1},{4,2},{5,3},{6,4},{7,5},{8,14},{9,15},{10,... | collective-permute-start | bytes 983048 | tf_op jit(solution)/shard_map/ppermute | solution.py:80
  31.3 6.9 %collective-permute-start.2 = (bf16[2,128,640]{1,2,0:T(8,128)(2,1)S(1)}, bf16[2,128,640]{1,2,0:T(8,128)(2,1)S(1)}, u32[]{:S(2)}, u32[]{:S(2)}) collective-permute-start(bf16[2,128,640]{1,2,0:T(8,128)(2,1)S(1)} %pad_maximum_fusion.1), channel_id=1, source_target_pairs={{0,5},{1,6},{2,7},{3,0},{4,1},{5,2},{6,3},{7,4},{8,13},{9,14},{10,... | collective-permute-start | bytes 983048 | tf_op jit(solution)/shard_map/ppermute | solution.py:80
  38.2 23.7 %collective-permute-done.8 = bf16[720,128]{1,0:T(8,128)(2,1)S(1)} collective-permute-done((bf16[720,128]{1,0:T(8,128)(2,1)S(1)}, bf16[720,128]{1,0:T(8,128)(2,1)S(1)}, u32[]{:S(2)}, u32[]{:S(2)}) %collective-permute-start.8) | collective-permute-done | bytes 184352 | tf_op jit(solution)/shard_map/ppermute | solution.py:80
  62.0 1.9 collective-permute-start.3
  63.9 1.9 collective-permute-start.4
  66.0 1.9 collective-permute-start.5
  68.7 8.4 %collective-permute-start.6 = (bf16[2,128,640]{1,2,0:T(8,128)(2,1)S(1)}, bf16[2,128,640]{1,2,0:T(8,128)(2,1)S(1)}, u32[]{:S(2)}, u32[]{:S(2)}) collective-permute-start(bf16[2,128,640]{1,2,0:T(8,128)(2,1)S(1)} %pad_maximum_fusion.1), channel_id=1, source_target_pairs={{0,1},{1,2},{2,3},{3,4},{4,5},{5,6},{6,7},{7,0},{8,9},{9,10},{10,1... | collective-permute-start | bytes 983048 | tf_op jit(solution)/shard_map/ppermute | solution.py:80
  77.9 10.7 %collective-permute-start.11 = (bf16[4,720,128]{2,1,0:T(8,128)(2,1)S(1)}, bf16[4,720,128]{2,1,0:T(8,128)(2,1)S(1)}, u32[]{:S(2)}, u32[]{:S(2)}) collective-permute-start(bf16[4,720,128]{2,1,0:T(8,128)(2,1)S(1)} %pad_maximum_fusion), channel_id=1, source_target_pairs={{0,112},{16,0},{32,16},{48,32},{64,48},{80,64},{96,80},{112,96},{1... | collective-permute-start | bytes 2211848 | tf_op jit(solution)/shard_map/ppermute | solution.py:80
  89.7 4.1 %collective-permute-start.10 = (bf16[4,720,128]{2,1,0:T(8,128)(2,1)S(1)}, bf16[4,720,128]{2,1,0:T(8,128)(2,1)S(1)}, u32[]{:S(2)}, u32[]{:S(2)}) collective-permute-start(bf16[4,720,128]{2,1,0:T(8,128)(2,1)S(1)} %pad_maximum_fusion), channel_id=1, source_target_pairs={{0,16},{16,32},{32,48},{48,64},{64,80},{80,96},{96,112},{112,0},{1... | collective-permute-start | bytes 2211848 | tf_op jit(solution)/shard_map/ppermute | solution.py:80
  94.5 3.0 %collective-permute-start.17 = (bf16[4,720,128]{2,1,0:T(8,128)(2,1)S(1)}, bf16[4,720,128]{2,1,0:T(8,128)(2,1)S(1)}, u32[]{:S(2)}, u32[]{:S(2)}) collective-permute-start(bf16[4,720,128]{2,1,0:T(8,128)(2,1)S(1)} %pad_maximum_fusion), channel_id=1, source_target_pairs={{0,8},{8,0},{1,9},{9,1},{2,10},{10,2},{3,11},{11,3},{4,12},{12,4},... | collective-permute-start | bytes 2211848 | tf_op jit(solution)/shard_map/ppermute | solution.py:80
  99.0 5.7 %collective-permute-done.6 = bf16[2,128,640]{1,2,0:T(8,128)(2,1)S(1)} collective-permute-done((bf16[2,128,640]{1,2,0:T(8,128)(2,1)S(1)}, bf16[2,128,640]{1,2,0:T(8,128)(2,1)S(1)}, u32[]{:S(2)}, u32[]{:S(2)}) %collective-permute-start.6) | collective-permute-done | bytes 327712 | tf_op jit(solution)/shard_map/ppermute | solution.py:80
  111.4 1.0 fusion.32
  112.4 1.0 fusion.31
  113.5 1.0 fusion.30
  114.5 1.0 fusion.29
  115.5 1.0 fusion.28
  116.5 1.0 fusion.27
  117.6 1.0 fusion.26
  118.6 1.0 fusion.25
  121.1 0.9 multiply_convert_fusion
  122.0 0.9 fusion.2
  122.9 0.9 fusion.1
  123.9 0.9 fusion
  126.5 9.9 %collective-permute-start.13 = (bf16[4,720,128]{2,1,0:T(8,128)(2,1)S(1)}, bf16[4,720,128]{2,1,0:T(8,128)(2,1)S(1)}, u32[]{:S(2)}, u32[]{:S(2)}) collective-permute-start(bf16[4,720,128]{2,1,0:T(8,128)(2,1)S(1)} %collective-permute-done.11), channel_id=1, source_target_pairs={{0,112},{16,0},{32,16},{48,32},{64,48},{80,64},{96,80},{112,96},{1... | collective-permute-start | bytes 2211848 | tf_op jit(solution)/shard_map/ppermute | solution.py:80
  136.4 1.9 collective-permute-start.12
  138.3 4.3 %collective-permute-start.19 = (bf16[4,720,128]{2,1,0:T(8,128)(2,1)S(1)}, bf16[4,720,128]{2,1,0:T(8,128)(2,1)S(1)}, u32[]{:S(2)}, u32[]{:S(2)}) collective-permute-start(bf16[4,720,128]{2,1,0:T(8,128)(2,1)S(1)} %collective-permute-done.11), channel_id=1, source_target_pairs={{0,8},{8,0},{1,9},{9,1},{2,10},{10,2},{3,11},{11,3},{4,12},{12,4},... | collective-permute-start | bytes 2211848 | tf_op jit(solution)/shard_map/ppermute | solution.py:80
  143.2 1.9 collective-permute-start.18
  145.1 4.9 %collective-permute-done.13 = bf16[4,720,128]{2,1,0:T(8,128)(2,1)S(1)} collective-permute-done((bf16[4,720,128]{2,1,0:T(8,128)(2,1)S(1)}, bf16[4,720,128]{2,1,0:T(8,128)(2,1)S(1)}, u32[]{:S(2)}, u32[]{:S(2)}) %collective-permute-start.13) | collective-permute-done | bytes 737312 | tf_op jit(solution)/shard_map/ppermute | solution.py:80
  150.0 5.3 %collective-permute-start.15 = (bf16[4,720,128]{2,1,0:T(8,128)(2,1)S(1)}, bf16[4,720,128]{2,1,0:T(8,128)(2,1)S(1)}, u32[]{:S(2)}, u32[]{:S(2)}) collective-permute-start(bf16[4,720,128]{2,1,0:T(8,128)(2,1)S(1)} %collective-permute-done.13), channel_id=1, source_target_pairs={{0,112},{16,0},{32,16},{48,32},{64,48},{80,64},{96,80},{112,96},{1... | collective-permute-start | bytes 2211848 | tf_op jit(solution)/shard_map/ppermute | solution.py:80
  155.3 5.2 %collective-permute-start.21 = (bf16[4,720,128]{2,1,0:T(8,128)(2,1)S(1)}, bf16[4,720,128]{2,1,0:T(8,128)(2,1)S(1)}, u32[]{:S(2)}, u32[]{:S(2)}) collective-permute-start(bf16[4,720,128]{2,1,0:T(8,128)(2,1)S(1)} %collective-permute-done.13), channel_id=1, source_target_pairs={{0,8},{8,0},{1,9},{9,1},{2,10},{10,2},{3,11},{11,3},{4,12},{12,4},... | collective-permute-start | bytes 2211848 | tf_op jit(solution)/shard_map/ppermute | solution.py:80
  160.6 1.9 collective-permute-start.14
  162.6 2.1 collective-permute-start.20
  166.9 14.9 %collective-permute-done.14 = bf16[4,720,128]{2,1,0:T(8,128)(2,1)S(1)} collective-permute-done((bf16[4,720,128]{2,1,0:T(8,128)(2,1)S(1)}, bf16[4,720,128]{2,1,0:T(8,128)(2,1)S(1)}, u32[]{:S(2)}, u32[]{:S(2)}) %collective-permute-start.14) | collective-permute-done | bytes 737312 | tf_op jit(solution)/shard_map/ppermute | solution.py:80
  183.0 2.7 %collective-permute-start.23 = (bf16[4,720,128]{2,1,0:T(8,128)(2,1)S(1)}, bf16[4,720,128]{2,1,0:T(8,128)(2,1)S(1)}, u32[]{:S(2)}, u32[]{:S(2)}) collective-permute-start(bf16[4,720,128]{2,1,0:T(8,128)(2,1)S(1)} %collective-permute-done.15), channel_id=1, source_target_pairs={{0,8},{8,0},{1,9},{9,1},{2,10},{10,2},{3,11},{11,3},{4,12},{12,4},... | collective-permute-start | bytes 2211848 | tf_op jit(solution)/shard_map/ppermute | solution.py:80
  185.7 1.9 collective-permute-start.22
  187.6 1.9 collective-permute-start.16
  190.6 17.6 %collective-permute-done.16 = bf16[4,720,128]{2,1,0:T(8,128)(2,1)S(1)} collective-permute-done((bf16[4,720,128]{2,1,0:T(8,128)(2,1)S(1)}, bf16[4,720,128]{2,1,0:T(8,128)(2,1)S(1)}, u32[]{:S(2)}, u32[]{:S(2)}) %collective-permute-start.16) | collective-permute-done | bytes 737312 | tf_op jit(solution)/shard_map/ppermute | solution.py:80
  209.1 3.3 %collective-permute-start.24 = (bf16[4,720,128]{2,1,0:T(8,128)(2,1)S(1)}, bf16[4,720,128]{2,1,0:T(8,128)(2,1)S(1)}, u32[]{:S(2)}, u32[]{:S(2)}) collective-permute-start(bf16[4,720,128]{2,1,0:T(8,128)(2,1)S(1)} %collective-permute-done.16), channel_id=1, source_target_pairs={{0,8},{8,0},{1,9},{9,1},{2,10},{10,2},{3,11},{11,3},{4,12},{12,4},... | collective-permute-start | bytes 2211848 | tf_op jit(solution)/shard_map/ppermute | solution.py:80
  213.0 1.1 fusion.16
  215.4 0.9 copy.69.q_ref
  218.5 15.5 %shard_map.149 = bf16[2,128,640]{2,1,0:T(8,128)(2,1)} custom-call(bf16[2,128,640]{2,1,0:T(8,128)(2,1)} %copy.69.q_ref, bf16[2,128,128]{2,1,0:T(8,128)(2,1)} %pad_maximum_fusion.3.ko_ref, bf16[2,128,128]{2,1,0:T(8,128)(2,1)} %add_convert_fusion.1.vo_ref, bf16[4096,128]{1,0:T(8,128)(2,1)} %get-tuple-element.65.kc_ref, ...), custom_call_target="tpu_custom_call" | custom-call | flops 2768240640 | bytes 3407872 | tf_op jit(solution)/shard_map/pallas_call | solution.py:57
  234.0 1.7 slice_bitcast_fusion
  (191 shorter events, 35.7 us)
Async XLA Ops:
  0.6 28.2 %copy-start.3 = (bf16[128]{0:T(256)(128)(2,1)S(1)}, bf16[128]{0:T(256)(128)(2,1)}, u32[]{:S(2)}) copy-start(bf16[128]{0:T(256)(128)(2,1)} %param.23) | copy-start | bytes 772
  0.6 28.6 %copy-start.4 = (bf16[128]{0:T(256)(128)(2,1)S(1)}, bf16[128]{0:T(256)(128)(2,1)}, u32[]{:S(2)}) copy-start(bf16[128]{0:T(256)(128)(2,1)} %param.25) | copy-start | bytes 772
  0.7 28.6 %copy-start.5 = (s32[1,64]{1,0:T(1,128)S(1)}, s32[1,64]{1,0:T(1,128)}, u32[]{:S(2)}) copy-start(s32[1,64]{1,0:T(1,128)} %param.18) | copy-start | bytes 772
  0.7 30.6 %copy-start.6 = (s32[128]{0:T(128)S(1)}, s32[128]{0:T(128)}, u32[]{:S(2)}) copy-start(s32[128]{0:T(128)} %param.16) | copy-start | bytes 1540
  7.3 24.0 %collective-permute-start.9 = (bf16[720,128]{1,0:T(8,128)(2,1)S(1)}, bf16[720,128]{1,0:T(8,128)(2,1)S(1)}, u32[]{:S(2)}, u32[]{:S(2)}) collective-permute-start(bf16[720,128]{1,0:T(8,128)(2,1)S(1)} %constant_dynamic-update-slice_fusion), channel_id=1, source_target_pairs={{0,128},{128,256},{256,384},{384,0},{1,129},{129,257},{257,385},{3... | collective-permute-start | bytes 552968 | tf_op jit(solution)/shard_map/ppermute | solution.py:80
  11.8 50.1 %collective-permute-start.8 = (bf16[720,128]{1,0:T(8,128)(2,1)S(1)}, bf16[720,128]{1,0:T(8,128)(2,1)S(1)}, u32[]{:S(2)}, u32[]{:S(2)}) collective-permute-start(bf16[720,128]{1,0:T(8,128)(2,1)S(1)} %constant_dynamic-update-slice_fusion), channel_id=1, source_target_pairs={{0,256},{128,384},{256,0},{384,128},{1,257},{129,385},{257,1},{385... | collective-permute-start | bytes 552968 | tf_op jit(solution)/shard_map/ppermute | solution.py:80
  13.8 50.1 %collective-permute-start.7 = (bf16[720,128]{1,0:T(8,128)(2,1)S(1)}, bf16[720,128]{1,0:T(8,128)(2,1)S(1)}, u32[]{:S(2)}, u32[]{:S(2)}) collective-permute-start(bf16[720,128]{1,0:T(8,128)(2,1)S(1)} %constant_dynamic-update-slice_fusion), channel_id=1, source_target_pairs={{0,384},{128,0},{256,128},{384,256},{1,385},{129,1},{257,129},{385... | collective-permute-start | bytes 552968 | tf_op jit(solution)/shard_map/ppermute | solution.py:80
  18.6 47.4 %collective-permute-start = (bf16[2,128,640]{1,2,0:T(8,128)(2,1)S(1)}, bf16[2,128,640]{1,2,0:T(8,128)(2,1)S(1)}, u32[]{:S(2)}, u32[]{:S(2)}) collective-permute-start(bf16[2,128,640]{1,2,0:T(8,128)(2,1)S(1)} %pad_maximum_fusion.1), channel_id=1, source_target_pairs={{0,7},{1,0},{2,1},{3,2},{4,3},{5,4},{6,5},{7,6},{8,15},{9,8},{10,9... | collective-permute-start | bytes 983048 | tf_op jit(solution)/shard_map/ppermute | solution.py:80
  23.4 45.3 %collective-permute-start.1 = (bf16[2,128,640]{1,2,0:T(8,128)(2,1)S(1)}, bf16[2,128,640]{1,2,0:T(8,128)(2,1)S(1)}, u32[]{:S(2)}, u32[]{:S(2)}) collective-permute-start(bf16[2,128,640]{1,2,0:T(8,128)(2,1)S(1)} %pad_maximum_fusion.1), channel_id=1, source_target_pairs={{0,6},{1,7},{2,0},{3,1},{4,2},{5,3},{6,4},{7,5},{8,14},{9,15},{10,... | collective-permute-start | bytes 983048 | tf_op jit(solution)/shard_map/ppermute | solution.py:80
  31.3 66.9 %copy-start.2 = (f32[1,4096]{1,0:T(1,128)}, f32[1,4096]{1,0:T(1,128)S(1)}, u32[]{:S(2)}) copy-start(f32[1,4096]{1,0:T(1,128)S(1)} %constant_dynamic-update-slice_fusion.43.bias_ref) | copy-start | bytes 49156
  31.3 46.5 %collective-permute-start.2 = (bf16[2,128,640]{1,2,0:T(8,128)(2,1)S(1)}, bf16[2,128,640]{1,2,0:T(8,128)(2,1)S(1)}, u32[]{:S(2)}, u32[]{:S(2)}) collective-permute-start(bf16[2,128,640]{1,2,0:T(8,128)(2,1)S(1)} %pad_maximum_fusion.1), channel_id=1, source_target_pairs={{0,5},{1,6},{2,7},{3,0},{4,1},{5,2},{6,3},{7,4},{8,13},{9,14},{10,... | collective-permute-start | bytes 983048 | tf_op jit(solution)/shard_map/ppermute | solution.py:80
  62.0 27.7 %collective-permute-start.3 = (bf16[2,128,640]{1,2,0:T(8,128)(2,1)S(1)}, bf16[2,128,640]{1,2,0:T(8,128)(2,1)S(1)}, u32[]{:S(2)}, u32[]{:S(2)}) collective-permute-start(bf16[2,128,640]{1,2,0:T(8,128)(2,1)S(1)} %pad_maximum_fusion.1), channel_id=1, source_target_pairs={{0,4},{1,5},{2,6},{3,7},{4,0},{5,1},{6,2},{7,3},{8,12},{9,13},{10,... | collective-permute-start | bytes 983048 | tf_op jit(solution)/shard_map/ppermute | solution.py:80
  63.9 30.6 %collective-permute-start.4 = (bf16[2,128,640]{1,2,0:T(8,128)(2,1)S(1)}, bf16[2,128,640]{1,2,0:T(8,128)(2,1)S(1)}, u32[]{:S(2)}, u32[]{:S(2)}) collective-permute-start(bf16[2,128,640]{1,2,0:T(8,128)(2,1)S(1)} %pad_maximum_fusion.1), channel_id=1, source_target_pairs={{0,3},{1,4},{2,5},{3,6},{4,7},{5,0},{6,1},{7,2},{8,11},{9,12},{10,... | collective-permute-start | bytes 983048 | tf_op jit(solution)/shard_map/ppermute | solution.py:80
  66.0 32.3 %collective-permute-start.5 = (bf16[2,128,640]{1,2,0:T(8,128)(2,1)S(1)}, bf16[2,128,640]{1,2,0:T(8,128)(2,1)S(1)}, u32[]{:S(2)}, u32[]{:S(2)}) collective-permute-start(bf16[2,128,640]{1,2,0:T(8,128)(2,1)S(1)} %pad_maximum_fusion.1), channel_id=1, source_target_pairs={{0,2},{1,3},{2,4},{3,5},{4,6},{5,7},{6,0},{7,1},{8,10},{9,11},{10,... | collective-permute-start | bytes 983048 | tf_op jit(solution)/shard_map/ppermute | solution.py:80
  68.7 36.0 %collective-permute-start.6 = (bf16[2,128,640]{1,2,0:T(8,128)(2,1)S(1)}, bf16[2,128,640]{1,2,0:T(8,128)(2,1)S(1)}, u32[]{:S(2)}, u32[]{:S(2)}) collective-permute-start(bf16[2,128,640]{1,2,0:T(8,128)(2,1)S(1)} %pad_maximum_fusion.1), channel_id=1, source_target_pairs={{0,1},{1,2},{2,3},{3,4},{4,5},{5,6},{6,7},{7,0},{8,9},{9,10},{10,1... | collective-permute-start | bytes 983048 | tf_op jit(solution)/shard_map/ppermute | solution.py:80
  77.9 47.5 %collective-permute-start.11 = (bf16[4,720,128]{2,1,0:T(8,128)(2,1)S(1)}, bf16[4,720,128]{2,1,0:T(8,128)(2,1)S(1)}, u32[]{:S(2)}, u32[]{:S(2)}) collective-permute-start(bf16[4,720,128]{2,1,0:T(8,128)(2,1)S(1)} %pad_maximum_fusion), channel_id=1, source_target_pairs={{0,112},{16,0},{32,16},{48,32},{64,48},{80,64},{96,80},{112,96},{1... | collective-permute-start | bytes 2211848 | tf_op jit(solution)/shard_map/ppermute | solution.py:80
  89.7 36.2 %collective-permute-start.10 = (bf16[4,720,128]{2,1,0:T(8,128)(2,1)S(1)}, bf16[4,720,128]{2,1,0:T(8,128)(2,1)S(1)}, u32[]{:S(2)}, u32[]{:S(2)}) collective-permute-start(bf16[4,720,128]{2,1,0:T(8,128)(2,1)S(1)} %pad_maximum_fusion), channel_id=1, source_target_pairs={{0,16},{16,32},{32,48},{48,64},{64,80},{80,96},{96,112},{112,0},{1... | collective-permute-start | bytes 2211848 | tf_op jit(solution)/shard_map/ppermute | solution.py:80
  94.5 30.4 %collective-permute-start.17 = (bf16[4,720,128]{2,1,0:T(8,128)(2,1)S(1)}, bf16[4,720,128]{2,1,0:T(8,128)(2,1)S(1)}, u32[]{:S(2)}, u32[]{:S(2)}) collective-permute-start(bf16[4,720,128]{2,1,0:T(8,128)(2,1)S(1)} %pad_maximum_fusion), channel_id=1, source_target_pairs={{0,8},{8,0},{1,9},{9,1},{2,10},{10,2},{3,11},{11,3},{4,12},{12,4},... | collective-permute-start | bytes 2211848 | tf_op jit(solution)/shard_map/ppermute | solution.py:80
  126.5 23.5 %collective-permute-start.13 = (bf16[4,720,128]{2,1,0:T(8,128)(2,1)S(1)}, bf16[4,720,128]{2,1,0:T(8,128)(2,1)S(1)}, u32[]{:S(2)}, u32[]{:S(2)}) collective-permute-start(bf16[4,720,128]{2,1,0:T(8,128)(2,1)S(1)} %collective-permute-done.11), channel_id=1, source_target_pairs={{0,112},{16,0},{32,16},{48,32},{64,48},{80,64},{96,80},{112,96},{1... | collective-permute-start | bytes 2211848 | tf_op jit(solution)/shard_map/ppermute | solution.py:80
  136.4 24.2 %collective-permute-start.12 = (bf16[4,720,128]{2,1,0:T(8,128)(2,1)S(1)}, bf16[4,720,128]{2,1,0:T(8,128)(2,1)S(1)}, u32[]{:S(2)}, u32[]{:S(2)}) collective-permute-start(bf16[4,720,128]{2,1,0:T(8,128)(2,1)S(1)} %collective-permute-done.10), channel_id=1, source_target_pairs={{0,16},{16,32},{32,48},{48,64},{64,80},{80,96},{96,112},{112,0},{1... | collective-permute-start | bytes 2211848 | tf_op jit(solution)/shard_map/ppermute | solution.py:80
  138.3 24.3 %collective-permute-start.19 = (bf16[4,720,128]{2,1,0:T(8,128)(2,1)S(1)}, bf16[4,720,128]{2,1,0:T(8,128)(2,1)S(1)}, u32[]{:S(2)}, u32[]{:S(2)}) collective-permute-start(bf16[4,720,128]{2,1,0:T(8,128)(2,1)S(1)} %collective-permute-done.11), channel_id=1, source_target_pairs={{0,8},{8,0},{1,9},{9,1},{2,10},{10,2},{3,11},{11,3},{4,12},{12,4},... | collective-permute-start | bytes 2211848 | tf_op jit(solution)/shard_map/ppermute | solution.py:80
  143.2 22.6 %collective-permute-start.18 = (bf16[4,720,128]{2,1,0:T(8,128)(2,1)S(1)}, bf16[4,720,128]{2,1,0:T(8,128)(2,1)S(1)}, u32[]{:S(2)}, u32[]{:S(2)}) collective-permute-start(bf16[4,720,128]{2,1,0:T(8,128)(2,1)S(1)} %collective-permute-done.10), channel_id=1, source_target_pairs={{0,8},{8,0},{1,9},{9,1},{2,10},{10,2},{3,11},{11,3},{4,12},{12,4},... | collective-permute-start | bytes 2211848 | tf_op jit(solution)/shard_map/ppermute | solution.py:80
  150.0 32.8 %collective-permute-start.15 = (bf16[4,720,128]{2,1,0:T(8,128)(2,1)S(1)}, bf16[4,720,128]{2,1,0:T(8,128)(2,1)S(1)}, u32[]{:S(2)}, u32[]{:S(2)}) collective-permute-start(bf16[4,720,128]{2,1,0:T(8,128)(2,1)S(1)} %collective-permute-done.13), channel_id=1, source_target_pairs={{0,112},{16,0},{32,16},{48,32},{64,48},{80,64},{96,80},{112,96},{1... | collective-permute-start | bytes 2211848 | tf_op jit(solution)/shard_map/ppermute | solution.py:80
  155.3 26.5 %collective-permute-start.21 = (bf16[4,720,128]{2,1,0:T(8,128)(2,1)S(1)}, bf16[4,720,128]{2,1,0:T(8,128)(2,1)S(1)}, u32[]{:S(2)}, u32[]{:S(2)}) collective-permute-start(bf16[4,720,128]{2,1,0:T(8,128)(2,1)S(1)} %collective-permute-done.13), channel_id=1, source_target_pairs={{0,8},{8,0},{1,9},{9,1},{2,10},{10,2},{3,11},{11,3},{4,12},{12,4},... | collective-permute-start | bytes 2211848 | tf_op jit(solution)/shard_map/ppermute | solution.py:80
  160.6 21.2 %collective-permute-start.14 = (bf16[4,720,128]{2,1,0:T(8,128)(2,1)S(1)}, bf16[4,720,128]{2,1,0:T(8,128)(2,1)S(1)}, u32[]{:S(2)}, u32[]{:S(2)}) collective-permute-start(bf16[4,720,128]{2,1,0:T(8,128)(2,1)S(1)} %collective-permute-done.12), channel_id=1, source_target_pairs={{0,16},{16,32},{32,48},{48,64},{64,80},{80,96},{96,112},{112,0},{1... | collective-permute-start | bytes 2211848 | tf_op jit(solution)/shard_map/ppermute | solution.py:80
  162.6 19.8 %collective-permute-start.20 = (bf16[4,720,128]{2,1,0:T(8,128)(2,1)S(1)}, bf16[4,720,128]{2,1,0:T(8,128)(2,1)S(1)}, u32[]{:S(2)}, u32[]{:S(2)}) collective-permute-start(bf16[4,720,128]{2,1,0:T(8,128)(2,1)S(1)} %collective-permute-done.12), channel_id=1, source_target_pairs={{0,8},{8,0},{1,9},{9,1},{2,10},{10,2},{3,11},{11,3},{4,12},{12,4},... | collective-permute-start | bytes 2211848 | tf_op jit(solution)/shard_map/ppermute | solution.py:80
  183.0 25.4 %collective-permute-start.23 = (bf16[4,720,128]{2,1,0:T(8,128)(2,1)S(1)}, bf16[4,720,128]{2,1,0:T(8,128)(2,1)S(1)}, u32[]{:S(2)}, u32[]{:S(2)}) collective-permute-start(bf16[4,720,128]{2,1,0:T(8,128)(2,1)S(1)} %collective-permute-done.15), channel_id=1, source_target_pairs={{0,8},{8,0},{1,9},{9,1},{2,10},{10,2},{3,11},{11,3},{4,12},{12,4},... | collective-permute-start | bytes 2211848 | tf_op jit(solution)/shard_map/ppermute | solution.py:80
  185.7 23.2 %collective-permute-start.22 = (bf16[4,720,128]{2,1,0:T(8,128)(2,1)S(1)}, bf16[4,720,128]{2,1,0:T(8,128)(2,1)S(1)}, u32[]{:S(2)}, u32[]{:S(2)}) collective-permute-start(bf16[4,720,128]{2,1,0:T(8,128)(2,1)S(1)} %collective-permute-done.14), channel_id=1, source_target_pairs={{0,8},{8,0},{1,9},{9,1},{2,10},{10,2},{3,11},{11,3},{4,12},{12,4},... | collective-permute-start | bytes 2211848 | tf_op jit(solution)/shard_map/ppermute | solution.py:80
  187.6 20.7 %collective-permute-start.16 = (bf16[4,720,128]{2,1,0:T(8,128)(2,1)S(1)}, bf16[4,720,128]{2,1,0:T(8,128)(2,1)S(1)}, u32[]{:S(2)}, u32[]{:S(2)}) collective-permute-start(bf16[4,720,128]{2,1,0:T(8,128)(2,1)S(1)} %collective-permute-done.14), channel_id=1, source_target_pairs={{0,16},{16,32},{32,48},{48,64},{64,80},{80,96},{96,112},{112,0},{1... | collective-permute-start | bytes 2211848 | tf_op jit(solution)/shard_map/ppermute | solution.py:80
  209.0 5.8 %copy-start.1 = (bf16[4096,128]{1,0:T(8,128)(2,1)}, bf16[4096,128]{1,0:T(8,128)(2,1)S(1)}, u32[]{:S(2)}) copy-start(bf16[4096,128]{1,0:T(8,128)(2,1)S(1)} %constant_dynamic-update-slice_fusion.12) | copy-start | bytes 3145732
  209.1 5.1 %collective-permute-start.24 = (bf16[4,720,128]{2,1,0:T(8,128)(2,1)S(1)}, bf16[4,720,128]{2,1,0:T(8,128)(2,1)S(1)}, u32[]{:S(2)}, u32[]{:S(2)}) collective-permute-start(bf16[4,720,128]{2,1,0:T(8,128)(2,1)S(1)} %collective-permute-done.16), channel_id=1, source_target_pairs={{0,8},{8,0},{1,9},{9,1},{2,10},{10,2},{3,11},{11,3},{4,12},{12,4},... | collective-permute-start | bytes 2211848 | tf_op jit(solution)/shard_map/ppermute | solution.py:80
  212.4 2.3 copy-start

commit v5 on v4

--- a/solution.py
+++ b/solution.py
@@ -102,14 +102,6 @@
     q_cols = w_query.shape[1]
     w_rows = w_query.shape[0]
 
-    tp_size = lax.axis_size("tp")
-    me_tp = lax.axis_index("tp")
-    mine = jnp.stack([embeds, given_embeds])
-    pieces = [mine] + [shifted(mine, "tp", tp_size, k) for k in range(1, tp_size)]
-    ordered = jnp.roll(jnp.stack(pieces), me_tp, axis=0)
-    both = jnp.concatenate([ordered[i] for i in range(tp_size)], axis=-1)
-    first_rows, given_rows = both[0], both[1]
-
     w_parts = [w_query[:, j * HD : (j + 1) * HD] for j in range(q_cols // HD)] + [w_key, w_value]
     w_len = len(w_parts) * w_rows
     key_start = -(-w_len // ctx_rows) * ctx_rows
@@ -130,14 +122,22 @@
     arrived = [(0, line)]
     forward = line
     backward = line
-    for step in range(1, n_z // 2 + 1):
+    far = n_z // 2
+    split = n_ylo // 2
+    for step in range(1, far):
         forward = shifted(forward, "z", n_z, -1)
-        arrived.append((-step, forward))
-        if step < n_z - n_z // 2:
-            backward = shifted(backward, "z", n_z, 1)
-            arrived.append((step, backward))
+        backward = shifted(backward, "z", n_z, 1)
+        arrived += [(-step, forward), (step, backward)]
+    far_front = shifted(forward[:split], "z", n_z, -1)
+    far_back = shifted(backward[split:], "z", n_z, 1)
+    arrived.append((far, jnp.concatenate([far_front, far_back], axis=0)))
     held = [(offset, 0, piece) for offset, piece in arrived]
     held += [(offset, 1, shifted(piece, "core", 2, 1)) for offset, piece in arrived]
+
+    mine = jnp.stack([embeds, given_embeds])
+    mine, ignored = lax.optimization_barrier((mine, line))
+    both = lax.all_gather(mine, "tp", axis=2, tiled=True)
+    first_rows, given_rows = both[0], both[1]
 
     revised = jnp.where(accept[:, None] == 1, given_rows, first_rows)
     normed = normalize(jnp.concatenate([first_rows, revised], axis=0), norm_gain)

time: 237 us -> 193 us (0.81)
  the two profiles are of different devices: /device:TPU:57 before, /device:TPU:1 now
where the time goes in v5:
time: 193 us; the launch traced here: 190 us
  starting transfers between devices  76.1 us (39%)
  local copies, waits for them, and re-layouts  51.5 us (27%)
  between operations  15.7 us (8%)
  Pallas kernels  15.5 us (8%)
  waiting for transfers between devices  12.7 us (7%)
  other arithmetic  9.81 us (5%)
  matrix products  8.69 us (5%)
    ppermute x19, starting transfers between devices, shifted(): return lax.ppermute(x, axis, pairs)  76.1 us
    unnamed x128, local copies, waits for them, and re-layouts  40.9 us
    pallas_call x1, Pallas kernels, attend(): pl.pallas_call(attend_kernel, grid=(passes, heads), in_specs=[pl.BlockSpe...  15.5 us
    ppermute x19, waiting for transfers between devices, shifted(): return lax.ppermute(x, axis, pairs)  12.7 us
    dot_general x16, matrix products, local(): jnp.einsum('rki,kjid->rjd', normed5[:, :, offset % n_z, core, :], piece.r...  8.69 us
  transfers between devices with their start and end apart: 20, of which 4 were waited for; matrix products, arithmetic and copies ran while one was open for 19% of the time, Pallas kernels for 0%

profile of v5, /device:TPU:1, one launch (start us, length us, event | category | flops | bytes accessed | tf_op | source)
XLA Modules:
  0.0 190.0 jit_solution(12219428133647413775)
XLA Ops:
  7.2 0.8 constant_dynamic-update-slice_fusion.10
  8.0 0.7 constant_dynamic-update-slice_fusion.9
  8.7 0.7 constant_dynamic-update-slice_fusion.8
  9.5 0.7 constant_dynamic-update-slice_fusion.7
  10.2 0.8 constant_dynamic-update-slice_fusion.6
  11.0 0.7 constant_dynamic-update-slice_fusion.5
  11.7 0.7 constant_dynamic-update-slice_fusion.4
  12.4 0.7 constant_dynamic-update-slice_fusion.2
  13.2 0.7 constant_dynamic-update-slice_fusion.1
  13.9 4.0 %collective-permute-start.2 = (bf16[720,128]{1,0:T(8,128)(2,1)S(1)}, bf16[720,128]{1,0:T(8,128)(2,1)S(1)}, u32[]{:S(2)}, u32[]{:S(2)}) collective-permute-start(bf16[720,128]{1,0:T(8,128)(2,1)S(1)} %constant_dynamic-update-slice_fusion), channel_id=1, source_target_pairs={{0,128},{128,256},{256,384},{384,0},{1,129},{129,257},{257,385},{3... | collective-permute-start | bytes 552968 | tf_op jit(solution)/shard_map/ppermute | solution.py:80
  17.9 4.2 %collective-permute-start.1 = (bf16[720,128]{1,0:T(8,128)(2,1)S(1)}, bf16[720,128]{1,0:T(8,128)(2,1)S(1)}, u32[]{:S(2)}, u32[]{:S(2)}) collective-permute-start(bf16[720,128]{1,0:T(8,128)(2,1)S(1)} %constant_dynamic-update-slice_fusion), channel_id=1, source_target_pairs={{0,256},{128,384},{256,0},{384,128},{1,257},{129,385},{257,1},{385... | collective-permute-start | bytes 552968 | tf_op jit(solution)/shard_map/ppermute | solution.py:80
  22.2 3.0 %collective-permute-start = (bf16[720,128]{1,0:T(8,128)(2,1)S(1)}, bf16[720,128]{1,0:T(8,128)(2,1)S(1)}, u32[]{:S(2)}, u32[]{:S(2)}) collective-permute-start(bf16[720,128]{1,0:T(8,128)(2,1)S(1)} %constant_dynamic-update-slice_fusion), channel_id=1, source_target_pairs={{0,384},{128,0},{256,128},{384,256},{1,385},{129,1},{257,129},{385... | collective-permute-start | bytes 552968 | tf_op jit(solution)/shard_map/ppermute | solution.py:80
  37.9 10.7 %collective-permute-start.4 = (bf16[4,720,128]{2,1,0:T(8,128)(2,1)S(1)}, bf16[4,720,128]{2,1,0:T(8,128)(2,1)S(1)}, u32[]{:S(2)}, u32[]{:S(2)}) collective-permute-start(bf16[4,720,128]{2,1,0:T(8,128)(2,1)S(1)} %pad_maximum_fusion), channel_id=1, source_target_pairs={{0,112},{16,0},{32,16},{48,32},{64,48},{80,64},{96,80},{112,96},{1... | collective-permute-start | bytes 2211848 | tf_op jit(solution)/shard_map/ppermute | solution.py:80
  49.6 0.8 pad_maximum_fusion.1
  50.4 1.9 %collective-permute-start.3 = (bf16[4,720,128]{2,1,0:T(8,128)(2,1)S(1)}, bf16[4,720,128]{2,1,0:T(8,128)(2,1)S(1)}, u32[]{:S(2)}, u32[]{:S(2)}) collective-permute-start(bf16[4,720,128]{2,1,0:T(8,128)(2,1)S(1)} %pad_maximum_fusion), channel_id=1, source_target_pairs={{0,16},{16,32},{32,48},{48,64},{64,80},{80,96},{96,112},{112,0},{1... | collective-permute-start | bytes 2211848 | tf_op jit(solution)/shard_map/ppermute | solution.py:80
  53.7 0.7 copy.66
  54.4 0.7 copy.67
  55.1 3.7 %collective-permute-start.11 = (bf16[4,720,128]{2,1,0:T(8,128)(2,1)S(1)}, bf16[4,720,128]{2,1,0:T(8,128)(2,1)S(1)}, u32[]{:S(2)}, u32[]{:S(2)}) collective-permute-start(bf16[4,720,128]{2,1,0:T(8,128)(2,1)S(1)} %pad_maximum_fusion), channel_id=1, source_target_pairs={{0,8},{8,0},{1,9},{9,1},{2,10},{10,2},{3,11},{11,3},{4,12},{12,4},... | collective-permute-start | bytes 2211848 | tf_op jit(solution)/shard_map/ppermute | solution.py:80
  60.1 2.7 %collective-permute-done.4 = bf16[4,720,128]{2,1,0:T(8,128)(2,1)S(1)} collective-permute-done((bf16[4,720,128]{2,1,0:T(8,128)(2,1)S(1)}, bf16[4,720,128]{2,1,0:T(8,128)(2,1)S(1)}, u32[]{:S(2)}, u32[]{:S(2)}) %collective-permute-start.4) | collective-permute-done | bytes 737312 | tf_op jit(solution)/shard_map/ppermute | solution.py:80
  62.8 5.3 %collective-permute-start.6 = (bf16[4,720,128]{2,1,0:T(8,128)(2,1)S(1)}, bf16[4,720,128]{2,1,0:T(8,128)(2,1)S(1)}, u32[]{:S(2)}, u32[]{:S(2)}) collective-permute-start(bf16[4,720,128]{2,1,0:T(8,128)(2,1)S(1)} %collective-permute-done.4), channel_id=1, source_target_pairs={{0,112},{16,0},{32,16},{48,32},{64,48},{80,64},{96,80},{112,96},{1... | collective-permute-start | bytes 2211848 | tf_op jit(solution)/shard_map/ppermute | solution.py:80
  68.2 1.5 collective-permute-done.3
  69.6 1.9 %collective-permute-start.5 = (bf16[4,720,128]{2,1,0:T(8,128)(2,1)S(1)}, bf16[4,720,128]{2,1,0:T(8,128)(2,1)S(1)}, u32[]{:S(2)}, u32[]{:S(2)}) collective-permute-start(bf16[4,720,128]{2,1,0:T(8,128)(2,1)S(1)} %collective-permute-done.3), channel_id=1, source_target_pairs={{0,16},{16,32},{32,48},{48,64},{64,80},{80,96},{96,112},{112,0},{1... | collective-permute-start | bytes 2211848 | tf_op jit(solution)/shard_map/ppermute | solution.py:80
  72.8 4.6 %collective-permute-start.13 = (bf16[4,720,128]{2,1,0:T(8,128)(2,1)S(1)}, bf16[4,720,128]{2,1,0:T(8,128)(2,1)S(1)}, u32[]{:S(2)}, u32[]{:S(2)}) collective-permute-start(bf16[4,720,128]{2,1,0:T(8,128)(2,1)S(1)} %collective-permute-done.4), channel_id=1, source_target_pairs={{0,8},{8,0},{1,9},{9,1},{2,10},{10,2},{3,11},{11,3},{4,12},{12,4},... | collective-permute-start | bytes 2211848 | tf_op jit(solution)/shard_map/ppermute | solution.py:80
  77.5 1.9 %collective-permute-start.12 = (bf16[4,720,128]{2,1,0:T(8,128)(2,1)S(1)}, bf16[4,720,128]{2,1,0:T(8,128)(2,1)S(1)}, u32[]{:S(2)}, u32[]{:S(2)}) collective-permute-start(bf16[4,720,128]{2,1,0:T(8,128)(2,1)S(1)} %collective-permute-done.3), channel_id=1, source_target_pairs={{0,8},{8,0},{1,9},{9,1},{2,10},{10,2},{3,11},{11,3},{4,12},{12,4},... | collective-permute-start | bytes 2211848 | tf_op jit(solution)/shard_map/ppermute | solution.py:80
  80.7 7.3 %collective-permute-done.5 = bf16[4,720,128]{2,1,0:T(8,128)(2,1)S(1)} collective-permute-done((bf16[4,720,128]{2,1,0:T(8,128)(2,1)S(1)}, bf16[4,720,128]{2,1,0:T(8,128)(2,1)S(1)}, u32[]{:S(2)}, u32[]{:S(2)}) %collective-permute-start.5) | collective-permute-done | bytes 737312 | tf_op jit(solution)/shard_map/ppermute | solution.py:80
  88.0 1.9 %collective-permute-start.7 = (bf16[4,720,128]{2,1,0:T(8,128)(2,1)S(1)}, bf16[4,720,128]{2,1,0:T(8,128)(2,1)S(1)}, u32[]{:S(2)}, u32[]{:S(2)}) collective-permute-start(bf16[4,720,128]{2,1,0:T(8,128)(2,1)S(1)} %collective-permute-done.5), channel_id=1, source_target_pairs={{0,16},{16,32},{32,48},{48,64},{64,80},{80,96},{96,112},{112,0},{1... | collective-permute-start | bytes 2211848 | tf_op jit(solution)/shard_map/ppermute | solution.py:80
  90.0 4.6 %collective-permute-start.8 = (bf16[4,720,128]{2,1,0:T(8,128)(2,1)S(1)}, bf16[4,720,128]{2,1,0:T(8,128)(2,1)S(1)}, u32[]{:S(2)}, u32[]{:S(2)}) collective-permute-start(bf16[4,720,128]{2,1,0:T(8,128)(2,1)S(1)} %collective-permute-done.6), channel_id=1, source_target_pairs={{0,112},{16,0},{32,16},{48,32},{64,48},{80,64},{96,80},{112,96},{1... | collective-permute-start | bytes 2211848 | tf_op jit(solution)/shard_map/ppermute | solution.py:80
  95.8 6.1 %collective-permute-start.15 = (bf16[4,720,128]{2,1,0:T(8,128)(2,1)S(1)}, bf16[4,720,128]{2,1,0:T(8,128)(2,1)S(1)}, u32[]{:S(2)}, u32[]{:S(2)}) collective-permute-start(bf16[4,720,128]{2,1,0:T(8,128)(2,1)S(1)} %collective-permute-done.6), channel_id=1, source_target_pairs={{0,8},{8,0},{1,9},{9,1},{2,10},{10,2},{3,11},{11,3},{4,12},{12,4},... | collective-permute-start | bytes 2211848 | tf_op jit(solution)/shard_map/ppermute | solution.py:80
  102.0 1.9 %collective-permute-start.14 = (bf16[4,720,128]{2,1,0:T(8,128)(2,1)S(1)}, bf16[4,720,128]{2,1,0:T(8,128)(2,1)S(1)}, u32[]{:S(2)}, u32[]{:S(2)}) collective-permute-start(bf16[4,720,128]{2,1,0:T(8,128)(2,1)S(1)} %collective-permute-done.5), channel_id=1, source_target_pairs={{0,8},{8,0},{1,9},{9,1},{2,10},{10,2},{3,11},{11,3},{4,12},{12,4},... | collective-permute-start | bytes 2211848 | tf_op jit(solution)/shard_map/ppermute | solution.py:80
  103.9 0.7 constant_dynamic-update-slice_fusion.41
  105.3 1.1 collective-permute-done.8
  106.4 5.4 %collective-permute-start.10 = (bf16[2,720,128]{2,1,0:T(8,128)(2,1)S(1)}, bf16[2,720,128]{2,1,0:T(8,128)(2,1)S(1)}, u32[]{:S(2)}, u32[]{:S(2)}) collective-permute-start(bf16[2,720,128]{2,1,0:T(8,128)(2,1)S(1)} %slice.339), channel_id=1, source_target_pairs={{0,112},{16,0},{32,16},{48,32},{64,48},{80,64},{96,80},{112,96},{1... | collective-permute-start | bytes 1105928 | tf_op jit(solution)/shard_map/ppermute | solution.py:80
  111.9 1.9 %collective-permute-start.9 = (bf16[2,720,128]{2,1,0:T(8,128)(2,1)S(1)}, bf16[2,720,128]{2,1,0:T(8,128)(2,1)S(1)}, u32[]{:S(2)}, u32[]{:S(2)}) collective-permute-start(bf16[2,720,128]{2,1,0:T(8,128)(2,1)S(1)} %slice.338), channel_id=1, source_target_pairs={{0,16},{16,32},{32,48},{48,64},{64,80},{80,96},{96,112},{112,0},{1... | collective-permute-start | bytes 1105928 | tf_op jit(solution)/shard_map/ppermute | solution.py:80
  113.9 6.9 %collective-permute-start.17 = (bf16[4,720,128]{2,1,0:T(8,128)(2,1)S(1)}, bf16[4,720,128]{2,1,0:T(8,128)(2,1)S(1)}, u32[]{:S(2)}, u32[]{:S(2)}) collective-permute-start(bf16[4,720,128]{2,1,0:T(8,128)(2,1)S(1)} %collective-permute-done.8), channel_id=1, source_target_pairs={{0,8},{8,0},{1,9},{9,1},{2,10},{10,2},{3,11},{11,3},{4,12},{12,4},... | collective-permute-start | bytes 2211848 | tf_op jit(solution)/shard_map/ppermute | solution.py:80
  123.4 1.9 %collective-permute-start.16 = (bf16[4,720,128]{2,1,0:T(8,128)(2,1)S(1)}, bf16[4,720,128]{2,1,0:T(8,128)(2,1)S(1)}, u32[]{:S(2)}, u32[]{:S(2)}) collective-permute-start(bf16[4,720,128]{2,1,0:T(8,128)(2,1)S(1)} %collective-permute-done.7), channel_id=1, source_target_pairs={{0,8},{8,0},{1,9},{9,1},{2,10},{10,2},{3,11},{11,3},{4,12},{12,4},... | collective-permute-start | bytes 2211848 | tf_op jit(solution)/shard_map/ppermute | solution.py:80
  125.4 4.1 %collective-permute-start.18 = (bf16[4,720,128]{2,1,0:T(8,128)(2,1)S(1)}, bf16[4,720,128]{2,1,0:T(8,128)(2,1)S(1)}, u32[]{:S(2)}, u32[]{:S(2)}) collective-permute-start(bf16[4,720,128]{2,1,0:T(8,128)(2,1)S(1)} %constant_dynamic-update-slice_fusion.11), channel_id=1, source_target_pairs={{0,8},{8,0},{1,9},{9,1},{2,10},{10,2},{3,11},{11,3},{4,12},{12,4},... | collective-permute-start | bytes 2211848 | tf_op jit(solution)/shard_map/ppermute | solution.py:80
  139.9 0.9 copy-done.21
  141.4 2.3 %slice_bitcast_fusion.34 = (bf16[128,5120]{0,1:T(8,128)(2,1)S(1)}, bf16[1,128,5120]{1,2,0:T(8,128)(2,1)S(1)}, bf16[1,128,5120]{1,2,0:T(8,128)(2,1)S(1)}) fusion(bf16[2,128,5120]{1,2,0:T(8,128)(2,1)} %all-gather.2.cloned.1.call-done), kind=kLoop, calls=%fused_computation.164 | loop fusion | bytes 6553600 | tf_op jit(solution)/shard_map/squeeze | solution.py:140
  144.1 0.7 multiply_reduce_fusion
  145.6 0.8 multiply_convert_fusion
  146.4 0.9 fusion.2
  147.4 0.9 fusion.1
  148.3 0.9 fusion
  160.7 0.9 fusion.14
  163.4 0.9 copy.69.q_ref
  165.2 0.7 pad_maximum_fusion.3.ko_ref
  165.9 15.5 %shard_map.149 = bf16[2,128,640]{2,1,0:T(8,128)(2,1)} custom-call(bf16[2,128,640]{2,1,0:T(8,128)(2,1)} %copy.69.q_ref, bf16[2,128,128]{2,1,0:T(8,128)(2,1)} %pad_maximum_fusion.3.ko_ref, bf16[2,128,128]{2,1,0:T(8,128)(2,1)} %add_convert_fusion.1.vo_ref, bf16[4096,128]{1,0:T(8,128)(2,1)} %get-tuple-element.67.kc_ref, ...), custom_call_target="tpu_custom_call" | custom-call | flops 2768240640 | bytes 3407872 | tf_op jit(solution)/shard_map/pallas_call | solution.py:57
  181.4 1.7 slice_bitcast_fusion
  (218 shorter events, 48.6 us)
Async XLA Ops:
  7.2 42.1 %copy-start.29 = (bf16[128,640]{1,0:T(8,128)(2,1)S(1)}, bf16[128,640]{1,0:T(8,128)(2,1)}, u32[]{:S(2)}) copy-start(bf16[128,640]{1,0:T(8,128)(2,1)} %param.14) | copy-start | bytes 491524
  7.2 134.2 %all-gather.2.cloned.1.call-start = ((), (), s32[]{:S(2)}) async-start(), calls=%async_computation | async-start | bytes 2949120 | tf_op jit(solution)/shard_map/all_gather | solution.py:139
  10.2 39.2 %copy-start.30 = (bf16[128,640]{1,0:T(8,128)(2,1)S(1)}, bf16[128,640]{1,0:T(8,128)(2,1)}, u32[]{:S(2)}) copy-start(bf16[128,640]{1,0:T(8,128)(2,1)} %param.15) | copy-start | bytes 491524
  13.9 23.8 %collective-permute-start.2 = (bf16[720,128]{1,0:T(8,128)(2,1)S(1)}, bf16[720,128]{1,0:T(8,128)(2,1)S(1)}, u32[]{:S(2)}, u32[]{:S(2)}) collective-permute-start(bf16[720,128]{1,0:T(8,128)(2,1)S(1)} %constant_dynamic-update-slice_fusion), channel_id=1, source_target_pairs={{0,128},{128,256},{256,384},{384,0},{1,129},{129,257},{257,385},{3... | collective-permute-start | bytes 552968 | tf_op jit(solution)/shard_map/ppermute | solution.py:80
  17.9 19.8 %collective-permute-start.1 = (bf16[720,128]{1,0:T(8,128)(2,1)S(1)}, bf16[720,128]{1,0:T(8,128)(2,1)S(1)}, u32[]{:S(2)}, u32[]{:S(2)}) collective-permute-start(bf16[720,128]{1,0:T(8,128)(2,1)S(1)} %constant_dynamic-update-slice_fusion), channel_id=1, source_target_pairs={{0,256},{128,384},{256,0},{384,128},{1,257},{129,385},{257,1},{385... | collective-permute-start | bytes 552968 | tf_op jit(solution)/shard_map/ppermute | solution.py:80
  22.2 15.6 %collective-permute-start = (bf16[720,128]{1,0:T(8,128)(2,1)S(1)}, bf16[720,128]{1,0:T(8,128)(2,1)S(1)}, u32[]{:S(2)}, u32[]{:S(2)}) collective-permute-start(bf16[720,128]{1,0:T(8,128)(2,1)S(1)} %constant_dynamic-update-slice_fusion), channel_id=1, source_target_pairs={{0,384},{128,0},{256,128},{384,256},{1,385},{129,1},{257,129},{385... | collective-permute-start | bytes 552968 | tf_op jit(solution)/shard_map/ppermute | solution.py:80
  37.0 17.3 %copy-start.25 = (f32[128,64]{0,1:T(8,128)}, f32[128,64]{0,1:T(8,128)S(1)}, u32[]{:S(2)}) copy-start(f32[128,64]{0,1:T(8,128)S(1)} %get-tuple-element.66) | copy-start | bytes 98308
  37.7 12.6 %copy-start.23 = (bf16[720,128]{1,0:T(8,128)(2,1)}, bf16[720,128]{1,0:T(8,128)(2,1)S(1)}, u32[]{:S(2)}) copy-start(bf16[720,128]{1,0:T(8,128)(2,1)S(1)} %collective-permute-done) | copy-start | bytes 552964
  37.8 15.1 %copy-start.33 = (bf16[128]{0:T(256)(128)(2,1)S(1)}, bf16[128]{0:T(256)(128)(2,1)}, u32[]{:S(2)}) copy-start(bf16[128]{0:T(256)(128)(2,1)} %param.23) | copy-start | bytes 772
  37.8 15.1 %copy-start.34 = (bf16[128]{0:T(256)(128)(2,1)S(1)}, bf16[128]{0:T(256)(128)(2,1)}, u32[]{:S(2)}) copy-start(bf16[128]{0:T(256)(128)(2,1)} %param.25) | copy-start | bytes 772
  37.8 15.1 %copy-start.32 = (bf16[5120]{0:T(1024)(128)(2,1)S(1)}, bf16[5120]{0:T(1024)(128)(2,1)}, u32[]{:S(2)}) copy-start(bf16[5120]{0:T(1024)(128)(2,1)} %param.19) | copy-start | bytes 30724
  37.9 24.9 %collective-permute-start.4 = (bf16[4,720,128]{2,1,0:T(8,128)(2,1)S(1)}, bf16[4,720,128]{2,1,0:T(8,128)(2,1)S(1)}, u32[]{:S(2)}, u32[]{:S(2)}) collective-permute-start(bf16[4,720,128]{2,1,0:T(8,128)(2,1)S(1)} %pad_maximum_fusion), channel_id=1, source_target_pairs={{0,112},{16,0},{32,16},{48,32},{64,48},{80,64},{96,80},{112,96},{1... | collective-permute-start | bytes 2211848 | tf_op jit(solution)/shard_map/ppermute | solution.py:80
  50.4 19.3 %collective-permute-start.3 = (bf16[4,720,128]{2,1,0:T(8,128)(2,1)S(1)}, bf16[4,720,128]{2,1,0:T(8,128)(2,1)S(1)}, u32[]{:S(2)}, u32[]{:S(2)}) collective-permute-start(bf16[4,720,128]{2,1,0:T(8,128)(2,1)S(1)} %pad_maximum_fusion), channel_id=1, source_target_pairs={{0,16},{16,32},{32,48},{48,64},{64,80},{80,96},{96,112},{112,0},{1... | collective-permute-start | bytes 2211848 | tf_op jit(solution)/shard_map/ppermute | solution.py:80
  55.1 25.5 %collective-permute-start.11 = (bf16[4,720,128]{2,1,0:T(8,128)(2,1)S(1)}, bf16[4,720,128]{2,1,0:T(8,128)(2,1)S(1)}, u32[]{:S(2)}, u32[]{:S(2)}) collective-permute-start(bf16[4,720,128]{2,1,0:T(8,128)(2,1)S(1)} %pad_maximum_fusion), channel_id=1, source_target_pairs={{0,8},{8,0},{1,9},{9,1},{2,10},{10,2},{3,11},{11,3},{4,12},{12,4},... | collective-permute-start | bytes 2211848 | tf_op jit(solution)/shard_map/ppermute | solution.py:80
  62.8 27.1 %collective-permute-start.6 = (bf16[4,720,128]{2,1,0:T(8,128)(2,1)S(1)}, bf16[4,720,128]{2,1,0:T(8,128)(2,1)S(1)}, u32[]{:S(2)}, u32[]{:S(2)}) collective-permute-start(bf16[4,720,128]{2,1,0:T(8,128)(2,1)S(1)} %collective-permute-done.4), channel_id=1, source_target_pairs={{0,112},{16,0},{32,16},{48,32},{64,48},{80,64},{96,80},{112,96},{1... | collective-permute-start | bytes 2211848 | tf_op jit(solution)/shard_map/ppermute | solution.py:80
  69.6 35.6 %copy-start.1 = (bf16[4,720,128]{2,1,0:T(8,128)(2,1)}, bf16[4,720,128]{2,1,0:T(8,128)(2,1)S(1)}, u32[]{:S(2)}) copy-start(bf16[4,720,128]{2,1,0:T(8,128)(2,1)S(1)} %collective-permute-done.3) | copy-start | bytes 2211844
  69.6 18.4 %collective-permute-start.5 = (bf16[4,720,128]{2,1,0:T(8,128)(2,1)S(1)}, bf16[4,720,128]{2,1,0:T(8,128)(2,1)S(1)}, u32[]{:S(2)}, u32[]{:S(2)}) collective-permute-start(bf16[4,720,128]{2,1,0:T(8,128)(2,1)S(1)} %collective-permute-done.3), channel_id=1, source_target_pairs={{0,16},{16,32},{32,48},{48,64},{64,80},{80,96},{96,112},{112,0},{1... | collective-permute-start | bytes 2211848 | tf_op jit(solution)/shard_map/ppermute | solution.py:80
  72.8 29.1 %collective-permute-start.13 = (bf16[4,720,128]{2,1,0:T(8,128)(2,1)S(1)}, bf16[4,720,128]{2,1,0:T(8,128)(2,1)S(1)}, u32[]{:S(2)}, u32[]{:S(2)}) collective-permute-start(bf16[4,720,128]{2,1,0:T(8,128)(2,1)S(1)} %collective-permute-done.4), channel_id=1, source_target_pairs={{0,8},{8,0},{1,9},{9,1},{2,10},{10,2},{3,11},{11,3},{4,12},{12,4},... | collective-permute-start | bytes 2211848 | tf_op jit(solution)/shard_map/ppermute | solution.py:80
  77.5 26.4 %collective-permute-start.12 = (bf16[4,720,128]{2,1,0:T(8,128)(2,1)S(1)}, bf16[4,720,128]{2,1,0:T(8,128)(2,1)S(1)}, u32[]{:S(2)}, u32[]{:S(2)}) collective-permute-start(bf16[4,720,128]{2,1,0:T(8,128)(2,1)S(1)} %collective-permute-done.3), channel_id=1, source_target_pairs={{0,8},{8,0},{1,9},{9,1},{2,10},{10,2},{3,11},{11,3},{4,12},{12,4},... | collective-permute-start | bytes 2211848 | tf_op jit(solution)/shard_map/ppermute | solution.py:80
  80.6 7.4 %copy-start.3 = (bf16[4,720,128]{2,1,0:T(8,128)(2,1)}, bf16[4,720,128]{2,1,0:T(8,128)(2,1)S(1)}, u32[]{:S(2)}) copy-start(bf16[4,720,128]{2,1,0:T(8,128)(2,1)S(1)} %collective-permute-done.11) | copy-start | bytes 2211844
  88.0 23.9 %copy-start.5 = (bf16[4,720,128]{2,1,0:T(8,128)(2,1)}, bf16[4,720,128]{2,1,0:T(8,128)(2,1)S(1)}, u32[]{:S(2)}) copy-start(bf16[4,720,128]{2,1,0:T(8,128)(2,1)S(1)} %collective-permute-done.5) | copy-start | bytes 2211844
  88.0 23.8 %collective-permute-start.7 = (bf16[4,720,128]{2,1,0:T(8,128)(2,1)S(1)}, bf16[4,720,128]{2,1,0:T(8,128)(2,1)S(1)}, u32[]{:S(2)}, u32[]{:S(2)}) collective-permute-start(bf16[4,720,128]{2,1,0:T(8,128)(2,1)S(1)} %collective-permute-done.5), channel_id=1, source_target_pairs={{0,16},{16,32},{32,48},{48,64},{64,80},{80,96},{96,112},{112,0},{1... | collective-permute-start | bytes 2211848 | tf_op jit(solution)/shard_map/ppermute | solution.py:80
  90.0 21.9 %copy-start.7 = (bf16[4,720,128]{2,1,0:T(8,128)(2,1)}, bf16[4,720,128]{2,1,0:T(8,128)(2,1)S(1)}, u32[]{:S(2)}) copy-start(bf16[4,720,128]{2,1,0:T(8,128)(2,1)S(1)} %collective-permute-done.6) | copy-start | bytes 2211844
  90.0 16.4 %collective-permute-start.8 = (bf16[4,720,128]{2,1,0:T(8,128)(2,1)S(1)}, bf16[4,720,128]{2,1,0:T(8,128)(2,1)S(1)}, u32[]{:S(2)}, u32[]{:S(2)}) collective-permute-start(bf16[4,720,128]{2,1,0:T(8,128)(2,1)S(1)} %collective-permute-done.6), channel_id=1, source_target_pairs={{0,112},{16,0},{32,16},{48,32},{64,48},{80,64},{96,80},{112,96},{1... | collective-permute-start | bytes 2211848 | tf_op jit(solution)/shard_map/ppermute | solution.py:80
  95.8 27.5 %collective-permute-start.15 = (bf16[4,720,128]{2,1,0:T(8,128)(2,1)S(1)}, bf16[4,720,128]{2,1,0:T(8,128)(2,1)S(1)}, u32[]{:S(2)}, u32[]{:S(2)}) collective-permute-start(bf16[4,720,128]{2,1,0:T(8,128)(2,1)S(1)} %collective-permute-done.6), channel_id=1, source_target_pairs={{0,8},{8,0},{1,9},{9,1},{2,10},{10,2},{3,11},{11,3},{4,12},{12,4},... | collective-permute-start | bytes 2211848 | tf_op jit(solution)/shard_map/ppermute | solution.py:80
  102.0 2.7 %copy-start.9 = (bf16[4,720,128]{2,1,0:T(8,128)(2,1)}, bf16[4,720,128]{2,1,0:T(8,128)(2,1)S(1)}, u32[]{:S(2)}) copy-start(bf16[4,720,128]{2,1,0:T(8,128)(2,1)S(1)} %collective-permute-done.13) | copy-start | bytes 2211844
  102.0 23.3 %collective-permute-start.14 = (bf16[4,720,128]{2,1,0:T(8,128)(2,1)S(1)}, bf16[4,720,128]{2,1,0:T(8,128)(2,1)S(1)}, u32[]{:S(2)}, u32[]{:S(2)}) collective-permute-start(bf16[4,720,128]{2,1,0:T(8,128)(2,1)S(1)} %collective-permute-done.5), channel_id=1, source_target_pairs={{0,8},{8,0},{1,9},{9,1},{2,10},{10,2},{3,11},{11,3},{4,12},{12,4},... | collective-permute-start | bytes 2211848 | tf_op jit(solution)/shard_map/ppermute | solution.py:80
  103.9 1.4 copy-start.11
  106.4 19.0 %collective-permute-start.10 = (bf16[2,720,128]{2,1,0:T(8,128)(2,1)S(1)}, bf16[2,720,128]{2,1,0:T(8,128)(2,1)S(1)}, u32[]{:S(2)}, u32[]{:S(2)}) collective-permute-start(bf16[2,720,128]{2,1,0:T(8,128)(2,1)S(1)} %slice.339), channel_id=1, source_target_pairs={{0,112},{16,0},{32,16},{48,32},{64,48},{80,64},{96,80},{112,96},{1... | collective-permute-start | bytes 1105928 | tf_op jit(solution)/shard_map/ppermute | solution.py:80
  111.9 13.4 %collective-permute-start.9 = (bf16[2,720,128]{2,1,0:T(8,128)(2,1)S(1)}, bf16[2,720,128]{2,1,0:T(8,128)(2,1)S(1)}, u32[]{:S(2)}, u32[]{:S(2)}) collective-permute-start(bf16[2,720,128]{2,1,0:T(8,128)(2,1)S(1)} %slice.338), channel_id=1, source_target_pairs={{0,16},{16,32},{32,48},{48,64},{64,80},{80,96},{96,112},{112,0},{1... | collective-permute-start | bytes 1105928 | tf_op jit(solution)/shard_map/ppermute | solution.py:80
  113.9 24.0 %collective-permute-start.17 = (bf16[4,720,128]{2,1,0:T(8,128)(2,1)S(1)}, bf16[4,720,128]{2,1,0:T(8,128)(2,1)S(1)}, u32[]{:S(2)}, u32[]{:S(2)}) collective-permute-start(bf16[4,720,128]{2,1,0:T(8,128)(2,1)S(1)} %collective-permute-done.8), channel_id=1, source_target_pairs={{0,8},{8,0},{1,9},{9,1},{2,10},{10,2},{3,11},{11,3},{4,12},{12,4},... | collective-permute-start | bytes 2211848 | tf_op jit(solution)/shard_map/ppermute | solution.py:80
  123.3 8.1 %copy-start.13 = (bf16[4,720,128]{2,1,0:T(8,128)(2,1)}, bf16[4,720,128]{2,1,0:T(8,128)(2,1)S(1)}, u32[]{:S(2)}) copy-start(bf16[4,720,128]{2,1,0:T(8,128)(2,1)S(1)} %collective-permute-done.15) | copy-start | bytes 2211844
  123.4 13.8 %collective-permute-start.16 = (bf16[4,720,128]{2,1,0:T(8,128)(2,1)S(1)}, bf16[4,720,128]{2,1,0:T(8,128)(2,1)S(1)}, u32[]{:S(2)}, u32[]{:S(2)}) collective-permute-start(bf16[4,720,128]{2,1,0:T(8,128)(2,1)S(1)} %collective-permute-done.7), channel_id=1, source_target_pairs={{0,8},{8,0},{1,9},{9,1},{2,10},{10,2},{3,11},{11,3},{4,12},{12,4},... | collective-permute-start | bytes 2211848 | tf_op jit(solution)/shard_map/ppermute | solution.py:80
  125.3 7.5 %copy-start.15 = (bf16[4,720,128]{2,1,0:T(8,128)(2,1)}, bf16[4,720,128]{2,1,0:T(8,128)(2,1)S(1)}, u32[]{:S(2)}) copy-start(bf16[4,720,128]{2,1,0:T(8,128)(2,1)S(1)} %collective-permute-done.14) | copy-start | bytes 2211844
  125.4 14.4 %collective-permute-start.18 = (bf16[4,720,128]{2,1,0:T(8,128)(2,1)S(1)}, bf16[4,720,128]{2,1,0:T(8,128)(2,1)S(1)}, u32[]{:S(2)}, u32[]{:S(2)}) collective-permute-start(bf16[4,720,128]{2,1,0:T(8,128)(2,1)S(1)} %constant_dynamic-update-slice_fusion.11), channel_id=1, source_target_pairs={{0,8},{8,0},{1,9},{9,1},{2,10},{10,2},{3,11},{11,3},{4,12},{12,4},... | collective-permute-start | bytes 2211848 | tf_op jit(solution)/shard_map/ppermute | solution.py:80
  137.2 2.7 %copy-start.17 = (bf16[4,720,128]{2,1,0:T(8,128)(2,1)}, bf16[4,720,128]{2,1,0:T(8,128)(2,1)S(1)}, u32[]{:S(2)}) copy-start(bf16[4,720,128]{2,1,0:T(8,128)(2,1)S(1)} %collective-permute-done.16) | copy-start | bytes 2211844
  137.8 2.0 %copy-start.19 = (bf16[4,720,128]{2,1,0:T(8,128)(2,1)}, bf16[4,720,128]{2,1,0:T(8,128)(2,1)S(1)}, u32[]{:S(2)}) copy-start(bf16[4,720,128]{2,1,0:T(8,128)(2,1)S(1)} %collective-permute-done.17) | copy-start | bytes 2211844
  141.4 2.5 %copy-start = (bf16[2,128,5120]{1,2,0:T(8,128)(2,1)S(1)}, bf16[2,128,5120]{1,2,0:T(8,128)(2,1)}, u32[]{:S(2)}) copy-start(bf16[2,128,5120]{1,2,0:T(8,128)(2,1)} %all-gather.2.cloned.1.call-done) | copy-start | bytes 7864324
  148.3 1.1 copy-start.20
  149.3 1.2 copy-start.14
  150.0 1.2 copy-start.16
  151.0 1.2 copy-start.10
  151.6 1.2 copy-start.12
  152.6 1.2 copy-start.4
  154.8 1.1 copy-start.8
  157.0 1.2 copy-start.22
  163.3 1.7 copy-start.27
  163.3 1.7 copy-start.28
  (7 other events, 6.7 us)
Sparse Core Ops, SparseCore 0:
  59.0 78.3 all-gather.1

commit v6 on v5

--- a/solution.py
+++ b/solution.py
@@ -118,6 +118,16 @@
     me_z = lax.axis_index("z")
     me_core = lax.axis_index("core")
 
+    mine = jnp.stack([embeds, given_embeds])
+    both = lax.all_gather(mine, "tp", axis=2, tiled=True)
+    first_rows, given_rows = both[0], both[1]
+
+    revised = jnp.where(accept[:, None] == 1, given_rows, first_rows)
+    normed = normalize(jnp.concatenate([first_rows, revised], axis=0), norm_gain)
+    normed5 = normed.reshape(normed.shape[0], n_ylo, n_z, 2, w_rows)
+    normed5 = jnp.roll(normed5, -me_ylo, axis=1)
+    normed5 = jnp.roll(normed5, -me_z, axis=2)
+    normed5 = jnp.roll(normed5, -me_core, axis=3)
     line = jnp.stack([packed] + [shifted(packed, "ylo", n_ylo, k) for k in range(1, n_ylo)])
     arrived = [(0, line)]
     forward = line
@@ -128,23 +138,13 @@
         forward = shifted(forward, "z", n_z, -1)
         backward = shifted(backward, "z", n_z, 1)
         arrived += [(-step, forward), (step, backward)]
+    normed5, forward, backward = lax.optimization_barrier((normed5, forward, backward))
     far_front = shifted(forward[:split], "z", n_z, -1)
     far_back = shifted(backward[split:], "z", n_z, 1)
     arrived.append((far, jnp.concatenate([far_front, far_back], axis=0)))
     held = [(offset, 0, piece) for offset, piece in arrived]
     held += [(offset, 1, shifted(piece, "core", 2, 1)) for offset, piece in arrived]
 
-    mine = jnp.stack([embeds, given_embeds])
-    mine, ignored = lax.optimization_barrier((mine, line))
-    both = lax.all_gather(mine, "tp", axis=2, tiled=True)
-    first_rows, given_rows = both[0], both[1]
-
-    revised = jnp.where(accept[:, None] == 1, given_rows, first_rows)
-    normed = normalize(jnp.concatenate([first_rows, revised], axis=0), norm_gain)
-    normed5 = normed.reshape(normed.shape[0], n_ylo, n_z, 2, w_rows)
-    normed5 = jnp.roll(normed5, -me_ylo, axis=1)
-    normed5 = jnp.roll(normed5, -me_z, axis=2)
-    normed5 = jnp.roll(normed5, -me_core, axis=3)
     proj = None
     for offset, core, piece in held:
         part = jnp.einsum(

time: 193 us -> 190 us (0.984)
  waiting for transfers between devices: 12.7 us -> 25 us
  local copies, waits for them, and re-layouts: 51.5 us -> 40.5 us
  other arithmetic: 9.81 us -> 7.8 us
    unnamed x128 -> x156, local copies, waits for them, and re-layouts: 40.9 us -> 25.8 us
    ppermute x19, waiting for transfers between devices: 12.7 us -> 23.1 us  [shifted(): return lax.ppermute(x, axis, pairs)]
    slice x16, local copies, waits for them, and re-layouts: 0.17 us -> 4.91 us  [local(): piece[:, value_start:used, :].reshape(-1, HD)]
  transfers between devices with their start and end apart: 20 -> 20, of which waited for: 4 -> 5; matrix products, arithmetic and copies ran while one was open for 19% -> 16% of each run, Pallas kernels for 0% -> 0%
where the time goes in v6:
time: 190 us; the launch traced here: 188 us
  starting transfers between devices  74.4 us (39%)
  local copies, waits for them, and re-layouts  40.5 us (21%)
  waiting for transfers between devices  25 us (13%)
  between operations  16 us (8%)
  Pallas kernels  15.5 us (8%)
  matrix products  8.57 us (5%)
  other arithmetic  7.8 us (4%)
    ppermute x19, starting transfers between devices, shifted(): return lax.ppermute(x, axis, pairs)  74.4 us
    unnamed x156, local copies, waits for them, and re-layouts  25.8 us
    ppermute x19, waiting for transfers between devices, shifted(): return lax.ppermute(x, axis, pairs)  23.1 us
    pallas_call x1, Pallas kernels, attend(): pl.pallas_call(attend_kernel, grid=(passes, heads), in_specs=[pl.BlockSpe...  15.5 us
    dot_general x16, matrix products, local(): jnp.einsum('rki,kjid->rjd', normed5[:, :, offset % n_z, core, :], piece.r...  8.57 us
    slice x16, local copies, waits for them, and re-layouts, local(): piece[:, value_start:used, :].reshape(-1, HD)  4.91 us
  transfers between devices with their start and end apart: 20, of which 5 were waited for; matrix products, arithmetic and copies ran while one was open for 16% of the time, Pallas kernels for 0%

profile of v6, /device:TPU:1, one launch (start us, length us, event | category | flops | bytes accessed | tf_op | source)
XLA Modules:
  0.0 187.7 jit_solution(11522973696300153877)
XLA Ops:
  7.2 0.7 constant_dynamic-update-slice_fusion.10
  8.0 0.7 constant_dynamic-update-slice_fusion.9
  8.7 0.7 constant_dynamic-update-slice_fusion.8
  9.4 0.7 constant_dynamic-update-slice_fusion.7
  10.2 0.8 constant_dynamic-update-slice_fusion.6
  10.9 0.7 constant_dynamic-update-slice_fusion.5
  11.7 0.7 constant_dynamic-update-slice_fusion.4
  12.4 0.7 constant_dynamic-update-slice_fusion.2
  13.9 6.0 %collective-permute-start = (bf16[720,128]{1,0:T(8,128)(2,1)S(1)}, bf16[720,128]{1,0:T(8,128)(2,1)S(1)}, u32[]{:S(2)}, u32[]{:S(2)}) collective-permute-start(bf16[720,128]{1,0:T(8,128)(2,1)S(1)} %constant_dynamic-update-slice_fusion), channel_id=1, source_target_pairs={{0,384},{128,0},{256,128},{384,256},{1,385},{129,1},{257,129},{385... | collective-permute-start | bytes 552968 | tf_op jit(solution)/shard_map/ppermute | solution.py:80
  19.9 1.9 %collective-permute-start.1 = (bf16[720,128]{1,0:T(8,128)(2,1)S(1)}, bf16[720,128]{1,0:T(8,128)(2,1)S(1)}, u32[]{:S(2)}, u32[]{:S(2)}) collective-permute-start(bf16[720,128]{1,0:T(8,128)(2,1)S(1)} %constant_dynamic-update-slice_fusion), channel_id=1, source_target_pairs={{0,256},{128,384},{256,0},{384,128},{1,257},{129,385},{257,1},{385... | collective-permute-start | bytes 552968 | tf_op jit(solution)/shard_map/ppermute | solution.py:80
  21.9 2.3 %collective-permute-start.2 = (bf16[720,128]{1,0:T(8,128)(2,1)S(1)}, bf16[720,128]{1,0:T(8,128)(2,1)S(1)}, u32[]{:S(2)}, u32[]{:S(2)}) collective-permute-start(bf16[720,128]{1,0:T(8,128)(2,1)S(1)} %constant_dynamic-update-slice_fusion), channel_id=1, source_target_pairs={{0,128},{128,256},{256,384},{384,0},{1,129},{129,257},{257,385},{3... | collective-permute-start | bytes 552968 | tf_op jit(solution)/shard_map/ppermute | solution.py:80
  24.2 1.1 copy.44
  25.3 1.1 copy.45
  26.4 0.8 pad_maximum_fusion.1
  30.1 4.9 %collective-permute-done.1 = bf16[720,128]{1,0:T(8,128)(2,1)S(1)} collective-permute-done((bf16[720,128]{1,0:T(8,128)(2,1)S(1)}, bf16[720,128]{1,0:T(8,128)(2,1)S(1)}, u32[]{:S(2)}, u32[]{:S(2)}) %collective-permute-start.1) | collective-permute-done | bytes 184352 | tf_op jit(solution)/shard_map/ppermute | solution.py:80
  35.1 5.0 %collective-permute-start.3 = (bf16[4,720,128]{2,1,0:T(8,128)(2,1)S(1)}, bf16[4,720,128]{2,1,0:T(8,128)(2,1)S(1)}, u32[]{:S(2)}, u32[]{:S(2)}) collective-permute-start(bf16[4,720,128]{2,1,0:T(8,128)(2,1)S(1)} %pad_maximum_fusion), channel_id=1, source_target_pairs={{0,16},{16,32},{32,48},{48,64},{64,80},{80,96},{96,112},{112,0},{1... | collective-permute-start | bytes 2211848 | tf_op jit(solution)/shard_map/ppermute | solution.py:80
  40.3 8.6 %collective-permute-start.6 = (bf16[4,720,128]{2,1,0:T(8,128)(2,1)S(1)}, bf16[4,720,128]{2,1,0:T(8,128)(2,1)S(1)}, u32[]{:S(2)}, u32[]{:S(2)}) collective-permute-start(bf16[4,720,128]{2,1,0:T(8,128)(2,1)S(1)} %pad_maximum_fusion), channel_id=1, source_target_pairs={{0,112},{16,0},{32,16},{48,32},{64,48},{80,64},{96,80},{112,96},{1... | collective-permute-start | bytes 2211848 | tf_op jit(solution)/shard_map/ppermute | solution.py:80
  49.6 0.7 copy.66
  50.4 0.7 copy.67
  51.1 3.2 %collective-permute-start.11 = (bf16[4,720,128]{2,1,0:T(8,128)(2,1)S(1)}, bf16[4,720,128]{2,1,0:T(8,128)(2,1)S(1)}, u32[]{:S(2)}, u32[]{:S(2)}) collective-permute-start(bf16[4,720,128]{2,1,0:T(8,128)(2,1)S(1)} %pad_maximum_fusion), channel_id=1, source_target_pairs={{0,8},{8,0},{1,9},{9,1},{2,10},{10,2},{3,11},{11,3},{4,12},{12,4},... | collective-permute-start | bytes 2211848 | tf_op jit(solution)/shard_map/ppermute | solution.py:80
  54.4 8.2 %collective-permute-done.3 = bf16[4,720,128]{2,1,0:T(8,128)(2,1)S(1)} collective-permute-done((bf16[4,720,128]{2,1,0:T(8,128)(2,1)S(1)}, bf16[4,720,128]{2,1,0:T(8,128)(2,1)S(1)}, u32[]{:S(2)}, u32[]{:S(2)}) %collective-permute-start.3) | collective-permute-done | bytes 737312 | tf_op jit(solution)/shard_map/ppermute | solution.py:80
  62.5 1.9 %collective-permute-start.4 = (bf16[4,720,128]{2,1,0:T(8,128)(2,1)S(1)}, bf16[4,720,128]{2,1,0:T(8,128)(2,1)S(1)}, u32[]{:S(2)}, u32[]{:S(2)}) collective-permute-start(bf16[4,720,128]{2,1,0:T(8,128)(2,1)S(1)} %collective-permute-done.3), channel_id=1, source_target_pairs={{0,16},{16,32},{32,48},{48,64},{64,80},{80,96},{96,112},{112,0},{1... | collective-permute-start | bytes 2211848 | tf_op jit(solution)/shard_map/ppermute | solution.py:80
  64.5 4.6 %collective-permute-start.7 = (bf16[4,720,128]{2,1,0:T(8,128)(2,1)S(1)}, bf16[4,720,128]{2,1,0:T(8,128)(2,1)S(1)}, u32[]{:S(2)}, u32[]{:S(2)}) collective-permute-start(bf16[4,720,128]{2,1,0:T(8,128)(2,1)S(1)} %collective-permute-done.6), channel_id=1, source_target_pairs={{0,112},{16,0},{32,16},{48,32},{64,48},{80,64},{96,80},{112,96},{1... | collective-permute-start | bytes 2211848 | tf_op jit(solution)/shard_map/ppermute | solution.py:80
  69.1 4.1 %collective-permute-start.12 = (bf16[4,720,128]{2,1,0:T(8,128)(2,1)S(1)}, bf16[4,720,128]{2,1,0:T(8,128)(2,1)S(1)}, u32[]{:S(2)}, u32[]{:S(2)}) collective-permute-start(bf16[4,720,128]{2,1,0:T(8,128)(2,1)S(1)} %collective-permute-done.3), channel_id=1, source_target_pairs={{0,8},{8,0},{1,9},{9,1},{2,10},{10,2},{3,11},{11,3},{4,12},{12,4},... | collective-permute-start | bytes 2211848 | tf_op jit(solution)/shard_map/ppermute | solution.py:80
  73.3 1.9 %collective-permute-start.13 = (bf16[4,720,128]{2,1,0:T(8,128)(2,1)S(1)}, bf16[4,720,128]{2,1,0:T(8,128)(2,1)S(1)}, u32[]{:S(2)}, u32[]{:S(2)}) collective-permute-start(bf16[4,720,128]{2,1,0:T(8,128)(2,1)S(1)} %collective-permute-done.6), channel_id=1, source_target_pairs={{0,8},{8,0},{1,9},{9,1},{2,10},{10,2},{3,11},{11,3},{4,12},{12,4},... | collective-permute-start | bytes 2211848 | tf_op jit(solution)/shard_map/ppermute | solution.py:80
  75.9 6.1 %collective-permute-done.4 = bf16[4,720,128]{2,1,0:T(8,128)(2,1)S(1)} collective-permute-done((bf16[4,720,128]{2,1,0:T(8,128)(2,1)S(1)}, bf16[4,720,128]{2,1,0:T(8,128)(2,1)S(1)}, u32[]{:S(2)}, u32[]{:S(2)}) %collective-permute-start.4) | collective-permute-done | bytes 737312 | tf_op jit(solution)/shard_map/ppermute | solution.py:80
  82.1 1.9 %collective-permute-start.5 = (bf16[4,720,128]{2,1,0:T(8,128)(2,1)S(1)}, bf16[4,720,128]{2,1,0:T(8,128)(2,1)S(1)}, u32[]{:S(2)}, u32[]{:S(2)}) collective-permute-start(bf16[4,720,128]{2,1,0:T(8,128)(2,1)S(1)} %collective-permute-done.4), channel_id=1, source_target_pairs={{0,16},{16,32},{32,48},{48,64},{64,80},{80,96},{96,112},{112,0},{1... | collective-permute-start | bytes 2211848 | tf_op jit(solution)/shard_map/ppermute | solution.py:80
  84.1 4.6 %collective-permute-start.8 = (bf16[4,720,128]{2,1,0:T(8,128)(2,1)S(1)}, bf16[4,720,128]{2,1,0:T(8,128)(2,1)S(1)}, u32[]{:S(2)}, u32[]{:S(2)}) collective-permute-start(bf16[4,720,128]{2,1,0:T(8,128)(2,1)S(1)} %collective-permute-done.7), channel_id=1, source_target_pairs={{0,112},{16,0},{32,16},{48,32},{64,48},{80,64},{96,80},{112,96},{1... | collective-permute-start | bytes 2211848 | tf_op jit(solution)/shard_map/ppermute | solution.py:80
  88.7 4.9 %collective-permute-start.14 = (bf16[4,720,128]{2,1,0:T(8,128)(2,1)S(1)}, bf16[4,720,128]{2,1,0:T(8,128)(2,1)S(1)}, u32[]{:S(2)}, u32[]{:S(2)}) collective-permute-start(bf16[4,720,128]{2,1,0:T(8,128)(2,1)S(1)} %collective-permute-done.4), channel_id=1, source_target_pairs={{0,8},{8,0},{1,9},{9,1},{2,10},{10,2},{3,11},{11,3},{4,12},{12,4},... | collective-permute-start | bytes 2211848 | tf_op jit(solution)/shard_map/ppermute | solution.py:80
  93.7 1.9 %collective-permute-start.15 = (bf16[4,720,128]{2,1,0:T(8,128)(2,1)S(1)}, bf16[4,720,128]{2,1,0:T(8,128)(2,1)S(1)}, u32[]{:S(2)}, u32[]{:S(2)}) collective-permute-start(bf16[4,720,128]{2,1,0:T(8,128)(2,1)S(1)} %collective-permute-done.7), channel_id=1, source_target_pairs={{0,8},{8,0},{1,9},{9,1},{2,10},{10,2},{3,11},{11,3},{4,12},{12,4},... | collective-permute-start | bytes 2211848 | tf_op jit(solution)/shard_map/ppermute | solution.py:80
  97.0 3.8 %collective-permute-done.5 = bf16[4,720,128]{2,1,0:T(8,128)(2,1)S(1)} collective-permute-done((bf16[4,720,128]{2,1,0:T(8,128)(2,1)S(1)}, bf16[4,720,128]{2,1,0:T(8,128)(2,1)S(1)}, u32[]{:S(2)}, u32[]{:S(2)}) %collective-permute-start.5) | collective-permute-done | bytes 737312 | tf_op jit(solution)/shard_map/ppermute | solution.py:80
  100.8 5.2 %collective-permute-start.16 = (bf16[4,720,128]{2,1,0:T(8,128)(2,1)S(1)}, bf16[4,720,128]{2,1,0:T(8,128)(2,1)S(1)}, u32[]{:S(2)}, u32[]{:S(2)}) collective-permute-start(bf16[4,720,128]{2,1,0:T(8,128)(2,1)S(1)} %collective-permute-done.5), channel_id=1, source_target_pairs={{0,8},{8,0},{1,9},{9,1},{2,10},{10,2},{3,11},{11,3},{4,12},{12,4},... | collective-permute-start | bytes 2211848 | tf_op jit(solution)/shard_map/ppermute | solution.py:80
  106.1 1.9 %collective-permute-start.17 = (bf16[4,720,128]{2,1,0:T(8,128)(2,1)S(1)}, bf16[4,720,128]{2,1,0:T(8,128)(2,1)S(1)}, u32[]{:S(2)}, u32[]{:S(2)}) collective-permute-start(bf16[4,720,128]{2,1,0:T(8,128)(2,1)S(1)} %collective-permute-done.8), channel_id=1, source_target_pairs={{0,8},{8,0},{1,9},{9,1},{2,10},{10,2},{3,11},{11,3},{4,12},{12,4},... | collective-permute-start | bytes 2211848 | tf_op jit(solution)/shard_map/ppermute | solution.py:80
  110.5 0.9 copy-done.17
  112.0 1.9 all-gather.2.cloned.1.call-done
  113.9 2.3 %slice_bitcast_fusion.2 = (bf16[128,5120]{0,1:T(8,128)(2,1)S(1)}, bf16[1,128,5120]{1,2,0:T(8,128)(2,1)S(1)}, bf16[1,128,5120]{1,2,0:T(8,128)(2,1)S(1)}) fusion(bf16[2,128,5120]{1,2,0:T(8,128)(2,1)} %all-gather.2.cloned.1.call-done), kind=kLoop, calls=%fused_computation.180 | loop fusion | bytes 6553600 | tf_op jit(solution)/shard_map/squeeze | solution.py:123
  116.5 0.7 multiply_reduce_fusion
  118.0 0.8 multiply_convert_fusion
  118.9 0.9 fusion.2
  119.8 0.9 fusion.1
  120.8 0.9 fusion
  121.8 2.0 %collective-permute-start.9 = (bf16[2,720,128]{2,1,0:T(8,128)(2,1)S(1)}, bf16[2,720,128]{2,1,0:T(8,128)(2,1)S(1)}, u32[]{:S(2)}, u32[]{:S(2)}) collective-permute-start(bf16[2,720,128]{2,1,0:T(8,128)(2,1)S(1)} %slice.261), channel_id=1, source_target_pairs={{0,16},{16,32},{32,48},{48,64},{64,80},{80,96},{96,112},{112,0},{1... | collective-permute-start | bytes 1105928 | tf_op jit(solution)/shard_map/ppermute | solution.py:80
  123.8 4.7 %collective-permute-start.10 = (bf16[2,720,128]{2,1,0:T(8,128)(2,1)S(1)}, bf16[2,720,128]{2,1,0:T(8,128)(2,1)S(1)}, u32[]{:S(2)}, u32[]{:S(2)}) collective-permute-start(bf16[2,720,128]{2,1,0:T(8,128)(2,1)S(1)} %slice.262), channel_id=1, source_target_pairs={{0,112},{16,0},{32,16},{48,32},{64,48},{80,64},{96,80},{112,96},{1... | collective-permute-start | bytes 1105928 | tf_op jit(solution)/shard_map/ppermute | solution.py:80
  138.6 7.7 %collective-permute-start.18 = (bf16[4,720,128]{2,1,0:T(8,128)(2,1)S(1)}, bf16[4,720,128]{2,1,0:T(8,128)(2,1)S(1)}, u32[]{:S(2)}, u32[]{:S(2)}) collective-permute-start(bf16[4,720,128]{2,1,0:T(8,128)(2,1)S(1)} %constant_dynamic-update-slice_fusion.11), channel_id=1, source_target_pairs={{0,8},{8,0},{1,9},{9,1},{2,10},{10,2},{3,11},{11,3},{4,12},{12,4},... | collective-permute-start | bytes 2211848 | tf_op jit(solution)/shard_map/ppermute | solution.py:80
  157.0 0.9 fusion.14
  160.5 0.9 copy.69.q_ref
  163.6 15.5 %shard_map.149 = bf16[2,128,640]{2,1,0:T(8,128)(2,1)} custom-call(bf16[2,128,640]{2,1,0:T(8,128)(2,1)} %copy.69.q_ref, bf16[2,128,128]{2,1,0:T(8,128)(2,1)} %pad_maximum_fusion.3.ko_ref, bf16[2,128,128]{2,1,0:T(8,128)(2,1)} %add_convert_fusion.1.vo_ref, bf16[4096,128]{1,0:T(8,128)(2,1)} %get-tuple-element.71.kc_ref, ...), custom_call_target="tpu_custom_call" | custom-call | flops 2768240640 | bytes 3407872 | tf_op jit(solution)/shard_map/pallas_call | solution.py:57
  179.1 1.7 slice_bitcast_fusion
  (246 shorter events, 35.5 us)
Async XLA Ops:
  7.2 20.8 %copy-start.43 = (bf16[640]{0:T(1024)(128)(2,1)S(1)}, bf16[640]{0:T(1024)(128)(2,1)}, u32[]{:S(2)}) copy-start(bf16[640]{0:T(1024)(128)(2,1)} %param.21) | copy-start | bytes 3844
  7.2 20.8 %copy-start.45 = (s32[1,64]{1,0:T(1,128)S(1)}, s32[1,64]{1,0:T(1,128)}, u32[]{:S(2)}) copy-start(s32[1,64]{1,0:T(1,128)} %param.18) | copy-start | bytes 772
  7.2 22.8 %copy-start.46 = (s32[128]{0:T(128)S(1)}, s32[128]{0:T(128)}, u32[]{:S(2)}) copy-start(s32[128]{0:T(128)} %param.16) | copy-start | bytes 1540
  7.2 106.7 %all-gather.2.cloned.1.call-start = ((), (), s32[]{:S(2)}) async-start(), calls=%async_computation | async-start | bytes 2949120 | tf_op jit(solution)/shard_map/all_gather | solution.py:122
  13.9 16.2 %collective-permute-start = (bf16[720,128]{1,0:T(8,128)(2,1)S(1)}, bf16[720,128]{1,0:T(8,128)(2,1)S(1)}, u32[]{:S(2)}, u32[]{:S(2)}) collective-permute-start(bf16[720,128]{1,0:T(8,128)(2,1)S(1)} %constant_dynamic-update-slice_fusion), channel_id=1, source_target_pairs={{0,384},{128,0},{256,128},{384,256},{1,385},{129,1},{257,129},{385... | collective-permute-start | bytes 552968 | tf_op jit(solution)/shard_map/ppermute | solution.py:80
  19.9 15.1 %collective-permute-start.1 = (bf16[720,128]{1,0:T(8,128)(2,1)S(1)}, bf16[720,128]{1,0:T(8,128)(2,1)S(1)}, u32[]{:S(2)}, u32[]{:S(2)}) collective-permute-start(bf16[720,128]{1,0:T(8,128)(2,1)S(1)} %constant_dynamic-update-slice_fusion), channel_id=1, source_target_pairs={{0,256},{128,384},{256,0},{384,128},{1,257},{129,385},{257,1},{385... | collective-permute-start | bytes 552968 | tf_op jit(solution)/shard_map/ppermute | solution.py:80
  21.9 13.1 %collective-permute-start.2 = (bf16[720,128]{1,0:T(8,128)(2,1)S(1)}, bf16[720,128]{1,0:T(8,128)(2,1)S(1)}, u32[]{:S(2)}, u32[]{:S(2)}) collective-permute-start(bf16[720,128]{1,0:T(8,128)(2,1)S(1)} %constant_dynamic-update-slice_fusion), channel_id=1, source_target_pairs={{0,128},{128,256},{256,384},{384,0},{1,129},{129,257},{257,385},{3... | collective-permute-start | bytes 552968 | tf_op jit(solution)/shard_map/ppermute | solution.py:80
  27.2 21.7 %copy-start.40 = (bf16[5120]{0:T(1024)(128)(2,1)S(1)}, bf16[5120]{0:T(1024)(128)(2,1)}, u32[]{:S(2)}) copy-start(bf16[5120]{0:T(1024)(128)(2,1)} %param.19) | copy-start | bytes 30724
  27.2 22.5 %copy-start.47 = (bf16[128]{0:T(256)(128)(2,1)S(1)}, bf16[128]{0:T(256)(128)(2,1)}, u32[]{:S(2)}) copy-start(bf16[128]{0:T(256)(128)(2,1)} %param.23) | copy-start | bytes 772
  27.2 23.9 %copy-start.48 = (bf16[128]{0:T(256)(128)(2,1)S(1)}, bf16[128]{0:T(256)(128)(2,1)}, u32[]{:S(2)}) copy-start(bf16[128]{0:T(256)(128)(2,1)} %param.25) | copy-start | bytes 772
  29.9 34.6 %copy-start.21 = (f32[128,64]{0,1:T(8,128)}, f32[128,64]{0,1:T(8,128)S(1)}, u32[]{:S(2)}) copy-start(f32[128,64]{0,1:T(8,128)S(1)} %get-tuple-element.70) | copy-start | bytes 98308
  35.0 34.1 %copy-start.19 = (bf16[720,128]{1,0:T(8,128)(2,1)}, bf16[720,128]{1,0:T(8,128)(2,1)S(1)}, u32[]{:S(2)}) copy-start(bf16[720,128]{1,0:T(8,128)(2,1)S(1)} %collective-permute-done.2) | copy-start | bytes 552964
  35.1 27.4 %collective-permute-start.3 = (bf16[4,720,128]{2,1,0:T(8,128)(2,1)S(1)}, bf16[4,720,128]{2,1,0:T(8,128)(2,1)S(1)}, u32[]{:S(2)}, u32[]{:S(2)}) collective-permute-start(bf16[4,720,128]{2,1,0:T(8,128)(2,1)S(1)} %pad_maximum_fusion), channel_id=1, source_target_pairs={{0,16},{16,32},{32,48},{48,64},{64,80},{80,96},{96,112},{112,0},{1... | collective-permute-start | bytes 2211848 | tf_op jit(solution)/shard_map/ppermute | solution.py:80
  40.3 24.2 %collective-permute-start.6 = (bf16[4,720,128]{2,1,0:T(8,128)(2,1)S(1)}, bf16[4,720,128]{2,1,0:T(8,128)(2,1)S(1)}, u32[]{:S(2)}, u32[]{:S(2)}) collective-permute-start(bf16[4,720,128]{2,1,0:T(8,128)(2,1)S(1)} %pad_maximum_fusion), channel_id=1, source_target_pairs={{0,112},{16,0},{32,16},{48,32},{64,48},{80,64},{96,80},{112,96},{1... | collective-permute-start | bytes 2211848 | tf_op jit(solution)/shard_map/ppermute | solution.py:80
  51.1 24.1 %collective-permute-start.11 = (bf16[4,720,128]{2,1,0:T(8,128)(2,1)S(1)}, bf16[4,720,128]{2,1,0:T(8,128)(2,1)S(1)}, u32[]{:S(2)}, u32[]{:S(2)}) collective-permute-start(bf16[4,720,128]{2,1,0:T(8,128)(2,1)S(1)} %pad_maximum_fusion), channel_id=1, source_target_pairs={{0,8},{8,0},{1,9},{9,1},{2,10},{10,2},{3,11},{11,3},{4,12},{12,4},... | collective-permute-start | bytes 2211848 | tf_op jit(solution)/shard_map/ppermute | solution.py:80
  62.5 19.5 %collective-permute-start.4 = (bf16[4,720,128]{2,1,0:T(8,128)(2,1)S(1)}, bf16[4,720,128]{2,1,0:T(8,128)(2,1)S(1)}, u32[]{:S(2)}, u32[]{:S(2)}) collective-permute-start(bf16[4,720,128]{2,1,0:T(8,128)(2,1)S(1)} %collective-permute-done.3), channel_id=1, source_target_pairs={{0,16},{16,32},{32,48},{48,64},{64,80},{80,96},{96,112},{112,0},{1... | collective-permute-start | bytes 2211848 | tf_op jit(solution)/shard_map/ppermute | solution.py:80
  64.5 19.5 %collective-permute-start.7 = (bf16[4,720,128]{2,1,0:T(8,128)(2,1)S(1)}, bf16[4,720,128]{2,1,0:T(8,128)(2,1)S(1)}, u32[]{:S(2)}, u32[]{:S(2)}) collective-permute-start(bf16[4,720,128]{2,1,0:T(8,128)(2,1)S(1)} %collective-permute-done.6), channel_id=1, source_target_pairs={{0,112},{16,0},{32,16},{48,32},{64,48},{80,64},{96,80},{112,96},{1... | collective-permute-start | bytes 2211848 | tf_op jit(solution)/shard_map/ppermute | solution.py:80
  69.1 24.5 %collective-permute-start.12 = (bf16[4,720,128]{2,1,0:T(8,128)(2,1)S(1)}, bf16[4,720,128]{2,1,0:T(8,128)(2,1)S(1)}, u32[]{:S(2)}, u32[]{:S(2)}) collective-permute-start(bf16[4,720,128]{2,1,0:T(8,128)(2,1)S(1)} %collective-permute-done.3), channel_id=1, source_target_pairs={{0,8},{8,0},{1,9},{9,1},{2,10},{10,2},{3,11},{11,3},{4,12},{12,4},... | collective-permute-start | bytes 2211848 | tf_op jit(solution)/shard_map/ppermute | solution.py:80
  73.3 23.0 %collective-permute-start.13 = (bf16[4,720,128]{2,1,0:T(8,128)(2,1)S(1)}, bf16[4,720,128]{2,1,0:T(8,128)(2,1)S(1)}, u32[]{:S(2)}, u32[]{:S(2)}) collective-permute-start(bf16[4,720,128]{2,1,0:T(8,128)(2,1)S(1)} %collective-permute-done.6), channel_id=1, source_target_pairs={{0,8},{8,0},{1,9},{9,1},{2,10},{10,2},{3,11},{11,3},{4,12},{12,4},... | collective-permute-start | bytes 2211848 | tf_op jit(solution)/shard_map/ppermute | solution.py:80
  75.2 30.8 %copy-start.1 = (bf16[4,720,128]{2,1,0:T(8,128)(2,1)}, bf16[4,720,128]{2,1,0:T(8,128)(2,1)S(1)}, u32[]{:S(2)}) copy-start(bf16[4,720,128]{2,1,0:T(8,128)(2,1)S(1)} %collective-permute-done.11) | copy-start | bytes 2211844
  82.1 26.0 %copy-start.3 = (bf16[4,720,128]{2,1,0:T(8,128)(2,1)}, bf16[4,720,128]{2,1,0:T(8,128)(2,1)S(1)}, u32[]{:S(2)}) copy-start(bf16[4,720,128]{2,1,0:T(8,128)(2,1)S(1)} %collective-permute-done.4) | copy-start | bytes 2211844
  82.1 18.7 %collective-permute-start.5 = (bf16[4,720,128]{2,1,0:T(8,128)(2,1)S(1)}, bf16[4,720,128]{2,1,0:T(8,128)(2,1)S(1)}, u32[]{:S(2)}, u32[]{:S(2)}) collective-permute-start(bf16[4,720,128]{2,1,0:T(8,128)(2,1)S(1)} %collective-permute-done.4), channel_id=1, source_target_pairs={{0,16},{16,32},{32,48},{48,64},{64,80},{80,96},{96,112},{112,0},{1... | collective-permute-start | bytes 2211848 | tf_op jit(solution)/shard_map/ppermute | solution.py:80
  84.0 24.8 %copy-start.7 = (bf16[4,720,128]{2,1,0:T(8,128)(2,1)}, bf16[4,720,128]{2,1,0:T(8,128)(2,1)S(1)}, u32[]{:S(2)}) copy-start(bf16[4,720,128]{2,1,0:T(8,128)(2,1)S(1)} %collective-permute-done.7) | copy-start | bytes 2211844
  84.1 21.9 %collective-permute-start.8 = (bf16[4,720,128]{2,1,0:T(8,128)(2,1)S(1)}, bf16[4,720,128]{2,1,0:T(8,128)(2,1)S(1)}, u32[]{:S(2)}, u32[]{:S(2)}) collective-permute-start(bf16[4,720,128]{2,1,0:T(8,128)(2,1)S(1)} %collective-permute-done.7), channel_id=1, source_target_pairs={{0,112},{16,0},{32,16},{48,32},{64,48},{80,64},{96,80},{112,96},{1... | collective-permute-start | bytes 2211848 | tf_op jit(solution)/shard_map/ppermute | solution.py:80
  88.7 19.4 %collective-permute-start.14 = (bf16[4,720,128]{2,1,0:T(8,128)(2,1)S(1)}, bf16[4,720,128]{2,1,0:T(8,128)(2,1)S(1)}, u32[]{:S(2)}, u32[]{:S(2)}) collective-permute-start(bf16[4,720,128]{2,1,0:T(8,128)(2,1)S(1)} %collective-permute-done.4), channel_id=1, source_target_pairs={{0,8},{8,0},{1,9},{9,1},{2,10},{10,2},{3,11},{11,3},{4,12},{12,4},... | collective-permute-start | bytes 2211848 | tf_op jit(solution)/shard_map/ppermute | solution.py:80
  93.7 7.1 %copy-start.9 = (bf16[4,720,128]{2,1,0:T(8,128)(2,1)}, bf16[4,720,128]{2,1,0:T(8,128)(2,1)S(1)}, u32[]{:S(2)}) copy-start(bf16[4,720,128]{2,1,0:T(8,128)(2,1)S(1)} %collective-permute-done.12) | copy-start | bytes 2211844
  93.7 15.2 %collective-permute-start.15 = (bf16[4,720,128]{2,1,0:T(8,128)(2,1)S(1)}, bf16[4,720,128]{2,1,0:T(8,128)(2,1)S(1)}, u32[]{:S(2)}, u32[]{:S(2)}) collective-permute-start(bf16[4,720,128]{2,1,0:T(8,128)(2,1)S(1)} %collective-permute-done.7), channel_id=1, source_target_pairs={{0,8},{8,0},{1,9},{9,1},{2,10},{10,2},{3,11},{11,3},{4,12},{12,4},... | collective-permute-start | bytes 2211848 | tf_op jit(solution)/shard_map/ppermute | solution.py:80
  96.3 14.0 %copy-start.11 = (bf16[4,720,128]{2,1,0:T(8,128)(2,1)}, bf16[4,720,128]{2,1,0:T(8,128)(2,1)S(1)}, u32[]{:S(2)}) copy-start(bf16[4,720,128]{2,1,0:T(8,128)(2,1)S(1)} %collective-permute-done.13) | copy-start | bytes 2211844
  100.8 8.7 %collective-permute-start.16 = (bf16[4,720,128]{2,1,0:T(8,128)(2,1)S(1)}, bf16[4,720,128]{2,1,0:T(8,128)(2,1)S(1)}, u32[]{:S(2)}, u32[]{:S(2)}) collective-permute-start(bf16[4,720,128]{2,1,0:T(8,128)(2,1)S(1)} %collective-permute-done.5), channel_id=1, source_target_pairs={{0,8},{8,0},{1,9},{9,1},{2,10},{10,2},{3,11},{11,3},{4,12},{12,4},... | collective-permute-start | bytes 2211848 | tf_op jit(solution)/shard_map/ppermute | solution.py:80
  106.1 4.1 %copy-start.42 = (bf16[4096,128]{1,0:T(8,128)(2,1)}, bf16[4096,128]{1,0:T(8,128)(2,1)S(1)}, u32[]{:S(2)}) copy-start(bf16[4096,128]{1,0:T(8,128)(2,1)S(1)} %constant_dynamic-update-slice_fusion.38) | copy-start | bytes 3145732
  106.1 4.1 %collective-permute-start.17 = (bf16[4,720,128]{2,1,0:T(8,128)(2,1)S(1)}, bf16[4,720,128]{2,1,0:T(8,128)(2,1)S(1)}, u32[]{:S(2)}, u32[]{:S(2)}) collective-permute-start(bf16[4,720,128]{2,1,0:T(8,128)(2,1)S(1)} %collective-permute-done.8), channel_id=1, source_target_pairs={{0,8},{8,0},{1,9},{9,1},{2,10},{10,2},{3,11},{11,3},{4,12},{12,4},... | collective-permute-start | bytes 2211848 | tf_op jit(solution)/shard_map/ppermute | solution.py:80
  121.8 16.6 %collective-permute-start.9 = (bf16[2,720,128]{2,1,0:T(8,128)(2,1)S(1)}, bf16[2,720,128]{2,1,0:T(8,128)(2,1)S(1)}, u32[]{:S(2)}, u32[]{:S(2)}) collective-permute-start(bf16[2,720,128]{2,1,0:T(8,128)(2,1)S(1)} %slice.261), channel_id=1, source_target_pairs={{0,16},{16,32},{32,48},{48,64},{64,80},{80,96},{96,112},{112,0},{1... | collective-permute-start | bytes 1105928 | tf_op jit(solution)/shard_map/ppermute | solution.py:80
  123.8 14.7 %collective-permute-start.10 = (bf16[2,720,128]{2,1,0:T(8,128)(2,1)S(1)}, bf16[2,720,128]{2,1,0:T(8,128)(2,1)S(1)}, u32[]{:S(2)}, u32[]{:S(2)}) collective-permute-start(bf16[2,720,128]{2,1,0:T(8,128)(2,1)S(1)} %slice.262), channel_id=1, source_target_pairs={{0,112},{16,0},{32,16},{48,32},{64,48},{80,64},{96,80},{112,96},{1... | collective-permute-start | bytes 1105928 | tf_op jit(solution)/shard_map/ppermute | solution.py:80
  138.3 8.6 %copy-start.24 = (bf16[4,64,128]{2,1,0:T(8,128)(2,1)S(1)}, bf16[4,64,128]{2,1,0:T(8,128)(2,1)}, u32[]{:S(2)}) copy-start(bf16[4,64,128]{2,1,0:T(8,128)(2,1)} %get-tuple-element.29) | copy-start | bytes 196612
  138.3 9.2 %copy-start.27 = (bf16[4,64,128]{2,1,0:T(8,128)(2,1)S(1)}, bf16[4,64,128]{2,1,0:T(8,128)(2,1)}, u32[]{:S(2)}) copy-start(bf16[4,64,128]{2,1,0:T(8,128)(2,1)} %get-tuple-element.27) | copy-start | bytes 196612
  138.3 9.8 %copy-start.28 = (bf16[4,64,128]{2,1,0:T(8,128)(2,1)S(1)}, bf16[4,64,128]{2,1,0:T(8,128)(2,1)}, u32[]{:S(2)}) copy-start(bf16[4,64,128]{2,1,0:T(8,128)(2,1)} %get-tuple-element.25) | copy-start | bytes 196612
  138.4 10.5 %copy-start.33 = (bf16[4,64,128]{2,1,0:T(8,128)(2,1)S(1)}, bf16[4,64,128]{2,1,0:T(8,128)(2,1)}, u32[]{:S(2)}) copy-start(bf16[4,64,128]{2,1,0:T(8,128)(2,1)} %get-tuple-element.23) | copy-start | bytes 196612
  138.4 11.1 %copy-start.34 = (bf16[4,64,128]{2,1,0:T(8,128)(2,1)S(1)}, bf16[4,64,128]{2,1,0:T(8,128)(2,1)}, u32[]{:S(2)}) copy-start(bf16[4,64,128]{2,1,0:T(8,128)(2,1)} %get-tuple-element.21) | copy-start | bytes 196612
  138.4 11.7 %copy-start.35 = (bf16[4,64,128]{2,1,0:T(8,128)(2,1)S(1)}, bf16[4,64,128]{2,1,0:T(8,128)(2,1)}, u32[]{:S(2)}) copy-start(bf16[4,64,128]{2,1,0:T(8,128)(2,1)} %get-tuple-element.19) | copy-start | bytes 196612
  138.4 12.3 %copy-start.36 = (bf16[4,64,128]{2,1,0:T(8,128)(2,1)S(1)}, bf16[4,64,128]{2,1,0:T(8,128)(2,1)}, u32[]{:S(2)}) copy-start(bf16[4,64,128]{2,1,0:T(8,128)(2,1)} %get-tuple-element.17) | copy-start | bytes 196612
  138.4 13.6 %copy-start.23 = (bf16[4,64,128]{2,1,0:T(8,128)(2,1)S(1)}, bf16[4,64,128]{2,1,0:T(8,128)(2,1)}, u32[]{:S(2)}) copy-start(bf16[4,64,128]{2,1,0:T(8,128)(2,1)} %get-tuple-element.30) | copy-start | bytes 196612
  138.5 14.2 %copy-start.25 = (bf16[4,64,128]{2,1,0:T(8,128)(2,1)S(1)}, bf16[4,64,128]{2,1,0:T(8,128)(2,1)}, u32[]{:S(2)}) copy-start(bf16[4,64,128]{2,1,0:T(8,128)(2,1)} %get-tuple-element.28) | copy-start | bytes 196612
  138.5 14.8 %copy-start.26 = (bf16[4,64,128]{2,1,0:T(8,128)(2,1)S(1)}, bf16[4,64,128]{2,1,0:T(8,128)(2,1)}, u32[]{:S(2)}) copy-start(bf16[4,64,128]{2,1,0:T(8,128)(2,1)} %get-tuple-element.26) | copy-start | bytes 196612
  138.5 15.4 %copy-start.29 = (bf16[4,64,128]{2,1,0:T(8,128)(2,1)S(1)}, bf16[4,64,128]{2,1,0:T(8,128)(2,1)}, u32[]{:S(2)}) copy-start(bf16[4,64,128]{2,1,0:T(8,128)(2,1)} %get-tuple-element.24) | copy-start | bytes 196612
  138.5 16.1 %copy-start.30 = (bf16[4,64,128]{2,1,0:T(8,128)(2,1)S(1)}, bf16[4,64,128]{2,1,0:T(8,128)(2,1)}, u32[]{:S(2)}) copy-start(bf16[4,64,128]{2,1,0:T(8,128)(2,1)} %get-tuple-element.22) | copy-start | bytes 196612
  138.5 16.7 %copy-start.31 = (bf16[4,64,128]{2,1,0:T(8,128)(2,1)S(1)}, bf16[4,64,128]{2,1,0:T(8,128)(2,1)}, u32[]{:S(2)}) copy-start(bf16[4,64,128]{2,1,0:T(8,128)(2,1)} %get-tuple-element.20) | copy-start | bytes 196612
  138.6 17.2 %copy-start.32 = (bf16[4,64,128]{2,1,0:T(8,128)(2,1)S(1)}, bf16[4,64,128]{2,1,0:T(8,128)(2,1)}, u32[]{:S(2)}) copy-start(bf16[4,64,128]{2,1,0:T(8,128)(2,1)} %get-tuple-element.18) | copy-start | bytes 196612
  138.6 19.3 %collective-permute-start.18 = (bf16[4,720,128]{2,1,0:T(8,128)(2,1)S(1)}, bf16[4,720,128]{2,1,0:T(8,128)(2,1)S(1)}, u32[]{:S(2)}, u32[]{:S(2)}) collective-permute-start(bf16[4,720,128]{2,1,0:T(8,128)(2,1)S(1)} %constant_dynamic-update-slice_fusion.11), channel_id=1, source_target_pairs={{0,8},{8,0},{1,9},{9,1},{2,10},{10,2},{3,11},{11,3},{4,12},{12,4},... | collective-permute-start | bytes 2211848 | tf_op jit(solution)/shard_map/ppermute | solution.py:80
  (21 other events, 27.3 us)
Sparse Core Ops, SparseCore 0:
  27.3 86.5 all-gather.1

commit v7 on v6

--- a/solution.py
+++ b/solution.py
@@ -138,9 +138,9 @@
         forward = shifted(forward, "z", n_z, -1)
         backward = shifted(backward, "z", n_z, 1)
         arrived += [(-step, forward), (step, backward)]
-    normed5, forward, backward = lax.optimization_barrier((normed5, forward, backward))
     far_front = shifted(forward[:split], "z", n_z, -1)
     far_back = shifted(backward[split:], "z", n_z, 1)
+    normed5, far_front, far_back = lax.optimization_barrier((normed5, far_front, far_back))
     arrived.append((far, jnp.concatenate([far_front, far_back], axis=0)))
     held = [(offset, 0, piece) for offset, piece in arrived]
     held += [(offset, 1, shifted(piece, "core", 2, 1)) for offset, piece in arrived]

time: 190 us -> 191 us (level)
  local copies, waits for them, and re-layouts: 40.5 us -> 45 us
  starting transfers between devices: 74.4 us -> 71.6 us
  waiting for transfers between devices: 25 us -> 22.2 us
    ppermute x19, starting transfers between devices: 74.4 us -> 71.5 us  [shifted(): return lax.ppermute(x, axis, pairs)]
    unnamed x156 -> x154, local copies, waits for them, and re-layouts: 25.8 us -> 26 us
  transfers between devices with their start and end apart: 20 -> 20, of which waited for: 5 -> 4; matrix products, arithmetic and copies ran while one was open for 16% -> 22% of each run, Pallas kernels for 0% -> 0%
where the time goes in v7:
time: 191 us; the launch traced here: 188 us
  starting transfers between devices  71.6 us (37%)
  local copies, waits for them, and re-layouts  45 us (24%)
  waiting for transfers between devices  22.2 us (12%)
  between operations  15.9 us (8%)
  Pallas kernels  15.5 us (8%)
  matrix products  9.93 us (5%)
  other arithmetic  7.79 us (4%)
    ppermute x19, starting transfers between devices, shifted(): return lax.ppermute(x, axis, pairs)  71.5 us
    unnamed x154, local copies, waits for them, and re-layouts  26 us
    ppermute x19, waiting for transfers between devices, shifted(): return lax.ppermute(x, axis, pairs)  22.2 us
    pallas_call x1, Pallas kernels, attend(): pl.pallas_call(attend_kernel, grid=(passes, heads), in_specs=[pl.BlockSpe...  15.5 us
    dot_general x16, matrix products, local(): jnp.einsum('rki,kjid->rjd', normed5[:, :, offset % n_z, core, :], piece.r...  9.93 us
    slice x16, local copies, waits for them, and re-layouts, local(): piece[:, value_start:used, :].reshape(-1, HD)  6.71 us
  transfers between devices with their start and end apart: 20, of which 4 were waited for; matrix products, arithmetic and copies ran while one was open for 22% of the time, Pallas kernels for 0%

profile of v7, /device:TPU:1, one launch (start us, length us, event | category | flops | bytes accessed | tf_op | source)
XLA Modules:
  0.0 188.0 jit_solution(9038244831286559071)
XLA Ops:
  8.0 0.7 constant_dynamic-update-slice_fusion.9
  8.7 0.7 constant_dynamic-update-slice_fusion.8
  10.2 0.7 constant_dynamic-update-slice_fusion.6
  10.9 0.7 constant_dynamic-update-slice_fusion.5
  13.9 6.0 %collective-permute-start = (bf16[720,128]{1,0:T(8,128)(2,1)S(1)}, bf16[720,128]{1,0:T(8,128)(2,1)S(1)}, u32[]{:S(2)}, u32[]{:S(2)}) collective-permute-start(bf16[720,128]{1,0:T(8,128)(2,1)S(1)} %constant_dynamic-update-slice_fusion), channel_id=1, source_target_pairs={{0,384},{128,0},{256,128},{384,256},{1,385},{129,1},{257,129},{385... | collective-permute-start | bytes 552968 | tf_op jit(solution)/shard_map/ppermute | solution.py:80
  19.9 1.9 %collective-permute-start.1 = (bf16[720,128]{1,0:T(8,128)(2,1)S(1)}, bf16[720,128]{1,0:T(8,128)(2,1)S(1)}, u32[]{:S(2)}, u32[]{:S(2)}) collective-permute-start(bf16[720,128]{1,0:T(8,128)(2,1)S(1)} %constant_dynamic-update-slice_fusion), channel_id=1, source_target_pairs={{0,256},{128,384},{256,0},{384,128},{1,257},{129,385},{257,1},{385... | collective-permute-start | bytes 552968 | tf_op jit(solution)/shard_map/ppermute | solution.py:80
  21.8 2.3 %collective-permute-start.2 = (bf16[720,128]{1,0:T(8,128)(2,1)S(1)}, bf16[720,128]{1,0:T(8,128)(2,1)S(1)}, u32[]{:S(2)}, u32[]{:S(2)}) collective-permute-start(bf16[720,128]{1,0:T(8,128)(2,1)S(1)} %constant_dynamic-update-slice_fusion), channel_id=1, source_target_pairs={{0,128},{128,256},{256,384},{384,0},{1,129},{129,257},{257,385},{3... | collective-permute-start | bytes 552968 | tf_op jit(solution)/shard_map/ppermute | solution.py:80
  24.2 1.1 copy.44
  25.3 1.1 copy.45
  26.3 0.8 pad_maximum_fusion.1
  30.0 4.9 %collective-permute-done.1 = bf16[720,128]{1,0:T(8,128)(2,1)S(1)} collective-permute-done((bf16[720,128]{1,0:T(8,128)(2,1)S(1)}, bf16[720,128]{1,0:T(8,128)(2,1)S(1)}, u32[]{:S(2)}, u32[]{:S(2)}) %collective-permute-start.1) | collective-permute-done | bytes 184352 | tf_op jit(solution)/shard_map/ppermute | solution.py:80
  35.1 5.0 %collective-permute-start.3 = (bf16[4,720,128]{2,1,0:T(8,128)(2,1)S(1)}, bf16[4,720,128]{2,1,0:T(8,128)(2,1)S(1)}, u32[]{:S(2)}, u32[]{:S(2)}) collective-permute-start(bf16[4,720,128]{2,1,0:T(8,128)(2,1)S(1)} %pad_maximum_fusion), channel_id=1, source_target_pairs={{0,16},{16,32},{32,48},{48,64},{64,80},{80,96},{96,112},{112,0},{1... | collective-permute-start | bytes 2211848 | tf_op jit(solution)/shard_map/ppermute | solution.py:80
  40.3 8.6 %collective-permute-start.7 = (bf16[4,720,128]{2,1,0:T(8,128)(2,1)S(1)}, bf16[4,720,128]{2,1,0:T(8,128)(2,1)}, u32[]{:S(2)}, u32[]{:S(2)}) collective-permute-start(bf16[4,720,128]{2,1,0:T(8,128)(2,1)S(1)} %pad_maximum_fusion), channel_id=1, source_target_pairs={{0,112},{16,0},{32,16},{48,32},{64,48},{80,64},{96,80},{112,96},{1... | collective-permute-start | bytes 2211848 | tf_op jit(solution)/shard_map/ppermute | solution.py:80
  51.1 3.2 %collective-permute-start.11 = (bf16[4,720,128]{2,1,0:T(8,128)(2,1)S(1)}, bf16[4,720,128]{2,1,0:T(8,128)(2,1)S(1)}, u32[]{:S(2)}, u32[]{:S(2)}) collective-permute-start(bf16[4,720,128]{2,1,0:T(8,128)(2,1)S(1)} %pad_maximum_fusion), channel_id=1, source_target_pairs={{0,8},{8,0},{1,9},{9,1},{2,10},{10,2},{3,11},{11,3},{4,12},{12,4},... | collective-permute-start | bytes 2211848 | tf_op jit(solution)/shard_map/ppermute | solution.py:80
  54.4 8.2 %collective-permute-done.3 = bf16[4,720,128]{2,1,0:T(8,128)(2,1)S(1)} collective-permute-done((bf16[4,720,128]{2,1,0:T(8,128)(2,1)S(1)}, bf16[4,720,128]{2,1,0:T(8,128)(2,1)S(1)}, u32[]{:S(2)}, u32[]{:S(2)}) %collective-permute-start.3) | collective-permute-done | bytes 737312 | tf_op jit(solution)/shard_map/ppermute | solution.py:80
  62.5 1.9 %collective-permute-start.4 = (bf16[4,720,128]{2,1,0:T(8,128)(2,1)S(1)}, bf16[4,720,128]{2,1,0:T(8,128)(2,1)S(1)}, u32[]{:S(2)}, u32[]{:S(2)}) collective-permute-start(bf16[4,720,128]{2,1,0:T(8,128)(2,1)S(1)} %collective-permute-done.3), channel_id=1, source_target_pairs={{0,16},{16,32},{32,48},{48,64},{64,80},{80,96},{96,112},{112,0},{1... | collective-permute-start | bytes 2211848 | tf_op jit(solution)/shard_map/ppermute | solution.py:80
  64.5 4.6 %collective-permute-start.8 = (bf16[4,720,128]{2,1,0:T(8,128)(2,1)}, bf16[4,720,128]{2,1,0:T(8,128)(2,1)S(1)}, u32[]{:S(2)}, u32[]{:S(2)}) collective-permute-start(bf16[4,720,128]{2,1,0:T(8,128)(2,1)} %collective-permute-done.7), channel_id=1, source_target_pairs={{0,112},{16,0},{32,16},{48,32},{64,48},{80,64},{96,80},{112,96},{1... | collective-permute-start | bytes 2211848 | tf_op jit(solution)/shard_map/ppermute | solution.py:80
  69.1 0.9 fusion.80
  70.0 4.1 %collective-permute-start.12 = (bf16[4,720,128]{2,1,0:T(8,128)(2,1)S(1)}, bf16[4,720,128]{2,1,0:T(8,128)(2,1)S(1)}, u32[]{:S(2)}, u32[]{:S(2)}) collective-permute-start(bf16[4,720,128]{2,1,0:T(8,128)(2,1)S(1)} %collective-permute-done.3), channel_id=1, source_target_pairs={{0,8},{8,0},{1,9},{9,1},{2,10},{10,2},{3,11},{11,3},{4,12},{12,4},... | collective-permute-start | bytes 2211848 | tf_op jit(solution)/shard_map/ppermute | solution.py:80
  74.1 1.9 %collective-permute-start.13 = (bf16[4,720,128]{2,1,0:T(8,128)(2,1)}, bf16[4,720,128]{2,1,0:T(8,128)(2,1)S(1)}, u32[]{:S(2)}, u32[]{:S(2)}) collective-permute-start(bf16[4,720,128]{2,1,0:T(8,128)(2,1)} %collective-permute-done.7), channel_id=1, source_target_pairs={{0,8},{8,0},{1,9},{9,1},{2,10},{10,2},{3,11},{11,3},{4,12},{12,4},... | collective-permute-start | bytes 2211848 | tf_op jit(solution)/shard_map/ppermute | solution.py:80
  76.8 6.4 %collective-permute-done.8 = bf16[4,720,128]{2,1,0:T(8,128)(2,1)S(1)} collective-permute-done((bf16[4,720,128]{2,1,0:T(8,128)(2,1)}, bf16[4,720,128]{2,1,0:T(8,128)(2,1)S(1)}, u32[]{:S(2)}, u32[]{:S(2)}) %collective-permute-start.8) | collective-permute-done | bytes 737312 | tf_op jit(solution)/shard_map/ppermute | solution.py:80
  83.2 5.3 %collective-permute-start.9 = (bf16[4,720,128]{2,1,0:T(8,128)(2,1)S(1)}, bf16[4,720,128]{2,1,0:T(8,128)(2,1)S(1)}, u32[]{:S(2)}, u32[]{:S(2)}) collective-permute-start(bf16[4,720,128]{2,1,0:T(8,128)(2,1)S(1)} %collective-permute-done.8), channel_id=1, source_target_pairs={{0,112},{16,0},{32,16},{48,32},{64,48},{80,64},{96,80},{112,96},{1... | collective-permute-start | bytes 2211848 | tf_op jit(solution)/shard_map/ppermute | solution.py:80
  88.6 1.9 %collective-permute-start.5 = (bf16[4,720,128]{2,1,0:T(8,128)(2,1)S(1)}, bf16[4,720,128]{2,1,0:T(8,128)(2,1)S(1)}, u32[]{:S(2)}, u32[]{:S(2)}) collective-permute-start(bf16[4,720,128]{2,1,0:T(8,128)(2,1)S(1)} %collective-permute-done.4), channel_id=1, source_target_pairs={{0,16},{16,32},{32,48},{48,64},{64,80},{80,96},{96,112},{112,0},{1... | collective-permute-start | bytes 2211848 | tf_op jit(solution)/shard_map/ppermute | solution.py:80
  90.6 4.9 %collective-permute-start.14 = (bf16[4,720,128]{2,1,0:T(8,128)(2,1)S(1)}, bf16[4,720,128]{2,1,0:T(8,128)(2,1)S(1)}, u32[]{:S(2)}, u32[]{:S(2)}) collective-permute-start(bf16[4,720,128]{2,1,0:T(8,128)(2,1)S(1)} %collective-permute-done.4), channel_id=1, source_target_pairs={{0,8},{8,0},{1,9},{9,1},{2,10},{10,2},{3,11},{11,3},{4,12},{12,4},... | collective-permute-start | bytes 2211848 | tf_op jit(solution)/shard_map/ppermute | solution.py:80
  95.5 1.9 %collective-permute-start.15 = (bf16[4,720,128]{2,1,0:T(8,128)(2,1)S(1)}, bf16[4,720,128]{2,1,0:T(8,128)(2,1)S(1)}, u32[]{:S(2)}, u32[]{:S(2)}) collective-permute-start(bf16[4,720,128]{2,1,0:T(8,128)(2,1)S(1)} %collective-permute-done.8), channel_id=1, source_target_pairs={{0,8},{8,0},{1,9},{9,1},{2,10},{10,2},{3,11},{11,3},{4,12},{12,4},... | collective-permute-start | bytes 2211848 | tf_op jit(solution)/shard_map/ppermute | solution.py:80
  98.8 2.7 %collective-permute-done.9 = bf16[4,720,128]{2,1,0:T(8,128)(2,1)S(1)} collective-permute-done((bf16[4,720,128]{2,1,0:T(8,128)(2,1)S(1)}, bf16[4,720,128]{2,1,0:T(8,128)(2,1)S(1)}, u32[]{:S(2)}, u32[]{:S(2)}) %collective-permute-start.9) | collective-permute-done | bytes 737312 | tf_op jit(solution)/shard_map/ppermute | solution.py:80
  101.5 0.8 slice.331
  102.3 5.4 %collective-permute-start.10 = (bf16[2,720,128]{2,1,0:T(8,128)(2,1)}, bf16[2,720,128]{2,1,0:T(8,128)(2,1)}, u32[]{:S(2)}, u32[]{:S(2)}) collective-permute-start(bf16[2,720,128]{2,1,0:T(8,128)(2,1)} %slice.331), channel_id=1, source_target_pairs={{0,112},{16,0},{32,16},{48,32},{64,48},{80,64},{96,80},{112,96},{1... | collective-permute-start | bytes 1105928 | tf_op jit(solution)/shard_map/ppermute | solution.py:80
  107.8 5.7 %collective-permute-start.16 = (bf16[4,720,128]{2,1,0:T(8,128)(2,1)S(1)}, bf16[4,720,128]{2,1,0:T(8,128)(2,1)S(1)}, u32[]{:S(2)}, u32[]{:S(2)}) collective-permute-start(bf16[4,720,128]{2,1,0:T(8,128)(2,1)S(1)} %collective-permute-done.5), channel_id=1, source_target_pairs={{0,8},{8,0},{1,9},{9,1},{2,10},{10,2},{3,11},{11,3},{4,12},{12,4},... | collective-permute-start | bytes 2211848 | tf_op jit(solution)/shard_map/ppermute | solution.py:80
  113.6 1.9 %collective-permute-start.17 = (bf16[4,720,128]{2,1,0:T(8,128)(2,1)S(1)}, bf16[4,720,128]{2,1,0:T(8,128)(2,1)S(1)}, u32[]{:S(2)}, u32[]{:S(2)}) collective-permute-start(bf16[4,720,128]{2,1,0:T(8,128)(2,1)S(1)} %collective-permute-done.9), channel_id=1, source_target_pairs={{0,8},{8,0},{1,9},{9,1},{2,10},{10,2},{3,11},{11,3},{4,12},{12,4},... | collective-permute-start | bytes 2211848 | tf_op jit(solution)/shard_map/ppermute | solution.py:80
  115.6 0.8 slice.330
  116.4 1.9 %collective-permute-start.6 = (bf16[2,720,128]{2,1,0:T(8,128)(2,1)}, bf16[2,720,128]{2,1,0:T(8,128)(2,1)}, u32[]{:S(2)}, u32[]{:S(2)}) collective-permute-start(bf16[2,720,128]{2,1,0:T(8,128)(2,1)} %slice.330), channel_id=1, source_target_pairs={{0,16},{16,32},{32,48},{48,64},{64,80},{80,96},{96,112},{112,0},{1... | collective-permute-start | bytes 1105928 | tf_op jit(solution)/shard_map/ppermute | solution.py:80
  120.6 0.9 copy-done.11
  122.2 2.3 %slice_bitcast_fusion.2 = (bf16[128,5120]{0,1:T(8,128)(2,1)S(1)}, bf16[1,128,5120]{1,2,0:T(8,128)(2,1)S(1)}, bf16[1,128,5120]{1,2,0:T(8,128)(2,1)S(1)}) fusion(bf16[2,128,5120]{1,2,0:T(8,128)(2,1)} %all-gather.2.cloned.1.call-done), kind=kLoop, calls=%fused_computation.180 | loop fusion | bytes 6553600 | tf_op jit(solution)/shard_map/squeeze | solution.py:123
  126.4 0.8 multiply_convert_fusion
  127.2 0.9 fusion.2
  128.2 0.9 fusion.1
  129.1 0.9 fusion
  130.1 1.0 constant_dynamic-update-slice_fusion.12
  131.1 1.0 constant_dynamic-update-slice_fusion.11
  132.2 2.8 %collective-permute-start.18 = (bf16[4,720,128]{2,1,0:T(8,128)(2,1)S(1)}, bf16[4,720,128]{2,1,0:T(8,128)(2,1)S(1)}, u32[]{:S(2)}, u32[]{:S(2)}) collective-permute-start(bf16[4,720,128]{2,1,0:T(8,128)(2,1)S(1)} %constant_dynamic-update-slice_fusion.11), channel_id=1, source_target_pairs={{0,8},{8,0},{1,9},{9,1},{2,10},{10,2},{3,11},{11,3},{4,12},{12,4},... | collective-permute-start | bytes 2211848 | tf_op jit(solution)/shard_map/ppermute | solution.py:80
  135.0 1.6 convolution_bitcast_fusion.13
  155.8 1.1 fusion.14
  157.5 0.8 copy-done.10
  159.9 0.9 copy.69.q_ref
  162.3 0.9 fusion.67
  163.9 15.5 %shard_map.149 = bf16[2,128,640]{2,1,0:T(8,128)(2,1)} custom-call(bf16[2,128,640]{2,1,0:T(8,128)(2,1)} %copy.69.q_ref, bf16[2,128,128]{2,1,0:T(8,128)(2,1)} %pad_maximum_fusion.3.ko_ref, bf16[2,128,128]{2,1,0:T(8,128)(2,1)} %add_convert_fusion.1.vo_ref, bf16[4096,128]{1,0:T(8,128)(2,1)} %get-tuple-element.71.kc_ref, ...), custom_call_target="tpu_custom_call" | custom-call | flops 2768240640 | bytes 3407872 | tf_op jit(solution)/shard_map/pallas_call | solution.py:57
  179.4 1.7 slice_bitcast_fusion
  (244 shorter events, 38.5 us)
Async XLA Ops:
  7.2 20.8 %copy-start.42 = (bf16[640]{0:T(1024)(128)(2,1)S(1)}, bf16[640]{0:T(1024)(128)(2,1)}, u32[]{:S(2)}) copy-start(bf16[640]{0:T(1024)(128)(2,1)} %param.21) | copy-start | bytes 3844
  7.2 20.8 %copy-start.44 = (s32[1,64]{1,0:T(1,128)S(1)}, s32[1,64]{1,0:T(1,128)}, u32[]{:S(2)}) copy-start(s32[1,64]{1,0:T(1,128)} %param.18) | copy-start | bytes 772
  7.2 22.8 %copy-start.45 = (s32[128]{0:T(128)S(1)}, s32[128]{0:T(128)}, u32[]{:S(2)}) copy-start(s32[128]{0:T(128)} %param.16) | copy-start | bytes 1540
  7.2 115.0 %all-gather.2.cloned.1.call-start = ((), (), s32[]{:S(2)}) async-start(), calls=%async_computation | async-start | bytes 2949120 | tf_op jit(solution)/shard_map/all_gather | solution.py:122
  13.9 16.2 %collective-permute-start = (bf16[720,128]{1,0:T(8,128)(2,1)S(1)}, bf16[720,128]{1,0:T(8,128)(2,1)S(1)}, u32[]{:S(2)}, u32[]{:S(2)}) collective-permute-start(bf16[720,128]{1,0:T(8,128)(2,1)S(1)} %constant_dynamic-update-slice_fusion), channel_id=1, source_target_pairs={{0,384},{128,0},{256,128},{384,256},{1,385},{129,1},{257,129},{385... | collective-permute-start | bytes 552968 | tf_op jit(solution)/shard_map/ppermute | solution.py:80
  19.9 15.1 %collective-permute-start.1 = (bf16[720,128]{1,0:T(8,128)(2,1)S(1)}, bf16[720,128]{1,0:T(8,128)(2,1)S(1)}, u32[]{:S(2)}, u32[]{:S(2)}) collective-permute-start(bf16[720,128]{1,0:T(8,128)(2,1)S(1)} %constant_dynamic-update-slice_fusion), channel_id=1, source_target_pairs={{0,256},{128,384},{256,0},{384,128},{1,257},{129,385},{257,1},{385... | collective-permute-start | bytes 552968 | tf_op jit(solution)/shard_map/ppermute | solution.py:80
  21.8 13.1 %collective-permute-start.2 = (bf16[720,128]{1,0:T(8,128)(2,1)S(1)}, bf16[720,128]{1,0:T(8,128)(2,1)S(1)}, u32[]{:S(2)}, u32[]{:S(2)}) collective-permute-start(bf16[720,128]{1,0:T(8,128)(2,1)S(1)} %constant_dynamic-update-slice_fusion), channel_id=1, source_target_pairs={{0,128},{128,256},{256,384},{384,0},{1,129},{129,257},{257,385},{3... | collective-permute-start | bytes 552968 | tf_op jit(solution)/shard_map/ppermute | solution.py:80
  27.1 21.7 %copy-start.39 = (bf16[5120]{0:T(1024)(128)(2,1)S(1)}, bf16[5120]{0:T(1024)(128)(2,1)}, u32[]{:S(2)}) copy-start(bf16[5120]{0:T(1024)(128)(2,1)} %param.19) | copy-start | bytes 30724
  27.1 22.5 %copy-start.46 = (bf16[128]{0:T(256)(128)(2,1)S(1)}, bf16[128]{0:T(256)(128)(2,1)}, u32[]{:S(2)}) copy-start(bf16[128]{0:T(256)(128)(2,1)} %param.23) | copy-start | bytes 772
  27.1 24.0 %copy-start.47 = (bf16[128]{0:T(256)(128)(2,1)S(1)}, bf16[128]{0:T(256)(128)(2,1)}, u32[]{:S(2)}) copy-start(bf16[128]{0:T(256)(128)(2,1)} %param.25) | copy-start | bytes 772
  29.8 34.6 %copy-start.20 = (f32[128,64]{0,1:T(8,128)}, f32[128,64]{0,1:T(8,128)S(1)}, u32[]{:S(2)}) copy-start(f32[128,64]{0,1:T(8,128)S(1)} %get-tuple-element.70) | copy-start | bytes 98308
  35.0 35.0 %copy-start.18 = (bf16[720,128]{1,0:T(8,128)(2,1)}, bf16[720,128]{1,0:T(8,128)(2,1)S(1)}, u32[]{:S(2)}) copy-start(bf16[720,128]{1,0:T(8,128)(2,1)S(1)} %collective-permute-done.2) | copy-start | bytes 552964
  35.1 27.4 %collective-permute-start.3 = (bf16[4,720,128]{2,1,0:T(8,128)(2,1)S(1)}, bf16[4,720,128]{2,1,0:T(8,128)(2,1)S(1)}, u32[]{:S(2)}, u32[]{:S(2)}) collective-permute-start(bf16[4,720,128]{2,1,0:T(8,128)(2,1)S(1)} %pad_maximum_fusion), channel_id=1, source_target_pairs={{0,16},{16,32},{32,48},{48,64},{64,80},{80,96},{96,112},{112,0},{1... | collective-permute-start | bytes 2211848 | tf_op jit(solution)/shard_map/ppermute | solution.py:80
  40.3 24.2 %collective-permute-start.7 = (bf16[4,720,128]{2,1,0:T(8,128)(2,1)S(1)}, bf16[4,720,128]{2,1,0:T(8,128)(2,1)}, u32[]{:S(2)}, u32[]{:S(2)}) collective-permute-start(bf16[4,720,128]{2,1,0:T(8,128)(2,1)S(1)} %pad_maximum_fusion), channel_id=1, source_target_pairs={{0,112},{16,0},{32,16},{48,32},{64,48},{80,64},{96,80},{112,96},{1... | collective-permute-start | bytes 2211848 | tf_op jit(solution)/shard_map/ppermute | solution.py:80
  51.1 25.0 %collective-permute-start.11 = (bf16[4,720,128]{2,1,0:T(8,128)(2,1)S(1)}, bf16[4,720,128]{2,1,0:T(8,128)(2,1)S(1)}, u32[]{:S(2)}, u32[]{:S(2)}) collective-permute-start(bf16[4,720,128]{2,1,0:T(8,128)(2,1)S(1)} %pad_maximum_fusion), channel_id=1, source_target_pairs={{0,8},{8,0},{1,9},{9,1},{2,10},{10,2},{3,11},{11,3},{4,12},{12,4},... | collective-permute-start | bytes 2211848 | tf_op jit(solution)/shard_map/ppermute | solution.py:80
  62.5 26.0 %collective-permute-start.4 = (bf16[4,720,128]{2,1,0:T(8,128)(2,1)S(1)}, bf16[4,720,128]{2,1,0:T(8,128)(2,1)S(1)}, u32[]{:S(2)}, u32[]{:S(2)}) collective-permute-start(bf16[4,720,128]{2,1,0:T(8,128)(2,1)S(1)} %collective-permute-done.3), channel_id=1, source_target_pairs={{0,16},{16,32},{32,48},{48,64},{64,80},{80,96},{96,112},{112,0},{1... | collective-permute-start | bytes 2211848 | tf_op jit(solution)/shard_map/ppermute | solution.py:80
  64.5 18.7 %collective-permute-start.8 = (bf16[4,720,128]{2,1,0:T(8,128)(2,1)}, bf16[4,720,128]{2,1,0:T(8,128)(2,1)S(1)}, u32[]{:S(2)}, u32[]{:S(2)}) collective-permute-start(bf16[4,720,128]{2,1,0:T(8,128)(2,1)} %collective-permute-done.7), channel_id=1, source_target_pairs={{0,112},{16,0},{32,16},{48,32},{64,48},{80,64},{96,80},{112,96},{1... | collective-permute-start | bytes 2211848 | tf_op jit(solution)/shard_map/ppermute | solution.py:80
  70.0 25.5 %collective-permute-start.12 = (bf16[4,720,128]{2,1,0:T(8,128)(2,1)S(1)}, bf16[4,720,128]{2,1,0:T(8,128)(2,1)S(1)}, u32[]{:S(2)}, u32[]{:S(2)}) collective-permute-start(bf16[4,720,128]{2,1,0:T(8,128)(2,1)S(1)} %collective-permute-done.3), channel_id=1, source_target_pairs={{0,8},{8,0},{1,9},{9,1},{2,10},{10,2},{3,11},{11,3},{4,12},{12,4},... | collective-permute-start | bytes 2211848 | tf_op jit(solution)/shard_map/ppermute | solution.py:80
  74.1 24.0 %collective-permute-start.13 = (bf16[4,720,128]{2,1,0:T(8,128)(2,1)}, bf16[4,720,128]{2,1,0:T(8,128)(2,1)S(1)}, u32[]{:S(2)}, u32[]{:S(2)}) collective-permute-start(bf16[4,720,128]{2,1,0:T(8,128)(2,1)} %collective-permute-done.7), channel_id=1, source_target_pairs={{0,8},{8,0},{1,9},{9,1},{2,10},{10,2},{3,11},{11,3},{4,12},{12,4},... | collective-permute-start | bytes 2211848 | tf_op jit(solution)/shard_map/ppermute | solution.py:80
  76.1 22.0 %copy-start.1 = (bf16[4,720,128]{2,1,0:T(8,128)(2,1)}, bf16[4,720,128]{2,1,0:T(8,128)(2,1)S(1)}, u32[]{:S(2)}) copy-start(bf16[4,720,128]{2,1,0:T(8,128)(2,1)S(1)} %collective-permute-done.11) | copy-start | bytes 2211844
  83.2 24.6 %copy-start.3 = (bf16[4,720,128]{2,1,0:T(8,128)(2,1)}, bf16[4,720,128]{2,1,0:T(8,128)(2,1)S(1)}, u32[]{:S(2)}) copy-start(bf16[4,720,128]{2,1,0:T(8,128)(2,1)S(1)} %collective-permute-done.8) | copy-start | bytes 2211844
  83.2 18.3 %collective-permute-start.9 = (bf16[4,720,128]{2,1,0:T(8,128)(2,1)S(1)}, bf16[4,720,128]{2,1,0:T(8,128)(2,1)S(1)}, u32[]{:S(2)}, u32[]{:S(2)}) collective-permute-start(bf16[4,720,128]{2,1,0:T(8,128)(2,1)S(1)} %collective-permute-done.8), channel_id=1, source_target_pairs={{0,112},{16,0},{32,16},{48,32},{64,48},{80,64},{96,80},{112,96},{1... | collective-permute-start | bytes 2211848 | tf_op jit(solution)/shard_map/ppermute | solution.py:80
  88.6 19.2 %collective-permute-start.5 = (bf16[4,720,128]{2,1,0:T(8,128)(2,1)S(1)}, bf16[4,720,128]{2,1,0:T(8,128)(2,1)S(1)}, u32[]{:S(2)}, u32[]{:S(2)}) collective-permute-start(bf16[4,720,128]{2,1,0:T(8,128)(2,1)S(1)} %collective-permute-done.4), channel_id=1, source_target_pairs={{0,16},{16,32},{32,48},{48,64},{64,80},{80,96},{96,112},{112,0},{1... | collective-permute-start | bytes 2211848 | tf_op jit(solution)/shard_map/ppermute | solution.py:80
  90.6 25.8 %collective-permute-start.14 = (bf16[4,720,128]{2,1,0:T(8,128)(2,1)S(1)}, bf16[4,720,128]{2,1,0:T(8,128)(2,1)S(1)}, u32[]{:S(2)}, u32[]{:S(2)}) collective-permute-start(bf16[4,720,128]{2,1,0:T(8,128)(2,1)S(1)} %collective-permute-done.4), channel_id=1, source_target_pairs={{0,8},{8,0},{1,9},{9,1},{2,10},{10,2},{3,11},{11,3},{4,12},{12,4},... | collective-permute-start | bytes 2211848 | tf_op jit(solution)/shard_map/ppermute | solution.py:80
  95.5 3.3 %copy-start.5 = (bf16[4,720,128]{2,1,0:T(8,128)(2,1)}, bf16[4,720,128]{2,1,0:T(8,128)(2,1)S(1)}, u32[]{:S(2)}) copy-start(bf16[4,720,128]{2,1,0:T(8,128)(2,1)S(1)} %collective-permute-done.12) | copy-start | bytes 2211844
  95.5 23.5 %collective-permute-start.15 = (bf16[4,720,128]{2,1,0:T(8,128)(2,1)S(1)}, bf16[4,720,128]{2,1,0:T(8,128)(2,1)S(1)}, u32[]{:S(2)}, u32[]{:S(2)}) collective-permute-start(bf16[4,720,128]{2,1,0:T(8,128)(2,1)S(1)} %collective-permute-done.8), channel_id=1, source_target_pairs={{0,8},{8,0},{1,9},{9,1},{2,10},{10,2},{3,11},{11,3},{4,12},{12,4},... | collective-permute-start | bytes 2211848 | tf_op jit(solution)/shard_map/ppermute | solution.py:80
  98.1 18.3 %copy-start.7 = (bf16[4,720,128]{2,1,0:T(8,128)(2,1)}, bf16[4,720,128]{2,1,0:T(8,128)(2,1)S(1)}, u32[]{:S(2)}) copy-start(bf16[4,720,128]{2,1,0:T(8,128)(2,1)S(1)} %collective-permute-done.13) | copy-start | bytes 2211844
  102.3 27.7 %collective-permute-start.10 = (bf16[2,720,128]{2,1,0:T(8,128)(2,1)}, bf16[2,720,128]{2,1,0:T(8,128)(2,1)}, u32[]{:S(2)}, u32[]{:S(2)}) collective-permute-start(bf16[2,720,128]{2,1,0:T(8,128)(2,1)} %slice.331), channel_id=1, source_target_pairs={{0,112},{16,0},{32,16},{48,32},{64,48},{80,64},{96,80},{112,96},{1... | collective-permute-start | bytes 1105928 | tf_op jit(solution)/shard_map/ppermute | solution.py:80
  107.8 11.9 %collective-permute-start.16 = (bf16[4,720,128]{2,1,0:T(8,128)(2,1)S(1)}, bf16[4,720,128]{2,1,0:T(8,128)(2,1)S(1)}, u32[]{:S(2)}, u32[]{:S(2)}) collective-permute-start(bf16[4,720,128]{2,1,0:T(8,128)(2,1)S(1)} %collective-permute-done.5), channel_id=1, source_target_pairs={{0,8},{8,0},{1,9},{9,1},{2,10},{10,2},{3,11},{11,3},{4,12},{12,4},... | collective-permute-start | bytes 2211848 | tf_op jit(solution)/shard_map/ppermute | solution.py:80
  113.6 6.9 %copy-start.41 = (bf16[4096,128]{1,0:T(8,128)(2,1)}, bf16[4096,128]{1,0:T(8,128)(2,1)S(1)}, u32[]{:S(2)}) copy-start(bf16[4096,128]{1,0:T(8,128)(2,1)S(1)} %constant_dynamic-update-slice_fusion.38) | copy-start | bytes 3145732
  113.6 6.9 %collective-permute-start.17 = (bf16[4,720,128]{2,1,0:T(8,128)(2,1)S(1)}, bf16[4,720,128]{2,1,0:T(8,128)(2,1)S(1)}, u32[]{:S(2)}, u32[]{:S(2)}) collective-permute-start(bf16[4,720,128]{2,1,0:T(8,128)(2,1)S(1)} %collective-permute-done.9), channel_id=1, source_target_pairs={{0,8},{8,0},{1,9},{9,1},{2,10},{10,2},{3,11},{11,3},{4,12},{12,4},... | collective-permute-start | bytes 2211848 | tf_op jit(solution)/shard_map/ppermute | solution.py:80
  115.6 4.9 %copy-start.40 = (bf16[4096,128]{1,0:T(8,128)(2,1)}, bf16[4096,128]{1,0:T(8,128)(2,1)S(1)}, u32[]{:S(2)}) copy-start(bf16[4096,128]{1,0:T(8,128)(2,1)S(1)} %constant_dynamic-update-slice_fusion.22) | copy-start | bytes 3145732
  116.4 4.1 %copy-start.13 = (bf16[4,720,128]{2,1,0:T(8,128)(2,1)}, bf16[4,720,128]{2,1,0:T(8,128)(2,1)S(1)}, u32[]{:S(2)}) copy-start(bf16[4,720,128]{2,1,0:T(8,128)(2,1)S(1)} %collective-permute-done.14) | copy-start | bytes 2211844
  116.4 13.7 %collective-permute-start.6 = (bf16[2,720,128]{2,1,0:T(8,128)(2,1)}, bf16[2,720,128]{2,1,0:T(8,128)(2,1)}, u32[]{:S(2)}, u32[]{:S(2)}) collective-permute-start(bf16[2,720,128]{2,1,0:T(8,128)(2,1)} %slice.330), channel_id=1, source_target_pairs={{0,16},{16,32},{32,48},{48,64},{64,80},{80,96},{96,112},{112,0},{1... | collective-permute-start | bytes 1105928 | tf_op jit(solution)/shard_map/ppermute | solution.py:80
  122.2 2.5 %copy-start = (bf16[2,128,5120]{1,2,0:T(8,128)(2,1)S(1)}, bf16[2,128,5120]{1,2,0:T(8,128)(2,1)}, u32[]{:S(2)}) copy-start(bf16[2,128,5120]{1,2,0:T(8,128)(2,1)} %all-gather.2.cloned.1.call-done) | copy-start | bytes 7864324
  132.2 24.8 %collective-permute-start.18 = (bf16[4,720,128]{2,1,0:T(8,128)(2,1)S(1)}, bf16[4,720,128]{2,1,0:T(8,128)(2,1)S(1)}, u32[]{:S(2)}, u32[]{:S(2)}) collective-permute-start(bf16[4,720,128]{2,1,0:T(8,128)(2,1)S(1)} %constant_dynamic-update-slice_fusion.11), channel_id=1, source_target_pairs={{0,8},{8,0},{1,9},{9,1},{2,10},{10,2},{3,11},{11,3},{4,12},{12,4},... | collective-permute-start | bytes 2211848 | tf_op jit(solution)/shard_map/ppermute | solution.py:80
  142.7 3.0 %copy-start.27 = (bf16[4,64,128]{2,1,0:T(8,128)(2,1)S(1)}, bf16[4,64,128]{2,1,0:T(8,128)(2,1)}, u32[]{:S(2)}) copy-start(bf16[4,64,128]{2,1,0:T(8,128)(2,1)} %get-tuple-element.25) | copy-start | bytes 196612
  143.2 3.1 %copy-start.32 = (bf16[4,64,128]{2,1,0:T(8,128)(2,1)S(1)}, bf16[4,64,128]{2,1,0:T(8,128)(2,1)}, u32[]{:S(2)}) copy-start(bf16[4,64,128]{2,1,0:T(8,128)(2,1)} %get-tuple-element.23) | copy-start | bytes 196612
  143.2 3.8 %copy-start.33 = (bf16[4,64,128]{2,1,0:T(8,128)(2,1)S(1)}, bf16[4,64,128]{2,1,0:T(8,128)(2,1)}, u32[]{:S(2)}) copy-start(bf16[4,64,128]{2,1,0:T(8,128)(2,1)} %get-tuple-element.21) | copy-start | bytes 196612
  143.2 4.4 %copy-start.34 = (bf16[4,64,128]{2,1,0:T(8,128)(2,1)S(1)}, bf16[4,64,128]{2,1,0:T(8,128)(2,1)}, u32[]{:S(2)}) copy-start(bf16[4,64,128]{2,1,0:T(8,128)(2,1)} %get-tuple-element.19) | copy-start | bytes 196612
  143.2 5.0 %copy-start.35 = (bf16[4,64,128]{2,1,0:T(8,128)(2,1)S(1)}, bf16[4,64,128]{2,1,0:T(8,128)(2,1)}, u32[]{:S(2)}) copy-start(bf16[4,64,128]{2,1,0:T(8,128)(2,1)} %get-tuple-element.17) | copy-start | bytes 196612
  143.2 6.3 %copy-start.22 = (bf16[4,64,128]{2,1,0:T(8,128)(2,1)S(1)}, bf16[4,64,128]{2,1,0:T(8,128)(2,1)}, u32[]{:S(2)}) copy-start(bf16[4,64,128]{2,1,0:T(8,128)(2,1)} %get-tuple-element.30) | copy-start | bytes 196612
  143.2 6.9 %copy-start.24 = (bf16[4,64,128]{2,1,0:T(8,128)(2,1)S(1)}, bf16[4,64,128]{2,1,0:T(8,128)(2,1)}, u32[]{:S(2)}) copy-start(bf16[4,64,128]{2,1,0:T(8,128)(2,1)} %get-tuple-element.28) | copy-start | bytes 196612
  143.2 7.5 %copy-start.25 = (bf16[4,64,128]{2,1,0:T(8,128)(2,1)S(1)}, bf16[4,64,128]{2,1,0:T(8,128)(2,1)}, u32[]{:S(2)}) copy-start(bf16[4,64,128]{2,1,0:T(8,128)(2,1)} %get-tuple-element.26) | copy-start | bytes 196612
  143.7 7.7 %copy-start.29 = (bf16[4,64,128]{2,1,0:T(8,128)(2,1)S(1)}, bf16[4,64,128]{2,1,0:T(8,128)(2,1)}, u32[]{:S(2)}) copy-start(bf16[4,64,128]{2,1,0:T(8,128)(2,1)} %get-tuple-element.24) | copy-start | bytes 196612
  143.8 8.3 %copy-start.30 = (bf16[4,64,128]{2,1,0:T(8,128)(2,1)S(1)}, bf16[4,64,128]{2,1,0:T(8,128)(2,1)}, u32[]{:S(2)}) copy-start(bf16[4,64,128]{2,1,0:T(8,128)(2,1)} %get-tuple-element.22) | copy-start | bytes 196612
  143.8 8.9 %copy-start.31 = (bf16[4,64,128]{2,1,0:T(8,128)(2,1)S(1)}, bf16[4,64,128]{2,1,0:T(8,128)(2,1)}, u32[]{:S(2)}) copy-start(bf16[4,64,128]{2,1,0:T(8,128)(2,1)} %get-tuple-element.20) | copy-start | bytes 196612
  143.8 9.5 %copy-start.19 = (bf16[720,128]{1,0:T(8,128)(2,1)S(1)}, bf16[720,128]{1,0:T(8,128)(2,1)}, u32[]{:S(2)}) copy-start(bf16[720,128]{1,0:T(8,128)(2,1)} %copy-done.18) | copy-start | bytes 552964
  (20 other events, 25.7 us)
Sparse Core Ops, SparseCore 0:
  27.3 86.8 all-gather.1

commit v8 on v7

--- a/solution.py
+++ b/solution.py
@@ -138,12 +138,23 @@
         forward = shifted(forward, "z", n_z, -1)
         backward = shifted(backward, "z", n_z, 1)
         arrived += [(-step, forward), (step, backward)]
-    far_front = shifted(forward[:split], "z", n_z, -1)
-    far_back = shifted(backward[split:], "z", n_z, 1)
-    normed5, far_front, far_back = lax.optimization_barrier((normed5, far_front, far_back))
-    arrived.append((far, jnp.concatenate([far_front, far_back], axis=0)))
+    pair_index = lambda z, core: (z % n_z) * 2 + core
+    to_partner_front = [(pair_index(z - 1, 1 - c), pair_index(z, c)) for z in range(n_z) for c in range(2)]
+    to_partner_back = [(pair_index(z + 1, 1 - c), pair_index(z, c)) for z in range(n_z) for c in range(2)]
+    far_own = jnp.concatenate(
+        [shifted(forward[:split], "z", n_z, -1), shifted(backward[split:], "z", n_z, 1)], axis=0
+    )
+    far_other = jnp.concatenate(
+        [
+            lax.ppermute(forward[:split], ("z", "core"), to_partner_front),
+            lax.ppermute(backward[split:], ("z", "core"), to_partner_back),
+        ],
+        axis=0,
+    )
+    normed5, far_own, far_other = lax.optimization_barrier((normed5, far_own, far_other))
     held = [(offset, 0, piece) for offset, piece in arrived]
     held += [(offset, 1, shifted(piece, "core", 2, 1)) for offset, piece in arrived]
+    held += [(far, 0, far_own), (far, 1, far_other)]
 
     proj = None
     for offset, core, piece in held:

time: 191 us -> 188 us (0.984)
  local copies, waits for them, and re-layouts: 45 us -> 38.5 us
    ppermute x0 -> x2, starting transfers between devices: none -> 6.08 us  [the longest x1 3.87 us: local(): lax.ppermute(forward[:split], ('z', 'core'), to_partner_front)]
    ppermute x19 -> x18, starting transfers between devices: 71.5 us -> 66.4 us  [shifted(): return lax.ppermute(x, axis, pairs)]
    slice x16 -> x15, local copies, waits for them, and re-layouts: 6.71 us -> 1.75 us  [local(): piece[:, value_start:used, :].reshape(-1, HD)]
    ppermute x0 -> x2, waiting for transfers between devices: none -> 2.59 us  [the longest x1 2.59 us: local(): lax.ppermute(backward[split:], ('z', 'core'), to_partner_back)]
    ppermute x19 -> x18, waiting for transfers between devices: 22.2 us -> 21.1 us  [shifted(): return lax.ppermute(x, axis, pairs)]
    unnamed x154 -> x137, local copies, waits for them, and re-layouts: 26 us -> 26.4 us
  transfers between devices with their start and end apart: 20 -> 21, of which waited for: 4 -> 5; matrix products, arithmetic and copies ran while one was open for 22% -> 10% of each run, Pallas kernels for 0% -> 0%
where the time goes in v8:
time: 188 us; the launch traced here: 184 us
  starting transfers between devices  72.5 us (39%)
  local copies, waits for them, and re-layouts  38.5 us (20%)
  waiting for transfers between devices  23.7 us (13%)
  between operations  15.9 us (8%)
  Pallas kernels  15.5 us (8%)
  matrix products  9.8 us (5%)
  other arithmetic  7.93 us (4%)
    ppermute x18, starting transfers between devices, shifted(): return lax.ppermute(x, axis, pairs)  66.4 us
    unnamed x137, local copies, waits for them, and re-layouts  26.4 us
    ppermute x18, waiting for transfers between devices, shifted(): return lax.ppermute(x, axis, pairs)  21.1 us
    pallas_call x1, Pallas kernels, attend(): pl.pallas_call(attend_kernel, grid=(passes, heads), in_specs=[pl.BlockSpe...  15.5 us
    dot_general x16, matrix products, local(): jnp.einsum('rki,kjid->rjd', normed5[:, :, offset % n_z, core, :], piece.r...  9.8 us
    ppermute x1, starting transfers between devices, local(): lax.ppermute(forward[:split], ('z', 'core'), to_partner_front)  3.87 us
  transfers between devices with their start and end apart: 21, of which 5 were waited for; matrix products, arithmetic and copies ran while one was open for 10% of the time, Pallas kernels for 0%

profile of v8, /device:TPU:1, one launch (start us, length us, event | category | flops | bytes accessed | tf_op | source)
XLA Modules:
  0.0 183.9 jit_solution(12755781501679608010)
XLA Ops:
  8.0 0.7 constant_dynamic-update-slice_fusion.9
  8.7 0.7 constant_dynamic-update-slice_fusion.8
  9.4 0.7 constant_dynamic-update-slice_fusion.7
  10.2 0.7 constant_dynamic-update-slice_fusion.6
  10.9 0.7 constant_dynamic-update-slice_fusion.5
  11.6 0.7 constant_dynamic-update-slice_fusion.4
  13.9 6.0 %collective-permute-start = (bf16[720,128]{1,0:T(8,128)(2,1)S(1)}, bf16[720,128]{1,0:T(8,128)(2,1)S(1)}, u32[]{:S(2)}, u32[]{:S(2)}) collective-permute-start(bf16[720,128]{1,0:T(8,128)(2,1)S(1)} %constant_dynamic-update-slice_fusion), channel_id=1, source_target_pairs={{0,384},{128,0},{256,128},{384,256},{1,385},{129,1},{257,129},{385... | collective-permute-start | bytes 552968 | tf_op jit(solution)/shard_map/ppermute | solution.py:80
  19.9 1.9 %collective-permute-start.1 = (bf16[720,128]{1,0:T(8,128)(2,1)S(1)}, bf16[720,128]{1,0:T(8,128)(2,1)S(1)}, u32[]{:S(2)}, u32[]{:S(2)}) collective-permute-start(bf16[720,128]{1,0:T(8,128)(2,1)S(1)} %constant_dynamic-update-slice_fusion), channel_id=1, source_target_pairs={{0,256},{128,384},{256,0},{384,128},{1,257},{129,385},{257,1},{385... | collective-permute-start | bytes 552968 | tf_op jit(solution)/shard_map/ppermute | solution.py:80
  21.8 2.3 %collective-permute-start.2 = (bf16[720,128]{1,0:T(8,128)(2,1)S(1)}, bf16[720,128]{1,0:T(8,128)(2,1)S(1)}, u32[]{:S(2)}, u32[]{:S(2)}) collective-permute-start(bf16[720,128]{1,0:T(8,128)(2,1)S(1)} %constant_dynamic-update-slice_fusion), channel_id=1, source_target_pairs={{0,128},{128,256},{256,384},{384,0},{1,129},{129,257},{257,385},{3... | collective-permute-start | bytes 552968 | tf_op jit(solution)/shard_map/ppermute | solution.py:80
  24.2 1.1 copy.46
  25.3 1.1 copy.47
  26.4 0.8 pad_maximum_fusion.3
  30.0 4.9 %collective-permute-done.1 = bf16[720,128]{1,0:T(8,128)(2,1)S(1)} collective-permute-done((bf16[720,128]{1,0:T(8,128)(2,1)S(1)}, bf16[720,128]{1,0:T(8,128)(2,1)S(1)}, u32[]{:S(2)}, u32[]{:S(2)}) %collective-permute-start.1) | collective-permute-done | bytes 184352 | tf_op jit(solution)/shard_map/ppermute | solution.py:80
  35.1 5.0 %collective-permute-start.3 = (bf16[4,720,128]{2,1,0:T(8,128)(2,1)S(1)}, bf16[4,720,128]{2,1,0:T(8,128)(2,1)S(1)}, u32[]{:S(2)}, u32[]{:S(2)}) collective-permute-start(bf16[4,720,128]{2,1,0:T(8,128)(2,1)S(1)} %pad_maximum_fusion), channel_id=1, source_target_pairs={{0,16},{16,32},{32,48},{48,64},{64,80},{80,96},{96,112},{112,0},{1... | collective-permute-start | bytes 2211848 | tf_op jit(solution)/shard_map/ppermute | solution.py:80
  40.3 8.6 %collective-permute-start.7 = (bf16[4,720,128]{2,1,0:T(8,128)(2,1)S(1)}, bf16[4,720,128]{2,1,0:T(8,128)(2,1)}, u32[]{:S(2)}, u32[]{:S(2)}) collective-permute-start(bf16[4,720,128]{2,1,0:T(8,128)(2,1)S(1)} %pad_maximum_fusion), channel_id=1, source_target_pairs={{0,112},{16,0},{32,16},{48,32},{64,48},{80,64},{96,80},{112,96},{1... | collective-permute-start | bytes 2211848 | tf_op jit(solution)/shard_map/ppermute | solution.py:80
  51.1 3.2 %collective-permute-start.13 = (bf16[4,720,128]{2,1,0:T(8,128)(2,1)S(1)}, bf16[4,720,128]{2,1,0:T(8,128)(2,1)S(1)}, u32[]{:S(2)}, u32[]{:S(2)}) collective-permute-start(bf16[4,720,128]{2,1,0:T(8,128)(2,1)S(1)} %pad_maximum_fusion), channel_id=1, source_target_pairs={{0,8},{8,0},{1,9},{9,1},{2,10},{10,2},{3,11},{11,3},{4,12},{12,4},... | collective-permute-start | bytes 2211848 | tf_op jit(solution)/shard_map/ppermute | solution.py:80
  55.0 7.5 %collective-permute-done.3 = bf16[4,720,128]{2,1,0:T(8,128)(2,1)S(1)} collective-permute-done((bf16[4,720,128]{2,1,0:T(8,128)(2,1)S(1)}, bf16[4,720,128]{2,1,0:T(8,128)(2,1)S(1)}, u32[]{:S(2)}, u32[]{:S(2)}) %collective-permute-start.3) | collective-permute-done | bytes 737312 | tf_op jit(solution)/shard_map/ppermute | solution.py:80
  62.5 1.9 %collective-permute-start.4 = (bf16[4,720,128]{2,1,0:T(8,128)(2,1)S(1)}, bf16[4,720,128]{2,1,0:T(8,128)(2,1)S(1)}, u32[]{:S(2)}, u32[]{:S(2)}) collective-permute-start(bf16[4,720,128]{2,1,0:T(8,128)(2,1)S(1)} %collective-permute-done.3), channel_id=1, source_target_pairs={{0,16},{16,32},{32,48},{48,64},{64,80},{80,96},{96,112},{112,0},{1... | collective-permute-start | bytes 2211848 | tf_op jit(solution)/shard_map/ppermute | solution.py:80
  64.5 4.6 %collective-permute-start.8 = (bf16[4,720,128]{2,1,0:T(8,128)(2,1)}, bf16[4,720,128]{2,1,0:T(8,128)(2,1)S(1)}, u32[]{:S(2)}, u32[]{:S(2)}) collective-permute-start(bf16[4,720,128]{2,1,0:T(8,128)(2,1)} %collective-permute-done.7), channel_id=1, source_target_pairs={{0,112},{16,0},{32,16},{48,32},{64,48},{80,64},{96,80},{112,96},{1... | collective-permute-start | bytes 2211848 | tf_op jit(solution)/shard_map/ppermute | solution.py:80
  69.1 0.9 fusion.80
  70.0 4.1 %collective-permute-start.14 = (bf16[4,720,128]{2,1,0:T(8,128)(2,1)S(1)}, bf16[4,720,128]{2,1,0:T(8,128)(2,1)S(1)}, u32[]{:S(2)}, u32[]{:S(2)}) collective-permute-start(bf16[4,720,128]{2,1,0:T(8,128)(2,1)S(1)} %collective-permute-done.3), channel_id=1, source_target_pairs={{0,8},{8,0},{1,9},{9,1},{2,10},{10,2},{3,11},{11,3},{4,12},{12,4},... | collective-permute-start | bytes 2211848 | tf_op jit(solution)/shard_map/ppermute | solution.py:80
  74.1 1.9 %collective-permute-start.15 = (bf16[4,720,128]{2,1,0:T(8,128)(2,1)}, bf16[4,720,128]{2,1,0:T(8,128)(2,1)S(1)}, u32[]{:S(2)}, u32[]{:S(2)}) collective-permute-start(bf16[4,720,128]{2,1,0:T(8,128)(2,1)} %collective-permute-done.7), channel_id=1, source_target_pairs={{0,8},{8,0},{1,9},{9,1},{2,10},{10,2},{3,11},{11,3},{4,12},{12,4},... | collective-permute-start | bytes 2211848 | tf_op jit(solution)/shard_map/ppermute | solution.py:80
  77.3 4.7 %collective-permute-done.4 = bf16[4,720,128]{2,1,0:T(8,128)(2,1)S(1)} collective-permute-done((bf16[4,720,128]{2,1,0:T(8,128)(2,1)S(1)}, bf16[4,720,128]{2,1,0:T(8,128)(2,1)S(1)}, u32[]{:S(2)}, u32[]{:S(2)}) %collective-permute-start.4) | collective-permute-done | bytes 737312 | tf_op jit(solution)/shard_map/ppermute | solution.py:80
  82.1 1.9 %collective-permute-start.5 = (bf16[4,720,128]{2,1,0:T(8,128)(2,1)S(1)}, bf16[4,720,128]{2,1,0:T(8,128)(2,1)S(1)}, u32[]{:S(2)}, u32[]{:S(2)}) collective-permute-start(bf16[4,720,128]{2,1,0:T(8,128)(2,1)S(1)} %collective-permute-done.4), channel_id=1, source_target_pairs={{0,16},{16,32},{32,48},{48,64},{64,80},{80,96},{96,112},{112,0},{1... | collective-permute-start | bytes 2211848 | tf_op jit(solution)/shard_map/ppermute | solution.py:80
  84.0 4.6 %collective-permute-start.9 = (bf16[4,720,128]{2,1,0:T(8,128)(2,1)S(1)}, bf16[4,720,128]{2,1,0:T(8,128)(2,1)S(1)}, u32[]{:S(2)}, u32[]{:S(2)}) collective-permute-start(bf16[4,720,128]{2,1,0:T(8,128)(2,1)S(1)} %collective-permute-done.8), channel_id=1, source_target_pairs={{0,112},{16,0},{32,16},{48,32},{64,48},{80,64},{96,80},{112,96},{1... | collective-permute-start | bytes 2211848 | tf_op jit(solution)/shard_map/ppermute | solution.py:80
  88.6 4.9 %collective-permute-start.16 = (bf16[4,720,128]{2,1,0:T(8,128)(2,1)S(1)}, bf16[4,720,128]{2,1,0:T(8,128)(2,1)S(1)}, u32[]{:S(2)}, u32[]{:S(2)}) collective-permute-start(bf16[4,720,128]{2,1,0:T(8,128)(2,1)S(1)} %collective-permute-done.4), channel_id=1, source_target_pairs={{0,8},{8,0},{1,9},{9,1},{2,10},{10,2},{3,11},{11,3},{4,12},{12,4},... | collective-permute-start | bytes 2211848 | tf_op jit(solution)/shard_map/ppermute | solution.py:80
  94.9 1.9 %collective-permute-start.17 = (bf16[4,720,128]{2,1,0:T(8,128)(2,1)S(1)}, bf16[4,720,128]{2,1,0:T(8,128)(2,1)S(1)}, u32[]{:S(2)}, u32[]{:S(2)}) collective-permute-start(bf16[4,720,128]{2,1,0:T(8,128)(2,1)S(1)} %collective-permute-done.8), channel_id=1, source_target_pairs={{0,8},{8,0},{1,9},{9,1},{2,10},{10,2},{3,11},{11,3},{4,12},{12,4},... | collective-permute-start | bytes 2211848 | tf_op jit(solution)/shard_map/ppermute | solution.py:80
  96.9 3.9 %collective-permute-done.5 = bf16[4,720,128]{2,1,0:T(8,128)(2,1)S(1)} collective-permute-done((bf16[4,720,128]{2,1,0:T(8,128)(2,1)S(1)}, bf16[4,720,128]{2,1,0:T(8,128)(2,1)S(1)}, u32[]{:S(2)}, u32[]{:S(2)}) %collective-permute-start.5) | collective-permute-done | bytes 737312 | tf_op jit(solution)/shard_map/ppermute | solution.py:80
  100.8 1.9 %collective-permute-start.6 = (bf16[2,720,128]{2,1,0:T(8,128)(2,1)S(1)}, bf16[2,720,128]{2,1,0:T(8,128)(2,1)S(1)}, u32[]{:S(2)}, u32[]{:S(2)}) collective-permute-start(bf16[2,720,128]{2,1,0:T(8,128)(2,1)S(1)} %slice.332), channel_id=1, source_target_pairs={{0,16},{16,32},{32,48},{48,64},{64,80},{80,96},{96,112},{112,0},{1... | collective-permute-start | bytes 1105928 | tf_op jit(solution)/shard_map/ppermute | solution.py:80
  102.7 3.9 %collective-permute-start.11 = (bf16[2,720,128]{2,1,0:T(8,128)(2,1)S(1)}, bf16[2,720,128]{2,1,0:T(8,128)(2,1)S(1)}, u32[]{:S(2)}, u32[]{:S(2)}) collective-permute-start(bf16[2,720,128]{2,1,0:T(8,128)(2,1)S(1)} %slice.332), channel_id=1, source_target_pairs={{120,0},{112,8},{8,16},{0,24},{24,32},{16,40},{40,48},{32,56},{56,... | collective-permute-start | bytes 1105928 | tf_op jit(solution)/shard_map/ppermute | solution.py:149
  106.7 5.8 %collective-permute-start.10 = (bf16[2,720,128]{2,1,0:T(8,128)(2,1)S(1)}, bf16[2,720,128]{2,1,0:T(8,128)(2,1)S(1)}, u32[]{:S(2)}, u32[]{:S(2)}) collective-permute-start(bf16[2,720,128]{2,1,0:T(8,128)(2,1)S(1)} %slice.333), channel_id=1, source_target_pairs={{0,112},{16,0},{32,16},{48,32},{64,48},{80,64},{96,80},{112,96},{1... | collective-permute-start | bytes 1105928 | tf_op jit(solution)/shard_map/ppermute | solution.py:80
  112.6 2.2 %collective-permute-start.12 = (bf16[2,720,128]{2,1,0:T(8,128)(2,1)S(1)}, bf16[2,720,128]{2,1,0:T(8,128)(2,1)S(1)}, u32[]{:S(2)}, u32[]{:S(2)}) collective-permute-start(bf16[2,720,128]{2,1,0:T(8,128)(2,1)S(1)} %slice.333), channel_id=1, source_target_pairs={{24,0},{16,8},{40,16},{32,24},{56,32},{48,40},{72,48},{64,56},{88,... | collective-permute-start | bytes 1105928 | tf_op jit(solution)/shard_map/ppermute | solution.py:150
  116.3 3.7 %collective-permute-start.18 = (bf16[4,720,128]{2,1,0:T(8,128)(2,1)S(1)}, bf16[4,720,128]{2,1,0:T(8,128)(2,1)S(1)}, u32[]{:S(2)}, u32[]{:S(2)}) collective-permute-start(bf16[4,720,128]{2,1,0:T(8,128)(2,1)S(1)} %collective-permute-done.5), channel_id=1, source_target_pairs={{0,8},{8,0},{1,9},{9,1},{2,10},{10,2},{3,11},{11,3},{4,12},{12,4},... | collective-permute-start | bytes 2211848 | tf_op jit(solution)/shard_map/ppermute | solution.py:80
  121.9 2.1 %collective-permute-start.19 = (bf16[4,720,128]{2,1,0:T(8,128)(2,1)S(1)}, bf16[4,720,128]{2,1,0:T(8,128)(2,1)S(1)}, u32[]{:S(2)}, u32[]{:S(2)}) collective-permute-start(bf16[4,720,128]{2,1,0:T(8,128)(2,1)S(1)} %collective-permute-done.9), channel_id=1, source_target_pairs={{0,8},{8,0},{1,9},{9,1},{2,10},{10,2},{3,11},{11,3},{4,12},{12,4},... | collective-permute-start | bytes 2211848 | tf_op jit(solution)/shard_map/ppermute | solution.py:80
  125.3 2.6 %collective-permute-done.12 = bf16[2,720,128]{2,1,0:T(8,128)(2,1)S(1)} collective-permute-done((bf16[2,720,128]{2,1,0:T(8,128)(2,1)S(1)}, bf16[2,720,128]{2,1,0:T(8,128)(2,1)S(1)}, u32[]{:S(2)}, u32[]{:S(2)}) %collective-permute-start.12) | collective-permute-done | bytes 368672 | tf_op jit(solution)/shard_map/ppermute | solution.py:150
  128.1 0.8 copy-done.1
  128.9 0.8 copy-done.19
  131.4 2.3 %slice_bitcast_fusion.2 = (bf16[128,5120]{0,1:T(8,128)(2,1)S(1)}, bf16[1,128,5120]{1,2,0:T(8,128)(2,1)S(1)}, bf16[1,128,5120]{1,2,0:T(8,128)(2,1)S(1)}) fusion(bf16[2,128,5120]{1,2,0:T(8,128)(2,1)} %all-gather.2.cloned.1.call-done), kind=kLoop, calls=%fused_computation.180 | loop fusion | bytes 6553600 | tf_op jit(solution)/shard_map/squeeze | solution.py:123
  134.1 0.7 multiply_reduce_fusion
  135.6 0.8 multiply_convert_fusion
  136.4 0.9 fusion.2
  137.4 0.9 fusion.1
  138.3 0.9 fusion
  139.3 1.7 convolution_bitcast_fusion.13
  152.0 0.8 fusion.13
  154.8 0.9 copy.71.q_ref
  159.8 15.5 %shard_map.149 = bf16[2,128,640]{2,1,0:T(8,128)(2,1)} custom-call(bf16[2,128,640]{2,1,0:T(8,128)(2,1)} %copy.71.q_ref, bf16[2,128,128]{2,1,0:T(8,128)(2,1)} %pad_maximum_fusion.5.ko_ref, bf16[2,128,128]{2,1,0:T(8,128)(2,1)} %add_convert_fusion.1.vo_ref, bf16[4096,128]{1,0:T(8,128)(2,1)} %constant_dynamic-update-slice_fusion.11.kc_ref, ...), custom_call_target="tpu_custom_call" | custom-call | flops 2768240640 | bytes 3407872 | tf_op jit(solution)/shard_map/pallas_call | solution.py:57
  175.3 1.7 slice_bitcast_fusion
  (230 shorter events, 34.5 us)
Async XLA Ops:
  7.2 20.8 %copy-start.34 = (bf16[640]{0:T(1024)(128)(2,1)S(1)}, bf16[640]{0:T(1024)(128)(2,1)}, u32[]{:S(2)}) copy-start(bf16[640]{0:T(1024)(128)(2,1)} %param.21) | copy-start | bytes 3844
  7.2 20.8 %copy-start.36 = (s32[1,64]{1,0:T(1,128)S(1)}, s32[1,64]{1,0:T(1,128)}, u32[]{:S(2)}) copy-start(s32[1,64]{1,0:T(1,128)} %param.18) | copy-start | bytes 772
  7.2 22.8 %copy-start.37 = (s32[128]{0:T(128)S(1)}, s32[128]{0:T(128)}, u32[]{:S(2)}) copy-start(s32[128]{0:T(128)} %param.16) | copy-start | bytes 1540
  7.2 124.2 %all-gather.2.cloned.1.call-start = ((), (), s32[]{:S(2)}) async-start(), calls=%async_computation | async-start | bytes 2949120 | tf_op jit(solution)/shard_map/all_gather | solution.py:122
  13.9 16.2 %collective-permute-start = (bf16[720,128]{1,0:T(8,128)(2,1)S(1)}, bf16[720,128]{1,0:T(8,128)(2,1)S(1)}, u32[]{:S(2)}, u32[]{:S(2)}) collective-permute-start(bf16[720,128]{1,0:T(8,128)(2,1)S(1)} %constant_dynamic-update-slice_fusion), channel_id=1, source_target_pairs={{0,384},{128,0},{256,128},{384,256},{1,385},{129,1},{257,129},{385... | collective-permute-start | bytes 552968 | tf_op jit(solution)/shard_map/ppermute | solution.py:80
  19.9 15.1 %collective-permute-start.1 = (bf16[720,128]{1,0:T(8,128)(2,1)S(1)}, bf16[720,128]{1,0:T(8,128)(2,1)S(1)}, u32[]{:S(2)}, u32[]{:S(2)}) collective-permute-start(bf16[720,128]{1,0:T(8,128)(2,1)S(1)} %constant_dynamic-update-slice_fusion), channel_id=1, source_target_pairs={{0,256},{128,384},{256,0},{384,128},{1,257},{129,385},{257,1},{385... | collective-permute-start | bytes 552968 | tf_op jit(solution)/shard_map/ppermute | solution.py:80
  21.8 13.1 %collective-permute-start.2 = (bf16[720,128]{1,0:T(8,128)(2,1)S(1)}, bf16[720,128]{1,0:T(8,128)(2,1)S(1)}, u32[]{:S(2)}, u32[]{:S(2)}) collective-permute-start(bf16[720,128]{1,0:T(8,128)(2,1)S(1)} %constant_dynamic-update-slice_fusion), channel_id=1, source_target_pairs={{0,128},{128,256},{256,384},{384,0},{1,129},{129,257},{257,385},{3... | collective-permute-start | bytes 552968 | tf_op jit(solution)/shard_map/ppermute | solution.py:80
  27.1 21.7 %copy-start.32 = (bf16[5120]{0:T(1024)(128)(2,1)S(1)}, bf16[5120]{0:T(1024)(128)(2,1)}, u32[]{:S(2)}) copy-start(bf16[5120]{0:T(1024)(128)(2,1)} %param.19) | copy-start | bytes 30724
  27.1 22.5 %copy-start.38 = (bf16[128]{0:T(256)(128)(2,1)S(1)}, bf16[128]{0:T(256)(128)(2,1)}, u32[]{:S(2)}) copy-start(bf16[128]{0:T(256)(128)(2,1)} %param.23) | copy-start | bytes 772
  27.1 23.9 %copy-start.39 = (bf16[128]{0:T(256)(128)(2,1)S(1)}, bf16[128]{0:T(256)(128)(2,1)}, u32[]{:S(2)}) copy-start(bf16[128]{0:T(256)(128)(2,1)} %param.25) | copy-start | bytes 772
  29.9 34.6 %copy-start.23 = (f32[128,64]{0,1:T(8,128)}, f32[128,64]{0,1:T(8,128)S(1)}, u32[]{:S(2)}) copy-start(f32[128,64]{0,1:T(8,128)S(1)} %get-tuple-element.70) | copy-start | bytes 98308
  35.0 35.0 %copy-start.21 = (bf16[720,128]{1,0:T(8,128)(2,1)}, bf16[720,128]{1,0:T(8,128)(2,1)S(1)}, u32[]{:S(2)}) copy-start(bf16[720,128]{1,0:T(8,128)(2,1)S(1)} %collective-permute-done.2) | copy-start | bytes 552964
  35.1 27.4 %collective-permute-start.3 = (bf16[4,720,128]{2,1,0:T(8,128)(2,1)S(1)}, bf16[4,720,128]{2,1,0:T(8,128)(2,1)S(1)}, u32[]{:S(2)}, u32[]{:S(2)}) collective-permute-start(bf16[4,720,128]{2,1,0:T(8,128)(2,1)S(1)} %pad_maximum_fusion), channel_id=1, source_target_pairs={{0,16},{16,32},{32,48},{48,64},{64,80},{80,96},{96,112},{112,0},{1... | collective-permute-start | bytes 2211848 | tf_op jit(solution)/shard_map/ppermute | solution.py:80
  40.3 24.2 %collective-permute-start.7 = (bf16[4,720,128]{2,1,0:T(8,128)(2,1)S(1)}, bf16[4,720,128]{2,1,0:T(8,128)(2,1)}, u32[]{:S(2)}, u32[]{:S(2)}) collective-permute-start(bf16[4,720,128]{2,1,0:T(8,128)(2,1)S(1)} %pad_maximum_fusion), channel_id=1, source_target_pairs={{0,112},{16,0},{32,16},{48,32},{64,48},{80,64},{96,80},{112,96},{1... | collective-permute-start | bytes 2211848 | tf_op jit(solution)/shard_map/ppermute | solution.py:80
  48.9 2.2 %copy-start.35 = (f32[1,4096]{1,0:T(1,128)}, f32[1,4096]{1,0:T(1,128)S(1)}, u32[]{:S(2)}) copy-start(f32[1,4096]{1,0:T(1,128)S(1)} %constant_dynamic-update-slice_fusion.43.bias_ref) | copy-start | bytes 49156
  51.1 26.2 %collective-permute-start.13 = (bf16[4,720,128]{2,1,0:T(8,128)(2,1)S(1)}, bf16[4,720,128]{2,1,0:T(8,128)(2,1)S(1)}, u32[]{:S(2)}, u32[]{:S(2)}) collective-permute-start(bf16[4,720,128]{2,1,0:T(8,128)(2,1)S(1)} %pad_maximum_fusion), channel_id=1, source_target_pairs={{0,8},{8,0},{1,9},{9,1},{2,10},{10,2},{3,11},{11,3},{4,12},{12,4},... | collective-permute-start | bytes 2211848 | tf_op jit(solution)/shard_map/ppermute | solution.py:80
  62.5 34.3 %copy-start.3 = (bf16[4,720,128]{2,1,0:T(8,128)(2,1)}, bf16[4,720,128]{2,1,0:T(8,128)(2,1)S(1)}, u32[]{:S(2)}) copy-start(bf16[4,720,128]{2,1,0:T(8,128)(2,1)S(1)} %collective-permute-done.3) | copy-start | bytes 2211844
  62.5 19.5 %collective-permute-start.4 = (bf16[4,720,128]{2,1,0:T(8,128)(2,1)S(1)}, bf16[4,720,128]{2,1,0:T(8,128)(2,1)S(1)}, u32[]{:S(2)}, u32[]{:S(2)}) collective-permute-start(bf16[4,720,128]{2,1,0:T(8,128)(2,1)S(1)} %collective-permute-done.3), channel_id=1, source_target_pairs={{0,16},{16,32},{32,48},{48,64},{64,80},{80,96},{96,112},{112,0},{1... | collective-permute-start | bytes 2211848 | tf_op jit(solution)/shard_map/ppermute | solution.py:80
  64.5 19.5 %collective-permute-start.8 = (bf16[4,720,128]{2,1,0:T(8,128)(2,1)}, bf16[4,720,128]{2,1,0:T(8,128)(2,1)S(1)}, u32[]{:S(2)}, u32[]{:S(2)}) collective-permute-start(bf16[4,720,128]{2,1,0:T(8,128)(2,1)} %collective-permute-done.7), channel_id=1, source_target_pairs={{0,112},{16,0},{32,16},{48,32},{64,48},{80,64},{96,80},{112,96},{1... | collective-permute-start | bytes 2211848 | tf_op jit(solution)/shard_map/ppermute | solution.py:80
  70.0 24.9 %collective-permute-start.14 = (bf16[4,720,128]{2,1,0:T(8,128)(2,1)S(1)}, bf16[4,720,128]{2,1,0:T(8,128)(2,1)S(1)}, u32[]{:S(2)}, u32[]{:S(2)}) collective-permute-start(bf16[4,720,128]{2,1,0:T(8,128)(2,1)S(1)} %collective-permute-done.3), channel_id=1, source_target_pairs={{0,8},{8,0},{1,9},{9,1},{2,10},{10,2},{3,11},{11,3},{4,12},{12,4},... | collective-permute-start | bytes 2211848 | tf_op jit(solution)/shard_map/ppermute | solution.py:80
  74.1 22.7 %collective-permute-start.15 = (bf16[4,720,128]{2,1,0:T(8,128)(2,1)}, bf16[4,720,128]{2,1,0:T(8,128)(2,1)S(1)}, u32[]{:S(2)}, u32[]{:S(2)}) collective-permute-start(bf16[4,720,128]{2,1,0:T(8,128)(2,1)} %collective-permute-done.7), channel_id=1, source_target_pairs={{0,8},{8,0},{1,9},{9,1},{2,10},{10,2},{3,11},{11,3},{4,12},{12,4},... | collective-permute-start | bytes 2211848 | tf_op jit(solution)/shard_map/ppermute | solution.py:80
  77.3 19.5 %copy-start.7 = (bf16[4,720,128]{2,1,0:T(8,128)(2,1)}, bf16[4,720,128]{2,1,0:T(8,128)(2,1)S(1)}, u32[]{:S(2)}) copy-start(bf16[4,720,128]{2,1,0:T(8,128)(2,1)S(1)} %collective-permute-done.13) | copy-start | bytes 2211844
  82.1 24.6 %copy-start.5 = (bf16[4,720,128]{2,1,0:T(8,128)(2,1)}, bf16[4,720,128]{2,1,0:T(8,128)(2,1)S(1)}, u32[]{:S(2)}) copy-start(bf16[4,720,128]{2,1,0:T(8,128)(2,1)S(1)} %collective-permute-done.4) | copy-start | bytes 2211844
  82.1 18.7 %collective-permute-start.5 = (bf16[4,720,128]{2,1,0:T(8,128)(2,1)S(1)}, bf16[4,720,128]{2,1,0:T(8,128)(2,1)S(1)}, u32[]{:S(2)}, u32[]{:S(2)}) collective-permute-start(bf16[4,720,128]{2,1,0:T(8,128)(2,1)S(1)} %collective-permute-done.4), channel_id=1, source_target_pairs={{0,16},{16,32},{32,48},{48,64},{64,80},{80,96},{96,112},{112,0},{1... | collective-permute-start | bytes 2211848 | tf_op jit(solution)/shard_map/ppermute | solution.py:80
  84.0 22.7 %copy-start.9 = (bf16[4,720,128]{2,1,0:T(8,128)(2,1)}, bf16[4,720,128]{2,1,0:T(8,128)(2,1)S(1)}, u32[]{:S(2)}) copy-start(bf16[4,720,128]{2,1,0:T(8,128)(2,1)S(1)} %collective-permute-done.8) | copy-start | bytes 2211844
  84.0 22.6 %collective-permute-start.9 = (bf16[4,720,128]{2,1,0:T(8,128)(2,1)S(1)}, bf16[4,720,128]{2,1,0:T(8,128)(2,1)S(1)}, u32[]{:S(2)}, u32[]{:S(2)}) collective-permute-start(bf16[4,720,128]{2,1,0:T(8,128)(2,1)S(1)} %collective-permute-done.8), channel_id=1, source_target_pairs={{0,112},{16,0},{32,16},{48,32},{64,48},{80,64},{96,80},{112,96},{1... | collective-permute-start | bytes 2211848 | tf_op jit(solution)/shard_map/ppermute | solution.py:80
  88.6 24.0 %collective-permute-start.16 = (bf16[4,720,128]{2,1,0:T(8,128)(2,1)S(1)}, bf16[4,720,128]{2,1,0:T(8,128)(2,1)S(1)}, u32[]{:S(2)}, u32[]{:S(2)}) collective-permute-start(bf16[4,720,128]{2,1,0:T(8,128)(2,1)S(1)} %collective-permute-done.4), channel_id=1, source_target_pairs={{0,8},{8,0},{1,9},{9,1},{2,10},{10,2},{3,11},{11,3},{4,12},{12,4},... | collective-permute-start | bytes 2211848 | tf_op jit(solution)/shard_map/ppermute | solution.py:80
  94.9 2.0 %copy-start.11 = (bf16[4,720,128]{2,1,0:T(8,128)(2,1)}, bf16[4,720,128]{2,1,0:T(8,128)(2,1)S(1)}, u32[]{:S(2)}) copy-start(bf16[4,720,128]{2,1,0:T(8,128)(2,1)S(1)} %collective-permute-done.14) | copy-start | bytes 2211844
  94.9 20.0 %collective-permute-start.17 = (bf16[4,720,128]{2,1,0:T(8,128)(2,1)S(1)}, bf16[4,720,128]{2,1,0:T(8,128)(2,1)S(1)}, u32[]{:S(2)}, u32[]{:S(2)}) collective-permute-start(bf16[4,720,128]{2,1,0:T(8,128)(2,1)S(1)} %collective-permute-done.8), channel_id=1, source_target_pairs={{0,8},{8,0},{1,9},{9,1},{2,10},{10,2},{3,11},{11,3},{4,12},{12,4},... | collective-permute-start | bytes 2211848 | tf_op jit(solution)/shard_map/ppermute | solution.py:80
  96.8 15.7 %copy-start.13 = (bf16[4,720,128]{2,1,0:T(8,128)(2,1)}, bf16[4,720,128]{2,1,0:T(8,128)(2,1)S(1)}, u32[]{:S(2)}) copy-start(bf16[4,720,128]{2,1,0:T(8,128)(2,1)S(1)} %collective-permute-done.15) | copy-start | bytes 2211844
  100.8 24.4 %collective-permute-start.6 = (bf16[2,720,128]{2,1,0:T(8,128)(2,1)S(1)}, bf16[2,720,128]{2,1,0:T(8,128)(2,1)S(1)}, u32[]{:S(2)}, u32[]{:S(2)}) collective-permute-start(bf16[2,720,128]{2,1,0:T(8,128)(2,1)S(1)} %slice.332), channel_id=1, source_target_pairs={{0,16},{16,32},{32,48},{48,64},{64,80},{80,96},{96,112},{112,0},{1... | collective-permute-start | bytes 1105928 | tf_op jit(solution)/shard_map/ppermute | solution.py:80
  102.7 22.6 %collective-permute-start.11 = (bf16[2,720,128]{2,1,0:T(8,128)(2,1)S(1)}, bf16[2,720,128]{2,1,0:T(8,128)(2,1)S(1)}, u32[]{:S(2)}, u32[]{:S(2)}) collective-permute-start(bf16[2,720,128]{2,1,0:T(8,128)(2,1)S(1)} %slice.332), channel_id=1, source_target_pairs={{120,0},{112,8},{8,16},{0,24},{24,32},{16,40},{40,48},{32,56},{56,... | collective-permute-start | bytes 1105928 | tf_op jit(solution)/shard_map/ppermute | solution.py:149
  106.7 15.2 %collective-permute-start.10 = (bf16[2,720,128]{2,1,0:T(8,128)(2,1)S(1)}, bf16[2,720,128]{2,1,0:T(8,128)(2,1)S(1)}, u32[]{:S(2)}, u32[]{:S(2)}) collective-permute-start(bf16[2,720,128]{2,1,0:T(8,128)(2,1)S(1)} %slice.333), channel_id=1, source_target_pairs={{0,112},{16,0},{32,16},{48,32},{64,48},{80,64},{96,80},{112,96},{1... | collective-permute-start | bytes 1105928 | tf_op jit(solution)/shard_map/ppermute | solution.py:80
  112.6 12.6 %copy-start.15 = (bf16[4,720,128]{2,1,0:T(8,128)(2,1)}, bf16[4,720,128]{2,1,0:T(8,128)(2,1)S(1)}, u32[]{:S(2)}) copy-start(bf16[4,720,128]{2,1,0:T(8,128)(2,1)S(1)} %collective-permute-done.16) | copy-start | bytes 2211844
  112.6 15.3 %collective-permute-start.12 = (bf16[2,720,128]{2,1,0:T(8,128)(2,1)S(1)}, bf16[2,720,128]{2,1,0:T(8,128)(2,1)S(1)}, u32[]{:S(2)}, u32[]{:S(2)}) collective-permute-start(bf16[2,720,128]{2,1,0:T(8,128)(2,1)S(1)} %slice.333), channel_id=1, source_target_pairs={{24,0},{16,8},{40,16},{32,24},{56,32},{48,40},{72,48},{64,56},{88,... | collective-permute-start | bytes 1105928 | tf_op jit(solution)/shard_map/ppermute | solution.py:150
  114.9 10.3 %copy-start.17 = (bf16[4,720,128]{2,1,0:T(8,128)(2,1)}, bf16[4,720,128]{2,1,0:T(8,128)(2,1)S(1)}, u32[]{:S(2)}) copy-start(bf16[4,720,128]{2,1,0:T(8,128)(2,1)S(1)} %collective-permute-done.17) | copy-start | bytes 2211844
  116.3 11.7 %collective-permute-start.18 = (bf16[4,720,128]{2,1,0:T(8,128)(2,1)S(1)}, bf16[4,720,128]{2,1,0:T(8,128)(2,1)S(1)}, u32[]{:S(2)}, u32[]{:S(2)}) collective-permute-start(bf16[4,720,128]{2,1,0:T(8,128)(2,1)S(1)} %collective-permute-done.5), channel_id=1, source_target_pairs={{0,8},{8,0},{1,9},{9,1},{2,10},{10,2},{3,11},{11,3},{4,12},{12,4},... | collective-permute-start | bytes 2211848 | tf_op jit(solution)/shard_map/ppermute | solution.py:80
  121.9 6.1 %collective-permute-start.19 = (bf16[4,720,128]{2,1,0:T(8,128)(2,1)S(1)}, bf16[4,720,128]{2,1,0:T(8,128)(2,1)S(1)}, u32[]{:S(2)}, u32[]{:S(2)}) collective-permute-start(bf16[4,720,128]{2,1,0:T(8,128)(2,1)S(1)} %collective-permute-done.9), channel_id=1, source_target_pairs={{0,8},{8,0},{1,9},{9,1},{2,10},{10,2},{3,11},{11,3},{4,12},{12,4},... | collective-permute-start | bytes 2211848 | tf_op jit(solution)/shard_map/ppermute | solution.py:80
  131.4 2.5 %copy-start = (bf16[2,128,5120]{1,2,0:T(8,128)(2,1)S(1)}, bf16[2,128,5120]{1,2,0:T(8,128)(2,1)}, u32[]{:S(2)}) copy-start(bf16[2,128,5120]{1,2,0:T(8,128)(2,1)} %all-gather.2.cloned.1.call-done) | copy-start | bytes 7864324
  139.3 1.7 copy-start.4
  143.2 1.2 copy-start.8
  144.9 1.2 copy-start.16
  146.5 1.2 copy-start.20
  154.7 1.7 copy-start.29
  154.7 2.4 %copy-start.28 = (bf16[4,64,128]{2,1,0:T(8,128)(2,1)S(1)}, bf16[4,64,128]{2,1,0:T(8,128)(2,1)}, u32[]{:S(2)}) copy-start(bf16[4,64,128]{2,1,0:T(8,128)(2,1)} %get-tuple-element.71) | copy-start | bytes 196612
  154.7 3.0 %copy-start.27 = (bf16[4,64,128]{2,1,0:T(8,128)(2,1)S(1)}, bf16[4,64,128]{2,1,0:T(8,128)(2,1)}, u32[]{:S(2)}) copy-start(bf16[4,64,128]{2,1,0:T(8,128)(2,1)} %get-tuple-element.16) | copy-start | bytes 196612
  154.8 3.5 %copy-start.25 = (f32[128,64]{1,0:T(8,128)S(1)}, f32[128,64]{1,0:T(8,128)}, u32[]{:S(2)}) copy-start(f32[128,64]{1,0:T(8,128)} %copy.68) | copy-start | bytes 98308
  154.8 3.5 %copy-start.26 = (f32[128,64]{1,0:T(8,128)S(1)}, f32[128,64]{1,0:T(8,128)}, u32[]{:S(2)}) copy-start(f32[128,64]{1,0:T(8,128)} %copy.69) | copy-start | bytes 98308
  (13 other events, 13.1 us)
Sparse Core Ops, SparseCore 0:
  27.3 86.7 all-gather.1

commit v9 on v8

--- a/solution.py
+++ b/solution.py
@@ -37,23 +37,28 @@
 def attend_kernel(q_ref, ko_ref, vo_ref, kc_ref, vc_ref, bias_ref, out_ref):
     inv_root = 1.0 / math.sqrt(HD)
     q = q_ref[...]
+    shards, ctx_rows, width = kc_ref.shape
+    cache_k = kc_ref[...].reshape(shards * ctx_rows, width)
+    cache_v = vc_ref[...].reshape(shards * ctx_rows, width)
     contract = (((1,), (1,)), ((), ()))
     own = lax.dot_general(q, ko_ref[...], contract, preferred_element_type=jnp.float32) * inv_root
-    far = lax.dot_general(q, kc_ref[...], contract, preferred_element_type=jnp.float32) * inv_root
+    far = lax.dot_general(q, cache_k, contract, preferred_element_type=jnp.float32) * inv_root
     far = far + bias_ref[...]
     highest = jnp.maximum(jnp.max(own, axis=-1, keepdims=True), jnp.max(far, axis=-1, keepdims=True))
     own_w = jnp.exp(own - highest)
     far_w = jnp.exp(far - highest)
     totals = jnp.sum(own_w, axis=-1, keepdims=True) + jnp.sum(far_w, axis=-1, keepdims=True)
     mixture = jnp.dot(own_w.astype(jnp.bfloat16), vo_ref[...], preferred_element_type=jnp.float32)
-    mixture = mixture + jnp.dot(far_w.astype(jnp.bfloat16), vc_ref[...], preferred_element_type=jnp.float32)
+    mixture = mixture + jnp.dot(far_w.astype(jnp.bfloat16), cache_v, preferred_element_type=jnp.float32)
     out_ref[...] = (mixture / totals).astype(out_ref.dtype)
 
 
-def attend(q_rot, k_rot, value_rows, cache_k, cache_v, bias):
+def attend(q_rot, k_rot, value_rows, stacked, bias, key_block):
     passes, rows, width = q_rot.shape
     heads = width // HD
-    ctx = cache_k.shape[0]
+    ctx = bias.shape[1]
+    shards = stacked.shape[0]
+    ctx_rows = ctx // shards
     return pl.pallas_call(
         attend_kernel,
         grid=(passes, heads),
@@ -61,8 +66,8 @@
             pl.BlockSpec((None, rows, HD), lambda p, h: (p, 0, h)),
             pl.BlockSpec((None, rows, HD), lambda p, h: (p, 0, 0)),
             pl.BlockSpec((None, rows, HD), lambda p, h: (p, 0, 0)),
-            pl.BlockSpec((ctx, HD), lambda p, h: (0, 0)),
-            pl.BlockSpec((ctx, HD), lambda p, h: (0, 0)),
+            pl.BlockSpec((shards, ctx_rows, HD), lambda p, h: (0, key_block, 0)),
+            pl.BlockSpec((shards, ctx_rows, HD), lambda p, h: (0, key_block + 1, 0)),
             pl.BlockSpec((1, ctx), lambda p, h: (0, 0)),
         ],
         out_specs=pl.BlockSpec((None, rows, HD), lambda p, h: (p, 0, h)),
@@ -72,7 +77,7 @@
             transcendentals=passes * heads * rows * (ctx + rows),
             bytes_accessed=2 * (2 * ctx * HD + 4 * passes * rows * width),
         ),
-    )(q_rot, k_rot, value_rows, cache_k, cache_v, bias)
+    )(q_rot, k_rot, value_rows, stacked, stacked, bias)
 
 
 def shifted(x, axis, size, shift):
@@ -156,15 +161,14 @@
     held += [(offset, 1, shifted(piece, "core", 2, 1)) for offset, piece in arrived]
     held += [(far, 0, far_own), (far, 1, far_other)]
 
-    proj = None
-    for offset, core, piece in held:
-        part = jnp.einsum(
-            "rki,kjid->rjd",
-            normed5[:, :, offset % n_z, core, :],
-            piece.reshape(n_ylo, total_blocks, w_rows, HD),
-            preferred_element_type=jnp.float32,
-        )
-        proj = part if proj is None else proj + part
+    stacked = jnp.stack([piece for ignored, ignored2, piece in held])
+    lhs = jnp.stack([normed5[:, :, offset % n_z, core, :] for offset, core, ignored in held], axis=1)
+    proj = jnp.einsum(
+        "rpki,pkjid->rjd",
+        lhs,
+        stacked.reshape(len(held), n_ylo, total_blocks, w_rows, HD),
+        preferred_element_type=jnp.float32,
+    )
     queries = proj[:, : q_cols // HD, :].reshape(-1, q_cols) + b_query.astype(jnp.float32)
     key_proj = proj[:, q_cols // HD, :] + b_key.astype(jnp.float32)
     value_proj = proj[:, q_cols // HD + 1, :] + b_value.astype(jnp.float32)
@@ -184,19 +188,13 @@
     bias4 = jnp.roll(bias4, -me_z, axis=1)
     bias4 = jnp.roll(bias4, -me_core, axis=2)
     bias = jnp.concatenate([bias4[:, offset % n_z, core, :].reshape(1, -1) for offset, core, ignored in held], axis=1)
-    cache_k = jnp.concatenate(
-        [piece[:, key_start:value_start, :].reshape(-1, HD) for ignored, ignored2, piece in held], axis=0
-    )
-    cache_v = jnp.concatenate(
-        [piece[:, value_start:used, :].reshape(-1, HD) for ignored, ignored2, piece in held], axis=0
-    )
     attended = attend(
         q_rot.reshape(2, block_rows, q_cols),
         k_rot.reshape(2, block_rows, local_kv * HD),
         value_rows.reshape(2, block_rows, local_kv * HD),
-        cache_k,
-        cache_v,
+        stacked.reshape(-1, total_blocks * w_rows, HD),
         bias,
+        key_start // ctx_rows,
     )
     return (attended[0], attended[1])
 

time: 188 us -> 199 us (1.059)
  the two profiles are of different devices: /device:TPU:1 before, /device:TPU:43 now
where the time goes in v9:
time: 199 us; the launch traced here: 197 us
  starting transfers between devices  66.4 us (33%)
  waiting for transfers between devices  49.8 us (25%)
  local copies, waits for them, and re-layouts  36.4 us (18%)
  between operations  15.7 us (8%)
  Pallas kernels  15.6 us (8%)
  other arithmetic  9.62 us (5%)
  matrix products  3.6 us (2%)
    ppermute x18, starting transfers between devices, shifted(): return lax.ppermute(x, axis, pairs)  62 us
    ppermute x18, waiting for transfers between devices, shifted(): return lax.ppermute(x, axis, pairs)  39.6 us
    unnamed x92, local copies, waits for them, and re-layouts  28.2 us
    pallas_call x1, Pallas kernels, attend(): pl.pallas_call(attend_kernel, grid=(passes, heads), in_specs=[pl.BlockSpe...  15.6 us
    ppermute x1, waiting for transfers between devices, local(): lax.ppermute(forward[:split], ('z', 'core'), to_partner_front)  10.2 us
  transfers between devices with their start and end apart: 21, of which 7 were waited for; matrix products, arithmetic and copies ran while one was open for 11% of the time, Pallas kernels for 0%

profile of v9, /device:TPU:43, one launch (start us, length us, event | category | flops | bytes accessed | tf_op | source)
XLA Modules:
  0.0 197.2 jit_solution(11975027189749160087)
XLA Ops:
  13.9 2.3 %collective-permute-start.2 = (bf16[720,128]{1,0:T(8,128)(2,1)S(1)}, bf16[720,128]{1,0:T(8,128)(2,1)S(1)}, u32[]{:S(2)}, u32[]{:S(2)}) collective-permute-start(bf16[720,128]{1,0:T(8,128)(2,1)S(1)} %constant_dynamic-update-slice_fusion), channel_id=1, source_target_pairs={{0,128},{128,256},{256,384},{384,0},{1,129},{129,257},{257,385},{3... | collective-permute-start | bytes 552968 | tf_op jit(solution)/shard_map/ppermute | solution.py:85
  16.2 4.7 %collective-permute-start.1 = (bf16[720,128]{1,0:T(8,128)(2,1)S(1)}, bf16[720,128]{1,0:T(8,128)(2,1)S(1)}, u32[]{:S(2)}, u32[]{:S(2)}) collective-permute-start(bf16[720,128]{1,0:T(8,128)(2,1)S(1)} %constant_dynamic-update-slice_fusion), channel_id=1, source_target_pairs={{0,256},{128,384},{256,0},{384,128},{1,257},{129,385},{257,1},{385... | collective-permute-start | bytes 552968 | tf_op jit(solution)/shard_map/ppermute | solution.py:85
  20.8 1.9 collective-permute-start
  22.8 1.1 copy.75
  23.8 1.1 copy.74
  29.3 2.5 %collective-permute-done.1 = bf16[720,128]{1,0:T(8,128)(2,1)S(1)} collective-permute-done((bf16[720,128]{1,0:T(8,128)(2,1)S(1)}, bf16[720,128]{1,0:T(8,128)(2,1)S(1)}, u32[]{:S(2)}, u32[]{:S(2)}) %collective-permute-start.1) | collective-permute-done | bytes 184352 | tf_op jit(solution)/shard_map/ppermute | solution.py:85
  31.9 4.0 %collective-permute-done = bf16[720,128]{1,0:T(8,128)(2,1)S(1)} collective-permute-done((bf16[720,128]{1,0:T(8,128)(2,1)S(1)}, bf16[720,128]{1,0:T(8,128)(2,1)S(1)}, u32[]{:S(2)}, u32[]{:S(2)}) %collective-permute-start) | collective-permute-done | bytes 184352 | tf_op jit(solution)/shard_map/ppermute | solution.py:85
  36.0 4.0 %collective-permute-start.3 = (bf16[4,720,128]{2,1,0:T(8,128)(2,1)S(1)}, bf16[4,720,128]{2,1,0:T(8,128)(2,1)S(1)}, u32[]{:S(2)}, u32[]{:S(2)}) collective-permute-start(bf16[4,720,128]{2,1,0:T(8,128)(2,1)S(1)} %pad_maximum_fusion), channel_id=1, source_target_pairs={{0,16},{16,32},{32,48},{48,64},{64,80},{80,96},{96,112},{112,0},{1... | collective-permute-start | bytes 2211848 | tf_op jit(solution)/shard_map/ppermute | solution.py:85
  40.0 8.6 %collective-permute-start.7 = (bf16[4,720,128]{2,1,0:T(8,128)(2,1)S(1)}, bf16[4,720,128]{2,1,0:T(8,128)(2,1)S(1)}, u32[]{:S(2)}, u32[]{:S(2)}) collective-permute-start(bf16[4,720,128]{2,1,0:T(8,128)(2,1)S(1)} %pad_maximum_fusion), channel_id=1, source_target_pairs={{0,112},{16,0},{32,16},{48,32},{64,48},{80,64},{96,80},{112,96},{1... | collective-permute-start | bytes 2211848 | tf_op jit(solution)/shard_map/ppermute | solution.py:85
  49.1 2.7 %collective-permute-start.13 = (bf16[4,720,128]{2,1,0:T(8,128)(2,1)S(1)}, bf16[4,720,128]{2,1,0:T(8,128)(2,1)S(1)}, u32[]{:S(2)}, u32[]{:S(2)}) collective-permute-start(bf16[4,720,128]{2,1,0:T(8,128)(2,1)S(1)} %pad_maximum_fusion), channel_id=1, source_target_pairs={{0,8},{8,0},{1,9},{9,1},{2,10},{10,2},{3,11},{11,3},{4,12},{12,4},... | collective-permute-start | bytes 2211848 | tf_op jit(solution)/shard_map/ppermute | solution.py:85
  51.7 0.9 bitcast_dynamic-update-slice_fusion.15
  52.8 10.3 %collective-permute-done.3 = bf16[4,720,128]{2,1,0:T(8,128)(2,1)S(1)} collective-permute-done((bf16[4,720,128]{2,1,0:T(8,128)(2,1)S(1)}, bf16[4,720,128]{2,1,0:T(8,128)(2,1)S(1)}, u32[]{:S(2)}, u32[]{:S(2)}) %collective-permute-start.3) | collective-permute-done | bytes 737312 | tf_op jit(solution)/shard_map/ppermute | solution.py:85
  63.1 1.9 collective-permute-start.4
  65.0 2.9 %collective-permute-start.14 = (bf16[4,720,128]{2,1,0:T(8,128)(2,1)S(1)}, bf16[4,720,128]{2,1,0:T(8,128)(2,1)S(1)}, u32[]{:S(2)}, u32[]{:S(2)}) collective-permute-start(bf16[4,720,128]{2,1,0:T(8,128)(2,1)S(1)} %collective-permute-done.3), channel_id=1, source_target_pairs={{0,8},{8,0},{1,9},{9,1},{2,10},{10,2},{3,11},{11,3},{4,12},{12,4},... | collective-permute-start | bytes 2211848 | tf_op jit(solution)/shard_map/ppermute | solution.py:85
  67.9 4.9 %collective-permute-start.8 = (bf16[4,720,128]{2,1,0:T(8,128)(2,1)S(1)}, bf16[4,720,128]{2,1,0:T(8,128)(2,1)S(1)}, u32[]{:S(2)}, u32[]{:S(2)}) collective-permute-start(bf16[4,720,128]{2,1,0:T(8,128)(2,1)S(1)} %collective-permute-done.7), channel_id=1, source_target_pairs={{0,112},{16,0},{32,16},{48,32},{64,48},{80,64},{96,80},{112,96},{1... | collective-permute-start | bytes 2211848 | tf_op jit(solution)/shard_map/ppermute | solution.py:85
  72.8 2.2 %collective-permute-start.15 = (bf16[4,720,128]{2,1,0:T(8,128)(2,1)S(1)}, bf16[4,720,128]{2,1,0:T(8,128)(2,1)S(1)}, u32[]{:S(2)}, u32[]{:S(2)}) collective-permute-start(bf16[4,720,128]{2,1,0:T(8,128)(2,1)S(1)} %collective-permute-done.7), channel_id=1, source_target_pairs={{0,8},{8,0},{1,9},{9,1},{2,10},{10,2},{3,11},{11,3},{4,12},{12,4},... | collective-permute-start | bytes 2211848 | tf_op jit(solution)/shard_map/ppermute | solution.py:85
  75.2 1.0 bitcast_dynamic-update-slice_fusion.14
  77.1 6.1 %collective-permute-done.4 = bf16[4,720,128]{2,1,0:T(8,128)(2,1)S(1)} collective-permute-done((bf16[4,720,128]{2,1,0:T(8,128)(2,1)S(1)}, bf16[4,720,128]{2,1,0:T(8,128)(2,1)S(1)}, u32[]{:S(2)}, u32[]{:S(2)}) %collective-permute-start.4) | collective-permute-done | bytes 737312 | tf_op jit(solution)/shard_map/ppermute | solution.py:85
  83.2 1.9 collective-permute-start.5
  85.1 3.5 %collective-permute-done.8 = bf16[4,720,128]{2,1,0:T(8,128)(2,1)S(1)} collective-permute-done((bf16[4,720,128]{2,1,0:T(8,128)(2,1)S(1)}, bf16[4,720,128]{2,1,0:T(8,128)(2,1)S(1)}, u32[]{:S(2)}, u32[]{:S(2)}) %collective-permute-start.8) | collective-permute-done | bytes 737312 | tf_op jit(solution)/shard_map/ppermute | solution.py:85
  88.7 5.4 %collective-permute-start.9 = (bf16[4,720,128]{2,1,0:T(8,128)(2,1)S(1)}, bf16[4,720,128]{2,1,0:T(8,128)(2,1)S(1)}, u32[]{:S(2)}, u32[]{:S(2)}) collective-permute-start(bf16[4,720,128]{2,1,0:T(8,128)(2,1)S(1)} %collective-permute-done.8), channel_id=1, source_target_pairs={{0,112},{16,0},{32,16},{48,32},{64,48},{80,64},{96,80},{112,96},{1... | collective-permute-start | bytes 2211848 | tf_op jit(solution)/shard_map/ppermute | solution.py:85
  94.1 0.9 bitcast_dynamic-update-slice_fusion.12
  95.2 0.9 bitcast_dynamic-update-slice_fusion.11
  96.2 13.0 %collective-permute-done.9 = bf16[4,720,128]{2,1,0:T(8,128)(2,1)S(1)} collective-permute-done((bf16[4,720,128]{2,1,0:T(8,128)(2,1)S(1)}, bf16[4,720,128]{2,1,0:T(8,128)(2,1)S(1)}, u32[]{:S(2)}, u32[]{:S(2)}) %collective-permute-start.9) | collective-permute-done | bytes 737312 | tf_op jit(solution)/shard_map/ppermute | solution.py:85
  109.2 3.5 %collective-permute-start.16 = (bf16[4,720,128]{2,1,0:T(8,128)(2,1)S(1)}, bf16[4,720,128]{2,1,0:T(8,128)(2,1)S(1)}, u32[]{:S(2)}, u32[]{:S(2)}) collective-permute-start(bf16[4,720,128]{2,1,0:T(8,128)(2,1)S(1)} %collective-permute-done.4), channel_id=1, source_target_pairs={{0,8},{8,0},{1,9},{9,1},{2,10},{10,2},{3,11},{11,3},{4,12},{12,4},... | collective-permute-start | bytes 2211848 | tf_op jit(solution)/shard_map/ppermute | solution.py:85
  112.7 1.9 collective-permute-start.17
  114.9 5.3 %collective-permute-start.10 = (bf16[2,720,128]{2,1,0:T(8,128)(2,1)S(1)}, bf16[2,720,128]{2,1,0:T(8,128)(2,1)S(1)}, u32[]{:S(2)}, u32[]{:S(2)}) collective-permute-start(bf16[2,720,128]{2,1,0:T(8,128)(2,1)S(1)} %slice.205), channel_id=1, source_target_pairs={{0,112},{16,0},{32,16},{48,32},{64,48},{80,64},{96,80},{112,96},{1... | collective-permute-start | bytes 1105928 | tf_op jit(solution)/shard_map/ppermute | solution.py:85
  120.4 2.3 %collective-permute-start.12 = (bf16[2,720,128]{2,1,0:T(8,128)(2,1)S(1)}, bf16[2,720,128]{2,1,0:T(8,128)(2,1)S(1)}, u32[]{:S(2)}, u32[]{:S(2)}) collective-permute-start(bf16[2,720,128]{2,1,0:T(8,128)(2,1)S(1)} %slice.205), channel_id=1, source_target_pairs={{24,0},{16,8},{40,16},{32,24},{56,32},{48,40},{72,48},{64,56},{88,... | collective-permute-start | bytes 1105928 | tf_op jit(solution)/shard_map/ppermute | solution.py:155
  122.8 0.9 bitcast_dynamic-update-slice_fusion.10
  123.7 0.9 bitcast_dynamic-update-slice_fusion.9
  124.6 0.9 bitcast_dynamic-update-slice_fusion.8
  126.5 3.6 %collective-permute-start.6 = (bf16[2,720,128]{2,1,0:T(8,128)(2,1)S(1)}, bf16[2,720,128]{2,1,0:T(8,128)(2,1)S(1)}, u32[]{:S(2)}, u32[]{:S(2)}) collective-permute-start(bf16[2,720,128]{2,1,0:T(8,128)(2,1)S(1)} %slice.204), channel_id=1, source_target_pairs={{0,16},{16,32},{32,48},{48,64},{64,80},{80,96},{96,112},{112,0},{1... | collective-permute-start | bytes 1105928 | tf_op jit(solution)/shard_map/ppermute | solution.py:85
  131.0 1.9 collective-permute-start.18
  133.0 0.9 bitcast_dynamic-update-slice_fusion.5
  134.1 2.4 %collective-permute-start.19 = (bf16[4,720,128]{2,1,0:T(8,128)(2,1)S(1)}, bf16[4,720,128]{2,1,0:T(8,128)(2,1)S(1)}, u32[]{:S(2)}, u32[]{:S(2)}) collective-permute-start(bf16[4,720,128]{2,1,0:T(8,128)(2,1)S(1)} %collective-permute-done.9), channel_id=1, source_target_pairs={{0,8},{8,0},{1,9},{9,1},{2,10},{10,2},{3,11},{11,3},{4,12},{12,4},... | collective-permute-start | bytes 2211848 | tf_op jit(solution)/shard_map/ppermute | solution.py:85
  136.6 2.1 %collective-permute-start.11 = (bf16[2,720,128]{2,1,0:T(8,128)(2,1)S(1)}, bf16[2,720,128]{2,1,0:T(8,128)(2,1)S(1)}, u32[]{:S(2)}, u32[]{:S(2)}) collective-permute-start(bf16[2,720,128]{2,1,0:T(8,128)(2,1)S(1)} %slice.204), channel_id=1, source_target_pairs={{120,0},{112,8},{8,16},{0,24},{24,32},{16,40},{40,48},{32,56},{56,... | collective-permute-start | bytes 1105928 | tf_op jit(solution)/shard_map/ppermute | solution.py:154
  139.7 10.2 %collective-permute-done.11 = bf16[2,720,128]{2,1,0:T(8,128)(2,1)S(1)} collective-permute-done((bf16[2,720,128]{2,1,0:T(8,128)(2,1)S(1)}, bf16[2,720,128]{2,1,0:T(8,128)(2,1)S(1)}, u32[]{:S(2)}, u32[]{:S(2)}) %collective-permute-start.11) | collective-permute-done | bytes 368672 | tf_op jit(solution)/shard_map/ppermute | solution.py:154
  150.3 1.0 bitcast_dynamic-update-slice_fusion.3
  151.2 3.6 %copy-done.1 = bf16[16,4,9,80,128]{4,3,0,2,1:T(8,128)(2,1)} copy-done((bf16[16,4,9,80,128]{4,3,0,2,1:T(8,128)(2,1)}, bf16[16,4,9,80,128]{4,3,0,2,1:T(8,128)(2,1)S(1)}, u32[]{:S(2)}) %copy-start.1) | copy-done | bytes 11796504
  154.8 0.9 bitcast_dynamic-update-slice_fusion.2
  155.8 2.3 %slice_bitcast_fusion.2 = (bf16[128,5120]{0,1:T(8,128)(2,1)S(1)}, bf16[1,128,5120]{1,2,0:T(8,128)(2,1)S(1)}, bf16[1,128,5120]{1,2,0:T(8,128)(2,1)S(1)}) fusion(bf16[2,128,5120]{1,2,0:T(8,128)(2,1)} %all-gather.2.cloned.1.call-done), kind=kLoop, calls=%fused_computation.128 | loop fusion | bytes 6553600 | tf_op jit(solution)/shard_map/squeeze | solution.py:128
  160.2 0.9 fusion.2
  161.2 0.9 fusion.1
  162.2 0.9 fusion
  164.5 3.6 %fusion.5 = f32[256,9,128]{2,0,1:T(8,128)S(1)} fusion(bf16[16,4,9,80,128]{4,3,0,2,1:T(8,128)(2,1)S(1)} %constant_dynamic-update-slice_fusion.11, bf16[256,16,4,80]{0,3,1,2:T(8,128)(2,1)S(1)} %bitcast_dynamic-update-slice_fusion.31), kind=kOutput, calls=%fused_computation.13 | convolution fusion | flops 3019898880 | bytes 15597568 | tf_op jit(solution)/shard_map/rpki,pkjid->rjd/dot_general | solution.py:166
  169.7 0.9 bitcast_dynamic-update-slice_fusion.1
  173.0 15.6 %shard_map.149 = bf16[2,128,640]{2,1,0:T(8,128)(2,1)} custom-call(bf16[2,128,640]{2,1,0:T(8,128)(2,1)} %copy.114.q_ref, bf16[2,128,128]{2,1,0:T(8,128)(2,1)} %pad_maximum_fusion.5.ko_ref, bf16[2,128,128]{2,1,0:T(8,128)(2,1)} %add_convert_fusion.1.vo_ref, bf16[64,720,128]{2,1,0:T(8,128)(2,1)} %bitcast.104.kc_ref.vc_ref, ...), custom_call_target="tpu_custom_call" | custom-call | flops 2768240640 | bytes 3407872 | tf_op jit(solution)/shard_map/pallas_call | solution.py:62
  188.7 1.7 slice_bitcast_fusion
  (159 shorter events, 23.2 us)
Async XLA Ops:
  7.2 41.4 %copy-start.3 = (bf16[5120]{0:T(1024)(128)(2,1)S(1)}, bf16[5120]{0:T(1024)(128)(2,1)}, u32[]{:S(2)}) copy-start(bf16[5120]{0:T(1024)(128)(2,1)} %param.19) | copy-start | bytes 30724
  7.2 41.6 %copy-start.5 = (bf16[128]{0:T(256)(128)(2,1)S(1)}, bf16[128]{0:T(256)(128)(2,1)}, u32[]{:S(2)}) copy-start(bf16[128]{0:T(256)(128)(2,1)} %param.23) | copy-start | bytes 772
  7.2 41.8 %copy-start.6 = (bf16[128]{0:T(256)(128)(2,1)S(1)}, bf16[128]{0:T(256)(128)(2,1)}, u32[]{:S(2)}) copy-start(bf16[128]{0:T(256)(128)(2,1)} %param.25) | copy-start | bytes 772
  7.2 41.8 %copy-start.7 = (s32[128]{0:T(128)S(1)}, s32[128]{0:T(128)}, u32[]{:S(2)}) copy-start(s32[128]{0:T(128)} %param.16) | copy-start | bytes 1540
  7.2 41.8 %copy-start.4 = (bf16[640]{0:T(1024)(128)(2,1)S(1)}, bf16[640]{0:T(1024)(128)(2,1)}, u32[]{:S(2)}) copy-start(bf16[640]{0:T(1024)(128)(2,1)} %param.21) | copy-start | bytes 3844
  7.2 148.5 %all-gather.2.cloned.1.call-start = ((), (), s32[]{:S(2)}) async-start(), calls=%async_computation | async-start | bytes 2949120 | tf_op jit(solution)/shard_map/all_gather | solution.py:127
  13.9 15.5 %collective-permute-start.2 = (bf16[720,128]{1,0:T(8,128)(2,1)S(1)}, bf16[720,128]{1,0:T(8,128)(2,1)S(1)}, u32[]{:S(2)}, u32[]{:S(2)}) collective-permute-start(bf16[720,128]{1,0:T(8,128)(2,1)S(1)} %constant_dynamic-update-slice_fusion), channel_id=1, source_target_pairs={{0,128},{128,256},{256,384},{384,0},{1,129},{129,257},{257,385},{3... | collective-permute-start | bytes 552968 | tf_op jit(solution)/shard_map/ppermute | solution.py:85
  16.2 15.7 %collective-permute-start.1 = (bf16[720,128]{1,0:T(8,128)(2,1)S(1)}, bf16[720,128]{1,0:T(8,128)(2,1)S(1)}, u32[]{:S(2)}, u32[]{:S(2)}) collective-permute-start(bf16[720,128]{1,0:T(8,128)(2,1)S(1)} %constant_dynamic-update-slice_fusion), channel_id=1, source_target_pairs={{0,256},{128,384},{256,0},{384,128},{1,257},{129,385},{257,1},{385... | collective-permute-start | bytes 552968 | tf_op jit(solution)/shard_map/ppermute | solution.py:85
  20.8 15.0 %collective-permute-start = (bf16[720,128]{1,0:T(8,128)(2,1)S(1)}, bf16[720,128]{1,0:T(8,128)(2,1)S(1)}, u32[]{:S(2)}, u32[]{:S(2)}) collective-permute-start(bf16[720,128]{1,0:T(8,128)(2,1)S(1)} %constant_dynamic-update-slice_fusion), channel_id=1, source_target_pairs={{0,384},{128,0},{256,128},{384,256},{1,385},{129,1},{257,129},{385... | collective-permute-start | bytes 552968 | tf_op jit(solution)/shard_map/ppermute | solution.py:85
  36.0 27.1 %collective-permute-start.3 = (bf16[4,720,128]{2,1,0:T(8,128)(2,1)S(1)}, bf16[4,720,128]{2,1,0:T(8,128)(2,1)S(1)}, u32[]{:S(2)}, u32[]{:S(2)}) collective-permute-start(bf16[4,720,128]{2,1,0:T(8,128)(2,1)S(1)} %pad_maximum_fusion), channel_id=1, source_target_pairs={{0,16},{16,32},{32,48},{48,64},{64,80},{80,96},{96,112},{112,0},{1... | collective-permute-start | bytes 2211848 | tf_op jit(solution)/shard_map/ppermute | solution.py:85
  40.0 27.9 %collective-permute-start.7 = (bf16[4,720,128]{2,1,0:T(8,128)(2,1)S(1)}, bf16[4,720,128]{2,1,0:T(8,128)(2,1)S(1)}, u32[]{:S(2)}, u32[]{:S(2)}) collective-permute-start(bf16[4,720,128]{2,1,0:T(8,128)(2,1)S(1)} %pad_maximum_fusion), channel_id=1, source_target_pairs={{0,112},{16,0},{32,16},{48,32},{64,48},{80,64},{96,80},{112,96},{1... | collective-permute-start | bytes 2211848 | tf_op jit(solution)/shard_map/ppermute | solution.py:85
  48.6 26.6 %copy-start.2 = (f32[1,4096]{1,0:T(1,128)}, f32[1,4096]{1,0:T(1,128)S(1)}, u32[]{:S(2)}) copy-start(f32[1,4096]{1,0:T(1,128)S(1)} %constant_dynamic-update-slice_fusion.26.bias_ref) | copy-start | bytes 49156
  49.1 65.8 %collective-permute-start.13 = (bf16[4,720,128]{2,1,0:T(8,128)(2,1)S(1)}, bf16[4,720,128]{2,1,0:T(8,128)(2,1)S(1)}, u32[]{:S(2)}, u32[]{:S(2)}) collective-permute-start(bf16[4,720,128]{2,1,0:T(8,128)(2,1)S(1)} %pad_maximum_fusion), channel_id=1, source_target_pairs={{0,8},{8,0},{1,9},{9,1},{2,10},{10,2},{3,11},{11,3},{4,12},{12,4},... | collective-permute-start | bytes 2211848 | tf_op jit(solution)/shard_map/ppermute | solution.py:85
  63.1 20.2 %collective-permute-start.4 = (bf16[4,720,128]{2,1,0:T(8,128)(2,1)S(1)}, bf16[4,720,128]{2,1,0:T(8,128)(2,1)S(1)}, u32[]{:S(2)}, u32[]{:S(2)}) collective-permute-start(bf16[4,720,128]{2,1,0:T(8,128)(2,1)S(1)} %collective-permute-done.3), channel_id=1, source_target_pairs={{0,16},{16,32},{32,48},{48,64},{64,80},{80,96},{96,112},{112,0},{1... | collective-permute-start | bytes 2211848 | tf_op jit(solution)/shard_map/ppermute | solution.py:85
  65.0 55.4 %collective-permute-start.14 = (bf16[4,720,128]{2,1,0:T(8,128)(2,1)S(1)}, bf16[4,720,128]{2,1,0:T(8,128)(2,1)S(1)}, u32[]{:S(2)}, u32[]{:S(2)}) collective-permute-start(bf16[4,720,128]{2,1,0:T(8,128)(2,1)S(1)} %collective-permute-done.3), channel_id=1, source_target_pairs={{0,8},{8,0},{1,9},{9,1},{2,10},{10,2},{3,11},{11,3},{4,12},{12,4},... | collective-permute-start | bytes 2211848 | tf_op jit(solution)/shard_map/ppermute | solution.py:85
  67.9 20.7 %collective-permute-start.8 = (bf16[4,720,128]{2,1,0:T(8,128)(2,1)S(1)}, bf16[4,720,128]{2,1,0:T(8,128)(2,1)S(1)}, u32[]{:S(2)}, u32[]{:S(2)}) collective-permute-start(bf16[4,720,128]{2,1,0:T(8,128)(2,1)S(1)} %collective-permute-done.7), channel_id=1, source_target_pairs={{0,112},{16,0},{32,16},{48,32},{64,48},{80,64},{96,80},{112,96},{1... | collective-permute-start | bytes 2211848 | tf_op jit(solution)/shard_map/ppermute | solution.py:85
  72.8 53.7 %collective-permute-start.15 = (bf16[4,720,128]{2,1,0:T(8,128)(2,1)S(1)}, bf16[4,720,128]{2,1,0:T(8,128)(2,1)S(1)}, u32[]{:S(2)}, u32[]{:S(2)}) collective-permute-start(bf16[4,720,128]{2,1,0:T(8,128)(2,1)S(1)} %collective-permute-done.7), channel_id=1, source_target_pairs={{0,8},{8,0},{1,9},{9,1},{2,10},{10,2},{3,11},{11,3},{4,12},{12,4},... | collective-permute-start | bytes 2211848 | tf_op jit(solution)/shard_map/ppermute | solution.py:85
  83.2 29.5 %collective-permute-start.5 = (bf16[4,720,128]{2,1,0:T(8,128)(2,1)S(1)}, bf16[4,720,128]{2,1,0:T(8,128)(2,1)S(1)}, u32[]{:S(2)}, u32[]{:S(2)}) collective-permute-start(bf16[4,720,128]{2,1,0:T(8,128)(2,1)S(1)} %collective-permute-done.4), channel_id=1, source_target_pairs={{0,16},{16,32},{32,48},{48,64},{64,80},{80,96},{96,112},{112,0},{1... | collective-permute-start | bytes 2211848 | tf_op jit(solution)/shard_map/ppermute | solution.py:85
  88.7 20.5 %collective-permute-start.9 = (bf16[4,720,128]{2,1,0:T(8,128)(2,1)S(1)}, bf16[4,720,128]{2,1,0:T(8,128)(2,1)S(1)}, u32[]{:S(2)}, u32[]{:S(2)}) collective-permute-start(bf16[4,720,128]{2,1,0:T(8,128)(2,1)S(1)} %collective-permute-done.8), channel_id=1, source_target_pairs={{0,112},{16,0},{32,16},{48,32},{64,48},{80,64},{96,80},{112,96},{1... | collective-permute-start | bytes 2211848 | tf_op jit(solution)/shard_map/ppermute | solution.py:85
  109.2 21.8 %collective-permute-start.16 = (bf16[4,720,128]{2,1,0:T(8,128)(2,1)S(1)}, bf16[4,720,128]{2,1,0:T(8,128)(2,1)S(1)}, u32[]{:S(2)}, u32[]{:S(2)}) collective-permute-start(bf16[4,720,128]{2,1,0:T(8,128)(2,1)S(1)} %collective-permute-done.4), channel_id=1, source_target_pairs={{0,8},{8,0},{1,9},{9,1},{2,10},{10,2},{3,11},{11,3},{4,12},{12,4},... | collective-permute-start | bytes 2211848 | tf_op jit(solution)/shard_map/ppermute | solution.py:85
  112.7 21.4 %collective-permute-start.17 = (bf16[4,720,128]{2,1,0:T(8,128)(2,1)S(1)}, bf16[4,720,128]{2,1,0:T(8,128)(2,1)S(1)}, u32[]{:S(2)}, u32[]{:S(2)}) collective-permute-start(bf16[4,720,128]{2,1,0:T(8,128)(2,1)S(1)} %collective-permute-done.8), channel_id=1, source_target_pairs={{0,8},{8,0},{1,9},{9,1},{2,10},{10,2},{3,11},{11,3},{4,12},{12,4},... | collective-permute-start | bytes 2211848 | tf_op jit(solution)/shard_map/ppermute | solution.py:85
  114.9 21.7 %collective-permute-start.10 = (bf16[2,720,128]{2,1,0:T(8,128)(2,1)S(1)}, bf16[2,720,128]{2,1,0:T(8,128)(2,1)S(1)}, u32[]{:S(2)}, u32[]{:S(2)}) collective-permute-start(bf16[2,720,128]{2,1,0:T(8,128)(2,1)S(1)} %slice.205), channel_id=1, source_target_pairs={{0,112},{16,0},{32,16},{48,32},{64,48},{80,64},{96,80},{112,96},{1... | collective-permute-start | bytes 1105928 | tf_op jit(solution)/shard_map/ppermute | solution.py:85
  120.4 19.4 %collective-permute-start.12 = (bf16[2,720,128]{2,1,0:T(8,128)(2,1)S(1)}, bf16[2,720,128]{2,1,0:T(8,128)(2,1)S(1)}, u32[]{:S(2)}, u32[]{:S(2)}) collective-permute-start(bf16[2,720,128]{2,1,0:T(8,128)(2,1)S(1)} %slice.205), channel_id=1, source_target_pairs={{24,0},{16,8},{40,16},{32,24},{56,32},{48,40},{72,48},{64,56},{88,... | collective-permute-start | bytes 1105928 | tf_op jit(solution)/shard_map/ppermute | solution.py:155
  126.5 13.2 %collective-permute-start.6 = (bf16[2,720,128]{2,1,0:T(8,128)(2,1)S(1)}, bf16[2,720,128]{2,1,0:T(8,128)(2,1)S(1)}, u32[]{:S(2)}, u32[]{:S(2)}) collective-permute-start(bf16[2,720,128]{2,1,0:T(8,128)(2,1)S(1)} %slice.204), channel_id=1, source_target_pairs={{0,16},{16,32},{32,48},{48,64},{64,80},{80,96},{96,112},{112,0},{1... | collective-permute-start | bytes 1105928 | tf_op jit(solution)/shard_map/ppermute | solution.py:85
  131.0 19.0 %collective-permute-start.18 = (bf16[4,720,128]{2,1,0:T(8,128)(2,1)S(1)}, bf16[4,720,128]{2,1,0:T(8,128)(2,1)S(1)}, u32[]{:S(2)}, u32[]{:S(2)}) collective-permute-start(bf16[4,720,128]{2,1,0:T(8,128)(2,1)S(1)} %collective-permute-done.5), channel_id=1, source_target_pairs={{0,8},{8,0},{1,9},{9,1},{2,10},{10,2},{3,11},{11,3},{4,12},{12,4},... | collective-permute-start | bytes 2211848 | tf_op jit(solution)/shard_map/ppermute | solution.py:85
  134.1 16.0 %collective-permute-start.19 = (bf16[4,720,128]{2,1,0:T(8,128)(2,1)S(1)}, bf16[4,720,128]{2,1,0:T(8,128)(2,1)S(1)}, u32[]{:S(2)}, u32[]{:S(2)}) collective-permute-start(bf16[4,720,128]{2,1,0:T(8,128)(2,1)S(1)} %collective-permute-done.9), channel_id=1, source_target_pairs={{0,8},{8,0},{1,9},{9,1},{2,10},{10,2},{3,11},{11,3},{4,12},{12,4},... | collective-permute-start | bytes 2211848 | tf_op jit(solution)/shard_map/ppermute | solution.py:85
  136.6 13.3 %collective-permute-start.11 = (bf16[2,720,128]{2,1,0:T(8,128)(2,1)S(1)}, bf16[2,720,128]{2,1,0:T(8,128)(2,1)S(1)}, u32[]{:S(2)}, u32[]{:S(2)}) collective-permute-start(bf16[2,720,128]{2,1,0:T(8,128)(2,1)S(1)} %slice.204), channel_id=1, source_target_pairs={{120,0},{112,8},{8,16},{0,24},{24,32},{16,40},{40,48},{32,56},{56,... | collective-permute-start | bytes 1105928 | tf_op jit(solution)/shard_map/ppermute | solution.py:154
  150.2 4.6 %copy-start.1 = (bf16[16,4,9,80,128]{4,3,0,2,1:T(8,128)(2,1)}, bf16[16,4,9,80,128]{4,3,0,2,1:T(8,128)(2,1)S(1)}, u32[]{:S(2)}) copy-start(bf16[16,4,9,80,128]{4,3,0,2,1:T(8,128)(2,1)S(1)} %constant_dynamic-update-slice_fusion.13) | copy-start | bytes 35389444
  155.8 2.5 %copy-start = (bf16[2,128,5120]{1,2,0:T(8,128)(2,1)S(1)}, bf16[2,128,5120]{1,2,0:T(8,128)(2,1)}, u32[]{:S(2)}) copy-start(bf16[2,128,5120]{1,2,0:T(8,128)(2,1)} %all-gather.2.cloned.1.call-done) | copy-start | bytes 7864324
  159.3 4.1 %slice-start = ((s8[11796480]{0:T(1024)(128)(4,1)}), s8[4194304]{0:T(1024)(128)(4,1)S(1)}, s32[]{:S(2)}) async-start(s8[11796480]{0:T(1024)(128)(4,1)} %bitcast.254), calls=%async_computation.1 | async-start | bytes 8388608
  160.2 3.2 %slice-start.1 = ((s8[11796480]{0:T(1024)(128)(4,1)}), s8[4194304]{0:T(1024)(128)(4,1)S(1)}, s32[]{:S(2)}) async-start(s8[11796480]{0:T(1024)(128)(4,1)} %bitcast.254), calls=%async_computation.2 | async-start | bytes 8388608
  162.1 2.2 %slice-start.2 = ((s8[11796480]{0:T(1024)(128)(4,1)}), s8[3407872]{0:T(1024)(128)(4,1)S(1)}, s32[]{:S(2)}) async-start(s8[11796480]{0:T(1024)(128)(4,1)} %bitcast.254), calls=%async_computation.3 | async-start | bytes 6815744
Sparse Core Ops, SparseCore 0:
  25.8 87.6 all-gather.1

commit v10 on v8

--- a/solution.py
+++ b/solution.py
@@ -36,18 +36,25 @@
 
 def attend_kernel(q_ref, ko_ref, vo_ref, kc_ref, vc_ref, bias_ref, out_ref):
     inv_root = 1.0 / math.sqrt(HD)
-    q = q_ref[...]
     contract = (((1,), (1,)), ((), ()))
-    own = lax.dot_general(q, ko_ref[...], contract, preferred_element_type=jnp.float32) * inv_root
-    far = lax.dot_general(q, kc_ref[...], contract, preferred_element_type=jnp.float32) * inv_root
-    far = far + bias_ref[...]
-    highest = jnp.maximum(jnp.max(own, axis=-1, keepdims=True), jnp.max(far, axis=-1, keepdims=True))
-    own_w = jnp.exp(own - highest)
-    far_w = jnp.exp(far - highest)
-    totals = jnp.sum(own_w, axis=-1, keepdims=True) + jnp.sum(far_w, axis=-1, keepdims=True)
-    mixture = jnp.dot(own_w.astype(jnp.bfloat16), vo_ref[...], preferred_element_type=jnp.float32)
-    mixture = mixture + jnp.dot(far_w.astype(jnp.bfloat16), vc_ref[...], preferred_element_type=jnp.float32)
-    out_ref[...] = (mixture / totals).astype(out_ref.dtype)
+    own_keys = ko_ref[...]
+    own_values = vo_ref[...]
+    cache_k = kc_ref[...]
+    cache_v = vc_ref[...]
+    bias = bias_ref[...]
+    for head in range(q_ref.shape[1] // HD):
+        lanes = slice(head * HD, (head + 1) * HD)
+        q = q_ref[:, lanes]
+        own = lax.dot_general(q, own_keys, contract, preferred_element_type=jnp.float32) * inv_root
+        far = lax.dot_general(q, cache_k, contract, preferred_element_type=jnp.float32) * inv_root
+        far = far + bias
+        highest = jnp.maximum(jnp.max(own, axis=-1, keepdims=True), jnp.max(far, axis=-1, keepdims=True))
+        own_w = jnp.exp(own - highest)
+        far_w = jnp.exp(far - highest)
+        totals = jnp.sum(own_w, axis=-1, keepdims=True) + jnp.sum(far_w, axis=-1, keepdims=True)
+        mixture = jnp.dot(own_w.astype(jnp.bfloat16), own_values, preferred_element_type=jnp.float32)
+        mixture = mixture + jnp.dot(far_w.astype(jnp.bfloat16), cache_v, preferred_element_type=jnp.float32)
+        out_ref[:, lanes] = (mixture / totals).astype(out_ref.dtype)
 
 
 def attend(q_rot, k_rot, value_rows, cache_k, cache_v, bias):
@@ -56,16 +63,16 @@
     ctx = cache_k.shape[0]
     return pl.pallas_call(
         attend_kernel,
-        grid=(passes, heads),
+        grid=(passes,),
         in_specs=[
-            pl.BlockSpec((None, rows, HD), lambda p, h: (p, 0, h)),
-            pl.BlockSpec((None, rows, HD), lambda p, h: (p, 0, 0)),
-            pl.BlockSpec((None, rows, HD), lambda p, h: (p, 0, 0)),
-            pl.BlockSpec((ctx, HD), lambda p, h: (0, 0)),
-            pl.BlockSpec((ctx, HD), lambda p, h: (0, 0)),
-            pl.BlockSpec((1, ctx), lambda p, h: (0, 0)),
+            pl.BlockSpec((None, rows, width), lambda p: (p, 0, 0)),
+            pl.BlockSpec((None, rows, HD), lambda p: (p, 0, 0)),
+            pl.BlockSpec((None, rows, HD), lambda p: (p, 0, 0)),
+            pl.BlockSpec((ctx, HD), lambda p: (0, 0)),
+            pl.BlockSpec((ctx, HD), lambda p: (0, 0)),
+            pl.BlockSpec((1, ctx), lambda p: (0, 0)),
         ],
-        out_specs=pl.BlockSpec((None, rows, HD), lambda p, h: (p, 0, h)),
+        out_specs=pl.BlockSpec((None, rows, width), lambda p: (p, 0, 0)),
         out_shape=jax.ShapeDtypeStruct((passes, rows, width), jnp.bfloat16),
         cost_estimate=pl.CostEstimate(
             flops=4 * passes * heads * rows * (ctx + rows) * HD,

time: 188 us -> 186 us (0.989)
  the two profiles are of different devices: /device:TPU:1 before, /device:TPU:22 now
where the time goes in v10:
time: 186 us; the launch traced here: 184 us
  starting transfers between devices  63.9 us (34%)
  local copies, waits for them, and re-layouts  38.5 us (21%)
  waiting for transfers between devices  34.3 us (18%)
  between operations  15.9 us (9%)
  Pallas kernels  13.4 us (7%)
  matrix products  9.8 us (5%)
  other arithmetic  7.93 us (4%)
    ppermute x18, starting transfers between devices, shifted(): return lax.ppermute(x, axis, pairs)  58.6 us
    ppermute x18, waiting for transfers between devices, shifted(): return lax.ppermute(x, axis, pairs)  31 us
    unnamed x137, local copies, waits for them, and re-layouts  26.4 us
    pallas_call x1, Pallas kernels, attend(): pl.pallas_call(attend_kernel, grid=(passes,), in_specs=[pl.BlockSpec((Non...  13.4 us
    dot_general x16, matrix products, local(): jnp.einsum('rki,kjid->rjd', normed5[:, :, offset % n_z, core, :], piece.r...  9.8 us
  transfers between devices with their start and end apart: 21, of which 7 were waited for; matrix products, arithmetic and copies ran while one was open for 10% of the time, Pallas kernels for 0%

profile of v10, /device:TPU:22, one launch (start us, length us, event | category | flops | bytes accessed | tf_op | source)
XLA Modules:
  0.0 183.8 jit_solution(3404825403992675952)
XLA Ops:
  8.0 0.7 constant_dynamic-update-slice_fusion.9
  8.7 0.7 constant_dynamic-update-slice_fusion.8
  9.4 0.7 constant_dynamic-update-slice_fusion.7
  10.2 0.7 constant_dynamic-update-slice_fusion.6
  10.9 0.7 constant_dynamic-update-slice_fusion.5
  11.6 0.7 constant_dynamic-update-slice_fusion.4
  13.9 2.3 %collective-permute-start = (bf16[720,128]{1,0:T(8,128)(2,1)S(1)}, bf16[720,128]{1,0:T(8,128)(2,1)S(1)}, u32[]{:S(2)}, u32[]{:S(2)}) collective-permute-start(bf16[720,128]{1,0:T(8,128)(2,1)S(1)} %constant_dynamic-update-slice_fusion), channel_id=1, source_target_pairs={{0,384},{128,0},{256,128},{384,256},{1,385},{129,1},{257,129},{385... | collective-permute-start | bytes 552968 | tf_op jit(solution)/shard_map/ppermute | solution.py:87
  16.2 5.4 %collective-permute-start.1 = (bf16[720,128]{1,0:T(8,128)(2,1)S(1)}, bf16[720,128]{1,0:T(8,128)(2,1)S(1)}, u32[]{:S(2)}, u32[]{:S(2)}) collective-permute-start(bf16[720,128]{1,0:T(8,128)(2,1)S(1)} %constant_dynamic-update-slice_fusion), channel_id=1, source_target_pairs={{0,256},{128,384},{256,0},{384,128},{1,257},{129,385},{257,1},{385... | collective-permute-start | bytes 552968 | tf_op jit(solution)/shard_map/ppermute | solution.py:87
  21.6 1.9 %collective-permute-start.2 = (bf16[720,128]{1,0:T(8,128)(2,1)S(1)}, bf16[720,128]{1,0:T(8,128)(2,1)S(1)}, u32[]{:S(2)}, u32[]{:S(2)}) collective-permute-start(bf16[720,128]{1,0:T(8,128)(2,1)S(1)} %constant_dynamic-update-slice_fusion), channel_id=1, source_target_pairs={{0,128},{128,256},{256,384},{384,0},{1,129},{129,257},{257,385},{3... | collective-permute-start | bytes 552968 | tf_op jit(solution)/shard_map/ppermute | solution.py:87
  23.5 1.1 copy.46
  24.6 1.1 copy.47
  25.7 0.8 pad_maximum_fusion.3
  29.4 3.1 %collective-permute-done.1 = bf16[720,128]{1,0:T(8,128)(2,1)S(1)} collective-permute-done((bf16[720,128]{1,0:T(8,128)(2,1)S(1)}, bf16[720,128]{1,0:T(8,128)(2,1)S(1)}, u32[]{:S(2)}, u32[]{:S(2)}) %collective-permute-start.1) | collective-permute-done | bytes 184352 | tf_op jit(solution)/shard_map/ppermute | solution.py:87
  32.4 3.5 %collective-permute-done.2 = bf16[720,128]{1,0:T(8,128)(2,1)S(1)} collective-permute-done((bf16[720,128]{1,0:T(8,128)(2,1)S(1)}, bf16[720,128]{1,0:T(8,128)(2,1)S(1)}, u32[]{:S(2)}, u32[]{:S(2)}) %collective-permute-start.2) | collective-permute-done | bytes 184352 | tf_op jit(solution)/shard_map/ppermute | solution.py:87
  36.0 4.3 %collective-permute-start.3 = (bf16[4,720,128]{2,1,0:T(8,128)(2,1)S(1)}, bf16[4,720,128]{2,1,0:T(8,128)(2,1)S(1)}, u32[]{:S(2)}, u32[]{:S(2)}) collective-permute-start(bf16[4,720,128]{2,1,0:T(8,128)(2,1)S(1)} %pad_maximum_fusion), channel_id=1, source_target_pairs={{0,16},{16,32},{32,48},{48,64},{64,80},{80,96},{96,112},{112,0},{1... | collective-permute-start | bytes 2211848 | tf_op jit(solution)/shard_map/ppermute | solution.py:87
  40.5 8.6 %collective-permute-start.7 = (bf16[4,720,128]{2,1,0:T(8,128)(2,1)S(1)}, bf16[4,720,128]{2,1,0:T(8,128)(2,1)}, u32[]{:S(2)}, u32[]{:S(2)}) collective-permute-start(bf16[4,720,128]{2,1,0:T(8,128)(2,1)S(1)} %pad_maximum_fusion), channel_id=1, source_target_pairs={{0,112},{16,0},{32,16},{48,32},{64,48},{80,64},{96,80},{112,96},{1... | collective-permute-start | bytes 2211848 | tf_op jit(solution)/shard_map/ppermute | solution.py:87
  51.3 1.9 %collective-permute-start.13 = (bf16[4,720,128]{2,1,0:T(8,128)(2,1)S(1)}, bf16[4,720,128]{2,1,0:T(8,128)(2,1)S(1)}, u32[]{:S(2)}, u32[]{:S(2)}) collective-permute-start(bf16[4,720,128]{2,1,0:T(8,128)(2,1)S(1)} %pad_maximum_fusion), channel_id=1, source_target_pairs={{0,8},{8,0},{1,9},{9,1},{2,10},{10,2},{3,11},{11,3},{4,12},{12,4},... | collective-permute-start | bytes 2211848 | tf_op jit(solution)/shard_map/ppermute | solution.py:87
  53.9 9.7 %collective-permute-done.3 = bf16[4,720,128]{2,1,0:T(8,128)(2,1)S(1)} collective-permute-done((bf16[4,720,128]{2,1,0:T(8,128)(2,1)S(1)}, bf16[4,720,128]{2,1,0:T(8,128)(2,1)S(1)}, u32[]{:S(2)}, u32[]{:S(2)}) %collective-permute-start.3) | collective-permute-done | bytes 737312 | tf_op jit(solution)/shard_map/ppermute | solution.py:87
  63.6 1.9 %collective-permute-start.4 = (bf16[4,720,128]{2,1,0:T(8,128)(2,1)S(1)}, bf16[4,720,128]{2,1,0:T(8,128)(2,1)S(1)}, u32[]{:S(2)}, u32[]{:S(2)}) collective-permute-start(bf16[4,720,128]{2,1,0:T(8,128)(2,1)S(1)} %collective-permute-done.3), channel_id=1, source_target_pairs={{0,16},{16,32},{32,48},{48,64},{64,80},{80,96},{96,112},{112,0},{1... | collective-permute-start | bytes 2211848 | tf_op jit(solution)/shard_map/ppermute | solution.py:87
  65.6 5.1 %collective-permute-start.8 = (bf16[4,720,128]{2,1,0:T(8,128)(2,1)}, bf16[4,720,128]{2,1,0:T(8,128)(2,1)S(1)}, u32[]{:S(2)}, u32[]{:S(2)}) collective-permute-start(bf16[4,720,128]{2,1,0:T(8,128)(2,1)} %collective-permute-done.7), channel_id=1, source_target_pairs={{0,112},{16,0},{32,16},{48,32},{64,48},{80,64},{96,80},{112,96},{1... | collective-permute-start | bytes 2211848 | tf_op jit(solution)/shard_map/ppermute | solution.py:87
  70.7 0.9 fusion.80
  71.7 1.9 %collective-permute-start.14 = (bf16[4,720,128]{2,1,0:T(8,128)(2,1)S(1)}, bf16[4,720,128]{2,1,0:T(8,128)(2,1)S(1)}, u32[]{:S(2)}, u32[]{:S(2)}) collective-permute-start(bf16[4,720,128]{2,1,0:T(8,128)(2,1)S(1)} %collective-permute-done.3), channel_id=1, source_target_pairs={{0,8},{8,0},{1,9},{9,1},{2,10},{10,2},{3,11},{11,3},{4,12},{12,4},... | collective-permute-start | bytes 2211848 | tf_op jit(solution)/shard_map/ppermute | solution.py:87
  73.6 2.4 %collective-permute-start.15 = (bf16[4,720,128]{2,1,0:T(8,128)(2,1)}, bf16[4,720,128]{2,1,0:T(8,128)(2,1)S(1)}, u32[]{:S(2)}, u32[]{:S(2)}) collective-permute-start(bf16[4,720,128]{2,1,0:T(8,128)(2,1)} %collective-permute-done.7), channel_id=1, source_target_pairs={{0,8},{8,0},{1,9},{9,1},{2,10},{10,2},{3,11},{11,3},{4,12},{12,4},... | collective-permute-start | bytes 2211848 | tf_op jit(solution)/shard_map/ppermute | solution.py:87
  77.3 7.3 %collective-permute-done.4 = bf16[4,720,128]{2,1,0:T(8,128)(2,1)S(1)} collective-permute-done((bf16[4,720,128]{2,1,0:T(8,128)(2,1)S(1)}, bf16[4,720,128]{2,1,0:T(8,128)(2,1)S(1)}, u32[]{:S(2)}, u32[]{:S(2)}) %collective-permute-start.4) | collective-permute-done | bytes 737312 | tf_op jit(solution)/shard_map/ppermute | solution.py:87
  84.6 1.9 %collective-permute-start.5 = (bf16[4,720,128]{2,1,0:T(8,128)(2,1)S(1)}, bf16[4,720,128]{2,1,0:T(8,128)(2,1)S(1)}, u32[]{:S(2)}, u32[]{:S(2)}) collective-permute-start(bf16[4,720,128]{2,1,0:T(8,128)(2,1)S(1)} %collective-permute-done.4), channel_id=1, source_target_pairs={{0,16},{16,32},{32,48},{48,64},{64,80},{80,96},{96,112},{112,0},{1... | collective-permute-start | bytes 2211848 | tf_op jit(solution)/shard_map/ppermute | solution.py:87
  86.6 5.1 %collective-permute-start.9 = (bf16[4,720,128]{2,1,0:T(8,128)(2,1)S(1)}, bf16[4,720,128]{2,1,0:T(8,128)(2,1)S(1)}, u32[]{:S(2)}, u32[]{:S(2)}) collective-permute-start(bf16[4,720,128]{2,1,0:T(8,128)(2,1)S(1)} %collective-permute-done.8), channel_id=1, source_target_pairs={{0,112},{16,0},{32,16},{48,32},{64,48},{80,64},{96,80},{112,96},{1... | collective-permute-start | bytes 2211848 | tf_op jit(solution)/shard_map/ppermute | solution.py:87
  91.8 1.9 %collective-permute-start.16 = (bf16[4,720,128]{2,1,0:T(8,128)(2,1)S(1)}, bf16[4,720,128]{2,1,0:T(8,128)(2,1)S(1)}, u32[]{:S(2)}, u32[]{:S(2)}) collective-permute-start(bf16[4,720,128]{2,1,0:T(8,128)(2,1)S(1)} %collective-permute-done.4), channel_id=1, source_target_pairs={{0,8},{8,0},{1,9},{9,1},{2,10},{10,2},{3,11},{11,3},{4,12},{12,4},... | collective-permute-start | bytes 2211848 | tf_op jit(solution)/shard_map/ppermute | solution.py:87
  95.0 2.4 %collective-permute-start.17 = (bf16[4,720,128]{2,1,0:T(8,128)(2,1)S(1)}, bf16[4,720,128]{2,1,0:T(8,128)(2,1)S(1)}, u32[]{:S(2)}, u32[]{:S(2)}) collective-permute-start(bf16[4,720,128]{2,1,0:T(8,128)(2,1)S(1)} %collective-permute-done.8), channel_id=1, source_target_pairs={{0,8},{8,0},{1,9},{9,1},{2,10},{10,2},{3,11},{11,3},{4,12},{12,4},... | collective-permute-start | bytes 2211848 | tf_op jit(solution)/shard_map/ppermute | solution.py:87
  97.4 7.3 %collective-permute-done.5 = bf16[4,720,128]{2,1,0:T(8,128)(2,1)S(1)} collective-permute-done((bf16[4,720,128]{2,1,0:T(8,128)(2,1)S(1)}, bf16[4,720,128]{2,1,0:T(8,128)(2,1)S(1)}, u32[]{:S(2)}, u32[]{:S(2)}) %collective-permute-start.5) | collective-permute-done | bytes 737312 | tf_op jit(solution)/shard_map/ppermute | solution.py:87
  104.8 1.9 %collective-permute-start.6 = (bf16[2,720,128]{2,1,0:T(8,128)(2,1)S(1)}, bf16[2,720,128]{2,1,0:T(8,128)(2,1)S(1)}, u32[]{:S(2)}, u32[]{:S(2)}) collective-permute-start(bf16[2,720,128]{2,1,0:T(8,128)(2,1)S(1)} %slice.332), channel_id=1, source_target_pairs={{0,16},{16,32},{32,48},{48,64},{64,80},{80,96},{96,112},{112,0},{1... | collective-permute-start | bytes 1105928 | tf_op jit(solution)/shard_map/ppermute | solution.py:87
  106.7 1.9 %collective-permute-start.11 = (bf16[2,720,128]{2,1,0:T(8,128)(2,1)S(1)}, bf16[2,720,128]{2,1,0:T(8,128)(2,1)S(1)}, u32[]{:S(2)}, u32[]{:S(2)}) collective-permute-start(bf16[2,720,128]{2,1,0:T(8,128)(2,1)S(1)} %slice.332), channel_id=1, source_target_pairs={{120,0},{112,8},{8,16},{0,24},{24,32},{16,40},{40,48},{32,56},{56,... | collective-permute-start | bytes 1105928 | tf_op jit(solution)/shard_map/ppermute | solution.py:156
  108.7 5.1 %collective-permute-start.10 = (bf16[2,720,128]{2,1,0:T(8,128)(2,1)S(1)}, bf16[2,720,128]{2,1,0:T(8,128)(2,1)S(1)}, u32[]{:S(2)}, u32[]{:S(2)}) collective-permute-start(bf16[2,720,128]{2,1,0:T(8,128)(2,1)S(1)} %slice.333), channel_id=1, source_target_pairs={{0,112},{16,0},{32,16},{48,32},{64,48},{80,64},{96,80},{112,96},{1... | collective-permute-start | bytes 1105928 | tf_op jit(solution)/shard_map/ppermute | solution.py:87
  114.0 3.4 %collective-permute-start.12 = (bf16[2,720,128]{2,1,0:T(8,128)(2,1)S(1)}, bf16[2,720,128]{2,1,0:T(8,128)(2,1)S(1)}, u32[]{:S(2)}, u32[]{:S(2)}) collective-permute-start(bf16[2,720,128]{2,1,0:T(8,128)(2,1)S(1)} %slice.333), channel_id=1, source_target_pairs={{24,0},{16,8},{40,16},{32,24},{56,32},{48,40},{72,48},{64,56},{88,... | collective-permute-start | bytes 1105928 | tf_op jit(solution)/shard_map/ppermute | solution.py:157
  118.8 1.9 %collective-permute-start.18 = (bf16[4,720,128]{2,1,0:T(8,128)(2,1)S(1)}, bf16[4,720,128]{2,1,0:T(8,128)(2,1)S(1)}, u32[]{:S(2)}, u32[]{:S(2)}) collective-permute-start(bf16[4,720,128]{2,1,0:T(8,128)(2,1)S(1)} %collective-permute-done.5), channel_id=1, source_target_pairs={{0,8},{8,0},{1,9},{9,1},{2,10},{10,2},{3,11},{11,3},{4,12},{12,4},... | collective-permute-start | bytes 2211848 | tf_op jit(solution)/shard_map/ppermute | solution.py:87
  122.8 2.4 %collective-permute-start.19 = (bf16[4,720,128]{2,1,0:T(8,128)(2,1)S(1)}, bf16[4,720,128]{2,1,0:T(8,128)(2,1)S(1)}, u32[]{:S(2)}, u32[]{:S(2)}) collective-permute-start(bf16[4,720,128]{2,1,0:T(8,128)(2,1)S(1)} %collective-permute-done.9), channel_id=1, source_target_pairs={{0,8},{8,0},{1,9},{9,1},{2,10},{10,2},{3,11},{11,3},{4,12},{12,4},... | collective-permute-start | bytes 2211848 | tf_op jit(solution)/shard_map/ppermute | solution.py:87
  126.6 3.3 %collective-permute-done.12 = bf16[2,720,128]{2,1,0:T(8,128)(2,1)S(1)} collective-permute-done((bf16[2,720,128]{2,1,0:T(8,128)(2,1)S(1)}, bf16[2,720,128]{2,1,0:T(8,128)(2,1)S(1)}, u32[]{:S(2)}, u32[]{:S(2)}) %collective-permute-start.12) | collective-permute-done | bytes 368672 | tf_op jit(solution)/shard_map/ppermute | solution.py:157
  130.0 0.8 copy-done.1
  130.9 0.8 copy-done.19
  133.4 2.3 %slice_bitcast_fusion.2 = (bf16[128,5120]{0,1:T(8,128)(2,1)S(1)}, bf16[1,128,5120]{1,2,0:T(8,128)(2,1)S(1)}, bf16[1,128,5120]{1,2,0:T(8,128)(2,1)S(1)}) fusion(bf16[2,128,5120]{1,2,0:T(8,128)(2,1)} %all-gather.2.cloned.1.call-done), kind=kLoop, calls=%fused_computation.180 | loop fusion | bytes 6553600 | tf_op jit(solution)/shard_map/squeeze | solution.py:130
  137.5 0.8 multiply_convert_fusion
  138.4 0.9 fusion.2
  139.3 0.9 fusion.1
  140.3 0.9 fusion
  141.2 1.7 convolution_bitcast_fusion.13
  154.0 0.8 fusion.13
  156.8 0.9 copy.71.q_ref
  161.8 13.4 %shard_map.149 = bf16[2,128,640]{2,1,0:T(8,128)(2,1)} custom-call(bf16[2,128,640]{2,1,0:T(8,128)(2,1)} %copy.71.q_ref, bf16[2,128,128]{2,1,0:T(8,128)(2,1)} %pad_maximum_fusion.5.ko_ref, bf16[2,128,128]{2,1,0:T(8,128)(2,1)} %add_convert_fusion.1.vo_ref, bf16[4096,128]{1,0:T(8,128)(2,1)} %constant_dynamic-update-slice_fusion.11.kc_ref, ...), custom_call_target="tpu_custom_call" | custom-call | flops 2768240640 | bytes 3407872 | tf_op jit(solution)/shard_map/pallas_call | solution.py:64
  175.2 1.7 slice_bitcast_fusion
  (230 shorter events, 35.4 us)
Async XLA Ops:
  7.2 20.1 %copy-start.34 = (bf16[640]{0:T(1024)(128)(2,1)S(1)}, bf16[640]{0:T(1024)(128)(2,1)}, u32[]{:S(2)}) copy-start(bf16[640]{0:T(1024)(128)(2,1)} %param.21) | copy-start | bytes 3844
  7.2 20.1 %copy-start.36 = (s32[1,64]{1,0:T(1,128)S(1)}, s32[1,64]{1,0:T(1,128)}, u32[]{:S(2)}) copy-start(s32[1,64]{1,0:T(1,128)} %param.18) | copy-start | bytes 772
  7.2 22.2 %copy-start.37 = (s32[128]{0:T(128)S(1)}, s32[128]{0:T(128)}, u32[]{:S(2)}) copy-start(s32[128]{0:T(128)} %param.16) | copy-start | bytes 1540
  7.2 126.2 %all-gather.2.cloned.1.call-start = ((), (), s32[]{:S(2)}) async-start(), calls=%async_computation | async-start | bytes 2949120 | tf_op jit(solution)/shard_map/all_gather | solution.py:129
  13.9 15.5 %collective-permute-start = (bf16[720,128]{1,0:T(8,128)(2,1)S(1)}, bf16[720,128]{1,0:T(8,128)(2,1)S(1)}, u32[]{:S(2)}, u32[]{:S(2)}) collective-permute-start(bf16[720,128]{1,0:T(8,128)(2,1)S(1)} %constant_dynamic-update-slice_fusion), channel_id=1, source_target_pairs={{0,384},{128,0},{256,128},{384,256},{1,385},{129,1},{257,129},{385... | collective-permute-start | bytes 552968 | tf_op jit(solution)/shard_map/ppermute | solution.py:87
  16.2 16.2 %collective-permute-start.1 = (bf16[720,128]{1,0:T(8,128)(2,1)S(1)}, bf16[720,128]{1,0:T(8,128)(2,1)S(1)}, u32[]{:S(2)}, u32[]{:S(2)}) collective-permute-start(bf16[720,128]{1,0:T(8,128)(2,1)S(1)} %constant_dynamic-update-slice_fusion), channel_id=1, source_target_pairs={{0,256},{128,384},{256,0},{384,128},{1,257},{129,385},{257,1},{385... | collective-permute-start | bytes 552968 | tf_op jit(solution)/shard_map/ppermute | solution.py:87
  21.6 14.3 %collective-permute-start.2 = (bf16[720,128]{1,0:T(8,128)(2,1)S(1)}, bf16[720,128]{1,0:T(8,128)(2,1)S(1)}, u32[]{:S(2)}, u32[]{:S(2)}) collective-permute-start(bf16[720,128]{1,0:T(8,128)(2,1)S(1)} %constant_dynamic-update-slice_fusion), channel_id=1, source_target_pairs={{0,128},{128,256},{256,384},{384,0},{1,129},{129,257},{257,385},{3... | collective-permute-start | bytes 552968 | tf_op jit(solution)/shard_map/ppermute | solution.py:87
  26.5 22.6 %copy-start.32 = (bf16[5120]{0:T(1024)(128)(2,1)S(1)}, bf16[5120]{0:T(1024)(128)(2,1)}, u32[]{:S(2)}) copy-start(bf16[5120]{0:T(1024)(128)(2,1)} %param.19) | copy-start | bytes 30724
  26.5 23.4 %copy-start.38 = (bf16[128]{0:T(256)(128)(2,1)S(1)}, bf16[128]{0:T(256)(128)(2,1)}, u32[]{:S(2)}) copy-start(bf16[128]{0:T(256)(128)(2,1)} %param.23) | copy-start | bytes 772
  26.5 24.8 %copy-start.39 = (bf16[128]{0:T(256)(128)(2,1)S(1)}, bf16[128]{0:T(256)(128)(2,1)}, u32[]{:S(2)}) copy-start(bf16[128]{0:T(256)(128)(2,1)} %param.25) | copy-start | bytes 772
  29.2 36.4 %copy-start.23 = (f32[128,64]{0,1:T(8,128)}, f32[128,64]{0,1:T(8,128)S(1)}, u32[]{:S(2)}) copy-start(f32[128,64]{0,1:T(8,128)S(1)} %get-tuple-element.70) | copy-start | bytes 98308
  35.9 35.7 %copy-start.21 = (bf16[720,128]{1,0:T(8,128)(2,1)}, bf16[720,128]{1,0:T(8,128)(2,1)S(1)}, u32[]{:S(2)}) copy-start(bf16[720,128]{1,0:T(8,128)(2,1)S(1)} %collective-permute-done.2) | copy-start | bytes 552964
  36.0 27.6 %collective-permute-start.3 = (bf16[4,720,128]{2,1,0:T(8,128)(2,1)S(1)}, bf16[4,720,128]{2,1,0:T(8,128)(2,1)S(1)}, u32[]{:S(2)}, u32[]{:S(2)}) collective-permute-start(bf16[4,720,128]{2,1,0:T(8,128)(2,1)S(1)} %pad_maximum_fusion), channel_id=1, source_target_pairs={{0,16},{16,32},{32,48},{48,64},{64,80},{80,96},{96,112},{112,0},{1... | collective-permute-start | bytes 2211848 | tf_op jit(solution)/shard_map/ppermute | solution.py:87
  40.5 25.1 %collective-permute-start.7 = (bf16[4,720,128]{2,1,0:T(8,128)(2,1)S(1)}, bf16[4,720,128]{2,1,0:T(8,128)(2,1)}, u32[]{:S(2)}, u32[]{:S(2)}) collective-permute-start(bf16[4,720,128]{2,1,0:T(8,128)(2,1)S(1)} %pad_maximum_fusion), channel_id=1, source_target_pairs={{0,112},{16,0},{32,16},{48,32},{64,48},{80,64},{96,80},{112,96},{1... | collective-permute-start | bytes 2211848 | tf_op jit(solution)/shard_map/ppermute | solution.py:87
  49.1 2.2 %copy-start.35 = (f32[1,4096]{1,0:T(1,128)}, f32[1,4096]{1,0:T(1,128)S(1)}, u32[]{:S(2)}) copy-start(f32[1,4096]{1,0:T(1,128)S(1)} %constant_dynamic-update-slice_fusion.43.bias_ref) | copy-start | bytes 49156
  51.3 26.0 %collective-permute-start.13 = (bf16[4,720,128]{2,1,0:T(8,128)(2,1)S(1)}, bf16[4,720,128]{2,1,0:T(8,128)(2,1)S(1)}, u32[]{:S(2)}, u32[]{:S(2)}) collective-permute-start(bf16[4,720,128]{2,1,0:T(8,128)(2,1)S(1)} %pad_maximum_fusion), channel_id=1, source_target_pairs={{0,8},{8,0},{1,9},{9,1},{2,10},{10,2},{3,11},{11,3},{4,12},{12,4},... | collective-permute-start | bytes 2211848 | tf_op jit(solution)/shard_map/ppermute | solution.py:87
  63.6 33.8 %copy-start.3 = (bf16[4,720,128]{2,1,0:T(8,128)(2,1)}, bf16[4,720,128]{2,1,0:T(8,128)(2,1)S(1)}, u32[]{:S(2)}) copy-start(bf16[4,720,128]{2,1,0:T(8,128)(2,1)S(1)} %collective-permute-done.3) | copy-start | bytes 2211844
  63.6 21.0 %collective-permute-start.4 = (bf16[4,720,128]{2,1,0:T(8,128)(2,1)S(1)}, bf16[4,720,128]{2,1,0:T(8,128)(2,1)S(1)}, u32[]{:S(2)}, u32[]{:S(2)}) collective-permute-start(bf16[4,720,128]{2,1,0:T(8,128)(2,1)S(1)} %collective-permute-done.3), channel_id=1, source_target_pairs={{0,16},{16,32},{32,48},{48,64},{64,80},{80,96},{96,112},{112,0},{1... | collective-permute-start | bytes 2211848 | tf_op jit(solution)/shard_map/ppermute | solution.py:87
  65.6 21.0 %collective-permute-start.8 = (bf16[4,720,128]{2,1,0:T(8,128)(2,1)}, bf16[4,720,128]{2,1,0:T(8,128)(2,1)S(1)}, u32[]{:S(2)}, u32[]{:S(2)}) collective-permute-start(bf16[4,720,128]{2,1,0:T(8,128)(2,1)} %collective-permute-done.7), channel_id=1, source_target_pairs={{0,112},{16,0},{32,16},{48,32},{64,48},{80,64},{96,80},{112,96},{1... | collective-permute-start | bytes 2211848 | tf_op jit(solution)/shard_map/ppermute | solution.py:87
  71.7 23.3 %collective-permute-start.14 = (bf16[4,720,128]{2,1,0:T(8,128)(2,1)S(1)}, bf16[4,720,128]{2,1,0:T(8,128)(2,1)S(1)}, u32[]{:S(2)}, u32[]{:S(2)}) collective-permute-start(bf16[4,720,128]{2,1,0:T(8,128)(2,1)S(1)} %collective-permute-done.3), channel_id=1, source_target_pairs={{0,8},{8,0},{1,9},{9,1},{2,10},{10,2},{3,11},{11,3},{4,12},{12,4},... | collective-permute-start | bytes 2211848 | tf_op jit(solution)/shard_map/ppermute | solution.py:87
  73.6 23.8 %collective-permute-start.15 = (bf16[4,720,128]{2,1,0:T(8,128)(2,1)}, bf16[4,720,128]{2,1,0:T(8,128)(2,1)S(1)}, u32[]{:S(2)}, u32[]{:S(2)}) collective-permute-start(bf16[4,720,128]{2,1,0:T(8,128)(2,1)} %collective-permute-done.7), channel_id=1, source_target_pairs={{0,8},{8,0},{1,9},{9,1},{2,10},{10,2},{3,11},{11,3},{4,12},{12,4},... | collective-permute-start | bytes 2211848 | tf_op jit(solution)/shard_map/ppermute | solution.py:87
  77.3 20.1 %copy-start.7 = (bf16[4,720,128]{2,1,0:T(8,128)(2,1)}, bf16[4,720,128]{2,1,0:T(8,128)(2,1)S(1)}, u32[]{:S(2)}) copy-start(bf16[4,720,128]{2,1,0:T(8,128)(2,1)S(1)} %collective-permute-done.13) | copy-start | bytes 2211844
  84.6 24.1 %copy-start.5 = (bf16[4,720,128]{2,1,0:T(8,128)(2,1)}, bf16[4,720,128]{2,1,0:T(8,128)(2,1)S(1)}, u32[]{:S(2)}) copy-start(bf16[4,720,128]{2,1,0:T(8,128)(2,1)S(1)} %collective-permute-done.4) | copy-start | bytes 2211844
  84.6 20.2 %collective-permute-start.5 = (bf16[4,720,128]{2,1,0:T(8,128)(2,1)S(1)}, bf16[4,720,128]{2,1,0:T(8,128)(2,1)S(1)}, u32[]{:S(2)}, u32[]{:S(2)}) collective-permute-start(bf16[4,720,128]{2,1,0:T(8,128)(2,1)S(1)} %collective-permute-done.4), channel_id=1, source_target_pairs={{0,16},{16,32},{32,48},{48,64},{64,80},{80,96},{96,112},{112,0},{1... | collective-permute-start | bytes 2211848 | tf_op jit(solution)/shard_map/ppermute | solution.py:87
  86.6 22.2 %copy-start.9 = (bf16[4,720,128]{2,1,0:T(8,128)(2,1)}, bf16[4,720,128]{2,1,0:T(8,128)(2,1)S(1)}, u32[]{:S(2)}) copy-start(bf16[4,720,128]{2,1,0:T(8,128)(2,1)S(1)} %collective-permute-done.8) | copy-start | bytes 2211844
  86.6 22.1 %collective-permute-start.9 = (bf16[4,720,128]{2,1,0:T(8,128)(2,1)S(1)}, bf16[4,720,128]{2,1,0:T(8,128)(2,1)S(1)}, u32[]{:S(2)}, u32[]{:S(2)}) collective-permute-start(bf16[4,720,128]{2,1,0:T(8,128)(2,1)S(1)} %collective-permute-done.8), channel_id=1, source_target_pairs={{0,112},{16,0},{32,16},{48,32},{64,48},{80,64},{96,80},{112,96},{1... | collective-permute-start | bytes 2211848 | tf_op jit(solution)/shard_map/ppermute | solution.py:87
  91.8 22.2 %collective-permute-start.16 = (bf16[4,720,128]{2,1,0:T(8,128)(2,1)S(1)}, bf16[4,720,128]{2,1,0:T(8,128)(2,1)S(1)}, u32[]{:S(2)}, u32[]{:S(2)}) collective-permute-start(bf16[4,720,128]{2,1,0:T(8,128)(2,1)S(1)} %collective-permute-done.4), channel_id=1, source_target_pairs={{0,8},{8,0},{1,9},{9,1},{2,10},{10,2},{3,11},{11,3},{4,12},{12,4},... | collective-permute-start | bytes 2211848 | tf_op jit(solution)/shard_map/ppermute | solution.py:87
  95.0 2.5 %copy-start.11 = (bf16[4,720,128]{2,1,0:T(8,128)(2,1)}, bf16[4,720,128]{2,1,0:T(8,128)(2,1)S(1)}, u32[]{:S(2)}) copy-start(bf16[4,720,128]{2,1,0:T(8,128)(2,1)S(1)} %collective-permute-done.14) | copy-start | bytes 2211844
  95.0 22.5 %collective-permute-start.17 = (bf16[4,720,128]{2,1,0:T(8,128)(2,1)S(1)}, bf16[4,720,128]{2,1,0:T(8,128)(2,1)S(1)}, u32[]{:S(2)}, u32[]{:S(2)}) collective-permute-start(bf16[4,720,128]{2,1,0:T(8,128)(2,1)S(1)} %collective-permute-done.8), channel_id=1, source_target_pairs={{0,8},{8,0},{1,9},{9,1},{2,10},{10,2},{3,11},{11,3},{4,12},{12,4},... | collective-permute-start | bytes 2211848 | tf_op jit(solution)/shard_map/ppermute | solution.py:87
  97.4 16.5 %copy-start.13 = (bf16[4,720,128]{2,1,0:T(8,128)(2,1)}, bf16[4,720,128]{2,1,0:T(8,128)(2,1)S(1)}, u32[]{:S(2)}) copy-start(bf16[4,720,128]{2,1,0:T(8,128)(2,1)S(1)} %collective-permute-done.15) | copy-start | bytes 2211844
  104.8 21.7 %collective-permute-start.6 = (bf16[2,720,128]{2,1,0:T(8,128)(2,1)S(1)}, bf16[2,720,128]{2,1,0:T(8,128)(2,1)S(1)}, u32[]{:S(2)}, u32[]{:S(2)}) collective-permute-start(bf16[2,720,128]{2,1,0:T(8,128)(2,1)S(1)} %slice.332), channel_id=1, source_target_pairs={{0,16},{16,32},{32,48},{48,64},{64,80},{80,96},{96,112},{112,0},{1... | collective-permute-start | bytes 1105928 | tf_op jit(solution)/shard_map/ppermute | solution.py:87
  106.7 19.8 %collective-permute-start.11 = (bf16[2,720,128]{2,1,0:T(8,128)(2,1)S(1)}, bf16[2,720,128]{2,1,0:T(8,128)(2,1)S(1)}, u32[]{:S(2)}, u32[]{:S(2)}) collective-permute-start(bf16[2,720,128]{2,1,0:T(8,128)(2,1)S(1)} %slice.332), channel_id=1, source_target_pairs={{120,0},{112,8},{8,16},{0,24},{24,32},{16,40},{40,48},{32,56},{56,... | collective-permute-start | bytes 1105928 | tf_op jit(solution)/shard_map/ppermute | solution.py:156
  108.7 14.1 %collective-permute-start.10 = (bf16[2,720,128]{2,1,0:T(8,128)(2,1)S(1)}, bf16[2,720,128]{2,1,0:T(8,128)(2,1)S(1)}, u32[]{:S(2)}, u32[]{:S(2)}) collective-permute-start(bf16[2,720,128]{2,1,0:T(8,128)(2,1)S(1)} %slice.333), channel_id=1, source_target_pairs={{0,112},{16,0},{32,16},{48,32},{64,48},{80,64},{96,80},{112,96},{1... | collective-permute-start | bytes 1105928 | tf_op jit(solution)/shard_map/ppermute | solution.py:87
  114.0 12.5 %copy-start.15 = (bf16[4,720,128]{2,1,0:T(8,128)(2,1)}, bf16[4,720,128]{2,1,0:T(8,128)(2,1)S(1)}, u32[]{:S(2)}) copy-start(bf16[4,720,128]{2,1,0:T(8,128)(2,1)S(1)} %collective-permute-done.16) | copy-start | bytes 2211844
  114.0 15.8 %collective-permute-start.12 = (bf16[2,720,128]{2,1,0:T(8,128)(2,1)S(1)}, bf16[2,720,128]{2,1,0:T(8,128)(2,1)S(1)}, u32[]{:S(2)}, u32[]{:S(2)}) collective-permute-start(bf16[2,720,128]{2,1,0:T(8,128)(2,1)S(1)} %slice.333), channel_id=1, source_target_pairs={{24,0},{16,8},{40,16},{32,24},{56,32},{48,40},{72,48},{64,56},{88,... | collective-permute-start | bytes 1105928 | tf_op jit(solution)/shard_map/ppermute | solution.py:157
  117.4 9.0 %copy-start.17 = (bf16[4,720,128]{2,1,0:T(8,128)(2,1)}, bf16[4,720,128]{2,1,0:T(8,128)(2,1)S(1)}, u32[]{:S(2)}) copy-start(bf16[4,720,128]{2,1,0:T(8,128)(2,1)S(1)} %collective-permute-done.17) | copy-start | bytes 2211844
  118.8 11.1 %collective-permute-start.18 = (bf16[4,720,128]{2,1,0:T(8,128)(2,1)S(1)}, bf16[4,720,128]{2,1,0:T(8,128)(2,1)S(1)}, u32[]{:S(2)}, u32[]{:S(2)}) collective-permute-start(bf16[4,720,128]{2,1,0:T(8,128)(2,1)S(1)} %collective-permute-done.5), channel_id=1, source_target_pairs={{0,8},{8,0},{1,9},{9,1},{2,10},{10,2},{3,11},{11,3},{4,12},{12,4},... | collective-permute-start | bytes 2211848 | tf_op jit(solution)/shard_map/ppermute | solution.py:87
  122.8 7.2 %collective-permute-start.19 = (bf16[4,720,128]{2,1,0:T(8,128)(2,1)S(1)}, bf16[4,720,128]{2,1,0:T(8,128)(2,1)S(1)}, u32[]{:S(2)}, u32[]{:S(2)}) collective-permute-start(bf16[4,720,128]{2,1,0:T(8,128)(2,1)S(1)} %collective-permute-done.9), channel_id=1, source_target_pairs={{0,8},{8,0},{1,9},{9,1},{2,10},{10,2},{3,11},{11,3},{4,12},{12,4},... | collective-permute-start | bytes 2211848 | tf_op jit(solution)/shard_map/ppermute | solution.py:87
  133.4 2.5 %copy-start = (bf16[2,128,5120]{1,2,0:T(8,128)(2,1)S(1)}, bf16[2,128,5120]{1,2,0:T(8,128)(2,1)}, u32[]{:S(2)}) copy-start(bf16[2,128,5120]{1,2,0:T(8,128)(2,1)} %all-gather.2.cloned.1.call-done) | copy-start | bytes 7864324
  141.2 1.7 copy-start.4
  145.1 1.2 copy-start.8
  146.8 1.2 copy-start.16
  148.5 1.2 copy-start.20
  156.6 1.7 copy-start.29
  156.6 2.4 %copy-start.28 = (bf16[4,64,128]{2,1,0:T(8,128)(2,1)S(1)}, bf16[4,64,128]{2,1,0:T(8,128)(2,1)}, u32[]{:S(2)}) copy-start(bf16[4,64,128]{2,1,0:T(8,128)(2,1)} %get-tuple-element.71) | copy-start | bytes 196612
  156.6 3.0 %copy-start.27 = (bf16[4,64,128]{2,1,0:T(8,128)(2,1)S(1)}, bf16[4,64,128]{2,1,0:T(8,128)(2,1)}, u32[]{:S(2)}) copy-start(bf16[4,64,128]{2,1,0:T(8,128)(2,1)} %get-tuple-element.16) | copy-start | bytes 196612
  156.7 3.5 %copy-start.25 = (f32[128,64]{1,0:T(8,128)S(1)}, f32[128,64]{1,0:T(8,128)}, u32[]{:S(2)}) copy-start(f32[128,64]{1,0:T(8,128)} %copy.68) | copy-start | bytes 98308
  156.7 3.5 %copy-start.26 = (f32[128,64]{1,0:T(8,128)S(1)}, f32[128,64]{1,0:T(8,128)}, u32[]{:S(2)}) copy-start(f32[128,64]{1,0:T(8,128)} %copy.69) | copy-start | bytes 98308
  (13 other events, 13.1 us)
Sparse Core Ops, SparseCore 0:
  26.6 90.0 all-gather.1

commit v11 on v10

--- a/solution.py
+++ b/solution.py
@@ -126,7 +126,10 @@
     me_core = lax.axis_index("core")
 
     mine = jnp.stack([embeds, given_embeds])
-    both = lax.all_gather(mine, "tp", axis=2, tiled=True)
+    me_yhi = lax.axis_index("yhi")
+    pair = jnp.roll(jnp.stack([mine, shifted(mine, "yhi", 2, 1)]), me_yhi, axis=0)
+    spread = lax.all_gather(pair, "x", axis=1, tiled=False)
+    both = jnp.transpose(spread, (2, 3, 0, 1, 4)).reshape(mine.shape[0], mine.shape[1], -1)
     first_rows, given_rows = both[0], both[1]
 
     revised = jnp.where(accept[:, None] == 1, given_rows, first_rows)
@@ -142,6 +145,8 @@
     far = n_z // 2
     split = n_ylo // 2
     for step in range(1, far):
+        if step == far - 1:
+            normed5, forward, backward = lax.optimization_barrier((normed5, forward, backward))
         forward = shifted(forward, "z", n_z, -1)
         backward = shifted(backward, "z", n_z, 1)
         arrived += [(-step, forward), (step, backward)]
@@ -158,7 +163,6 @@
         ],
         axis=0,
     )
-    normed5, far_own, far_other = lax.optimization_barrier((normed5, far_own, far_other))
     held = [(offset, 0, piece) for offset, piece in arrived]
     held += [(offset, 1, shifted(piece, "core", 2, 1)) for offset, piece in arrived]
     held += [(far, 0, far_own), (far, 1, far_other)]
@@ -210,27 +214,28 @@
 
 def solution(mesh):
     blk_size, tp_size = mesh.devices.shape
-    fine = Mesh(mesh.devices.reshape(4, blk_size // 8, 2, tp_size), ("ylo", "z", "core", "tp"))
+    fine = Mesh(mesh.devices.reshape(4, blk_size // 8, 2, 2, tp_size // 2), ("ylo", "z", "core", "yhi", "x"))
     rows = ("ylo", "z", "core")
+    cols = ("yhi", "x")
     return jax.shard_map(
         local,
         mesh=fine,
         in_specs=(
-            P(rows, "tp"),
-            P(rows, "tp"),
+            P(rows, cols),
+            P(rows, cols),
             P(rows),
             P(rows),
             P(rows, None),
             P(),
-            P(rows, "tp"),
-            P("tp"),
-            P(rows, "tp"),
-            P("tp"),
-            P(rows, "tp"),
-            P("tp"),
-            P(rows, "tp"),
-            P(rows, "tp"),
+            P(rows, cols),
+            P(cols),
+            P(rows, cols),
+            P(cols),
+            P(rows, cols),
+            P(cols),
+            P(rows, cols),
+            P(rows, cols),
         ),
-        out_specs=(P(rows, "tp"), P(rows, "tp")),
+        out_specs=(P(rows, cols), P(rows, cols)),
         check_vma=False,
     )

time: 186 us -> 212 us (1.14)
  the two profiles are of different devices: /device:TPU:22 before, /device:TPU:15 now
where the time goes in v11:
time: 212 us; the launch traced here: 211 us
  starting transfers between devices  73.2 us (35%)
  local copies, waits for them, and re-layouts  56.8 us (27%)
  waiting for transfers between devices  32.4 us (15%)
  between operations  15.9 us (8%)
  Pallas kernels  13.4 us (6%)
  other arithmetic  10.2 us (5%)
  matrix products  8.73 us (4%)
    ppermute x19, starting transfers between devices, shifted(): return lax.ppermute(x, axis, pairs)  67.3 us
    unnamed x151, local copies, waits for them, and re-layouts  38.7 us
    ppermute x19, waiting for transfers between devices, shifted(): return lax.ppermute(x, axis, pairs)  32.4 us
    pallas_call x1, Pallas kernels, attend(): pl.pallas_call(attend_kernel, grid=(passes,), in_specs=[pl.BlockSpec((Non...  13.4 us
    dot_general x16, matrix products, local(): jnp.einsum('rki,kjid->rjd', normed5[:, :, offset % n_z, core, :], piece.r...  8.73 us
    slice x3, local copies, waits for them, and re-layouts, local(): first_rows, given_rows = (both[0], both[1])  5.62 us
    slice x16, local copies, waits for them, and re-layouts, local(): piece[:, value_start:used, :].reshape(-1, HD)  4.42 us
  transfers between devices with their start and end apart: 22, of which 6 were waited for; matrix products, arithmetic and copies ran while one was open for 20% of the time, Pallas kernels for 0%

profile of v11, /device:TPU:15, one launch (start us, length us, event | category | flops | bytes accessed | tf_op | source)
XLA Modules:
  0.0 210.5 jit_solution(10010719348992431839)
XLA Ops:
  8.0 0.7 constant_dynamic-update-slice_fusion.9
  8.7 0.7 constant_dynamic-update-slice_fusion.8
  9.4 0.7 constant_dynamic-update-slice_fusion.7
  10.2 0.7 constant_dynamic-update-slice_fusion.6
  10.9 0.7 constant_dynamic-update-slice_fusion.5
  11.6 0.7 constant_dynamic-update-slice_fusion.4
  13.9 2.1 collective-permute-start.1
  15.9 4.2 %collective-permute-start.2 = (bf16[720,128]{1,0:T(8,128)(2,1)S(1)}, bf16[720,128]{1,0:T(8,128)(2,1)S(1)}, u32[]{:S(2)}, u32[]{:S(2)}) collective-permute-start(bf16[720,128]{1,0:T(8,128)(2,1)S(1)} %constant_dynamic-update-slice_fusion), channel_id=1, source_target_pairs={{0,256},{128,384},{256,0},{384,128},{1,257},{129,385},{257,1},{385... | collective-permute-start | bytes 552968 | tf_op jit(solution)/shard_map/ppermute | solution.py:87
  20.1 4.1 %collective-permute-start.3 = (bf16[720,128]{1,0:T(8,128)(2,1)S(1)}, bf16[720,128]{1,0:T(8,128)(2,1)S(1)}, u32[]{:S(2)}, u32[]{:S(2)}) collective-permute-start(bf16[720,128]{1,0:T(8,128)(2,1)S(1)} %constant_dynamic-update-slice_fusion), channel_id=1, source_target_pairs={{0,128},{128,256},{256,384},{384,0},{1,129},{129,257},{257,385},{3... | collective-permute-start | bytes 552968 | tf_op jit(solution)/shard_map/ppermute | solution.py:87
  24.3 1.1 pad_maximum_fusion.1
  25.3 4.8 %collective-permute-start = (bf16[2,128,640]{2,1,0:T(8,128)(2,1)S(1)}, bf16[2,128,640]{2,1,0:T(8,128)(2,1)S(1)}, u32[]{:S(2)}, u32[]{:S(2)}) collective-permute-start(bf16[2,128,640]{2,1,0:T(8,128)(2,1)S(1)} %get-tuple-element.50), channel_id=1, source_target_pairs={{0,4},{4,0},{1,5},{5,1},{2,6},{6,2},{3,7},{7,3},{8,12},{12,8},{9,1... | collective-permute-start | bytes 983048 | tf_op jit(solution)/shard_map/ppermute | solution.py:87
  39.4 12.9 %collective-permute-done = bf16[2,128,640]{2,1,0:T(8,128)(2,1)S(1)} collective-permute-done((bf16[2,128,640]{2,1,0:T(8,128)(2,1)S(1)}, bf16[2,128,640]{2,1,0:T(8,128)(2,1)S(1)}, u32[]{:S(2)}, u32[]{:S(2)}) %collective-permute-start) | collective-permute-done | bytes 327712 | tf_op jit(solution)/shard_map/ppermute | solution.py:87
  52.4 1.4 fusion.27
  55.2 4.0 %collective-permute-start.4 = (bf16[4,720,128]{2,1,0:T(8,128)(2,1)S(1)}, bf16[4,720,128]{2,1,0:T(8,128)(2,1)S(1)}, u32[]{:S(2)}, u32[]{:S(2)}) collective-permute-start(bf16[4,720,128]{2,1,0:T(8,128)(2,1)S(1)} %pad_maximum_fusion), channel_id=1, source_target_pairs={{0,16},{16,32},{32,48},{48,64},{64,80},{80,96},{96,112},{112,0},{1... | collective-permute-start | bytes 2211848 | tf_op jit(solution)/shard_map/ppermute | solution.py:87
  60.5 8.6 %collective-permute-start.6 = (bf16[4,720,128]{2,1,0:T(8,128)(2,1)S(1)}, bf16[4,720,128]{2,1,0:T(8,128)(2,1)S(1)}, u32[]{:S(2)}, u32[]{:S(2)}) collective-permute-start(bf16[4,720,128]{2,1,0:T(8,128)(2,1)S(1)} %pad_maximum_fusion), channel_id=1, source_target_pairs={{0,112},{16,0},{32,16},{48,32},{64,48},{80,64},{96,80},{112,96},{1... | collective-permute-start | bytes 2211848 | tf_op jit(solution)/shard_map/ppermute | solution.py:87
  72.5 2.7 %collective-permute-start.10 = (bf16[4,720,128]{2,1,0:T(8,128)(2,1)S(1)}, bf16[4,720,128]{2,1,0:T(8,128)(2,1)S(1)}, u32[]{:S(2)}, u32[]{:S(2)}) collective-permute-start(bf16[4,720,128]{2,1,0:T(8,128)(2,1)S(1)} %pad_maximum_fusion), channel_id=1, source_target_pairs={{0,8},{8,0},{1,9},{9,1},{2,10},{10,2},{3,11},{11,3},{4,12},{12,4},... | collective-permute-start | bytes 2211848 | tf_op jit(solution)/shard_map/ppermute | solution.py:87
  76.4 6.0 %collective-permute-done.4 = bf16[4,720,128]{2,1,0:T(8,128)(2,1)S(1)} collective-permute-done((bf16[4,720,128]{2,1,0:T(8,128)(2,1)S(1)}, bf16[4,720,128]{2,1,0:T(8,128)(2,1)S(1)}, u32[]{:S(2)}, u32[]{:S(2)}) %collective-permute-start.4) | collective-permute-done | bytes 737312 | tf_op jit(solution)/shard_map/ppermute | solution.py:87
  82.4 1.9 collective-permute-start.5
  84.5 5.4 %collective-permute-start.7 = (bf16[4,720,128]{2,1,0:T(8,128)(2,1)S(1)}, bf16[4,720,128]{2,1,0:T(8,128)(2,1)S(1)}, u32[]{:S(2)}, u32[]{:S(2)}) collective-permute-start(bf16[4,720,128]{2,1,0:T(8,128)(2,1)S(1)} %collective-permute-done.6), channel_id=1, source_target_pairs={{0,112},{16,0},{32,16},{48,32},{64,48},{80,64},{96,80},{112,96},{1... | collective-permute-start | bytes 2211848 | tf_op jit(solution)/shard_map/ppermute | solution.py:87
  91.2 3.4 %collective-permute-start.11 = (bf16[4,720,128]{2,1,0:T(8,128)(2,1)S(1)}, bf16[4,720,128]{2,1,0:T(8,128)(2,1)S(1)}, u32[]{:S(2)}, u32[]{:S(2)}) collective-permute-start(bf16[4,720,128]{2,1,0:T(8,128)(2,1)S(1)} %collective-permute-done.4), channel_id=1, source_target_pairs={{0,8},{8,0},{1,9},{9,1},{2,10},{10,2},{3,11},{11,3},{4,12},{12,4},... | collective-permute-start | bytes 2211848 | tf_op jit(solution)/shard_map/ppermute | solution.py:87
  94.6 1.9 collective-permute-start.12
  98.5 4.1 %collective-permute-done.5 = bf16[4,720,128]{2,1,0:T(8,128)(2,1)S(1)} collective-permute-done((bf16[4,720,128]{2,1,0:T(8,128)(2,1)S(1)}, bf16[4,720,128]{2,1,0:T(8,128)(2,1)S(1)}, u32[]{:S(2)}, u32[]{:S(2)}) %collective-permute-start.5) | collective-permute-done | bytes 737312 | tf_op jit(solution)/shard_map/ppermute | solution.py:87
  102.6 3.7 %collective-permute-start.13 = (bf16[4,720,128]{2,1,0:T(8,128)(2,1)S(1)}, bf16[4,720,128]{2,1,0:T(8,128)(2,1)S(1)}, u32[]{:S(2)}, u32[]{:S(2)}) collective-permute-start(bf16[4,720,128]{2,1,0:T(8,128)(2,1)S(1)} %collective-permute-done.5), channel_id=1, source_target_pairs={{0,8},{8,0},{1,9},{9,1},{2,10},{10,2},{3,11},{11,3},{4,12},{12,4},... | collective-permute-start | bytes 2211848 | tf_op jit(solution)/shard_map/ppermute | solution.py:87
  107.7 2.1 collective-permute-start.14
  113.1 0.9 copy-done.14
  114.7 3.1 %fusion.69 = (bf16[1,128,2,4,640]{4,1,0,3,2:T(8,128)(2,1)S(1)}, bf16[1,128,2,4,640]{4,1,0,3,2:T(8,128)(2,1)}) fusion(bf16[2,128,2,4,640]{4,1,0,3,2:T(8,128)(2,1)} %bitcast.355), kind=kLoop, calls=%fused_computation.190 | loop fusion | bytes 5242880 | tf_op jit(solution)/shard_map/slice | solution.py:133
  117.8 0.8 copy.70
  118.6 1.8 copy.71
  120.7 0.7 multiply_reduce_fusion
  122.2 0.8 multiply_convert_fusion
  123.0 0.9 fusion.2
  124.0 0.9 fusion.1
  124.9 0.9 fusion
  126.0 2.0 collective-permute-start.8
  128.1 5.5 %collective-permute-start.9 = (bf16[4,720,128]{2,1,0:T(8,128)(2,1)S(1)}, bf16[4,720,128]{2,1,0:T(8,128)(2,1)S(1)}, u32[]{:S(2)}, u32[]{:S(2)}) collective-permute-start(bf16[4,720,128]{2,1,0:T(8,128)(2,1)S(1)} %copy-done.9), channel_id=1, source_target_pairs={{0,112},{16,0},{32,16},{48,32},{64,48},{80,64},{96,80},{112,96},{1... | collective-permute-start | bytes 2211848 | tf_op jit(solution)/shard_map/ppermute | solution.py:87
  139.5 8.8 %collective-permute-done.8 = bf16[4,720,128]{2,1,0:T(8,128)(2,1)S(1)} collective-permute-done((bf16[4,720,128]{2,1,0:T(8,128)(2,1)S(1)}, bf16[4,720,128]{2,1,0:T(8,128)(2,1)S(1)}, u32[]{:S(2)}, u32[]{:S(2)}) %collective-permute-start.8) | collective-permute-done | bytes 737312 | tf_op jit(solution)/shard_map/ppermute | solution.py:87
  148.3 1.9 collective-permute-start.17
  150.3 2.4 %collective-permute-start.19 = (bf16[2,720,128]{2,1,0:T(8,128)(2,1)S(1)}, bf16[2,720,128]{2,1,0:T(8,128)(2,1)S(1)}, u32[]{:S(2)}, u32[]{:S(2)}) collective-permute-start(bf16[2,720,128]{2,1,0:T(8,128)(2,1)S(1)} %slice.334), channel_id=1, source_target_pairs={{120,0},{112,8},{8,16},{0,24},{24,32},{16,40},{40,48},{32,56},{56,... | collective-permute-start | bytes 1105928 | tf_op jit(solution)/shard_map/ppermute | solution.py:161
  152.7 4.6 %collective-permute-start.18 = (bf16[2,720,128]{2,1,0:T(8,128)(2,1)S(1)}, bf16[2,720,128]{2,1,0:T(8,128)(2,1)S(1)}, u32[]{:S(2)}, u32[]{:S(2)}) collective-permute-start(bf16[2,720,128]{2,1,0:T(8,128)(2,1)S(1)} %slice.335), channel_id=1, source_target_pairs={{0,112},{16,0},{32,16},{48,32},{64,48},{80,64},{96,80},{112,96},{1... | collective-permute-start | bytes 1105928 | tf_op jit(solution)/shard_map/ppermute | solution.py:87
  157.3 3.4 %collective-permute-start.20 = (bf16[2,720,128]{2,1,0:T(8,128)(2,1)S(1)}, bf16[2,720,128]{2,1,0:T(8,128)(2,1)S(1)}, u32[]{:S(2)}, u32[]{:S(2)}) collective-permute-start(bf16[2,720,128]{2,1,0:T(8,128)(2,1)S(1)} %slice.335), channel_id=1, source_target_pairs={{24,0},{16,8},{40,16},{32,24},{56,32},{48,40},{72,48},{64,56},{88,... | collective-permute-start | bytes 1105928 | tf_op jit(solution)/shard_map/ppermute | solution.py:162
  168.1 0.8 fusion.11
  170.8 2.5 %collective-permute-start.15 = (bf16[4,720,128]{2,1,0:T(8,128)(2,1)S(1)}, bf16[4,720,128]{2,1,0:T(8,128)(2,1)S(1)}, u32[]{:S(2)}, u32[]{:S(2)}) collective-permute-start(bf16[4,720,128]{2,1,0:T(8,128)(2,1)S(1)} %collective-permute-done.8), channel_id=1, source_target_pairs={{0,8},{8,0},{1,9},{9,1},{2,10},{10,2},{3,11},{11,3},{4,12},{12,4},... | collective-permute-start | bytes 2211848 | tf_op jit(solution)/shard_map/ppermute | solution.py:87
  174.0 1.9 collective-permute-start.16
  178.9 0.8 fusion.17
  180.8 0.9 copy.97.q_ref
  182.3 0.9 fusion.74
  188.5 13.4 %shard_map.149 = bf16[2,128,640]{2,1,0:T(8,128)(2,1)} custom-call(bf16[2,128,640]{2,1,0:T(8,128)(2,1)} %copy.97.q_ref, bf16[2,128,128]{2,1,0:T(8,128)(2,1)} %pad_maximum_fusion.3.ko_ref, bf16[2,128,128]{2,1,0:T(8,128)(2,1)} %add_convert_fusion.1.vo_ref, bf16[4096,128]{1,0:T(8,128)(2,1)} %get-tuple-element.72.kc_ref, ...), custom_call_target="tpu_custom_call" | custom-call | flops 2768240640 | bytes 3407872 | tf_op jit(solution)/shard_map/pallas_call | solution.py:64
  201.9 1.7 slice_bitcast_fusion
  (249 shorter events, 53.3 us)
Async XLA Ops:
  7.2 23.0 %copy-start.43 = (s32[128]{0:T(128)S(1)}, s32[128]{0:T(128)}, u32[]{:S(2)}) copy-start(s32[128]{0:T(128)} %param.16) | copy-start | bytes 1540
  7.2 23.7 %copy-start.41 = (bf16[640]{0:T(1024)(128)(2,1)S(1)}, bf16[640]{0:T(1024)(128)(2,1)}, u32[]{:S(2)}) copy-start(bf16[640]{0:T(1024)(128)(2,1)} %param.21) | copy-start | bytes 3844
  7.2 23.7 %copy-start.44 = (s32[1,64]{1,0:T(1,128)S(1)}, s32[1,64]{1,0:T(1,128)}, u32[]{:S(2)}) copy-start(s32[1,64]{1,0:T(1,128)} %param.18) | copy-start | bytes 772
  7.2 107.5 %all-gather.3.cloned.1.call-start = ((), (), s32[]{:S(2)}) async-start(), calls=%async_computation | async-start | bytes 3276800 | tf_op jit(solution)/shard_map/all_gather | solution.py:131
  13.9 40.5 %collective-permute-start.1 = (bf16[720,128]{1,0:T(8,128)(2,1)S(1)}, bf16[720,128]{1,0:T(8,128)(2,1)S(1)}, u32[]{:S(2)}, u32[]{:S(2)}) collective-permute-start(bf16[720,128]{1,0:T(8,128)(2,1)S(1)} %constant_dynamic-update-slice_fusion), channel_id=1, source_target_pairs={{0,384},{128,0},{256,128},{384,256},{1,385},{129,1},{257,129},{385... | collective-permute-start | bytes 552968 | tf_op jit(solution)/shard_map/ppermute | solution.py:87
  15.9 38.5 %collective-permute-start.2 = (bf16[720,128]{1,0:T(8,128)(2,1)S(1)}, bf16[720,128]{1,0:T(8,128)(2,1)S(1)}, u32[]{:S(2)}, u32[]{:S(2)}) collective-permute-start(bf16[720,128]{1,0:T(8,128)(2,1)S(1)} %constant_dynamic-update-slice_fusion), channel_id=1, source_target_pairs={{0,256},{128,384},{256,0},{384,128},{1,257},{129,385},{257,1},{385... | collective-permute-start | bytes 552968 | tf_op jit(solution)/shard_map/ppermute | solution.py:87
  20.1 34.2 %collective-permute-start.3 = (bf16[720,128]{1,0:T(8,128)(2,1)S(1)}, bf16[720,128]{1,0:T(8,128)(2,1)S(1)}, u32[]{:S(2)}, u32[]{:S(2)}) collective-permute-start(bf16[720,128]{1,0:T(8,128)(2,1)S(1)} %constant_dynamic-update-slice_fusion), channel_id=1, source_target_pairs={{0,128},{128,256},{256,384},{384,0},{1,129},{129,257},{257,385},{3... | collective-permute-start | bytes 552968 | tf_op jit(solution)/shard_map/ppermute | solution.py:87
  25.3 27.1 %collective-permute-start = (bf16[2,128,640]{2,1,0:T(8,128)(2,1)S(1)}, bf16[2,128,640]{2,1,0:T(8,128)(2,1)S(1)}, u32[]{:S(2)}, u32[]{:S(2)}) collective-permute-start(bf16[2,128,640]{2,1,0:T(8,128)(2,1)S(1)} %get-tuple-element.50), channel_id=1, source_target_pairs={{0,4},{4,0},{1,5},{5,1},{2,6},{6,2},{3,7},{7,3},{8,12},{12,8},{9,1... | collective-permute-start | bytes 983048 | tf_op jit(solution)/shard_map/ppermute | solution.py:87
  39.4 31.6 %copy-start.23 = (f32[128,64]{0,1:T(8,128)}, f32[128,64]{0,1:T(8,128)S(1)}, u32[]{:S(2)}) copy-start(f32[128,64]{0,1:T(8,128)S(1)} %get-tuple-element.70) | copy-start | bytes 98308
  39.4 32.3 %copy-start.25 = (f32[128,64]{0,1:T(8,128)}, f32[128,64]{0,1:T(8,128)S(1)}, u32[]{:S(2)}) copy-start(f32[128,64]{0,1:T(8,128)S(1)} %get-tuple-element.71) | copy-start | bytes 98308
  53.7 16.0 %copy-start.40 = (bf16[5120]{0:T(1024)(128)(2,1)S(1)}, bf16[5120]{0:T(1024)(128)(2,1)}, u32[]{:S(2)}) copy-start(bf16[5120]{0:T(1024)(128)(2,1)} %param.19) | copy-start | bytes 30724
  53.7 16.7 %copy-start.45 = (bf16[128]{0:T(256)(128)(2,1)S(1)}, bf16[128]{0:T(256)(128)(2,1)}, u32[]{:S(2)}) copy-start(bf16[128]{0:T(256)(128)(2,1)} %param.23) | copy-start | bytes 772
  53.7 18.7 %copy-start.46 = (bf16[128]{0:T(256)(128)(2,1)S(1)}, bf16[128]{0:T(256)(128)(2,1)}, u32[]{:S(2)}) copy-start(bf16[128]{0:T(256)(128)(2,1)} %param.25) | copy-start | bytes 772
  54.4 35.5 %copy-start.17 = (bf16[720,128]{1,0:T(8,128)(2,1)}, bf16[720,128]{1,0:T(8,128)(2,1)S(1)}, u32[]{:S(2)}) copy-start(bf16[720,128]{1,0:T(8,128)(2,1)S(1)} %collective-permute-done.1) | copy-start | bytes 552964
  54.4 35.5 %copy-start.19 = (bf16[720,128]{1,0:T(8,128)(2,1)}, bf16[720,128]{1,0:T(8,128)(2,1)S(1)}, u32[]{:S(2)}) copy-start(bf16[720,128]{1,0:T(8,128)(2,1)S(1)} %collective-permute-done.2) | copy-start | bytes 552964
  55.2 27.2 %collective-permute-start.4 = (bf16[4,720,128]{2,1,0:T(8,128)(2,1)S(1)}, bf16[4,720,128]{2,1,0:T(8,128)(2,1)S(1)}, u32[]{:S(2)}, u32[]{:S(2)}) collective-permute-start(bf16[4,720,128]{2,1,0:T(8,128)(2,1)S(1)} %pad_maximum_fusion), channel_id=1, source_target_pairs={{0,16},{16,32},{32,48},{48,64},{64,80},{80,96},{96,112},{112,0},{1... | collective-permute-start | bytes 2211848 | tf_op jit(solution)/shard_map/ppermute | solution.py:87
  60.5 23.9 %collective-permute-start.6 = (bf16[4,720,128]{2,1,0:T(8,128)(2,1)S(1)}, bf16[4,720,128]{2,1,0:T(8,128)(2,1)S(1)}, u32[]{:S(2)}, u32[]{:S(2)}) collective-permute-start(bf16[4,720,128]{2,1,0:T(8,128)(2,1)S(1)} %pad_maximum_fusion), channel_id=1, source_target_pairs={{0,112},{16,0},{32,16},{48,32},{64,48},{80,64},{96,80},{112,96},{1... | collective-permute-start | bytes 2211848 | tf_op jit(solution)/shard_map/ppermute | solution.py:87
  72.5 25.3 %collective-permute-start.10 = (bf16[4,720,128]{2,1,0:T(8,128)(2,1)S(1)}, bf16[4,720,128]{2,1,0:T(8,128)(2,1)S(1)}, u32[]{:S(2)}, u32[]{:S(2)}) collective-permute-start(bf16[4,720,128]{2,1,0:T(8,128)(2,1)S(1)} %pad_maximum_fusion), channel_id=1, source_target_pairs={{0,8},{8,0},{1,9},{9,1},{2,10},{10,2},{3,11},{11,3},{4,12},{12,4},... | collective-permute-start | bytes 2211848 | tf_op jit(solution)/shard_map/ppermute | solution.py:87
  82.4 29.3 %copy-start.2 = (bf16[4,720,128]{2,1,0:T(8,128)(2,1)}, bf16[4,720,128]{2,1,0:T(8,128)(2,1)S(1)}, u32[]{:S(2)}) copy-start(bf16[4,720,128]{2,1,0:T(8,128)(2,1)S(1)} %collective-permute-done.4) | copy-start | bytes 2211844
  82.4 20.2 %collective-permute-start.5 = (bf16[4,720,128]{2,1,0:T(8,128)(2,1)S(1)}, bf16[4,720,128]{2,1,0:T(8,128)(2,1)S(1)}, u32[]{:S(2)}, u32[]{:S(2)}) collective-permute-start(bf16[4,720,128]{2,1,0:T(8,128)(2,1)S(1)} %collective-permute-done.4), channel_id=1, source_target_pairs={{0,16},{16,32},{32,48},{48,64},{64,80},{80,96},{96,112},{112,0},{1... | collective-permute-start | bytes 2211848 | tf_op jit(solution)/shard_map/ppermute | solution.py:87
  84.5 28.0 %copy-start.4 = (bf16[4,720,128]{2,1,0:T(8,128)(2,1)}, bf16[4,720,128]{2,1,0:T(8,128)(2,1)S(1)}, u32[]{:S(2)}) copy-start(bf16[4,720,128]{2,1,0:T(8,128)(2,1)S(1)} %collective-permute-done.6) | copy-start | bytes 2211844
  84.5 21.9 %collective-permute-start.7 = (bf16[4,720,128]{2,1,0:T(8,128)(2,1)S(1)}, bf16[4,720,128]{2,1,0:T(8,128)(2,1)S(1)}, u32[]{:S(2)}, u32[]{:S(2)}) collective-permute-start(bf16[4,720,128]{2,1,0:T(8,128)(2,1)S(1)} %collective-permute-done.6), channel_id=1, source_target_pairs={{0,112},{16,0},{32,16},{48,32},{64,48},{80,64},{96,80},{112,96},{1... | collective-permute-start | bytes 2211848 | tf_op jit(solution)/shard_map/ppermute | solution.py:87
  91.2 19.8 %collective-permute-start.11 = (bf16[4,720,128]{2,1,0:T(8,128)(2,1)S(1)}, bf16[4,720,128]{2,1,0:T(8,128)(2,1)S(1)}, u32[]{:S(2)}, u32[]{:S(2)}) collective-permute-start(bf16[4,720,128]{2,1,0:T(8,128)(2,1)S(1)} %collective-permute-done.4), channel_id=1, source_target_pairs={{0,8},{8,0},{1,9},{9,1},{2,10},{10,2},{3,11},{11,3},{4,12},{12,4},... | collective-permute-start | bytes 2211848 | tf_op jit(solution)/shard_map/ppermute | solution.py:87
  94.6 17.2 %collective-permute-start.12 = (bf16[4,720,128]{2,1,0:T(8,128)(2,1)S(1)}, bf16[4,720,128]{2,1,0:T(8,128)(2,1)S(1)}, u32[]{:S(2)}, u32[]{:S(2)}) collective-permute-start(bf16[4,720,128]{2,1,0:T(8,128)(2,1)S(1)} %collective-permute-done.6), channel_id=1, source_target_pairs={{0,8},{8,0},{1,9},{9,1},{2,10},{10,2},{3,11},{11,3},{4,12},{12,4},... | collective-permute-start | bytes 2211848 | tf_op jit(solution)/shard_map/ppermute | solution.py:87
  97.8 15.3 %copy-start.6 = (bf16[4,720,128]{2,1,0:T(8,128)(2,1)}, bf16[4,720,128]{2,1,0:T(8,128)(2,1)S(1)}, u32[]{:S(2)}) copy-start(bf16[4,720,128]{2,1,0:T(8,128)(2,1)S(1)} %collective-permute-done.10) | copy-start | bytes 2211844
  102.6 9.8 %copy-start = (bf16[4,720,128]{2,1,0:T(8,128)(2,1)}, bf16[4,720,128]{2,1,0:T(8,128)(2,1)S(1)}, u32[]{:S(2)}) copy-start(bf16[4,720,128]{2,1,0:T(8,128)(2,1)S(1)} %collective-permute-done.5) | copy-start | bytes 2211844
  102.6 9.8 %collective-permute-start.13 = (bf16[4,720,128]{2,1,0:T(8,128)(2,1)S(1)}, bf16[4,720,128]{2,1,0:T(8,128)(2,1)S(1)}, u32[]{:S(2)}, u32[]{:S(2)}) collective-permute-start(bf16[4,720,128]{2,1,0:T(8,128)(2,1)S(1)} %collective-permute-done.5), channel_id=1, source_target_pairs={{0,8},{8,0},{1,9},{9,1},{2,10},{10,2},{3,11},{11,3},{4,12},{12,4},... | collective-permute-start | bytes 2211848 | tf_op jit(solution)/shard_map/ppermute | solution.py:87
  106.4 8.4 %copy-start.8 = (bf16[4,720,128]{2,1,0:T(8,128)(2,1)}, bf16[4,720,128]{2,1,0:T(8,128)(2,1)S(1)}, u32[]{:S(2)}) copy-start(bf16[4,720,128]{2,1,0:T(8,128)(2,1)S(1)} %collective-permute-done.7) | copy-start | bytes 2211844
  107.7 5.4 %collective-permute-start.14 = (bf16[4,720,128]{2,1,0:T(8,128)(2,1)S(1)}, bf16[4,720,128]{2,1,0:T(8,128)(2,1)S(1)}, u32[]{:S(2)}, u32[]{:S(2)}) collective-permute-start(bf16[4,720,128]{2,1,0:T(8,128)(2,1)S(1)} %collective-permute-done.7), channel_id=1, source_target_pairs={{0,8},{8,0},{1,9},{9,1},{2,10},{10,2},{3,11},{11,3},{4,12},{12,4},... | collective-permute-start | bytes 2211848 | tf_op jit(solution)/shard_map/ppermute | solution.py:87
  124.9 3.2 %copy-start.9 = (bf16[4,720,128]{2,1,0:T(8,128)(2,1)S(1)}, bf16[4,720,128]{2,1,0:T(8,128)(2,1)}, u32[]{:S(2)}) copy-start(bf16[4,720,128]{2,1,0:T(8,128)(2,1)} %copy-done.8) | copy-start | bytes 2211844
  124.9 8.7 %copy-start.5 = (bf16[4,720,128]{2,1,0:T(8,128)(2,1)S(1)}, bf16[4,720,128]{2,1,0:T(8,128)(2,1)}, u32[]{:S(2)}) copy-start(bf16[4,720,128]{2,1,0:T(8,128)(2,1)} %copy-done.4) | copy-start | bytes 2211844
  126.0 8.1 %copy-start.3 = (bf16[4,720,128]{2,1,0:T(8,128)(2,1)S(1)}, bf16[4,720,128]{2,1,0:T(8,128)(2,1)}, u32[]{:S(2)}) copy-start(bf16[4,720,128]{2,1,0:T(8,128)(2,1)} %copy-done.2) | copy-start | bytes 2211844
  126.0 22.3 %collective-permute-start.8 = (bf16[4,720,128]{2,1,0:T(8,128)(2,1)S(1)}, bf16[4,720,128]{2,1,0:T(8,128)(2,1)S(1)}, u32[]{:S(2)}, u32[]{:S(2)}) collective-permute-start(bf16[4,720,128]{2,1,0:T(8,128)(2,1)S(1)} %copy-done.1), channel_id=1, source_target_pairs={{0,16},{16,32},{32,48},{48,64},{64,80},{80,96},{96,112},{112,0},{1... | collective-permute-start | bytes 2211848 | tf_op jit(solution)/shard_map/ppermute | solution.py:87
  128.1 24.6 %collective-permute-start.9 = (bf16[4,720,128]{2,1,0:T(8,128)(2,1)S(1)}, bf16[4,720,128]{2,1,0:T(8,128)(2,1)S(1)}, u32[]{:S(2)}, u32[]{:S(2)}) collective-permute-start(bf16[4,720,128]{2,1,0:T(8,128)(2,1)S(1)} %copy-done.9), channel_id=1, source_target_pairs={{0,112},{16,0},{32,16},{48,32},{64,48},{80,64},{96,80},{112,96},{1... | collective-permute-start | bytes 2211848 | tf_op jit(solution)/shard_map/ppermute | solution.py:87
  148.3 25.6 %collective-permute-start.17 = (bf16[2,720,128]{2,1,0:T(8,128)(2,1)S(1)}, bf16[2,720,128]{2,1,0:T(8,128)(2,1)S(1)}, u32[]{:S(2)}, u32[]{:S(2)}) collective-permute-start(bf16[2,720,128]{2,1,0:T(8,128)(2,1)S(1)} %slice.334), channel_id=1, source_target_pairs={{0,16},{16,32},{32,48},{48,64},{64,80},{80,96},{96,112},{112,0},{1... | collective-permute-start | bytes 1105928 | tf_op jit(solution)/shard_map/ppermute | solution.py:87
  150.3 25.6 %collective-permute-start.19 = (bf16[2,720,128]{2,1,0:T(8,128)(2,1)S(1)}, bf16[2,720,128]{2,1,0:T(8,128)(2,1)S(1)}, u32[]{:S(2)}, u32[]{:S(2)}) collective-permute-start(bf16[2,720,128]{2,1,0:T(8,128)(2,1)S(1)} %slice.334), channel_id=1, source_target_pairs={{120,0},{112,8},{8,16},{0,24},{24,32},{16,40},{40,48},{32,56},{56,... | collective-permute-start | bytes 1105928 | tf_op jit(solution)/shard_map/ppermute | solution.py:161
  152.7 23.2 %collective-permute-start.18 = (bf16[2,720,128]{2,1,0:T(8,128)(2,1)S(1)}, bf16[2,720,128]{2,1,0:T(8,128)(2,1)S(1)}, u32[]{:S(2)}, u32[]{:S(2)}) collective-permute-start(bf16[2,720,128]{2,1,0:T(8,128)(2,1)S(1)} %slice.335), channel_id=1, source_target_pairs={{0,112},{16,0},{32,16},{48,32},{64,48},{80,64},{96,80},{112,96},{1... | collective-permute-start | bytes 1105928 | tf_op jit(solution)/shard_map/ppermute | solution.py:87
  157.3 19.2 %collective-permute-start.20 = (bf16[2,720,128]{2,1,0:T(8,128)(2,1)S(1)}, bf16[2,720,128]{2,1,0:T(8,128)(2,1)S(1)}, u32[]{:S(2)}, u32[]{:S(2)}) collective-permute-start(bf16[2,720,128]{2,1,0:T(8,128)(2,1)S(1)} %slice.335), channel_id=1, source_target_pairs={{24,0},{16,8},{40,16},{32,24},{56,32},{48,40},{72,48},{64,56},{88,... | collective-permute-start | bytes 1105928 | tf_op jit(solution)/shard_map/ppermute | solution.py:162
  161.3 3.1 %copy-start.34 = (bf16[4,64,128]{2,1,0:T(8,128)(2,1)S(1)}, bf16[4,64,128]{2,1,0:T(8,128)(2,1)}, u32[]{:S(2)}) copy-start(bf16[4,64,128]{2,1,0:T(8,128)(2,1)} %get-tuple-element.26) | copy-start | bytes 196612
  161.3 3.7 %copy-start.35 = (bf16[4,64,128]{2,1,0:T(8,128)(2,1)S(1)}, bf16[4,64,128]{2,1,0:T(8,128)(2,1)}, u32[]{:S(2)}) copy-start(bf16[4,64,128]{2,1,0:T(8,128)(2,1)} %get-tuple-element.24) | copy-start | bytes 196612
  161.3 4.3 %copy-start.36 = (bf16[4,64,128]{2,1,0:T(8,128)(2,1)S(1)}, bf16[4,64,128]{2,1,0:T(8,128)(2,1)}, u32[]{:S(2)}) copy-start(bf16[4,64,128]{2,1,0:T(8,128)(2,1)} %get-tuple-element.22) | copy-start | bytes 196612
  161.8 5.7 %copy-start.27 = (bf16[4,64,128]{2,1,0:T(8,128)(2,1)S(1)}, bf16[4,64,128]{2,1,0:T(8,128)(2,1)}, u32[]{:S(2)}) copy-start(bf16[4,64,128]{2,1,0:T(8,128)(2,1)} %get-tuple-element.31) | copy-start | bytes 196612
  168.1 5.2 %copy-start.31 = (bf16[4,64,128]{2,1,0:T(8,128)(2,1)S(1)}, bf16[4,64,128]{2,1,0:T(8,128)(2,1)}, u32[]{:S(2)}) copy-start(bf16[4,64,128]{2,1,0:T(8,128)(2,1)} %get-tuple-element.23) | copy-start | bytes 196612
  170.8 6.3 %collective-permute-start.15 = (bf16[4,720,128]{2,1,0:T(8,128)(2,1)S(1)}, bf16[4,720,128]{2,1,0:T(8,128)(2,1)S(1)}, u32[]{:S(2)}, u32[]{:S(2)}) collective-permute-start(bf16[4,720,128]{2,1,0:T(8,128)(2,1)S(1)} %collective-permute-done.8), channel_id=1, source_target_pairs={{0,8},{8,0},{1,9},{9,1},{2,10},{10,2},{3,11},{11,3},{4,12},{12,4},... | collective-permute-start | bytes 2211848 | tf_op jit(solution)/shard_map/ppermute | solution.py:87
  174.0 4.1 %collective-permute-start.16 = (bf16[4,720,128]{2,1,0:T(8,128)(2,1)S(1)}, bf16[4,720,128]{2,1,0:T(8,128)(2,1)S(1)}, u32[]{:S(2)}, u32[]{:S(2)}) collective-permute-start(bf16[4,720,128]{2,1,0:T(8,128)(2,1)S(1)} %collective-permute-done.9), channel_id=1, source_target_pairs={{0,8},{8,0},{1,9},{9,1},{2,10},{10,2},{3,11},{11,3},{4,12},{12,4},... | collective-permute-start | bytes 2211848 | tf_op jit(solution)/shard_map/ppermute | solution.py:87
  180.7 5.6 %copy-start.42 = (f32[128]{0:T(128)S(1)}, f32[128]{0:T(128)}, u32[]{:S(2)}) copy-start(f32[128]{0:T(128)} %convert_element_type.39) | copy-start | bytes 1540
  180.8 5.6 %copy-start.37 = (f32[128,64]{1,0:T(8,128)S(1)}, f32[128,64]{1,0:T(8,128)}, u32[]{:S(2)}) copy-start(f32[128,64]{1,0:T(8,128)} %copy.94) | copy-start | bytes 98308
  180.8 5.6 %copy-start.38 = (f32[128,64]{1,0:T(8,128)S(1)}, f32[128,64]{1,0:T(8,128)}, u32[]{:S(2)}) copy-start(f32[128,64]{1,0:T(8,128)} %copy.95) | copy-start | bytes 98308
  (21 other events, 25.7 us)
Sparse Core Ops, SparseCore 0:
  53.9 39.0 all-gather.2

commit v12 on v11

--- a/solution.py
+++ b/solution.py
@@ -145,8 +145,6 @@
     far = n_z // 2
     split = n_ylo // 2
     for step in range(1, far):
-        if step == far - 1:
-            normed5, forward, backward = lax.optimization_barrier((normed5, forward, backward))
         forward = shifted(forward, "z", n_z, -1)
         backward = shifted(backward, "z", n_z, 1)
         arrived += [(-step, forward), (step, backward)]
@@ -163,6 +161,7 @@
         ],
         axis=0,
     )
+    normed5, far_own, far_other = lax.optimization_barrier((normed5, far_own, far_other))
     held = [(offset, 0, piece) for offset, piece in arrived]
     held += [(offset, 1, shifted(piece, "core", 2, 1)) for offset, piece in arrived]
     held += [(far, 0, far_own), (far, 1, far_other)]

time: 212 us -> 205 us (0.967)
  the two profiles are of different devices: /device:TPU:15 before, /device:TPU:23 now
where the time goes in v12:
time: 205 us; the launch traced here: 204 us
  starting transfers between devices  75.2 us (37%)
  local copies, waits for them, and re-layouts  48.7 us (24%)
  waiting for transfers between devices  28.9 us (14%)
  between operations  15.9 us (8%)
  Pallas kernels  13.4 us (7%)
  other arithmetic  12.9 us (6%)
  matrix products  8.56 us (4%)
    ppermute x19, starting transfers between devices, shifted(): return lax.ppermute(x, axis, pairs)  69.6 us
    unnamed x151, local copies, waits for them, and re-layouts  34.8 us
    ppermute x19, waiting for transfers between devices, shifted(): return lax.ppermute(x, axis, pairs)  28.8 us
    pallas_call x1, Pallas kernels, attend(): pl.pallas_call(attend_kernel, grid=(passes,), in_specs=[pl.BlockSpec((Non...  13.4 us
    dot_general x16, matrix products, local(): jnp.einsum('rki,kjid->rjd', normed5[:, :, offset % n_z, core, :], piece.r...  8.56 us
    slice x3, local copies, waits for them, and re-layouts, local(): first_rows, given_rows = (both[0], both[1])  5.66 us
  transfers between devices with their start and end apart: 22, of which 6 were waited for; matrix products, arithmetic and copies ran while one was open for 14% of the time, Pallas kernels for 0%

profile of v12, /device:TPU:23, one launch (start us, length us, event | category | flops | bytes accessed | tf_op | source)
XLA Modules:
  0.0 203.6 jit_solution(436732394378749420)
XLA Ops:
  8.0 0.7 constant_dynamic-update-slice_fusion.9
  8.7 0.7 constant_dynamic-update-slice_fusion.8
  9.4 0.7 constant_dynamic-update-slice_fusion.7
  10.2 0.7 constant_dynamic-update-slice_fusion.6
  10.9 0.7 constant_dynamic-update-slice_fusion.5
  13.9 2.1 %collective-permute-start.1 = (bf16[720,128]{1,0:T(8,128)(2,1)S(1)}, bf16[720,128]{1,0:T(8,128)(2,1)S(1)}, u32[]{:S(2)}, u32[]{:S(2)}) collective-permute-start(bf16[720,128]{1,0:T(8,128)(2,1)S(1)} %constant_dynamic-update-slice_fusion), channel_id=1, source_target_pairs={{0,384},{128,0},{256,128},{384,256},{1,385},{129,1},{257,129},{385... | collective-permute-start | bytes 552968 | tf_op jit(solution)/shard_map/ppermute | solution.py:87
  15.9 5.1 %collective-permute-start.2 = (bf16[720,128]{1,0:T(8,128)(2,1)S(1)}, bf16[720,128]{1,0:T(8,128)(2,1)S(1)}, u32[]{:S(2)}, u32[]{:S(2)}) collective-permute-start(bf16[720,128]{1,0:T(8,128)(2,1)S(1)} %constant_dynamic-update-slice_fusion), channel_id=1, source_target_pairs={{0,256},{128,384},{256,0},{384,128},{1,257},{129,385},{257,1},{385... | collective-permute-start | bytes 552968 | tf_op jit(solution)/shard_map/ppermute | solution.py:87
  21.0 1.9 collective-permute-start.3
  23.0 1.8 pad_maximum_fusion.3
  24.8 5.7 %collective-permute-start = (bf16[2,128,640]{2,1,0:T(8,128)(2,1)}, bf16[2,128,640]{2,1,0:T(8,128)(2,1)}, u32[]{:S(2)}, u32[]{:S(2)}) collective-permute-start(bf16[2,128,640]{2,1,0:T(8,128)(2,1)} %get-tuple-element.50), channel_id=1, source_target_pairs={{0,4},{4,0},{1,5},{5,1},{2,6},{6,2},{3,7},{7,3},{8,12},{12,8},{9,1... | collective-permute-start | bytes 983048 | tf_op jit(solution)/shard_map/ppermute | solution.py:87
  33.5 16.6 %collective-permute-done.3 = bf16[720,128]{1,0:T(8,128)(2,1)S(1)} collective-permute-done((bf16[720,128]{1,0:T(8,128)(2,1)S(1)}, bf16[720,128]{1,0:T(8,128)(2,1)S(1)}, u32[]{:S(2)}, u32[]{:S(2)}) %collective-permute-start.3) | collective-permute-done | bytes 184352 | tf_op jit(solution)/shard_map/ppermute | solution.py:87
  50.9 4.0 %collective-permute-start.4 = (bf16[4,720,128]{2,1,0:T(8,128)(2,1)S(1)}, bf16[4,720,128]{2,1,0:T(8,128)(2,1)S(1)}, u32[]{:S(2)}, u32[]{:S(2)}) collective-permute-start(bf16[4,720,128]{2,1,0:T(8,128)(2,1)S(1)} %pad_maximum_fusion), channel_id=1, source_target_pairs={{0,16},{16,32},{32,48},{48,64},{64,80},{80,96},{96,112},{112,0},{1... | collective-permute-start | bytes 2211848 | tf_op jit(solution)/shard_map/ppermute | solution.py:87
  57.8 8.6 %collective-permute-start.8 = (bf16[4,720,128]{2,1,0:T(8,128)(2,1)S(1)}, bf16[4,720,128]{2,1,0:T(8,128)(2,1)S(1)}, u32[]{:S(2)}, u32[]{:S(2)}) collective-permute-start(bf16[4,720,128]{2,1,0:T(8,128)(2,1)S(1)} %pad_maximum_fusion), channel_id=1, source_target_pairs={{0,112},{16,0},{32,16},{48,32},{64,48},{80,64},{96,80},{112,96},{1... | collective-permute-start | bytes 2211848 | tf_op jit(solution)/shard_map/ppermute | solution.py:87
  66.4 2.7 %collective-permute-start.14 = (bf16[4,720,128]{2,1,0:T(8,128)(2,1)S(1)}, bf16[4,720,128]{2,1,0:T(8,128)(2,1)S(1)}, u32[]{:S(2)}, u32[]{:S(2)}) collective-permute-start(bf16[4,720,128]{2,1,0:T(8,128)(2,1)S(1)} %pad_maximum_fusion), channel_id=1, source_target_pairs={{0,8},{8,0},{1,9},{9,1},{2,10},{10,2},{3,11},{11,3},{4,12},{12,4},... | collective-permute-start | bytes 2211848 | tf_op jit(solution)/shard_map/ppermute | solution.py:87
  70.4 2.4 %fusion.27 = bf16[2,2,128,640]{3,2,1,0:T(8,128)(2,1)} fusion(s32[]{:T(128)S(6)} %select_n.73, bf16[1,2,128,640]{3,2,1,0:T(8,128)(2,1)S(1)} %get-tuple-element.51, bf16[1,2,128,640]{3,2,1,0:T(8,128)(2,1)} %bitcast.3), kind=kLoop, calls=%fused_computation.60 | loop fusion | flops 983040 | bytes 1310724 | tf_op jit(solution)/shard_map/jit(_roll_dynamic)/concatenate | solution.py:130
  72.9 5.1 %collective-permute-done.4 = bf16[4,720,128]{2,1,0:T(8,128)(2,1)S(1)} collective-permute-done((bf16[4,720,128]{2,1,0:T(8,128)(2,1)S(1)}, bf16[4,720,128]{2,1,0:T(8,128)(2,1)S(1)}, u32[]{:S(2)}, u32[]{:S(2)}) %collective-permute-start.4) | collective-permute-done | bytes 737312 | tf_op jit(solution)/shard_map/ppermute | solution.py:87
  78.0 1.9 collective-permute-start.5
  79.9 1.8 collective-permute-done.8
  81.7 5.3 %collective-permute-start.9 = (bf16[4,720,128]{2,1,0:T(8,128)(2,1)S(1)}, bf16[4,720,128]{2,1,0:T(8,128)(2,1)S(1)}, u32[]{:S(2)}, u32[]{:S(2)}) collective-permute-start(bf16[4,720,128]{2,1,0:T(8,128)(2,1)S(1)} %collective-permute-done.8), channel_id=1, source_target_pairs={{0,112},{16,0},{32,16},{48,32},{64,48},{80,64},{96,80},{112,96},{1... | collective-permute-start | bytes 2211848 | tf_op jit(solution)/shard_map/ppermute | solution.py:87
  88.3 3.5 %collective-permute-start.15 = (bf16[4,720,128]{2,1,0:T(8,128)(2,1)S(1)}, bf16[4,720,128]{2,1,0:T(8,128)(2,1)S(1)}, u32[]{:S(2)}, u32[]{:S(2)}) collective-permute-start(bf16[4,720,128]{2,1,0:T(8,128)(2,1)S(1)} %collective-permute-done.4), channel_id=1, source_target_pairs={{0,8},{8,0},{1,9},{9,1},{2,10},{10,2},{3,11},{11,3},{4,12},{12,4},... | collective-permute-start | bytes 2211848 | tf_op jit(solution)/shard_map/ppermute | solution.py:87
  91.9 1.9 collective-permute-start.16
  95.1 3.1 %collective-permute-done.5 = bf16[4,720,128]{2,1,0:T(8,128)(2,1)S(1)} collective-permute-done((bf16[4,720,128]{2,1,0:T(8,128)(2,1)S(1)}, bf16[4,720,128]{2,1,0:T(8,128)(2,1)S(1)}, u32[]{:S(2)}, u32[]{:S(2)}) %collective-permute-start.5) | collective-permute-done | bytes 737312 | tf_op jit(solution)/shard_map/ppermute | solution.py:87
  98.2 1.9 collective-permute-start.6
  100.1 1.4 collective-permute-done.9
  101.5 5.4 %collective-permute-start.10 = (bf16[4,720,128]{2,1,0:T(8,128)(2,1)S(1)}, bf16[4,720,128]{2,1,0:T(8,128)(2,1)S(1)}, u32[]{:S(2)}, u32[]{:S(2)}) collective-permute-start(bf16[4,720,128]{2,1,0:T(8,128)(2,1)S(1)} %collective-permute-done.9), channel_id=1, source_target_pairs={{0,112},{16,0},{32,16},{48,32},{64,48},{80,64},{96,80},{112,96},{1... | collective-permute-start | bytes 2211848 | tf_op jit(solution)/shard_map/ppermute | solution.py:87
  108.2 4.3 %collective-permute-start.17 = (bf16[4,720,128]{2,1,0:T(8,128)(2,1)S(1)}, bf16[4,720,128]{2,1,0:T(8,128)(2,1)S(1)}, u32[]{:S(2)}, u32[]{:S(2)}) collective-permute-start(bf16[4,720,128]{2,1,0:T(8,128)(2,1)S(1)} %collective-permute-done.5), channel_id=1, source_target_pairs={{0,8},{8,0},{1,9},{9,1},{2,10},{10,2},{3,11},{11,3},{4,12},{12,4},... | collective-permute-start | bytes 2211848 | tf_op jit(solution)/shard_map/ppermute | solution.py:87
  113.8 1.9 collective-permute-start.18
  115.8 0.8 copy-done.19
  116.6 0.8 collective-permute-done.6
  117.4 1.9 collective-permute-start.7
  119.4 3.4 %collective-permute-start.12 = (bf16[2,720,128]{2,1,0:T(8,128)(2,1)S(1)}, bf16[2,720,128]{2,1,0:T(8,128)(2,1)S(1)}, u32[]{:S(2)}, u32[]{:S(2)}) collective-permute-start(bf16[2,720,128]{2,1,0:T(8,128)(2,1)S(1)} %slice.334), channel_id=1, source_target_pairs={{120,0},{112,8},{8,16},{0,24},{24,32},{16,40},{40,48},{32,56},{56,... | collective-permute-start | bytes 1105928 | tf_op jit(solution)/shard_map/ppermute | solution.py:159
  122.8 5.8 %collective-permute-start.11 = (bf16[2,720,128]{2,1,0:T(8,128)(2,1)S(1)}, bf16[2,720,128]{2,1,0:T(8,128)(2,1)S(1)}, u32[]{:S(2)}, u32[]{:S(2)}) collective-permute-start(bf16[2,720,128]{2,1,0:T(8,128)(2,1)S(1)} %slice.335), channel_id=1, source_target_pairs={{0,112},{16,0},{32,16},{48,32},{64,48},{80,64},{96,80},{112,96},{1... | collective-permute-start | bytes 1105928 | tf_op jit(solution)/shard_map/ppermute | solution.py:87
  131.8 2.2 %collective-permute-start.13 = (bf16[2,720,128]{2,1,0:T(8,128)(2,1)S(1)}, bf16[2,720,128]{2,1,0:T(8,128)(2,1)S(1)}, u32[]{:S(2)}, u32[]{:S(2)}) collective-permute-start(bf16[2,720,128]{2,1,0:T(8,128)(2,1)S(1)} %slice.335), channel_id=1, source_target_pairs={{24,0},{16,8},{40,16},{32,24},{56,32},{48,40},{72,48},{64,56},{88,... | collective-permute-start | bytes 1105928 | tf_op jit(solution)/shard_map/ppermute | solution.py:160
  136.6 3.7 %collective-permute-start.19 = (bf16[4,720,128]{2,1,0:T(8,128)(2,1)S(1)}, bf16[4,720,128]{2,1,0:T(8,128)(2,1)S(1)}, u32[]{:S(2)}, u32[]{:S(2)}) collective-permute-start(bf16[4,720,128]{2,1,0:T(8,128)(2,1)S(1)} %collective-permute-done.6), channel_id=1, source_target_pairs={{0,8},{8,0},{1,9},{9,1},{2,10},{10,2},{3,11},{11,3},{4,12},{12,4},... | collective-permute-start | bytes 2211848 | tf_op jit(solution)/shard_map/ppermute | solution.py:87
  142.3 1.9 collective-permute-start.20
  145.6 0.9 pad_maximum_fusion.2
  147.4 0.9 copy-done.25
  150.2 3.1 %fusion.69 = (bf16[1,128,2,4,640]{4,1,0,3,2:T(8,128)(2,1)S(1)}, bf16[1,128,2,4,640]{4,1,0,3,2:T(8,128)(2,1)}) fusion(bf16[2,128,2,4,640]{4,1,0,3,2:T(8,128)(2,1)} %bitcast.357), kind=kLoop, calls=%fused_computation.188 | loop fusion | bytes 5242880 | tf_op jit(solution)/shard_map/slice | solution.py:133
  153.3 0.8 copy.72
  154.1 1.8 copy.73
  157.7 0.8 multiply_convert_fusion
  158.5 0.9 fusion.2
  159.5 0.9 fusion.1
  160.4 0.9 fusion
  173.9 0.8 fusion.13
  176.6 0.9 copy.99.q_ref
  181.6 13.4 %shard_map.149 = bf16[2,128,640]{2,1,0:T(8,128)(2,1)} custom-call(bf16[2,128,640]{2,1,0:T(8,128)(2,1)} %copy.99.q_ref, bf16[2,128,128]{2,1,0:T(8,128)(2,1)} %pad_maximum_fusion.5.ko_ref, bf16[2,128,128]{2,1,0:T(8,128)(2,1)} %add_convert_fusion.1.vo_ref, bf16[4096,128]{1,0:T(8,128)(2,1)} %constant_dynamic-update-slice_fusion.11.kc_ref, ...), custom_call_target="tpu_custom_call" | custom-call | flops 2768240640 | bytes 3407872 | tf_op jit(solution)/shard_map/pallas_call | solution.py:64
  195.0 1.7 slice_bitcast_fusion
  (249 shorter events, 47.0 us)
Async XLA Ops:
  7.2 24.1 %copy-start.41 = (bf16[640]{0:T(1024)(128)(2,1)S(1)}, bf16[640]{0:T(1024)(128)(2,1)}, u32[]{:S(2)}) copy-start(bf16[640]{0:T(1024)(128)(2,1)} %param.21) | copy-start | bytes 3844
  7.2 24.1 %copy-start.44 = (s32[1,64]{1,0:T(1,128)S(1)}, s32[1,64]{1,0:T(1,128)}, u32[]{:S(2)}) copy-start(s32[1,64]{1,0:T(1,128)} %param.18) | copy-start | bytes 772
  7.2 26.3 %copy-start.45 = (s32[128]{0:T(128)S(1)}, s32[128]{0:T(128)}, u32[]{:S(2)}) copy-start(s32[128]{0:T(128)} %param.16) | copy-start | bytes 1540
  7.2 143.0 %all-gather.3.cloned.1.call-start = ((), (), s32[]{:S(2)}) async-start(), calls=%async_computation | async-start | bytes 3276800 | tf_op jit(solution)/shard_map/all_gather | solution.py:131
  13.9 19.6 %collective-permute-start.1 = (bf16[720,128]{1,0:T(8,128)(2,1)S(1)}, bf16[720,128]{1,0:T(8,128)(2,1)S(1)}, u32[]{:S(2)}, u32[]{:S(2)}) collective-permute-start(bf16[720,128]{1,0:T(8,128)(2,1)S(1)} %constant_dynamic-update-slice_fusion), channel_id=1, source_target_pairs={{0,384},{128,0},{256,128},{384,256},{1,385},{129,1},{257,129},{385... | collective-permute-start | bytes 552968 | tf_op jit(solution)/shard_map/ppermute | solution.py:87
  15.9 17.6 %collective-permute-start.2 = (bf16[720,128]{1,0:T(8,128)(2,1)S(1)}, bf16[720,128]{1,0:T(8,128)(2,1)S(1)}, u32[]{:S(2)}, u32[]{:S(2)}) collective-permute-start(bf16[720,128]{1,0:T(8,128)(2,1)S(1)} %constant_dynamic-update-slice_fusion), channel_id=1, source_target_pairs={{0,256},{128,384},{256,0},{384,128},{1,257},{129,385},{257,1},{385... | collective-permute-start | bytes 552968 | tf_op jit(solution)/shard_map/ppermute | solution.py:87
  21.0 29.1 %collective-permute-start.3 = (bf16[720,128]{1,0:T(8,128)(2,1)S(1)}, bf16[720,128]{1,0:T(8,128)(2,1)S(1)}, u32[]{:S(2)}, u32[]{:S(2)}) collective-permute-start(bf16[720,128]{1,0:T(8,128)(2,1)S(1)} %constant_dynamic-update-slice_fusion), channel_id=1, source_target_pairs={{0,128},{128,256},{256,384},{384,0},{1,129},{129,257},{257,385},{3... | collective-permute-start | bytes 552968 | tf_op jit(solution)/shard_map/ppermute | solution.py:87
  24.8 30.2 %copy-start.40 = (bf16[5120]{0:T(1024)(128)(2,1)S(1)}, bf16[5120]{0:T(1024)(128)(2,1)}, u32[]{:S(2)}) copy-start(bf16[5120]{0:T(1024)(128)(2,1)} %param.19) | copy-start | bytes 30724
  24.8 30.9 %copy-start.46 = (bf16[128]{0:T(256)(128)(2,1)S(1)}, bf16[128]{0:T(256)(128)(2,1)}, u32[]{:S(2)}) copy-start(bf16[128]{0:T(256)(128)(2,1)} %param.23) | copy-start | bytes 772
  24.8 32.9 %copy-start.47 = (bf16[128]{0:T(256)(128)(2,1)S(1)}, bf16[128]{0:T(256)(128)(2,1)}, u32[]{:S(2)}) copy-start(bf16[128]{0:T(256)(128)(2,1)} %param.25) | copy-start | bytes 772
  24.8 45.6 %collective-permute-start = (bf16[2,128,640]{2,1,0:T(8,128)(2,1)}, bf16[2,128,640]{2,1,0:T(8,128)(2,1)}, u32[]{:S(2)}, u32[]{:S(2)}) collective-permute-start(bf16[2,128,640]{2,1,0:T(8,128)(2,1)} %get-tuple-element.50), channel_id=1, source_target_pairs={{0,4},{4,0},{1,5},{5,1},{2,6},{6,2},{3,7},{7,3},{8,12},{12,8},{9,1... | collective-permute-start | bytes 983048 | tf_op jit(solution)/shard_map/ppermute | solution.py:87
  33.3 33.1 %copy-start.33 = (f32[128,64]{0,1:T(8,128)}, f32[128,64]{0,1:T(8,128)S(1)}, u32[]{:S(2)}) copy-start(f32[128,64]{0,1:T(8,128)S(1)} %get-tuple-element.70) | copy-start | bytes 98308
  33.3 33.1 %copy-start.35 = (f32[128,64]{0,1:T(8,128)}, f32[128,64]{0,1:T(8,128)S(1)}, u32[]{:S(2)}) copy-start(f32[128,64]{0,1:T(8,128)S(1)} %get-tuple-element.71) | copy-start | bytes 98308
  33.5 16.7 %copy-start.27 = (bf16[720,128]{1,0:T(8,128)(2,1)}, bf16[720,128]{1,0:T(8,128)(2,1)S(1)}, u32[]{:S(2)}) copy-start(bf16[720,128]{1,0:T(8,128)(2,1)S(1)} %collective-permute-done.1) | copy-start | bytes 552964
  33.5 16.7 %copy-start.29 = (bf16[720,128]{1,0:T(8,128)(2,1)}, bf16[720,128]{1,0:T(8,128)(2,1)S(1)}, u32[]{:S(2)}) copy-start(bf16[720,128]{1,0:T(8,128)(2,1)S(1)} %collective-permute-done.2) | copy-start | bytes 552964
  50.9 27.1 %collective-permute-start.4 = (bf16[4,720,128]{2,1,0:T(8,128)(2,1)S(1)}, bf16[4,720,128]{2,1,0:T(8,128)(2,1)S(1)}, u32[]{:S(2)}, u32[]{:S(2)}) collective-permute-start(bf16[4,720,128]{2,1,0:T(8,128)(2,1)S(1)} %pad_maximum_fusion), channel_id=1, source_target_pairs={{0,16},{16,32},{32,48},{48,64},{64,80},{80,96},{96,112},{112,0},{1... | collective-permute-start | bytes 2211848 | tf_op jit(solution)/shard_map/ppermute | solution.py:87
  57.8 8.6 %copy-start.43 = (f32[1,4096]{1,0:T(1,128)}, f32[1,4096]{1,0:T(1,128)S(1)}, u32[]{:S(2)}) copy-start(f32[1,4096]{1,0:T(1,128)S(1)} %constant_dynamic-update-slice_fusion.43.bias_ref) | copy-start | bytes 49156
  57.8 23.9 %collective-permute-start.8 = (bf16[4,720,128]{2,1,0:T(8,128)(2,1)S(1)}, bf16[4,720,128]{2,1,0:T(8,128)(2,1)S(1)}, u32[]{:S(2)}, u32[]{:S(2)}) collective-permute-start(bf16[4,720,128]{2,1,0:T(8,128)(2,1)S(1)} %pad_maximum_fusion), channel_id=1, source_target_pairs={{0,112},{16,0},{32,16},{48,32},{64,48},{80,64},{96,80},{112,96},{1... | collective-permute-start | bytes 2211848 | tf_op jit(solution)/shard_map/ppermute | solution.py:87
  66.4 28.6 %collective-permute-start.14 = (bf16[4,720,128]{2,1,0:T(8,128)(2,1)S(1)}, bf16[4,720,128]{2,1,0:T(8,128)(2,1)S(1)}, u32[]{:S(2)}, u32[]{:S(2)}) collective-permute-start(bf16[4,720,128]{2,1,0:T(8,128)(2,1)S(1)} %pad_maximum_fusion), channel_id=1, source_target_pairs={{0,8},{8,0},{1,9},{9,1},{2,10},{10,2},{3,11},{11,3},{4,12},{12,4},... | collective-permute-start | bytes 2211848 | tf_op jit(solution)/shard_map/ppermute | solution.py:87
  78.0 37.7 %copy-start.7 = (bf16[4,720,128]{2,1,0:T(8,128)(2,1)}, bf16[4,720,128]{2,1,0:T(8,128)(2,1)S(1)}, u32[]{:S(2)}) copy-start(bf16[4,720,128]{2,1,0:T(8,128)(2,1)S(1)} %collective-permute-done.4) | copy-start | bytes 2211844
  78.0 20.2 %collective-permute-start.5 = (bf16[4,720,128]{2,1,0:T(8,128)(2,1)S(1)}, bf16[4,720,128]{2,1,0:T(8,128)(2,1)S(1)}, u32[]{:S(2)}, u32[]{:S(2)}) collective-permute-start(bf16[4,720,128]{2,1,0:T(8,128)(2,1)S(1)} %collective-permute-done.4), channel_id=1, source_target_pairs={{0,16},{16,32},{32,48},{48,64},{64,80},{80,96},{96,112},{112,0},{1... | collective-permute-start | bytes 2211848 | tf_op jit(solution)/shard_map/ppermute | solution.py:87
  81.7 34.1 %copy-start.11 = (bf16[4,720,128]{2,1,0:T(8,128)(2,1)}, bf16[4,720,128]{2,1,0:T(8,128)(2,1)S(1)}, u32[]{:S(2)}) copy-start(bf16[4,720,128]{2,1,0:T(8,128)(2,1)S(1)} %collective-permute-done.8) | copy-start | bytes 2211844
  81.7 19.7 %collective-permute-start.9 = (bf16[4,720,128]{2,1,0:T(8,128)(2,1)S(1)}, bf16[4,720,128]{2,1,0:T(8,128)(2,1)S(1)}, u32[]{:S(2)}, u32[]{:S(2)}) collective-permute-start(bf16[4,720,128]{2,1,0:T(8,128)(2,1)S(1)} %collective-permute-done.8), channel_id=1, source_target_pairs={{0,112},{16,0},{32,16},{48,32},{64,48},{80,64},{96,80},{112,96},{1... | collective-permute-start | bytes 2211848 | tf_op jit(solution)/shard_map/ppermute | solution.py:87
  88.3 25.5 %collective-permute-start.15 = (bf16[4,720,128]{2,1,0:T(8,128)(2,1)S(1)}, bf16[4,720,128]{2,1,0:T(8,128)(2,1)S(1)}, u32[]{:S(2)}, u32[]{:S(2)}) collective-permute-start(bf16[4,720,128]{2,1,0:T(8,128)(2,1)S(1)} %collective-permute-done.4), channel_id=1, source_target_pairs={{0,8},{8,0},{1,9},{9,1},{2,10},{10,2},{3,11},{11,3},{4,12},{12,4},... | collective-permute-start | bytes 2211848 | tf_op jit(solution)/shard_map/ppermute | solution.py:87
  91.9 23.9 %collective-permute-start.16 = (bf16[4,720,128]{2,1,0:T(8,128)(2,1)S(1)}, bf16[4,720,128]{2,1,0:T(8,128)(2,1)S(1)}, u32[]{:S(2)}, u32[]{:S(2)}) collective-permute-start(bf16[4,720,128]{2,1,0:T(8,128)(2,1)S(1)} %collective-permute-done.8), channel_id=1, source_target_pairs={{0,8},{8,0},{1,9},{9,1},{2,10},{10,2},{3,11},{11,3},{4,12},{12,4},... | collective-permute-start | bytes 2211848 | tf_op jit(solution)/shard_map/ppermute | solution.py:87
  95.1 27.7 %copy-start.9 = (bf16[4,720,128]{2,1,0:T(8,128)(2,1)}, bf16[4,720,128]{2,1,0:T(8,128)(2,1)S(1)}, u32[]{:S(2)}) copy-start(bf16[4,720,128]{2,1,0:T(8,128)(2,1)S(1)} %collective-permute-done.14) | copy-start | bytes 2211844
  98.2 24.6 %copy-start.13 = (bf16[4,720,128]{2,1,0:T(8,128)(2,1)}, bf16[4,720,128]{2,1,0:T(8,128)(2,1)S(1)}, u32[]{:S(2)}) copy-start(bf16[4,720,128]{2,1,0:T(8,128)(2,1)S(1)} %collective-permute-done.5) | copy-start | bytes 2211844
  98.2 19.2 %collective-permute-start.6 = (bf16[4,720,128]{2,1,0:T(8,128)(2,1)S(1)}, bf16[4,720,128]{2,1,0:T(8,128)(2,1)S(1)}, u32[]{:S(2)}, u32[]{:S(2)}) collective-permute-start(bf16[4,720,128]{2,1,0:T(8,128)(2,1)S(1)} %collective-permute-done.5), channel_id=1, source_target_pairs={{0,16},{16,32},{32,48},{48,64},{64,80},{80,96},{96,112},{112,0},{1... | collective-permute-start | bytes 2211848 | tf_op jit(solution)/shard_map/ppermute | solution.py:87
  101.5 21.3 %copy-start.15 = (bf16[4,720,128]{2,1,0:T(8,128)(2,1)}, bf16[4,720,128]{2,1,0:T(8,128)(2,1)S(1)}, u32[]{:S(2)}) copy-start(bf16[4,720,128]{2,1,0:T(8,128)(2,1)S(1)} %collective-permute-done.9) | copy-start | bytes 2211844
  101.5 21.2 %collective-permute-start.10 = (bf16[4,720,128]{2,1,0:T(8,128)(2,1)S(1)}, bf16[4,720,128]{2,1,0:T(8,128)(2,1)S(1)}, u32[]{:S(2)}, u32[]{:S(2)}) collective-permute-start(bf16[4,720,128]{2,1,0:T(8,128)(2,1)S(1)} %collective-permute-done.9), channel_id=1, source_target_pairs={{0,112},{16,0},{32,16},{48,32},{64,48},{80,64},{96,80},{112,96},{1... | collective-permute-start | bytes 2211848 | tf_op jit(solution)/shard_map/ppermute | solution.py:87
  108.2 23.6 %collective-permute-start.17 = (bf16[4,720,128]{2,1,0:T(8,128)(2,1)S(1)}, bf16[4,720,128]{2,1,0:T(8,128)(2,1)S(1)}, u32[]{:S(2)}, u32[]{:S(2)}) collective-permute-start(bf16[4,720,128]{2,1,0:T(8,128)(2,1)S(1)} %collective-permute-done.5), channel_id=1, source_target_pairs={{0,8},{8,0},{1,9},{9,1},{2,10},{10,2},{3,11},{11,3},{4,12},{12,4},... | collective-permute-start | bytes 2211848 | tf_op jit(solution)/shard_map/ppermute | solution.py:87
  113.8 2.0 copy-start.17
  113.8 20.8 %collective-permute-start.18 = (bf16[4,720,128]{2,1,0:T(8,128)(2,1)S(1)}, bf16[4,720,128]{2,1,0:T(8,128)(2,1)S(1)}, u32[]{:S(2)}, u32[]{:S(2)}) collective-permute-start(bf16[4,720,128]{2,1,0:T(8,128)(2,1)S(1)} %collective-permute-done.9), channel_id=1, source_target_pairs={{0,8},{8,0},{1,9},{9,1},{2,10},{10,2},{3,11},{11,3},{4,12},{12,4},... | collective-permute-start | bytes 2211848 | tf_op jit(solution)/shard_map/ppermute | solution.py:87
  117.4 19.2 %copy-start.1 = (bf16[4,720,128]{2,1,0:T(8,128)(2,1)}, bf16[4,720,128]{2,1,0:T(8,128)(2,1)S(1)}, u32[]{:S(2)}) copy-start(bf16[4,720,128]{2,1,0:T(8,128)(2,1)S(1)} %collective-permute-done.6) | copy-start | bytes 2211844
  117.4 28.0 %collective-permute-start.7 = (bf16[2,720,128]{2,1,0:T(8,128)(2,1)S(1)}, bf16[2,720,128]{2,1,0:T(8,128)(2,1)S(1)}, u32[]{:S(2)}, u32[]{:S(2)}) collective-permute-start(bf16[2,720,128]{2,1,0:T(8,128)(2,1)S(1)} %slice.334), channel_id=1, source_target_pairs={{0,16},{16,32},{32,48},{48,64},{64,80},{80,96},{96,112},{112,0},{1... | collective-permute-start | bytes 1105928 | tf_op jit(solution)/shard_map/ppermute | solution.py:87
  119.4 26.2 %collective-permute-start.12 = (bf16[2,720,128]{2,1,0:T(8,128)(2,1)S(1)}, bf16[2,720,128]{2,1,0:T(8,128)(2,1)S(1)}, u32[]{:S(2)}, u32[]{:S(2)}) collective-permute-start(bf16[2,720,128]{2,1,0:T(8,128)(2,1)S(1)} %slice.334), channel_id=1, source_target_pairs={{120,0},{112,8},{8,16},{0,24},{24,32},{16,40},{40,48},{32,56},{56,... | collective-permute-start | bytes 1105928 | tf_op jit(solution)/shard_map/ppermute | solution.py:159
  122.7 19.5 %copy-start.3 = (bf16[4,720,128]{2,1,0:T(8,128)(2,1)}, bf16[4,720,128]{2,1,0:T(8,128)(2,1)S(1)}, u32[]{:S(2)}) copy-start(bf16[4,720,128]{2,1,0:T(8,128)(2,1)S(1)} %collective-permute-done.10) | copy-start | bytes 2211844
  122.8 19.5 %collective-permute-start.11 = (bf16[2,720,128]{2,1,0:T(8,128)(2,1)S(1)}, bf16[2,720,128]{2,1,0:T(8,128)(2,1)S(1)}, u32[]{:S(2)}, u32[]{:S(2)}) collective-permute-start(bf16[2,720,128]{2,1,0:T(8,128)(2,1)S(1)} %slice.335), channel_id=1, source_target_pairs={{0,112},{16,0},{32,16},{48,32},{64,48},{80,64},{96,80},{112,96},{1... | collective-permute-start | bytes 1105928 | tf_op jit(solution)/shard_map/ppermute | solution.py:87
  131.8 13.7 %copy-start.21 = (bf16[4,720,128]{2,1,0:T(8,128)(2,1)}, bf16[4,720,128]{2,1,0:T(8,128)(2,1)S(1)}, u32[]{:S(2)}) copy-start(bf16[4,720,128]{2,1,0:T(8,128)(2,1)S(1)} %collective-permute-done.17) | copy-start | bytes 2211844
  131.8 13.8 %collective-permute-start.13 = (bf16[2,720,128]{2,1,0:T(8,128)(2,1)S(1)}, bf16[2,720,128]{2,1,0:T(8,128)(2,1)S(1)}, u32[]{:S(2)}, u32[]{:S(2)}) collective-permute-start(bf16[2,720,128]{2,1,0:T(8,128)(2,1)S(1)} %slice.335), channel_id=1, source_target_pairs={{24,0},{16,8},{40,16},{32,24},{56,32},{48,40},{72,48},{64,56},{88,... | collective-permute-start | bytes 1105928 | tf_op jit(solution)/shard_map/ppermute | solution.py:160
  134.6 10.8 %copy-start.23 = (bf16[4,720,128]{2,1,0:T(8,128)(2,1)}, bf16[4,720,128]{2,1,0:T(8,128)(2,1)S(1)}, u32[]{:S(2)}) copy-start(bf16[4,720,128]{2,1,0:T(8,128)(2,1)S(1)} %collective-permute-done.18) | copy-start | bytes 2211844
  136.6 9.9 %collective-permute-start.19 = (bf16[4,720,128]{2,1,0:T(8,128)(2,1)S(1)}, bf16[4,720,128]{2,1,0:T(8,128)(2,1)S(1)}, u32[]{:S(2)}, u32[]{:S(2)}) collective-permute-start(bf16[4,720,128]{2,1,0:T(8,128)(2,1)S(1)} %collective-permute-done.6), channel_id=1, source_target_pairs={{0,8},{8,0},{1,9},{9,1},{2,10},{10,2},{3,11},{11,3},{4,12},{12,4},... | collective-permute-start | bytes 2211848 | tf_op jit(solution)/shard_map/ppermute | solution.py:87
  142.3 4.9 %collective-permute-start.20 = (bf16[4,720,128]{2,1,0:T(8,128)(2,1)S(1)}, bf16[4,720,128]{2,1,0:T(8,128)(2,1)S(1)}, u32[]{:S(2)}, u32[]{:S(2)}) collective-permute-start(bf16[4,720,128]{2,1,0:T(8,128)(2,1)S(1)} %collective-permute-done.10), channel_id=1, source_target_pairs={{0,8},{8,0},{1,9},{9,1},{2,10},{10,2},{3,11},{11,3},{4,12},{12,4},... | collective-permute-start | bytes 2211848 | tf_op jit(solution)/shard_map/ppermute | solution.py:87
  162.1 1.2 copy-start.16
  168.8 1.2 copy-start
  176.4 3.6 %copy-start.42 = (f32[128]{0:T(128)S(1)}, f32[128]{0:T(128)}, u32[]{:S(2)}) copy-start(f32[128]{0:T(128)} %convert_element_type.39) | copy-start | bytes 1540
  176.5 3.5 %copy-start.37 = (f32[128,64]{1,0:T(8,128)S(1)}, f32[128,64]{1,0:T(8,128)}, u32[]{:S(2)}) copy-start(f32[128,64]{1,0:T(8,128)} %copy.96) | copy-start | bytes 98308
  176.5 3.5 %copy-start.38 = (f32[128,64]{1,0:T(8,128)S(1)}, f32[128,64]{1,0:T(8,128)}, u32[]{:S(2)}) copy-start(f32[128,64]{1,0:T(8,128)} %copy.97) | copy-start | bytes 98308
  (22 other events, 22.4 us)
Sparse Core Ops, SparseCore 0:
  73.0 34.3 all-gather.2

commit v13 on v10

--- a/solution.py
+++ b/solution.py
@@ -109,6 +109,10 @@
     q_cols = w_query.shape[1]
     w_rows = w_query.shape[0]
 
+    mine = jnp.stack([embeds, given_embeds])
+    mine, w_query, w_key, w_value, cache_keys, cache_values = lax.optimization_barrier(
+        (mine, w_query, w_key, w_value, cache_keys, cache_values)
+    )
     w_parts = [w_query[:, j * HD : (j + 1) * HD] for j in range(q_cols // HD)] + [w_key, w_value]
     w_len = len(w_parts) * w_rows
     key_start = -(-w_len // ctx_rows) * ctx_rows
@@ -125,7 +129,6 @@
     me_z = lax.axis_index("z")
     me_core = lax.axis_index("core")
 
-    mine = jnp.stack([embeds, given_embeds])
     both = lax.all_gather(mine, "tp", axis=2, tiled=True)
     first_rows, given_rows = both[0], both[1]
 

time: 186 us -> 184 us (0.989)
  the two profiles are of different devices: /device:TPU:22 before, /device:TPU:40 now
where the time goes in v13:
time: 184 us; the launch traced here: 183 us
  starting transfers between devices  65.2 us (35%)
  waiting for transfers between devices  39.8 us (22%)
  local copies, waits for them, and re-layouts  31.6 us (17%)
  between operations  16.1 us (9%)
  Pallas kernels  13.4 us (7%)
  matrix products  8.57 us (5%)
  other arithmetic  7.91 us (4%)
    ppermute x18, starting transfers between devices, shifted(): return lax.ppermute(x, axis, pairs)  59.1 us
    ppermute x18, waiting for transfers between devices, shifted(): return lax.ppermute(x, axis, pairs)  39.8 us
    unnamed x151, local copies, waits for them, and re-layouts  20.4 us
    pallas_call x1, Pallas kernels, attend(): pl.pallas_call(attend_kernel, grid=(passes,), in_specs=[pl.BlockSpec((Non...  13.4 us
    dot_general x16, matrix products, local(): jnp.einsum('rki,kjid->rjd', normed5[:, :, offset % n_z, core, :], piece.r...  8.57 us
  transfers between devices with their start and end apart: 21, of which 6 were waited for; matrix products, arithmetic and copies ran while one was open for 8% of the time, Pallas kernels for 0%

profile of v13, /device:TPU:40, one launch (start us, length us, event | category | flops | bytes accessed | tf_op | source)
XLA Modules:
  0.0 182.6 jit_solution(3774932915490858505)
XLA Ops:
  7.3 1.1 copy.46
  8.4 1.1 copy.47
  9.5 0.8 pad_maximum_fusion.3
  10.4 2.6 %collective-permute-start.2 = (bf16[720,128]{1,0:T(8,128)(2,1)S(1)}, bf16[720,128]{1,0:T(8,128)(2,1)S(1)}, u32[]{:S(2)}, u32[]{:S(2)}) collective-permute-start(bf16[720,128]{1,0:T(8,128)(2,1)S(1)} %constant_dynamic-update-slice_fusion), channel_id=1, source_target_pairs={{0,128},{128,256},{256,384},{384,0},{1,129},{129,257},{257,385},{3... | collective-permute-start | bytes 552968 | tf_op jit(solution)/shard_map/ppermute | solution.py:87
  13.0 4.9 %collective-permute-start.1 = (bf16[720,128]{1,0:T(8,128)(2,1)S(1)}, bf16[720,128]{1,0:T(8,128)(2,1)S(1)}, u32[]{:S(2)}, u32[]{:S(2)}) collective-permute-start(bf16[720,128]{1,0:T(8,128)(2,1)S(1)} %constant_dynamic-update-slice_fusion), channel_id=1, source_target_pairs={{0,256},{128,384},{256,0},{384,128},{1,257},{129,385},{257,1},{385... | collective-permute-start | bytes 552968 | tf_op jit(solution)/shard_map/ppermute | solution.py:87
  18.0 1.9 %collective-permute-start = (bf16[720,128]{1,0:T(8,128)(2,1)S(1)}, bf16[720,128]{1,0:T(8,128)(2,1)S(1)}, u32[]{:S(2)}, u32[]{:S(2)}) collective-permute-start(bf16[720,128]{1,0:T(8,128)(2,1)S(1)} %constant_dynamic-update-slice_fusion), channel_id=1, source_target_pairs={{0,384},{128,0},{256,128},{384,256},{1,385},{129,1},{257,129},{385... | collective-permute-start | bytes 552968 | tf_op jit(solution)/shard_map/ppermute | solution.py:87
  22.8 6.1 %collective-permute-done.1 = bf16[720,128]{1,0:T(8,128)(2,1)S(1)} collective-permute-done((bf16[720,128]{1,0:T(8,128)(2,1)S(1)}, bf16[720,128]{1,0:T(8,128)(2,1)S(1)}, u32[]{:S(2)}, u32[]{:S(2)}) %collective-permute-start.1) | collective-permute-done | bytes 184352 | tf_op jit(solution)/shard_map/ppermute | solution.py:87
  28.9 3.4 %collective-permute-done = bf16[720,128]{1,0:T(8,128)(2,1)S(1)} collective-permute-done((bf16[720,128]{1,0:T(8,128)(2,1)S(1)}, bf16[720,128]{1,0:T(8,128)(2,1)S(1)}, u32[]{:S(2)}, u32[]{:S(2)}) %collective-permute-start) | collective-permute-done | bytes 184352 | tf_op jit(solution)/shard_map/ppermute | solution.py:87
  32.4 10.9 %collective-permute-start.7 = (bf16[4,720,128]{2,1,0:T(8,128)(2,1)S(1)}, bf16[4,720,128]{2,1,0:T(8,128)(2,1)S(1)}, u32[]{:S(2)}, u32[]{:S(2)}) collective-permute-start(bf16[4,720,128]{2,1,0:T(8,128)(2,1)S(1)} %pad_maximum_fusion), channel_id=1, source_target_pairs={{0,112},{16,0},{32,16},{48,32},{64,48},{80,64},{96,80},{112,96},{1... | collective-permute-start | bytes 2211848 | tf_op jit(solution)/shard_map/ppermute | solution.py:87
  43.5 1.9 %collective-permute-start.3 = (bf16[4,720,128]{2,1,0:T(8,128)(2,1)S(1)}, bf16[4,720,128]{2,1,0:T(8,128)(2,1)S(1)}, u32[]{:S(2)}, u32[]{:S(2)}) collective-permute-start(bf16[4,720,128]{2,1,0:T(8,128)(2,1)S(1)} %pad_maximum_fusion), channel_id=1, source_target_pairs={{0,16},{16,32},{32,48},{48,64},{64,80},{80,96},{96,112},{112,0},{1... | collective-permute-start | bytes 2211848 | tf_op jit(solution)/shard_map/ppermute | solution.py:87
  46.3 0.7 copy.68
  47.0 0.7 copy.69
  47.7 1.9 %collective-permute-start.13 = (bf16[4,720,128]{2,1,0:T(8,128)(2,1)S(1)}, bf16[4,720,128]{2,1,0:T(8,128)(2,1)S(1)}, u32[]{:S(2)}, u32[]{:S(2)}) collective-permute-start(bf16[4,720,128]{2,1,0:T(8,128)(2,1)S(1)} %pad_maximum_fusion), channel_id=1, source_target_pairs={{0,8},{8,0},{1,9},{9,1},{2,10},{10,2},{3,11},{11,3},{4,12},{12,4},... | collective-permute-start | bytes 2211848 | tf_op jit(solution)/shard_map/ppermute | solution.py:87
  50.3 9.0 %collective-permute-done.7 = bf16[4,720,128]{2,1,0:T(8,128)(2,1)S(1)} collective-permute-done((bf16[4,720,128]{2,1,0:T(8,128)(2,1)S(1)}, bf16[4,720,128]{2,1,0:T(8,128)(2,1)S(1)}, u32[]{:S(2)}, u32[]{:S(2)}) %collective-permute-start.7) | collective-permute-done | bytes 737312 | tf_op jit(solution)/shard_map/ppermute | solution.py:87
  59.3 5.6 %collective-permute-start.8 = (bf16[4,720,128]{2,1,0:T(8,128)(2,1)S(1)}, bf16[4,720,128]{2,1,0:T(8,128)(2,1)S(1)}, u32[]{:S(2)}, u32[]{:S(2)}) collective-permute-start(bf16[4,720,128]{2,1,0:T(8,128)(2,1)S(1)} %collective-permute-done.7), channel_id=1, source_target_pairs={{0,112},{16,0},{32,16},{48,32},{64,48},{80,64},{96,80},{112,96},{1... | collective-permute-start | bytes 2211848 | tf_op jit(solution)/shard_map/ppermute | solution.py:87
  64.9 1.9 %collective-permute-start.4 = (bf16[4,720,128]{2,1,0:T(8,128)(2,1)S(1)}, bf16[4,720,128]{2,1,0:T(8,128)(2,1)S(1)}, u32[]{:S(2)}, u32[]{:S(2)}) collective-permute-start(bf16[4,720,128]{2,1,0:T(8,128)(2,1)S(1)} %collective-permute-done.3), channel_id=1, source_target_pairs={{0,16},{16,32},{32,48},{48,64},{64,80},{80,96},{96,112},{112,0},{1... | collective-permute-start | bytes 2211848 | tf_op jit(solution)/shard_map/ppermute | solution.py:87
  66.9 1.9 %collective-permute-start.15 = (bf16[4,720,128]{2,1,0:T(8,128)(2,1)S(1)}, bf16[4,720,128]{2,1,0:T(8,128)(2,1)S(1)}, u32[]{:S(2)}, u32[]{:S(2)}) collective-permute-start(bf16[4,720,128]{2,1,0:T(8,128)(2,1)S(1)} %collective-permute-done.7), channel_id=1, source_target_pairs={{0,8},{8,0},{1,9},{9,1},{2,10},{10,2},{3,11},{11,3},{4,12},{12,4},... | collective-permute-start | bytes 2211848 | tf_op jit(solution)/shard_map/ppermute | solution.py:87
  68.8 2.4 %collective-permute-start.14 = (bf16[4,720,128]{2,1,0:T(8,128)(2,1)S(1)}, bf16[4,720,128]{2,1,0:T(8,128)(2,1)S(1)}, u32[]{:S(2)}, u32[]{:S(2)}) collective-permute-start(bf16[4,720,128]{2,1,0:T(8,128)(2,1)S(1)} %collective-permute-done.3), channel_id=1, source_target_pairs={{0,8},{8,0},{1,9},{9,1},{2,10},{10,2},{3,11},{11,3},{4,12},{12,4},... | collective-permute-start | bytes 2211848 | tf_op jit(solution)/shard_map/ppermute | solution.py:87
  72.5 7.4 %collective-permute-done.8 = bf16[4,720,128]{2,1,0:T(8,128)(2,1)S(1)} collective-permute-done((bf16[4,720,128]{2,1,0:T(8,128)(2,1)S(1)}, bf16[4,720,128]{2,1,0:T(8,128)(2,1)S(1)}, u32[]{:S(2)}, u32[]{:S(2)}) %collective-permute-start.8) | collective-permute-done | bytes 737312 | tf_op jit(solution)/shard_map/ppermute | solution.py:87
  80.0 5.6 %collective-permute-start.9 = (bf16[4,720,128]{2,1,0:T(8,128)(2,1)S(1)}, bf16[4,720,128]{2,1,0:T(8,128)(2,1)S(1)}, u32[]{:S(2)}, u32[]{:S(2)}) collective-permute-start(bf16[4,720,128]{2,1,0:T(8,128)(2,1)S(1)} %collective-permute-done.8), channel_id=1, source_target_pairs={{0,112},{16,0},{32,16},{48,32},{64,48},{80,64},{96,80},{112,96},{1... | collective-permute-start | bytes 2211848 | tf_op jit(solution)/shard_map/ppermute | solution.py:87
  85.6 1.9 %collective-permute-start.5 = (bf16[4,720,128]{2,1,0:T(8,128)(2,1)S(1)}, bf16[4,720,128]{2,1,0:T(8,128)(2,1)S(1)}, u32[]{:S(2)}, u32[]{:S(2)}) collective-permute-start(bf16[4,720,128]{2,1,0:T(8,128)(2,1)S(1)} %collective-permute-done.4), channel_id=1, source_target_pairs={{0,16},{16,32},{32,48},{48,64},{64,80},{80,96},{96,112},{112,0},{1... | collective-permute-start | bytes 2211848 | tf_op jit(solution)/shard_map/ppermute | solution.py:87
  87.6 1.9 %collective-permute-start.17 = (bf16[4,720,128]{2,1,0:T(8,128)(2,1)S(1)}, bf16[4,720,128]{2,1,0:T(8,128)(2,1)S(1)}, u32[]{:S(2)}, u32[]{:S(2)}) collective-permute-start(bf16[4,720,128]{2,1,0:T(8,128)(2,1)S(1)} %collective-permute-done.8), channel_id=1, source_target_pairs={{0,8},{8,0},{1,9},{9,1},{2,10},{10,2},{3,11},{11,3},{4,12},{12,4},... | collective-permute-start | bytes 2211848 | tf_op jit(solution)/shard_map/ppermute | solution.py:87
  90.7 2.4 %collective-permute-start.16 = (bf16[4,720,128]{2,1,0:T(8,128)(2,1)S(1)}, bf16[4,720,128]{2,1,0:T(8,128)(2,1)S(1)}, u32[]{:S(2)}, u32[]{:S(2)}) collective-permute-start(bf16[4,720,128]{2,1,0:T(8,128)(2,1)S(1)} %collective-permute-done.4), channel_id=1, source_target_pairs={{0,8},{8,0},{1,9},{9,1},{2,10},{10,2},{3,11},{11,3},{4,12},{12,4},... | collective-permute-start | bytes 2211848 | tf_op jit(solution)/shard_map/ppermute | solution.py:87
  93.2 6.6 %collective-permute-done.9 = bf16[4,720,128]{2,1,0:T(8,128)(2,1)S(1)} collective-permute-done((bf16[4,720,128]{2,1,0:T(8,128)(2,1)S(1)}, bf16[4,720,128]{2,1,0:T(8,128)(2,1)S(1)}, u32[]{:S(2)}, u32[]{:S(2)}) %collective-permute-start.9) | collective-permute-done | bytes 737312 | tf_op jit(solution)/shard_map/ppermute | solution.py:87
  99.8 2.7 %collective-permute-start.12 = (bf16[2,720,128]{2,1,0:T(8,128)(2,1)S(1)}, bf16[2,720,128]{2,1,0:T(8,128)(2,1)S(1)}, u32[]{:S(2)}, u32[]{:S(2)}) collective-permute-start(bf16[2,720,128]{2,1,0:T(8,128)(2,1)S(1)} %slice.333), channel_id=1, source_target_pairs={{24,0},{16,8},{40,16},{32,24},{56,32},{48,40},{72,48},{64,56},{88,... | collective-permute-start | bytes 1105928 | tf_op jit(solution)/shard_map/ppermute | solution.py:160
  102.6 4.8 %collective-permute-start.10 = (bf16[2,720,128]{2,1,0:T(8,128)(2,1)S(1)}, bf16[2,720,128]{2,1,0:T(8,128)(2,1)S(1)}, u32[]{:S(2)}, u32[]{:S(2)}) collective-permute-start(bf16[2,720,128]{2,1,0:T(8,128)(2,1)S(1)} %slice.333), channel_id=1, source_target_pairs={{0,112},{16,0},{32,16},{48,32},{64,48},{80,64},{96,80},{112,96},{1... | collective-permute-start | bytes 1105928 | tf_op jit(solution)/shard_map/ppermute | solution.py:87
  107.4 3.4 %collective-permute-start.11 = (bf16[2,720,128]{2,1,0:T(8,128)(2,1)S(1)}, bf16[2,720,128]{2,1,0:T(8,128)(2,1)S(1)}, u32[]{:S(2)}, u32[]{:S(2)}) collective-permute-start(bf16[2,720,128]{2,1,0:T(8,128)(2,1)S(1)} %slice.332), channel_id=1, source_target_pairs={{120,0},{112,8},{8,16},{0,24},{24,32},{16,40},{40,48},{32,56},{56,... | collective-permute-start | bytes 1105928 | tf_op jit(solution)/shard_map/ppermute | solution.py:159
  111.0 1.9 %collective-permute-start.6 = (bf16[2,720,128]{2,1,0:T(8,128)(2,1)S(1)}, bf16[2,720,128]{2,1,0:T(8,128)(2,1)S(1)}, u32[]{:S(2)}, u32[]{:S(2)}) collective-permute-start(bf16[2,720,128]{2,1,0:T(8,128)(2,1)S(1)} %slice.332), channel_id=1, source_target_pairs={{0,16},{16,32},{32,48},{48,64},{64,80},{80,96},{96,112},{112,0},{1... | collective-permute-start | bytes 1105928 | tf_op jit(solution)/shard_map/ppermute | solution.py:87
  113.0 0.7 constant_dynamic-update-slice_fusion.37
  113.7 0.6 constant_dynamic-update-slice_fusion.36
  114.3 2.0 %collective-permute-start.18 = (bf16[4,720,128]{2,1,0:T(8,128)(2,1)S(1)}, bf16[4,720,128]{2,1,0:T(8,128)(2,1)S(1)}, u32[]{:S(2)}, u32[]{:S(2)}) collective-permute-start(bf16[4,720,128]{2,1,0:T(8,128)(2,1)S(1)} %collective-permute-done.5), channel_id=1, source_target_pairs={{0,8},{8,0},{1,9},{9,1},{2,10},{10,2},{3,11},{11,3},{4,12},{12,4},... | collective-permute-start | bytes 2211848 | tf_op jit(solution)/shard_map/ppermute | solution.py:87
  118.2 2.5 %collective-permute-start.19 = (bf16[4,720,128]{2,1,0:T(8,128)(2,1)S(1)}, bf16[4,720,128]{2,1,0:T(8,128)(2,1)S(1)}, u32[]{:S(2)}, u32[]{:S(2)}) collective-permute-start(bf16[4,720,128]{2,1,0:T(8,128)(2,1)S(1)} %collective-permute-done.9), channel_id=1, source_target_pairs={{0,8},{8,0},{1,9},{9,1},{2,10},{10,2},{3,11},{11,3},{4,12},{12,4},... | collective-permute-start | bytes 2211848 | tf_op jit(solution)/shard_map/ppermute | solution.py:87
  122.0 7.3 %collective-permute-done.6 = bf16[2,720,128]{2,1,0:T(8,128)(2,1)S(1)} collective-permute-done((bf16[2,720,128]{2,1,0:T(8,128)(2,1)S(1)}, bf16[2,720,128]{2,1,0:T(8,128)(2,1)S(1)}, u32[]{:S(2)}, u32[]{:S(2)}) %collective-permute-start.6) | collective-permute-done | bytes 368672 | tf_op jit(solution)/shard_map/ppermute | solution.py:87
  129.5 0.9 copy-done.1
  130.4 0.9 copy-done.21
  131.2 0.7 constant_dynamic-update-slice_fusion.30
  132.9 2.3 %slice_bitcast_fusion.2 = (bf16[128,5120]{0,1:T(8,128)(2,1)S(1)}, bf16[1,128,5120]{1,2,0:T(8,128)(2,1)S(1)}, bf16[1,128,5120]{1,2,0:T(8,128)(2,1)S(1)}) fusion(bf16[2,128,5120]{1,2,0:T(8,128)(2,1)} %all-gather.2.cloned.1.call-done), kind=kLoop, calls=%fused_computation.180 | loop fusion | bytes 6553600 | tf_op jit(solution)/shard_map/squeeze | solution.py:133
  135.5 0.7 multiply_reduce_fusion
  137.0 0.8 multiply_convert_fusion
  137.9 0.9 fusion.2
  138.8 0.9 fusion.1
  139.8 0.9 fusion
  149.0 0.7 fusion.67
  152.9 0.8 fusion.13
  155.6 0.9 copy.71.q_ref
  159.8 0.7 pad_maximum_fusion.5.ko_ref
  160.5 13.4 %shard_map.149 = bf16[2,128,640]{2,1,0:T(8,128)(2,1)} custom-call(bf16[2,128,640]{2,1,0:T(8,128)(2,1)} %copy.71.q_ref, bf16[2,128,128]{2,1,0:T(8,128)(2,1)} %pad_maximum_fusion.5.ko_ref, bf16[2,128,128]{2,1,0:T(8,128)(2,1)} %add_convert_fusion.1.vo_ref, bf16[4096,128]{1,0:T(8,128)(2,1)} %constant_dynamic-update-slice_fusion.11.kc_ref, ...), custom_call_target="tpu_custom_call" | custom-call | flops 2768240640 | bytes 3407872 | tf_op jit(solution)/shard_map/pallas_call | solution.py:64
  174.0 1.7 slice_bitcast_fusion
  (244 shorter events, 28.4 us)
Async XLA Ops:
  7.2 3.2 %copy-start.38 = (bf16[64,128]{1,0:T(8,128)(2,1)S(1)}, bf16[64,128]{1,0:T(8,128)(2,1)}, u32[]{:S(2)}) copy-start(bf16[64,128]{1,0:T(8,128)(2,1)} %param.27) | copy-start | bytes 49156
  7.2 3.2 %copy-start.37 = (bf16[64,128]{1,0:T(8,128)(2,1)S(1)}, bf16[64,128]{1,0:T(8,128)(2,1)}, u32[]{:S(2)}) copy-start(bf16[64,128]{1,0:T(8,128)(2,1)} %param.26) | copy-start | bytes 49156
  7.2 3.2 %copy-start.36 = (bf16[80,128]{1,0:T(8,128)(2,1)S(1)}, bf16[80,128]{1,0:T(8,128)(2,1)}, u32[]{:S(2)}) copy-start(bf16[80,128]{1,0:T(8,128)(2,1)} %param.24) | copy-start | bytes 61444
  7.2 3.1 %copy-start.35 = (bf16[80,128]{1,0:T(8,128)(2,1)S(1)}, bf16[80,128]{1,0:T(8,128)(2,1)}, u32[]{:S(2)}) copy-start(bf16[80,128]{1,0:T(8,128)(2,1)} %param.22) | copy-start | bytes 61444
  7.2 3.0 %copy-start.34 = (bf16[80,640]{1,0:T(8,128)(2,1)S(1)}, bf16[80,640]{1,0:T(8,128)(2,1)}, u32[]{:S(2)}) copy-start(bf16[80,640]{1,0:T(8,128)(2,1)} %param.20) | copy-start | bytes 307204
  7.2 13.5 %copy-start.43 = (s32[1,64]{1,0:T(1,128)S(1)}, s32[1,64]{1,0:T(1,128)}, u32[]{:S(2)}) copy-start(s32[1,64]{1,0:T(1,128)} %param.18) | copy-start | bytes 772
  7.2 13.8 %copy-start.41 = (bf16[640]{0:T(1024)(128)(2,1)S(1)}, bf16[640]{0:T(1024)(128)(2,1)}, u32[]{:S(2)}) copy-start(bf16[640]{0:T(1024)(128)(2,1)} %param.21) | copy-start | bytes 3844
  7.2 15.5 %copy-start.44 = (s32[128]{0:T(128)S(1)}, s32[128]{0:T(128)}, u32[]{:S(2)}) copy-start(s32[128]{0:T(128)} %param.16) | copy-start | bytes 1540
  7.2 125.6 %all-gather.2.cloned.1.call-start = ((), (), s32[]{:S(2)}) async-start(), calls=%async_computation | async-start | bytes 2949120 | tf_op jit(solution)/shard_map/all_gather | solution.py:132
  10.3 35.2 %copy-start.45 = (bf16[128]{0:T(256)(128)(2,1)S(1)}, bf16[128]{0:T(256)(128)(2,1)}, u32[]{:S(2)}) copy-start(bf16[128]{0:T(256)(128)(2,1)} %param.23) | copy-start | bytes 772
  10.3 35.2 %copy-start.46 = (bf16[128]{0:T(256)(128)(2,1)S(1)}, bf16[128]{0:T(256)(128)(2,1)}, u32[]{:S(2)}) copy-start(bf16[128]{0:T(256)(128)(2,1)} %param.25) | copy-start | bytes 772
  10.3 35.2 %copy-start.39 = (bf16[5120]{0:T(1024)(128)(2,1)S(1)}, bf16[5120]{0:T(1024)(128)(2,1)}, u32[]{:S(2)}) copy-start(bf16[5120]{0:T(1024)(128)(2,1)} %param.19) | copy-start | bytes 30724
  10.4 12.3 %collective-permute-start.2 = (bf16[720,128]{1,0:T(8,128)(2,1)S(1)}, bf16[720,128]{1,0:T(8,128)(2,1)S(1)}, u32[]{:S(2)}, u32[]{:S(2)}) collective-permute-start(bf16[720,128]{1,0:T(8,128)(2,1)S(1)} %constant_dynamic-update-slice_fusion), channel_id=1, source_target_pairs={{0,128},{128,256},{256,384},{384,0},{1,129},{129,257},{257,385},{3... | collective-permute-start | bytes 552968 | tf_op jit(solution)/shard_map/ppermute | solution.py:87
  13.0 15.9 %collective-permute-start.1 = (bf16[720,128]{1,0:T(8,128)(2,1)S(1)}, bf16[720,128]{1,0:T(8,128)(2,1)S(1)}, u32[]{:S(2)}, u32[]{:S(2)}) collective-permute-start(bf16[720,128]{1,0:T(8,128)(2,1)S(1)} %constant_dynamic-update-slice_fusion), channel_id=1, source_target_pairs={{0,256},{128,384},{256,0},{384,128},{1,257},{129,385},{257,1},{385... | collective-permute-start | bytes 552968 | tf_op jit(solution)/shard_map/ppermute | solution.py:87
  18.0 14.3 %collective-permute-start = (bf16[720,128]{1,0:T(8,128)(2,1)S(1)}, bf16[720,128]{1,0:T(8,128)(2,1)S(1)}, u32[]{:S(2)}, u32[]{:S(2)}) collective-permute-start(bf16[720,128]{1,0:T(8,128)(2,1)S(1)} %constant_dynamic-update-slice_fusion), channel_id=1, source_target_pairs={{0,384},{128,0},{256,128},{384,256},{1,385},{129,1},{257,129},{385... | collective-permute-start | bytes 552968 | tf_op jit(solution)/shard_map/ppermute | solution.py:87
  22.8 42.2 %copy-start.25 = (f32[128,64]{0,1:T(8,128)}, f32[128,64]{0,1:T(8,128)S(1)}, u32[]{:S(2)}) copy-start(f32[128,64]{0,1:T(8,128)S(1)} %get-tuple-element.82) | copy-start | bytes 98308
  32.3 32.6 %copy-start.23 = (bf16[720,128]{1,0:T(8,128)(2,1)}, bf16[720,128]{1,0:T(8,128)(2,1)S(1)}, u32[]{:S(2)}) copy-start(bf16[720,128]{1,0:T(8,128)(2,1)S(1)} %collective-permute-done) | copy-start | bytes 552964
  32.4 26.9 %collective-permute-start.7 = (bf16[4,720,128]{2,1,0:T(8,128)(2,1)S(1)}, bf16[4,720,128]{2,1,0:T(8,128)(2,1)S(1)}, u32[]{:S(2)}, u32[]{:S(2)}) collective-permute-start(bf16[4,720,128]{2,1,0:T(8,128)(2,1)S(1)} %pad_maximum_fusion), channel_id=1, source_target_pairs={{0,112},{16,0},{32,16},{48,32},{64,48},{80,64},{96,80},{112,96},{1... | collective-permute-start | bytes 2211848 | tf_op jit(solution)/shard_map/ppermute | solution.py:87
  43.5 21.3 %collective-permute-start.3 = (bf16[4,720,128]{2,1,0:T(8,128)(2,1)S(1)}, bf16[4,720,128]{2,1,0:T(8,128)(2,1)S(1)}, u32[]{:S(2)}, u32[]{:S(2)}) collective-permute-start(bf16[4,720,128]{2,1,0:T(8,128)(2,1)S(1)} %pad_maximum_fusion), channel_id=1, source_target_pairs={{0,16},{16,32},{32,48},{48,64},{64,80},{80,96},{96,112},{112,0},{1... | collective-permute-start | bytes 2211848 | tf_op jit(solution)/shard_map/ppermute | solution.py:87
  47.7 24.8 %collective-permute-start.13 = (bf16[4,720,128]{2,1,0:T(8,128)(2,1)S(1)}, bf16[4,720,128]{2,1,0:T(8,128)(2,1)S(1)}, u32[]{:S(2)}, u32[]{:S(2)}) collective-permute-start(bf16[4,720,128]{2,1,0:T(8,128)(2,1)S(1)} %pad_maximum_fusion), channel_id=1, source_target_pairs={{0,8},{8,0},{1,9},{9,1},{2,10},{10,2},{3,11},{11,3},{4,12},{12,4},... | collective-permute-start | bytes 2211848 | tf_op jit(solution)/shard_map/ppermute | solution.py:87
  59.3 33.9 %copy-start.3 = (bf16[4,720,128]{2,1,0:T(8,128)(2,1)}, bf16[4,720,128]{2,1,0:T(8,128)(2,1)S(1)}, u32[]{:S(2)}) copy-start(bf16[4,720,128]{2,1,0:T(8,128)(2,1)S(1)} %collective-permute-done.7) | copy-start | bytes 2211844
  59.3 20.7 %collective-permute-start.8 = (bf16[4,720,128]{2,1,0:T(8,128)(2,1)S(1)}, bf16[4,720,128]{2,1,0:T(8,128)(2,1)S(1)}, u32[]{:S(2)}, u32[]{:S(2)}) collective-permute-start(bf16[4,720,128]{2,1,0:T(8,128)(2,1)S(1)} %collective-permute-done.7), channel_id=1, source_target_pairs={{0,112},{16,0},{32,16},{48,32},{64,48},{80,64},{96,80},{112,96},{1... | collective-permute-start | bytes 2211848 | tf_op jit(solution)/shard_map/ppermute | solution.py:87
  64.9 28.3 %copy-start.5 = (bf16[4,720,128]{2,1,0:T(8,128)(2,1)}, bf16[4,720,128]{2,1,0:T(8,128)(2,1)S(1)}, u32[]{:S(2)}) copy-start(bf16[4,720,128]{2,1,0:T(8,128)(2,1)S(1)} %collective-permute-done.3) | copy-start | bytes 2211844
  64.9 20.6 %collective-permute-start.4 = (bf16[4,720,128]{2,1,0:T(8,128)(2,1)S(1)}, bf16[4,720,128]{2,1,0:T(8,128)(2,1)S(1)}, u32[]{:S(2)}, u32[]{:S(2)}) collective-permute-start(bf16[4,720,128]{2,1,0:T(8,128)(2,1)S(1)} %collective-permute-done.3), channel_id=1, source_target_pairs={{0,16},{16,32},{32,48},{48,64},{64,80},{80,96},{96,112},{112,0},{1... | collective-permute-start | bytes 2211848 | tf_op jit(solution)/shard_map/ppermute | solution.py:87
  66.9 23.8 %collective-permute-start.15 = (bf16[4,720,128]{2,1,0:T(8,128)(2,1)S(1)}, bf16[4,720,128]{2,1,0:T(8,128)(2,1)S(1)}, u32[]{:S(2)}, u32[]{:S(2)}) collective-permute-start(bf16[4,720,128]{2,1,0:T(8,128)(2,1)S(1)} %collective-permute-done.7), channel_id=1, source_target_pairs={{0,8},{8,0},{1,9},{9,1},{2,10},{10,2},{3,11},{11,3},{4,12},{12,4},... | collective-permute-start | bytes 2211848 | tf_op jit(solution)/shard_map/ppermute | solution.py:87
  68.8 24.3 %collective-permute-start.14 = (bf16[4,720,128]{2,1,0:T(8,128)(2,1)S(1)}, bf16[4,720,128]{2,1,0:T(8,128)(2,1)S(1)}, u32[]{:S(2)}, u32[]{:S(2)}) collective-permute-start(bf16[4,720,128]{2,1,0:T(8,128)(2,1)S(1)} %collective-permute-done.3), channel_id=1, source_target_pairs={{0,8},{8,0},{1,9},{9,1},{2,10},{10,2},{3,11},{11,3},{4,12},{12,4},... | collective-permute-start | bytes 2211848 | tf_op jit(solution)/shard_map/ppermute | solution.py:87
  72.5 20.7 %copy-start.7 = (bf16[4,720,128]{2,1,0:T(8,128)(2,1)}, bf16[4,720,128]{2,1,0:T(8,128)(2,1)S(1)}, u32[]{:S(2)}) copy-start(bf16[4,720,128]{2,1,0:T(8,128)(2,1)S(1)} %collective-permute-done.13) | copy-start | bytes 2211844
  79.9 27.5 %copy-start.11 = (bf16[4,720,128]{2,1,0:T(8,128)(2,1)}, bf16[4,720,128]{2,1,0:T(8,128)(2,1)S(1)}, u32[]{:S(2)}) copy-start(bf16[4,720,128]{2,1,0:T(8,128)(2,1)S(1)} %collective-permute-done.8) | copy-start | bytes 2211844
  80.0 19.9 %collective-permute-start.9 = (bf16[4,720,128]{2,1,0:T(8,128)(2,1)S(1)}, bf16[4,720,128]{2,1,0:T(8,128)(2,1)S(1)}, u32[]{:S(2)}, u32[]{:S(2)}) collective-permute-start(bf16[4,720,128]{2,1,0:T(8,128)(2,1)S(1)} %collective-permute-done.8), channel_id=1, source_target_pairs={{0,112},{16,0},{32,16},{48,32},{64,48},{80,64},{96,80},{112,96},{1... | collective-permute-start | bytes 2211848 | tf_op jit(solution)/shard_map/ppermute | solution.py:87
  85.6 21.9 %copy-start.9 = (bf16[4,720,128]{2,1,0:T(8,128)(2,1)}, bf16[4,720,128]{2,1,0:T(8,128)(2,1)S(1)}, u32[]{:S(2)}) copy-start(bf16[4,720,128]{2,1,0:T(8,128)(2,1)S(1)} %collective-permute-done.4) | copy-start | bytes 2211844
  85.6 21.8 %collective-permute-start.5 = (bf16[4,720,128]{2,1,0:T(8,128)(2,1)S(1)}, bf16[4,720,128]{2,1,0:T(8,128)(2,1)S(1)}, u32[]{:S(2)}, u32[]{:S(2)}) collective-permute-start(bf16[4,720,128]{2,1,0:T(8,128)(2,1)S(1)} %collective-permute-done.4), channel_id=1, source_target_pairs={{0,16},{16,32},{32,48},{48,64},{64,80},{80,96},{96,112},{112,0},{1... | collective-permute-start | bytes 2211848 | tf_op jit(solution)/shard_map/ppermute | solution.py:87
  87.6 25.4 %collective-permute-start.17 = (bf16[4,720,128]{2,1,0:T(8,128)(2,1)S(1)}, bf16[4,720,128]{2,1,0:T(8,128)(2,1)S(1)}, u32[]{:S(2)}, u32[]{:S(2)}) collective-permute-start(bf16[4,720,128]{2,1,0:T(8,128)(2,1)S(1)} %collective-permute-done.8), channel_id=1, source_target_pairs={{0,8},{8,0},{1,9},{9,1},{2,10},{10,2},{3,11},{11,3},{4,12},{12,4},... | collective-permute-start | bytes 2211848 | tf_op jit(solution)/shard_map/ppermute | solution.py:87
  90.7 2.5 %copy-start.13 = (bf16[4,720,128]{2,1,0:T(8,128)(2,1)}, bf16[4,720,128]{2,1,0:T(8,128)(2,1)S(1)}, u32[]{:S(2)}) copy-start(bf16[4,720,128]{2,1,0:T(8,128)(2,1)S(1)} %collective-permute-done.15) | copy-start | bytes 2211844
  90.7 20.2 %collective-permute-start.16 = (bf16[4,720,128]{2,1,0:T(8,128)(2,1)S(1)}, bf16[4,720,128]{2,1,0:T(8,128)(2,1)S(1)}, u32[]{:S(2)}, u32[]{:S(2)}) collective-permute-start(bf16[4,720,128]{2,1,0:T(8,128)(2,1)S(1)} %collective-permute-done.4), channel_id=1, source_target_pairs={{0,8},{8,0},{1,9},{9,1},{2,10},{10,2},{3,11},{11,3},{4,12},{12,4},... | collective-permute-start | bytes 2211848 | tf_op jit(solution)/shard_map/ppermute | solution.py:87
  93.2 17.7 %copy-start.15 = (bf16[4,720,128]{2,1,0:T(8,128)(2,1)}, bf16[4,720,128]{2,1,0:T(8,128)(2,1)S(1)}, u32[]{:S(2)}) copy-start(bf16[4,720,128]{2,1,0:T(8,128)(2,1)S(1)} %collective-permute-done.14) | copy-start | bytes 2211844
  99.8 18.4 %collective-permute-start.12 = (bf16[2,720,128]{2,1,0:T(8,128)(2,1)S(1)}, bf16[2,720,128]{2,1,0:T(8,128)(2,1)S(1)}, u32[]{:S(2)}, u32[]{:S(2)}) collective-permute-start(bf16[2,720,128]{2,1,0:T(8,128)(2,1)S(1)} %slice.333), channel_id=1, source_target_pairs={{24,0},{16,8},{40,16},{32,24},{56,32},{48,40},{72,48},{64,56},{88,... | collective-permute-start | bytes 1105928 | tf_op jit(solution)/shard_map/ppermute | solution.py:160
  102.6 19.5 %collective-permute-start.10 = (bf16[2,720,128]{2,1,0:T(8,128)(2,1)S(1)}, bf16[2,720,128]{2,1,0:T(8,128)(2,1)S(1)}, u32[]{:S(2)}, u32[]{:S(2)}) collective-permute-start(bf16[2,720,128]{2,1,0:T(8,128)(2,1)S(1)} %slice.333), channel_id=1, source_target_pairs={{0,112},{16,0},{32,16},{48,32},{64,48},{80,64},{96,80},{112,96},{1... | collective-permute-start | bytes 1105928 | tf_op jit(solution)/shard_map/ppermute | solution.py:87
  107.4 14.5 %collective-permute-start.11 = (bf16[2,720,128]{2,1,0:T(8,128)(2,1)S(1)}, bf16[2,720,128]{2,1,0:T(8,128)(2,1)S(1)}, u32[]{:S(2)}, u32[]{:S(2)}) collective-permute-start(bf16[2,720,128]{2,1,0:T(8,128)(2,1)S(1)} %slice.332), channel_id=1, source_target_pairs={{120,0},{112,8},{8,16},{0,24},{24,32},{16,40},{40,48},{32,56},{56,... | collective-permute-start | bytes 1105928 | tf_op jit(solution)/shard_map/ppermute | solution.py:159
  111.0 2.7 %copy-start.19 = (bf16[4,720,128]{2,1,0:T(8,128)(2,1)}, bf16[4,720,128]{2,1,0:T(8,128)(2,1)S(1)}, u32[]{:S(2)}) copy-start(bf16[4,720,128]{2,1,0:T(8,128)(2,1)S(1)} %collective-permute-done.16) | copy-start | bytes 2211844
  111.0 18.4 %collective-permute-start.6 = (bf16[2,720,128]{2,1,0:T(8,128)(2,1)S(1)}, bf16[2,720,128]{2,1,0:T(8,128)(2,1)S(1)}, u32[]{:S(2)}, u32[]{:S(2)}) collective-permute-start(bf16[2,720,128]{2,1,0:T(8,128)(2,1)S(1)} %slice.332), channel_id=1, source_target_pairs={{0,16},{16,32},{32,48},{48,64},{64,80},{80,96},{96,112},{112,0},{1... | collective-permute-start | bytes 1105928 | tf_op jit(solution)/shard_map/ppermute | solution.py:87
  112.9 9.0 %copy-start.17 = (bf16[4,720,128]{2,1,0:T(8,128)(2,1)}, bf16[4,720,128]{2,1,0:T(8,128)(2,1)S(1)}, u32[]{:S(2)}) copy-start(bf16[4,720,128]{2,1,0:T(8,128)(2,1)S(1)} %collective-permute-done.17) | copy-start | bytes 2211844
  114.3 15.1 %collective-permute-start.18 = (bf16[4,720,128]{2,1,0:T(8,128)(2,1)S(1)}, bf16[4,720,128]{2,1,0:T(8,128)(2,1)S(1)}, u32[]{:S(2)}, u32[]{:S(2)}) collective-permute-start(bf16[4,720,128]{2,1,0:T(8,128)(2,1)S(1)} %collective-permute-done.5), channel_id=1, source_target_pairs={{0,8},{8,0},{1,9},{9,1},{2,10},{10,2},{3,11},{11,3},{4,12},{12,4},... | collective-permute-start | bytes 2211848 | tf_op jit(solution)/shard_map/ppermute | solution.py:87
  118.2 11.2 %collective-permute-start.19 = (bf16[4,720,128]{2,1,0:T(8,128)(2,1)S(1)}, bf16[4,720,128]{2,1,0:T(8,128)(2,1)S(1)}, u32[]{:S(2)}, u32[]{:S(2)}) collective-permute-start(bf16[4,720,128]{2,1,0:T(8,128)(2,1)S(1)} %collective-permute-done.9), channel_id=1, source_target_pairs={{0,8},{8,0},{1,9},{9,1},{2,10},{10,2},{3,11},{11,3},{4,12},{12,4},... | collective-permute-start | bytes 2211848 | tf_op jit(solution)/shard_map/ppermute | solution.py:87
  132.9 2.5 %copy-start = (bf16[2,128,5120]{1,2,0:T(8,128)(2,1)S(1)}, bf16[2,128,5120]{1,2,0:T(8,128)(2,1)}, u32[]{:S(2)}) copy-start(bf16[2,128,5120]{1,2,0:T(8,128)(2,1)} %all-gather.2.cloned.1.call-done) | copy-start | bytes 7864324
  155.4 2.3 %copy-start.30 = (bf16[4,64,128]{2,1,0:T(8,128)(2,1)S(1)}, bf16[4,64,128]{2,1,0:T(8,128)(2,1)}, u32[]{:S(2)}) copy-start(bf16[4,64,128]{2,1,0:T(8,128)(2,1)} %get-tuple-element.27) | copy-start | bytes 196612
  155.4 3.0 %copy-start.29 = (bf16[4,64,128]{2,1,0:T(8,128)(2,1)S(1)}, bf16[4,64,128]{2,1,0:T(8,128)(2,1)}, u32[]{:S(2)}) copy-start(bf16[4,64,128]{2,1,0:T(8,128)(2,1)} %get-tuple-element.28) | copy-start | bytes 196612
  155.6 4.1 %copy-start.27 = (f32[128,64]{1,0:T(8,128)S(1)}, f32[128,64]{1,0:T(8,128)}, u32[]{:S(2)}) copy-start(f32[128,64]{1,0:T(8,128)} %copy.68) | copy-start | bytes 98308
  155.6 4.1 %copy-start.28 = (f32[128,64]{1,0:T(8,128)S(1)}, f32[128,64]{1,0:T(8,128)}, u32[]{:S(2)}) copy-start(f32[128,64]{1,0:T(8,128)} %copy.69) | copy-start | bytes 98308
  (20 other events, 22.9 us)
Sparse Core Ops, SparseCore 0:
  20.1 88.9 all-gather.1

commit v14 on v13

--- a/solution.py
+++ b/solution.py
@@ -121,7 +121,8 @@
     total_blocks = -(-used // w_rows)
     lead = jnp.zeros((key_start - w_len, HD), w_query.dtype)
     tail = jnp.zeros((total_blocks * w_rows - used, HD), w_query.dtype)
-    packed = jnp.concatenate(w_parts + [lead, cache_keys, cache_values, tail], axis=0)
+    q_blocks = jnp.transpose(w_query.reshape(w_rows, q_cols // HD, HD), (1, 0, 2)).reshape(-1, HD)
+    packed = jnp.concatenate([q_blocks, w_key, w_value, lead, cache_keys, cache_values, tail], axis=0)
 
     n_ylo = lax.axis_size("ylo")
     n_z = lax.axis_size("z")

time: 184 us -> 188 us (1.022)
  the two profiles are of different devices: /device:TPU:40 before, /device:TPU:1 now
where the time goes in v14:
time: 188 us; the launch traced here: 187 us
  starting transfers between devices  73.2 us (39%)
  waiting for transfers between devices  33.5 us (18%)
  local copies, waits for them, and re-layouts  33 us (18%)
  between operations  16 us (9%)
  Pallas kernels  13.4 us (7%)
  matrix products  9.78 us (5%)
  other arithmetic  7.9 us (4%)
    ppermute x18, starting transfers between devices, shifted(): return lax.ppermute(x, axis, pairs)  63 us
    ppermute x18, waiting for transfers between devices, shifted(): return lax.ppermute(x, axis, pairs)  30.6 us
    unnamed x139, local copies, waits for them, and re-layouts  20.8 us
    pallas_call x1, Pallas kernels, attend(): pl.pallas_call(attend_kernel, grid=(passes,), in_specs=[pl.BlockSpec((Non...  13.4 us
    dot_general x16, matrix products, local(): jnp.einsum('rki,kjid->rjd', normed5[:, :, offset % n_z, core, :], piece.r...  9.78 us
    ppermute x1, starting transfers between devices, local(): lax.ppermute(backward[split:], ('z', 'core'), to_partner_back)  8.24 us
  transfers between devices with their start and end apart: 21, of which 7 were waited for; matrix products, arithmetic and copies ran while one was open for 8% of the time, Pallas kernels for 0%

profile of v14, /device:TPU:1, one launch (start us, length us, event | category | flops | bytes accessed | tf_op | source)
XLA Modules:
  0.0 186.9 jit_solution(6155755193299920921)
XLA Ops:
  7.3 1.1 copy.72
  8.4 1.1 copy.73
  9.5 0.7 pad_maximum_fusion.3
  10.6 5.0 %collective-permute-start.1 = (bf16[720,128]{1,0:T(8,128)(2,1)S(1)}, bf16[720,128]{1,0:T(8,128)(2,1)S(1)}, u32[]{:S(2)}, u32[]{:S(2)}) collective-permute-start(bf16[720,128]{1,0:T(8,128)(2,1)S(1)} %constant_dynamic-update-slice_fusion), channel_id=1, source_target_pairs={{0,256},{128,384},{256,0},{384,128},{1,257},{129,385},{257,1},{385... | collective-permute-start | bytes 552968 | tf_op jit(solution)/shard_map/ppermute | solution.py:87
  15.6 3.2 %collective-permute-start.2 = (bf16[720,128]{1,0:T(8,128)(2,1)S(1)}, bf16[720,128]{1,0:T(8,128)(2,1)S(1)}, u32[]{:S(2)}, u32[]{:S(2)}) collective-permute-start(bf16[720,128]{1,0:T(8,128)(2,1)S(1)} %constant_dynamic-update-slice_fusion), channel_id=1, source_target_pairs={{0,128},{128,256},{256,384},{384,0},{1,129},{129,257},{257,385},{3... | collective-permute-start | bytes 552968 | tf_op jit(solution)/shard_map/ppermute | solution.py:87
  18.8 3.9 %collective-permute-start = (bf16[720,128]{1,0:T(8,128)(2,1)S(1)}, bf16[720,128]{1,0:T(8,128)(2,1)S(1)}, u32[]{:S(2)}, u32[]{:S(2)}) collective-permute-start(bf16[720,128]{1,0:T(8,128)(2,1)S(1)} %constant_dynamic-update-slice_fusion), channel_id=1, source_target_pairs={{0,384},{128,0},{256,128},{384,256},{1,385},{129,1},{257,129},{385... | collective-permute-start | bytes 552968 | tf_op jit(solution)/shard_map/ppermute | solution.py:87
  25.6 6.4 %collective-permute-done = bf16[720,128]{1,0:T(8,128)(2,1)S(1)} collective-permute-done((bf16[720,128]{1,0:T(8,128)(2,1)S(1)}, bf16[720,128]{1,0:T(8,128)(2,1)S(1)}, u32[]{:S(2)}, u32[]{:S(2)}) %collective-permute-start) | collective-permute-done | bytes 184352 | tf_op jit(solution)/shard_map/ppermute | solution.py:87
  32.8 4.5 %collective-permute-start.3 = (bf16[4,720,128]{2,1,0:T(8,128)(2,1)S(1)}, bf16[4,720,128]{2,1,0:T(8,128)(2,1)S(1)}, u32[]{:S(2)}, u32[]{:S(2)}) collective-permute-start(bf16[4,720,128]{2,1,0:T(8,128)(2,1)S(1)} %pad_maximum_fusion), channel_id=1, source_target_pairs={{0,16},{16,32},{32,48},{48,64},{64,80},{80,96},{96,112},{112,0},{1... | collective-permute-start | bytes 2211848 | tf_op jit(solution)/shard_map/ppermute | solution.py:87
  37.6 8.6 %collective-permute-start.7 = (bf16[4,720,128]{2,1,0:T(8,128)(2,1)S(1)}, bf16[4,720,128]{2,1,0:T(8,128)(2,1)}, u32[]{:S(2)}, u32[]{:S(2)}) collective-permute-start(bf16[4,720,128]{2,1,0:T(8,128)(2,1)S(1)} %pad_maximum_fusion), channel_id=1, source_target_pairs={{0,112},{16,0},{32,16},{48,32},{64,48},{80,64},{96,80},{112,96},{1... | collective-permute-start | bytes 2211848 | tf_op jit(solution)/shard_map/ppermute | solution.py:87
  46.9 0.7 copy.95
  47.6 0.7 copy.96
  48.4 2.7 %collective-permute-start.13 = (bf16[4,720,128]{2,1,0:T(8,128)(2,1)S(1)}, bf16[4,720,128]{2,1,0:T(8,128)(2,1)S(1)}, u32[]{:S(2)}, u32[]{:S(2)}) collective-permute-start(bf16[4,720,128]{2,1,0:T(8,128)(2,1)S(1)} %pad_maximum_fusion), channel_id=1, source_target_pairs={{0,8},{8,0},{1,9},{9,1},{2,10},{10,2},{3,11},{11,3},{4,12},{12,4},... | collective-permute-start | bytes 2211848 | tf_op jit(solution)/shard_map/ppermute | solution.py:87
  51.7 8.7 %collective-permute-done.3 = bf16[4,720,128]{2,1,0:T(8,128)(2,1)S(1)} collective-permute-done((bf16[4,720,128]{2,1,0:T(8,128)(2,1)S(1)}, bf16[4,720,128]{2,1,0:T(8,128)(2,1)S(1)}, u32[]{:S(2)}, u32[]{:S(2)}) %collective-permute-start.3) | collective-permute-done | bytes 737312 | tf_op jit(solution)/shard_map/ppermute | solution.py:87
  60.5 1.9 %collective-permute-start.4 = (bf16[4,720,128]{2,1,0:T(8,128)(2,1)S(1)}, bf16[4,720,128]{2,1,0:T(8,128)(2,1)S(1)}, u32[]{:S(2)}, u32[]{:S(2)}) collective-permute-start(bf16[4,720,128]{2,1,0:T(8,128)(2,1)S(1)} %collective-permute-done.3), channel_id=1, source_target_pairs={{0,16},{16,32},{32,48},{48,64},{64,80},{80,96},{96,112},{112,0},{1... | collective-permute-start | bytes 2211848 | tf_op jit(solution)/shard_map/ppermute | solution.py:87
  62.4 0.9 fusion.80
  63.3 4.6 %collective-permute-start.8 = (bf16[4,720,128]{2,1,0:T(8,128)(2,1)}, bf16[4,720,128]{2,1,0:T(8,128)(2,1)S(1)}, u32[]{:S(2)}, u32[]{:S(2)}) collective-permute-start(bf16[4,720,128]{2,1,0:T(8,128)(2,1)} %collective-permute-done.7), channel_id=1, source_target_pairs={{0,112},{16,0},{32,16},{48,32},{64,48},{80,64},{96,80},{112,96},{1... | collective-permute-start | bytes 2211848 | tf_op jit(solution)/shard_map/ppermute | solution.py:87
  67.9 3.5 %collective-permute-start.14 = (bf16[4,720,128]{2,1,0:T(8,128)(2,1)S(1)}, bf16[4,720,128]{2,1,0:T(8,128)(2,1)S(1)}, u32[]{:S(2)}, u32[]{:S(2)}) collective-permute-start(bf16[4,720,128]{2,1,0:T(8,128)(2,1)S(1)} %collective-permute-done.3), channel_id=1, source_target_pairs={{0,8},{8,0},{1,9},{9,1},{2,10},{10,2},{3,11},{11,3},{4,12},{12,4},... | collective-permute-start | bytes 2211848 | tf_op jit(solution)/shard_map/ppermute | solution.py:87
  71.4 1.9 %collective-permute-start.15 = (bf16[4,720,128]{2,1,0:T(8,128)(2,1)}, bf16[4,720,128]{2,1,0:T(8,128)(2,1)S(1)}, u32[]{:S(2)}, u32[]{:S(2)}) collective-permute-start(bf16[4,720,128]{2,1,0:T(8,128)(2,1)} %collective-permute-done.7), channel_id=1, source_target_pairs={{0,8},{8,0},{1,9},{9,1},{2,10},{10,2},{3,11},{11,3},{4,12},{12,4},... | collective-permute-start | bytes 2211848 | tf_op jit(solution)/shard_map/ppermute | solution.py:87
  74.6 6.0 %collective-permute-done.4 = bf16[4,720,128]{2,1,0:T(8,128)(2,1)S(1)} collective-permute-done((bf16[4,720,128]{2,1,0:T(8,128)(2,1)S(1)}, bf16[4,720,128]{2,1,0:T(8,128)(2,1)S(1)}, u32[]{:S(2)}, u32[]{:S(2)}) %collective-permute-start.4) | collective-permute-done | bytes 737312 | tf_op jit(solution)/shard_map/ppermute | solution.py:87
  80.7 1.9 %collective-permute-start.5 = (bf16[4,720,128]{2,1,0:T(8,128)(2,1)S(1)}, bf16[4,720,128]{2,1,0:T(8,128)(2,1)S(1)}, u32[]{:S(2)}, u32[]{:S(2)}) collective-permute-start(bf16[4,720,128]{2,1,0:T(8,128)(2,1)S(1)} %collective-permute-done.4), channel_id=1, source_target_pairs={{0,16},{16,32},{32,48},{48,64},{64,80},{80,96},{96,112},{112,0},{1... | collective-permute-start | bytes 2211848 | tf_op jit(solution)/shard_map/ppermute | solution.py:87
  82.7 5.3 %collective-permute-start.9 = (bf16[4,720,128]{2,1,0:T(8,128)(2,1)S(1)}, bf16[4,720,128]{2,1,0:T(8,128)(2,1)S(1)}, u32[]{:S(2)}, u32[]{:S(2)}) collective-permute-start(bf16[4,720,128]{2,1,0:T(8,128)(2,1)S(1)} %collective-permute-done.8), channel_id=1, source_target_pairs={{0,112},{16,0},{32,16},{48,32},{64,48},{80,64},{96,80},{112,96},{1... | collective-permute-start | bytes 2211848 | tf_op jit(solution)/shard_map/ppermute | solution.py:87
  88.0 4.3 %collective-permute-start.16 = (bf16[4,720,128]{2,1,0:T(8,128)(2,1)S(1)}, bf16[4,720,128]{2,1,0:T(8,128)(2,1)S(1)}, u32[]{:S(2)}, u32[]{:S(2)}) collective-permute-start(bf16[4,720,128]{2,1,0:T(8,128)(2,1)S(1)} %collective-permute-done.4), channel_id=1, source_target_pairs={{0,8},{8,0},{1,9},{9,1},{2,10},{10,2},{3,11},{11,3},{4,12},{12,4},... | collective-permute-start | bytes 2211848 | tf_op jit(solution)/shard_map/ppermute | solution.py:87
  93.6 1.9 %collective-permute-start.17 = (bf16[4,720,128]{2,1,0:T(8,128)(2,1)S(1)}, bf16[4,720,128]{2,1,0:T(8,128)(2,1)S(1)}, u32[]{:S(2)}, u32[]{:S(2)}) collective-permute-start(bf16[4,720,128]{2,1,0:T(8,128)(2,1)S(1)} %collective-permute-done.8), channel_id=1, source_target_pairs={{0,8},{8,0},{1,9},{9,1},{2,10},{10,2},{3,11},{11,3},{4,12},{12,4},... | collective-permute-start | bytes 2211848 | tf_op jit(solution)/shard_map/ppermute | solution.py:87
  95.6 0.8 copy-done.13
  96.4 5.2 %collective-permute-done.9 = bf16[4,720,128]{2,1,0:T(8,128)(2,1)S(1)} collective-permute-done((bf16[4,720,128]{2,1,0:T(8,128)(2,1)S(1)}, bf16[4,720,128]{2,1,0:T(8,128)(2,1)S(1)}, u32[]{:S(2)}, u32[]{:S(2)}) %collective-permute-start.9) | collective-permute-done | bytes 737312 | tf_op jit(solution)/shard_map/ppermute | solution.py:87
  101.7 8.2 %collective-permute-start.12 = (bf16[2,720,128]{2,1,0:T(8,128)(2,1)S(1)}, bf16[2,720,128]{2,1,0:T(8,128)(2,1)S(1)}, u32[]{:S(2)}, u32[]{:S(2)}) collective-permute-start(bf16[2,720,128]{2,1,0:T(8,128)(2,1)S(1)} %slice.313), channel_id=1, source_target_pairs={{24,0},{16,8},{40,16},{32,24},{56,32},{48,40},{72,48},{64,56},{88,... | collective-permute-start | bytes 1105928 | tf_op jit(solution)/shard_map/ppermute | solution.py:161
  109.9 1.9 %collective-permute-start.10 = (bf16[2,720,128]{2,1,0:T(8,128)(2,1)S(1)}, bf16[2,720,128]{2,1,0:T(8,128)(2,1)S(1)}, u32[]{:S(2)}, u32[]{:S(2)}) collective-permute-start(bf16[2,720,128]{2,1,0:T(8,128)(2,1)S(1)} %slice.313), channel_id=1, source_target_pairs={{0,112},{16,0},{32,16},{48,32},{64,48},{80,64},{96,80},{112,96},{1... | collective-permute-start | bytes 1105928 | tf_op jit(solution)/shard_map/ppermute | solution.py:87
  111.9 1.9 %collective-permute-start.11 = (bf16[2,720,128]{2,1,0:T(8,128)(2,1)S(1)}, bf16[2,720,128]{2,1,0:T(8,128)(2,1)S(1)}, u32[]{:S(2)}, u32[]{:S(2)}) collective-permute-start(bf16[2,720,128]{2,1,0:T(8,128)(2,1)S(1)} %slice.312), channel_id=1, source_target_pairs={{120,0},{112,8},{8,16},{0,24},{24,32},{16,40},{40,48},{32,56},{56,... | collective-permute-start | bytes 1105928 | tf_op jit(solution)/shard_map/ppermute | solution.py:160
  114.0 3.4 %collective-permute-start.6 = (bf16[2,720,128]{2,1,0:T(8,128)(2,1)S(1)}, bf16[2,720,128]{2,1,0:T(8,128)(2,1)S(1)}, u32[]{:S(2)}, u32[]{:S(2)}) collective-permute-start(bf16[2,720,128]{2,1,0:T(8,128)(2,1)S(1)} %slice.312), channel_id=1, source_target_pairs={{0,16},{16,32},{32,48},{48,64},{64,80},{80,96},{96,112},{112,0},{1... | collective-permute-start | bytes 1105928 | tf_op jit(solution)/shard_map/ppermute | solution.py:87
  117.5 0.7 constant_dynamic-update-slice_fusion.17
  118.8 2.3 %collective-permute-start.18 = (bf16[4,720,128]{2,1,0:T(8,128)(2,1)S(1)}, bf16[4,720,128]{2,1,0:T(8,128)(2,1)S(1)}, u32[]{:S(2)}, u32[]{:S(2)}) collective-permute-start(bf16[4,720,128]{2,1,0:T(8,128)(2,1)S(1)} %collective-permute-done.5), channel_id=1, source_target_pairs={{0,8},{8,0},{1,9},{9,1},{2,10},{10,2},{3,11},{11,3},{4,12},{12,4},... | collective-permute-start | bytes 2211848 | tf_op jit(solution)/shard_map/ppermute | solution.py:87
  123.0 2.9 %collective-permute-done.11 = bf16[2,720,128]{2,1,0:T(8,128)(2,1)S(1)} collective-permute-done((bf16[2,720,128]{2,1,0:T(8,128)(2,1)S(1)}, bf16[2,720,128]{2,1,0:T(8,128)(2,1)S(1)}, u32[]{:S(2)}, u32[]{:S(2)}) %collective-permute-start.11) | collective-permute-done | bytes 368672 | tf_op jit(solution)/shard_map/ppermute | solution.py:160
  125.9 2.2 %collective-permute-start.19 = (bf16[4,720,128]{2,1,0:T(8,128)(2,1)S(1)}, bf16[4,720,128]{2,1,0:T(8,128)(2,1)S(1)}, u32[]{:S(2)}, u32[]{:S(2)}) collective-permute-start(bf16[4,720,128]{2,1,0:T(8,128)(2,1)S(1)} %collective-permute-done.9), channel_id=1, source_target_pairs={{0,8},{8,0},{1,9},{9,1},{2,10},{10,2},{3,11},{11,3},{4,12},{12,4},... | collective-permute-start | bytes 2211848 | tf_op jit(solution)/shard_map/ppermute | solution.py:87
  129.4 4.1 %collective-permute-done.6 = bf16[2,720,128]{2,1,0:T(8,128)(2,1)S(1)} collective-permute-done((bf16[2,720,128]{2,1,0:T(8,128)(2,1)S(1)}, bf16[2,720,128]{2,1,0:T(8,128)(2,1)S(1)}, u32[]{:S(2)}, u32[]{:S(2)}) %collective-permute-start.6) | collective-permute-done | bytes 368672 | tf_op jit(solution)/shard_map/ppermute | solution.py:87
  133.6 0.9 copy-done.1
  134.5 0.8 copy-done.19
  137.0 2.3 %slice_bitcast_fusion.2 = (bf16[128,5120]{0,1:T(8,128)(2,1)S(1)}, bf16[1,128,5120]{1,2,0:T(8,128)(2,1)S(1)}, bf16[1,128,5120]{1,2,0:T(8,128)(2,1)S(1)}) fusion(bf16[2,128,5120]{1,2,0:T(8,128)(2,1)} %all-gather.2.cloned.1.call-done), kind=kLoop, calls=%fused_computation.176 | loop fusion | bytes 6553600 | tf_op jit(solution)/shard_map/squeeze | solution.py:134
  139.7 0.7 multiply_reduce_fusion
  141.2 0.8 multiply_convert_fusion
  142.0 0.9 fusion.2
  143.0 0.9 fusion.1
  143.9 0.9 fusion
  145.6 1.7 convolution_bitcast_fusion.13
  157.2 0.8 fusion.13
  159.9 0.9 copy.98.q_ref
  163.5 0.7 pad_maximum_fusion.5.ko_ref
  164.8 13.4 %shard_map.149 = bf16[2,128,640]{2,1,0:T(8,128)(2,1)} custom-call(bf16[2,128,640]{2,1,0:T(8,128)(2,1)} %copy.98.q_ref, bf16[2,128,128]{2,1,0:T(8,128)(2,1)} %pad_maximum_fusion.5.ko_ref, bf16[2,128,128]{2,1,0:T(8,128)(2,1)} %add_convert_fusion.1.vo_ref, bf16[4096,128]{1,0:T(8,128)(2,1)} %constant_dynamic-update-slice_fusion.7.kc_ref, ...), custom_call_target="tpu_custom_call" | custom-call | flops 2768240640 | bytes 3407872 | tf_op jit(solution)/shard_map/pallas_call | solution.py:64
  178.3 1.7 slice_bitcast_fusion
  (234 shorter events, 29.7 us)
Async XLA Ops:
  7.2 3.1 %copy-start.30 = (bf16[80,640]{1,0:T(8,128)(2,1)S(1)}, bf16[80,640]{1,0:T(8,128)(2,1)}, u32[]{:S(2)}) copy-start(bf16[80,640]{1,0:T(8,128)(2,1)} %param.20) | copy-start | bytes 307204
  7.2 3.2 %copy-start.31 = (bf16[80,128]{1,0:T(8,128)(2,1)S(1)}, bf16[80,128]{1,0:T(8,128)(2,1)}, u32[]{:S(2)}) copy-start(bf16[80,128]{1,0:T(8,128)(2,1)} %param.22) | copy-start | bytes 61444
  7.2 3.3 %copy-start.32 = (bf16[80,128]{1,0:T(8,128)(2,1)S(1)}, bf16[80,128]{1,0:T(8,128)(2,1)}, u32[]{:S(2)}) copy-start(bf16[80,128]{1,0:T(8,128)(2,1)} %param.24) | copy-start | bytes 61444
  7.2 3.3 %copy-start.33 = (bf16[64,128]{1,0:T(8,128)(2,1)S(1)}, bf16[64,128]{1,0:T(8,128)(2,1)}, u32[]{:S(2)}) copy-start(bf16[64,128]{1,0:T(8,128)(2,1)} %param.26) | copy-start | bytes 49156
  7.2 3.3 %copy-start.34 = (bf16[64,128]{1,0:T(8,128)(2,1)S(1)}, bf16[64,128]{1,0:T(8,128)(2,1)}, u32[]{:S(2)}) copy-start(bf16[64,128]{1,0:T(8,128)(2,1)} %param.27) | copy-start | bytes 49156
  7.2 16.3 %copy-start.37 = (bf16[640]{0:T(1024)(128)(2,1)S(1)}, bf16[640]{0:T(1024)(128)(2,1)}, u32[]{:S(2)}) copy-start(bf16[640]{0:T(1024)(128)(2,1)} %param.21) | copy-start | bytes 3844
  7.2 16.3 %copy-start.39 = (s32[1,64]{1,0:T(1,128)S(1)}, s32[1,64]{1,0:T(1,128)}, u32[]{:S(2)}) copy-start(s32[1,64]{1,0:T(1,128)} %param.18) | copy-start | bytes 772
  7.2 129.8 %all-gather.2.cloned.1.call-start = ((), (), s32[]{:S(2)}) async-start(), calls=%async_computation | async-start | bytes 2949120 | tf_op jit(solution)/shard_map/all_gather | solution.py:133
  9.5 16.1 %copy-start.40 = (s32[128]{0:T(128)S(1)}, s32[128]{0:T(128)}, u32[]{:S(2)}) copy-start(s32[128]{0:T(128)} %param.16) | copy-start | bytes 1540
  10.4 35.7 %copy-start.35 = (bf16[5120]{0:T(1024)(128)(2,1)S(1)}, bf16[5120]{0:T(1024)(128)(2,1)}, u32[]{:S(2)}) copy-start(bf16[5120]{0:T(1024)(128)(2,1)} %param.19) | copy-start | bytes 30724
  10.5 36.4 %copy-start.41 = (bf16[128]{0:T(256)(128)(2,1)S(1)}, bf16[128]{0:T(256)(128)(2,1)}, u32[]{:S(2)}) copy-start(bf16[128]{0:T(256)(128)(2,1)} %param.23) | copy-start | bytes 772
  10.6 37.8 %copy-start.42 = (bf16[128]{0:T(256)(128)(2,1)S(1)}, bf16[128]{0:T(256)(128)(2,1)}, u32[]{:S(2)}) copy-start(bf16[128]{0:T(256)(128)(2,1)} %param.25) | copy-start | bytes 772
  10.6 15.0 %collective-permute-start.1 = (bf16[720,128]{1,0:T(8,128)(2,1)S(1)}, bf16[720,128]{1,0:T(8,128)(2,1)S(1)}, u32[]{:S(2)}, u32[]{:S(2)}) collective-permute-start(bf16[720,128]{1,0:T(8,128)(2,1)S(1)} %constant_dynamic-update-slice_fusion), channel_id=1, source_target_pairs={{0,256},{128,384},{256,0},{384,128},{1,257},{129,385},{257,1},{385... | collective-permute-start | bytes 552968 | tf_op jit(solution)/shard_map/ppermute | solution.py:87
  15.6 10.0 %collective-permute-start.2 = (bf16[720,128]{1,0:T(8,128)(2,1)S(1)}, bf16[720,128]{1,0:T(8,128)(2,1)S(1)}, u32[]{:S(2)}, u32[]{:S(2)}) collective-permute-start(bf16[720,128]{1,0:T(8,128)(2,1)S(1)} %constant_dynamic-update-slice_fusion), channel_id=1, source_target_pairs={{0,128},{128,256},{256,384},{384,0},{1,129},{129,257},{257,385},{3... | collective-permute-start | bytes 552968 | tf_op jit(solution)/shard_map/ppermute | solution.py:87
  18.8 13.2 %collective-permute-start = (bf16[720,128]{1,0:T(8,128)(2,1)S(1)}, bf16[720,128]{1,0:T(8,128)(2,1)S(1)}, u32[]{:S(2)}, u32[]{:S(2)}) collective-permute-start(bf16[720,128]{1,0:T(8,128)(2,1)S(1)} %constant_dynamic-update-slice_fusion), channel_id=1, source_target_pairs={{0,384},{128,0},{256,128},{384,256},{1,385},{129,1},{257,129},{385... | collective-permute-start | bytes 552968 | tf_op jit(solution)/shard_map/ppermute | solution.py:87
  25.4 35.0 %copy-start.23 = (f32[128,64]{0,1:T(8,128)}, f32[128,64]{0,1:T(8,128)S(1)}, u32[]{:S(2)}) copy-start(f32[128,64]{0,1:T(8,128)S(1)} %get-tuple-element.82) | copy-start | bytes 98308
  32.8 27.6 %collective-permute-start.3 = (bf16[4,720,128]{2,1,0:T(8,128)(2,1)S(1)}, bf16[4,720,128]{2,1,0:T(8,128)(2,1)S(1)}, u32[]{:S(2)}, u32[]{:S(2)}) collective-permute-start(bf16[4,720,128]{2,1,0:T(8,128)(2,1)S(1)} %pad_maximum_fusion), channel_id=1, source_target_pairs={{0,16},{16,32},{32,48},{48,64},{64,80},{80,96},{96,112},{112,0},{1... | collective-permute-start | bytes 2211848 | tf_op jit(solution)/shard_map/ppermute | solution.py:87
  37.6 24.8 %collective-permute-start.7 = (bf16[4,720,128]{2,1,0:T(8,128)(2,1)S(1)}, bf16[4,720,128]{2,1,0:T(8,128)(2,1)}, u32[]{:S(2)}, u32[]{:S(2)}) collective-permute-start(bf16[4,720,128]{2,1,0:T(8,128)(2,1)S(1)} %pad_maximum_fusion), channel_id=1, source_target_pairs={{0,112},{16,0},{32,16},{48,32},{64,48},{80,64},{96,80},{112,96},{1... | collective-permute-start | bytes 2211848 | tf_op jit(solution)/shard_map/ppermute | solution.py:87
  46.2 2.2 %copy-start.38 = (f32[1,4096]{1,0:T(1,128)}, f32[1,4096]{1,0:T(1,128)S(1)}, u32[]{:S(2)}) copy-start(f32[1,4096]{1,0:T(1,128)S(1)} %constant_dynamic-update-slice_fusion.39.bias_ref) | copy-start | bytes 49156
  48.4 26.2 %collective-permute-start.13 = (bf16[4,720,128]{2,1,0:T(8,128)(2,1)S(1)}, bf16[4,720,128]{2,1,0:T(8,128)(2,1)S(1)}, u32[]{:S(2)}, u32[]{:S(2)}) collective-permute-start(bf16[4,720,128]{2,1,0:T(8,128)(2,1)S(1)} %pad_maximum_fusion), channel_id=1, source_target_pairs={{0,8},{8,0},{1,9},{9,1},{2,10},{10,2},{3,11},{11,3},{4,12},{12,4},... | collective-permute-start | bytes 2211848 | tf_op jit(solution)/shard_map/ppermute | solution.py:87
  60.4 35.1 %copy-start.3 = (bf16[4,720,128]{2,1,0:T(8,128)(2,1)}, bf16[4,720,128]{2,1,0:T(8,128)(2,1)S(1)}, u32[]{:S(2)}) copy-start(bf16[4,720,128]{2,1,0:T(8,128)(2,1)S(1)} %collective-permute-done.3) | copy-start | bytes 2211844
  60.5 20.2 %collective-permute-start.4 = (bf16[4,720,128]{2,1,0:T(8,128)(2,1)S(1)}, bf16[4,720,128]{2,1,0:T(8,128)(2,1)S(1)}, u32[]{:S(2)}, u32[]{:S(2)}) collective-permute-start(bf16[4,720,128]{2,1,0:T(8,128)(2,1)S(1)} %collective-permute-done.3), channel_id=1, source_target_pairs={{0,16},{16,32},{32,48},{48,64},{64,80},{80,96},{96,112},{112,0},{1... | collective-permute-start | bytes 2211848 | tf_op jit(solution)/shard_map/ppermute | solution.py:87
  63.3 19.4 %collective-permute-start.8 = (bf16[4,720,128]{2,1,0:T(8,128)(2,1)}, bf16[4,720,128]{2,1,0:T(8,128)(2,1)S(1)}, u32[]{:S(2)}, u32[]{:S(2)}) collective-permute-start(bf16[4,720,128]{2,1,0:T(8,128)(2,1)} %collective-permute-done.7), channel_id=1, source_target_pairs={{0,112},{16,0},{32,16},{48,32},{64,48},{80,64},{96,80},{112,96},{1... | collective-permute-start | bytes 2211848 | tf_op jit(solution)/shard_map/ppermute | solution.py:87
  67.9 25.7 %collective-permute-start.14 = (bf16[4,720,128]{2,1,0:T(8,128)(2,1)S(1)}, bf16[4,720,128]{2,1,0:T(8,128)(2,1)S(1)}, u32[]{:S(2)}, u32[]{:S(2)}) collective-permute-start(bf16[4,720,128]{2,1,0:T(8,128)(2,1)S(1)} %collective-permute-done.3), channel_id=1, source_target_pairs={{0,8},{8,0},{1,9},{9,1},{2,10},{10,2},{3,11},{11,3},{4,12},{12,4},... | collective-permute-start | bytes 2211848 | tf_op jit(solution)/shard_map/ppermute | solution.py:87
  71.4 24.1 %collective-permute-start.15 = (bf16[4,720,128]{2,1,0:T(8,128)(2,1)}, bf16[4,720,128]{2,1,0:T(8,128)(2,1)S(1)}, u32[]{:S(2)}, u32[]{:S(2)}) collective-permute-start(bf16[4,720,128]{2,1,0:T(8,128)(2,1)} %collective-permute-done.7), channel_id=1, source_target_pairs={{0,8},{8,0},{1,9},{9,1},{2,10},{10,2},{3,11},{11,3},{4,12},{12,4},... | collective-permute-start | bytes 2211848 | tf_op jit(solution)/shard_map/ppermute | solution.py:87
  74.6 6.1 %copy-start.7 = (bf16[4,720,128]{2,1,0:T(8,128)(2,1)}, bf16[4,720,128]{2,1,0:T(8,128)(2,1)S(1)}, u32[]{:S(2)}) copy-start(bf16[4,720,128]{2,1,0:T(8,128)(2,1)S(1)} %collective-permute-done.13) | copy-start | bytes 2211844
  80.6 31.2 %copy-start.5 = (bf16[4,720,128]{2,1,0:T(8,128)(2,1)}, bf16[4,720,128]{2,1,0:T(8,128)(2,1)S(1)}, u32[]{:S(2)}) copy-start(bf16[4,720,128]{2,1,0:T(8,128)(2,1)S(1)} %collective-permute-done.4) | copy-start | bytes 2211844
  80.7 31.2 %collective-permute-start.5 = (bf16[4,720,128]{2,1,0:T(8,128)(2,1)S(1)}, bf16[4,720,128]{2,1,0:T(8,128)(2,1)S(1)}, u32[]{:S(2)}, u32[]{:S(2)}) collective-permute-start(bf16[4,720,128]{2,1,0:T(8,128)(2,1)S(1)} %collective-permute-done.4), channel_id=1, source_target_pairs={{0,16},{16,32},{32,48},{48,64},{64,80},{80,96},{96,112},{112,0},{1... | collective-permute-start | bytes 2211848 | tf_op jit(solution)/shard_map/ppermute | solution.py:87
  82.7 29.2 %copy-start.9 = (bf16[4,720,128]{2,1,0:T(8,128)(2,1)}, bf16[4,720,128]{2,1,0:T(8,128)(2,1)S(1)}, u32[]{:S(2)}) copy-start(bf16[4,720,128]{2,1,0:T(8,128)(2,1)S(1)} %collective-permute-done.8) | copy-start | bytes 2211844
  82.7 19.0 %collective-permute-start.9 = (bf16[4,720,128]{2,1,0:T(8,128)(2,1)S(1)}, bf16[4,720,128]{2,1,0:T(8,128)(2,1)S(1)}, u32[]{:S(2)}, u32[]{:S(2)}) collective-permute-start(bf16[4,720,128]{2,1,0:T(8,128)(2,1)S(1)} %collective-permute-done.8), channel_id=1, source_target_pairs={{0,112},{16,0},{32,16},{48,32},{64,48},{80,64},{96,80},{112,96},{1... | collective-permute-start | bytes 2211848 | tf_op jit(solution)/shard_map/ppermute | solution.py:87
  88.0 25.9 %collective-permute-start.16 = (bf16[4,720,128]{2,1,0:T(8,128)(2,1)S(1)}, bf16[4,720,128]{2,1,0:T(8,128)(2,1)S(1)}, u32[]{:S(2)}, u32[]{:S(2)}) collective-permute-start(bf16[4,720,128]{2,1,0:T(8,128)(2,1)S(1)} %collective-permute-done.4), channel_id=1, source_target_pairs={{0,8},{8,0},{1,9},{9,1},{2,10},{10,2},{3,11},{11,3},{4,12},{12,4},... | collective-permute-start | bytes 2211848 | tf_op jit(solution)/shard_map/ppermute | solution.py:87
  93.6 2.0 %copy-start.11 = (bf16[4,720,128]{2,1,0:T(8,128)(2,1)}, bf16[4,720,128]{2,1,0:T(8,128)(2,1)S(1)}, u32[]{:S(2)}) copy-start(bf16[4,720,128]{2,1,0:T(8,128)(2,1)S(1)} %collective-permute-done.14) | copy-start | bytes 2211844
  93.6 23.8 %collective-permute-start.17 = (bf16[4,720,128]{2,1,0:T(8,128)(2,1)S(1)}, bf16[4,720,128]{2,1,0:T(8,128)(2,1)S(1)}, u32[]{:S(2)}, u32[]{:S(2)}) collective-permute-start(bf16[4,720,128]{2,1,0:T(8,128)(2,1)S(1)} %collective-permute-done.8), channel_id=1, source_target_pairs={{0,8},{8,0},{1,9},{9,1},{2,10},{10,2},{3,11},{11,3},{4,12},{12,4},... | collective-permute-start | bytes 2211848 | tf_op jit(solution)/shard_map/ppermute | solution.py:87
  101.7 27.7 %collective-permute-start.12 = (bf16[2,720,128]{2,1,0:T(8,128)(2,1)S(1)}, bf16[2,720,128]{2,1,0:T(8,128)(2,1)S(1)}, u32[]{:S(2)}, u32[]{:S(2)}) collective-permute-start(bf16[2,720,128]{2,1,0:T(8,128)(2,1)S(1)} %slice.313), channel_id=1, source_target_pairs={{24,0},{16,8},{40,16},{32,24},{56,32},{48,40},{72,48},{64,56},{88,... | collective-permute-start | bytes 1105928 | tf_op jit(solution)/shard_map/ppermute | solution.py:161
  109.9 19.5 %collective-permute-start.10 = (bf16[2,720,128]{2,1,0:T(8,128)(2,1)S(1)}, bf16[2,720,128]{2,1,0:T(8,128)(2,1)S(1)}, u32[]{:S(2)}, u32[]{:S(2)}) collective-permute-start(bf16[2,720,128]{2,1,0:T(8,128)(2,1)S(1)} %slice.313), channel_id=1, source_target_pairs={{0,112},{16,0},{32,16},{48,32},{64,48},{80,64},{96,80},{112,96},{1... | collective-permute-start | bytes 1105928 | tf_op jit(solution)/shard_map/ppermute | solution.py:87
  111.9 14.0 %collective-permute-start.11 = (bf16[2,720,128]{2,1,0:T(8,128)(2,1)S(1)}, bf16[2,720,128]{2,1,0:T(8,128)(2,1)S(1)}, u32[]{:S(2)}, u32[]{:S(2)}) collective-permute-start(bf16[2,720,128]{2,1,0:T(8,128)(2,1)S(1)} %slice.312), channel_id=1, source_target_pairs={{120,0},{112,8},{8,16},{0,24},{24,32},{16,40},{40,48},{32,56},{56,... | collective-permute-start | bytes 1105928 | tf_op jit(solution)/shard_map/ppermute | solution.py:160
  114.0 15.4 %copy-start.15 = (bf16[4,720,128]{2,1,0:T(8,128)(2,1)}, bf16[4,720,128]{2,1,0:T(8,128)(2,1)S(1)}, u32[]{:S(2)}) copy-start(bf16[4,720,128]{2,1,0:T(8,128)(2,1)S(1)} %collective-permute-done.16) | copy-start | bytes 2211844
  114.0 19.5 %collective-permute-start.6 = (bf16[2,720,128]{2,1,0:T(8,128)(2,1)S(1)}, bf16[2,720,128]{2,1,0:T(8,128)(2,1)S(1)}, u32[]{:S(2)}, u32[]{:S(2)}) collective-permute-start(bf16[2,720,128]{2,1,0:T(8,128)(2,1)S(1)} %slice.312), channel_id=1, source_target_pairs={{0,16},{16,32},{32,48},{48,64},{64,80},{80,96},{96,112},{112,0},{1... | collective-permute-start | bytes 1105928 | tf_op jit(solution)/shard_map/ppermute | solution.py:87
  117.4 11.9 %copy-start.17 = (bf16[4,720,128]{2,1,0:T(8,128)(2,1)}, bf16[4,720,128]{2,1,0:T(8,128)(2,1)S(1)}, u32[]{:S(2)}) copy-start(bf16[4,720,128]{2,1,0:T(8,128)(2,1)S(1)} %collective-permute-done.17) | copy-start | bytes 2211844
  118.8 14.8 %collective-permute-start.18 = (bf16[4,720,128]{2,1,0:T(8,128)(2,1)S(1)}, bf16[4,720,128]{2,1,0:T(8,128)(2,1)S(1)}, u32[]{:S(2)}, u32[]{:S(2)}) collective-permute-start(bf16[4,720,128]{2,1,0:T(8,128)(2,1)S(1)} %collective-permute-done.5), channel_id=1, source_target_pairs={{0,8},{8,0},{1,9},{9,1},{2,10},{10,2},{3,11},{11,3},{4,12},{12,4},... | collective-permute-start | bytes 2211848 | tf_op jit(solution)/shard_map/ppermute | solution.py:87
  125.9 7.7 %collective-permute-start.19 = (bf16[4,720,128]{2,1,0:T(8,128)(2,1)S(1)}, bf16[4,720,128]{2,1,0:T(8,128)(2,1)S(1)}, u32[]{:S(2)}, u32[]{:S(2)}) collective-permute-start(bf16[4,720,128]{2,1,0:T(8,128)(2,1)S(1)} %collective-permute-done.9), channel_id=1, source_target_pairs={{0,8},{8,0},{1,9},{9,1},{2,10},{10,2},{3,11},{11,3},{4,12},{12,4},... | collective-permute-start | bytes 2211848 | tf_op jit(solution)/shard_map/ppermute | solution.py:87
  137.0 2.5 %copy-start = (bf16[2,128,5120]{1,2,0:T(8,128)(2,1)S(1)}, bf16[2,128,5120]{1,2,0:T(8,128)(2,1)}, u32[]{:S(2)}) copy-start(bf16[2,128,5120]{1,2,0:T(8,128)(2,1)} %all-gather.2.cloned.1.call-done) | copy-start | bytes 7864324
  145.6 1.7 copy-start.10
  148.3 1.2 copy-start.12
  150.0 1.2 copy-start.16
  159.8 1.7 copy-start.27
  159.9 3.5 %copy-start.25 = (f32[128,64]{1,0:T(8,128)S(1)}, f32[128,64]{1,0:T(8,128)}, u32[]{:S(2)}) copy-start(f32[128,64]{1,0:T(8,128)} %copy.95) | copy-start | bytes 98308
  159.9 3.5 %copy-start.26 = (f32[128,64]{1,0:T(8,128)S(1)}, f32[128,64]{1,0:T(8,128)}, u32[]{:S(2)}) copy-start(f32[128,64]{1,0:T(8,128)} %copy.96) | copy-start | bytes 98308
  (16 other events, 15.7 us)
Sparse Core Ops, SparseCore 0:
  22.9 86.3 all-gather.1
